TPU v7x, 128 devices: a whole 4x4x4 slice. The times are simulated.
128 devices in a mesh: dp: 4 (over z), seq: 32 (over y, x, core).
Axes of the slice: x: 4, y: 4, z: 4, core: 2. Of those that a mesh axis runs over, the one named last changes fastest.
Arguments:
- queries: bfloat16 [49152, 2048], P(('dp', 'seq')), parts along dimension 0, may hold values from -6 to 6
- keys_in: bfloat16 [49152, 2048], P(('dp', 'seq')), parts along dimension 0, may hold values from -6 to 6
- values: bfloat16 [49152, 2048], P(('dp', 'seq')), parts along dimension 0, may hold values from -6 to 6
- stream: bfloat16 [49152, 2048], P(('dp', 'seq')), parts along dimension 0, may hold values from -6 to 6
- log_decay: float32 [49152, 16], P(('dp', 'seq')), parts along dimension 0, may hold values from -1 to 0
- token_index: int32 [128, 768], P('dp', 'seq'), parts along dimension 0, may hold values from 0 to 12287, as said below
- route_weight: float32 [128, 768], P('dp', 'seq'), parts along dimension 0, may hold values from 0.2 to 1
- moe_gain: float32 [2048], replicated, may hold values from 0.25 to 1.75
- out_weight: bfloat16 [2048, 2048], P('seq'), may hold values from -0.125 to 0.125
- gate_weight: bfloat16 [32, 2048, 1408], P('seq'), may hold values from -0.125 to 0.125
- up_weight: bfloat16 [32, 2048, 1408], P('seq'), may hold values from -0.125 to 0.125
- down_weight: bfloat16 [32, 1408, 2048], P('seq'), may hold values from -0.15625 to 0.15625
Outputs:
- mixed: bfloat16 [49152, 2048], P(('dp', 'seq')), parts along dimension 0
There are 4 independent parts, one for each index of `dp`. A program takes and returns all parts, laid end to end along the dimension named above; an argument that names none is the same for every part. Nothing has to cross between parts.
Inputs may be any that keep to these rules, and one draw needn't show every extreme that they name: `token_index`: for each expert and each j, positions j * 24 to (j + 1) * 24 - 1 of its row hold 24 different tokens of the j-th block of 384 tokens, in ascending order.
All inputs are finite; a program needn't handle non-finite values.
Results may differ from a plain program's by a relative error of at most 0.014.
Values may be sent and summed in bfloat16 or wider, within the bound.
No kernel may reach another device: no remote copies, remote signals or barrier semaphores. Data moves between devices by JAX's collectives and lax.ppermute only.
A program may use at most 192 MiB of HBM per device.

v0:
```python
import jax
import jax.numpy as jnp
from jax import lax
from jax.sharding import PartitionSpec as P


def carried_in(array, axis, combine, identity):
    count, index = (lax.axis_size(axis), lax.axis_index(axis))
    everything = jax.tree.map(
        lambda part, kind: lax.all_gather(part.astype(kind), axis),
        array,
        (jnp.bfloat16, jnp.bfloat16),
    )
    start = jax.tree.map(
        lambda part, zero: jnp.broadcast_to(jnp.asarray(zero, part.dtype), part.shape),
        array,
        identity,
    )

    def turn(k, before):
        reached = k < index
        new = combine(
            before, jax.tree.map(lambda part, own: part[k].astype(own.dtype), everything, array)
        )
        return jax.tree.map(lambda a, b: jnp.where(reached, a, b), new, before)

    return lax.fori_loop(0, count, turn, start)


def shards(
    queries,
    keys_in,
    values,
    stream,
    log_decay,
    token_index,
    route_weight,
    moe_gain,
    out_weight,
    gate_weight,
    up_weight,
    down_weight,
):
    length, model_width = queries.shape
    head_count = log_decay.shape[1]
    head_size = model_width // head_count
    scaling = head_size ** (-0.5)
    device = lax.axis_index("seq")
    query_heads = queries.reshape(length, head_count, head_size)
    key_heads = keys_in.reshape(length, head_count, head_size)
    value_heads = values.reshape(length, head_count, head_size)
    running = jnp.cumsum(log_decay, axis=0)
    ending = running[-1]
    shrink = jnp.exp(ending[None, :] - running)
    key_scaled = (key_heads.astype(jnp.float32) * shrink[:, :, None]).astype(jnp.bfloat16)
    local_state = jnp.einsum(
        "shd,she->hde", key_scaled, value_heads, preferred_element_type=jnp.float32
    )
    zero_state = jnp.zeros_like(local_state)

    def combine(earlier, latter):
        return (earlier[0] * jnp.exp(latter[1])[:, None, None] + latter[0], earlier[1] + latter[1])

    incoming, _ = carried_in(
        (local_state, ending), "seq", combine, (zero_state, jnp.zeros_like(ending))
    )
    scores = (
        jnp.einsum("thd,shd->hts", query_heads, key_heads, preferred_element_type=jnp.float32)
        * scaling
    )
    spacing = running.T[:, :, None] - running.T[:, None, :]
    causal = jnp.arange(length)[:, None] >= jnp.arange(length)[None, :]
    decay_mask = jnp.where(causal[None], jnp.exp(jnp.minimum(spacing, 0.0)), 0.0)
    attend_weights = (scores * decay_mask).astype(jnp.bfloat16)
    within = jnp.einsum(
        "hts,shd->thd", attend_weights, value_heads, preferred_element_type=jnp.float32
    )
    query_scaled = (
        query_heads.astype(jnp.float32) * (jnp.exp(running) * scaling)[:, :, None]
    ).astype(jnp.bfloat16)
    across = jnp.einsum(
        "thd,hde->the",
        query_scaled,
        incoming.astype(jnp.bfloat16),
        preferred_element_type=jnp.float32,
    )
    unnormed = within + across
    spread = jnp.mean(unnormed * unnormed, axis=2, keepdims=True)
    normed = (
        (unnormed * lax.rsqrt(spread + 1e-06)).astype(jnp.bfloat16).reshape(length, model_width)
    )
    attended = jnp.dot(
        normed,
        lax.all_gather(out_weight, "seq", axis=0, tiled=True),
        preferred_element_type=jnp.float32,
    )
    residual = (stream.astype(jnp.float32) + attended).astype(jnp.bfloat16)
    widened = residual.astype(jnp.float32)
    mixed_in = (
        widened * lax.rsqrt(jnp.mean(widened * widened, axis=1, keepdims=True) + 1e-06) * moe_gain
    ).astype(jnp.bfloat16)
    offsets = token_index - device * length
    picked = jnp.take(mixed_in, offsets, axis=0)
    arrived = lax.all_to_all(picked, "seq", split_axis=0, concat_axis=0, tiled=True)
    gating = jnp.einsum("snd,df->snf", arrived, gate_weight[0], preferred_element_type=jnp.float32)
    upward = jnp.einsum("snd,df->snf", arrived, up_weight[0], preferred_element_type=jnp.float32)
    activated = (jax.nn.silu(gating) * upward).astype(jnp.bfloat16)
    produced = jnp.einsum(
        "snf,fd->snd", activated, down_weight[0], preferred_element_type=jnp.float32
    ).astype(jnp.bfloat16)
    returned = lax.all_to_all(produced, "seq", split_axis=0, concat_axis=0, tiled=True)
    scaled = returned.astype(jnp.float32) * route_weight[:, :, None]
    total = widened.at[offsets.reshape(-1)].add(scaled.reshape(-1, model_width))
    return total.astype(jnp.bfloat16)


def solution(mesh):
    placed = (
        P(("dp", "seq"), None),
        P(("dp", "seq"), None),
        P(("dp", "seq"), None),
        P(("dp", "seq"), None),
        P(("dp", "seq"), None),
        P("dp", "seq"),
        P("dp", "seq"),
        P(),
        P("seq", None),
        P("seq", None, None),
        P("seq", None, None),
        P("seq", None, None),
    )
    return jax.shard_map(
        shards, mesh=mesh, in_specs=placed, out_specs=P(("dp", "seq"), None), check_vma=False
    )
```

profile of v0, /device:TPU:0, one launch (start us, length us, event | category | flops | bytes accessed | tf_op | source)
XLA Modules:
  0.0 305.1 jit_solution(13879910465764965656)
XLA Ops:
  6.5 0.9 copy_bitcast_fusion.1
  7.4 0.9 reduce-window.6
  8.3 0.2 slice_reduce_fusion
  8.5 0.2 slice_reduce_fusion.1
  8.7 0.1 subtract_exponential_fusion
  8.8 1.9 copy.70
  10.7 3.5 %fusion.31 = bf16[16,128,128]{2,1,0:T(8,128)(2,1)} fusion(bf16[384,16,128]{0,2,1:T(8,128)(2,1)S(1)} %bitcast.105, f32[384,16]{0,1:T(8,128)S(1)} %get-tuple-element.147, bf16[384,2048]{1,0:T(8,128)(2,1)} %param.16), kind=kOutput, calls=%fused_computation.40 | convolution fusion | flops 203948032 | bytes 3694592 | tf_op jit(solution)/shard_map/shd,she->hde/dot_general | solution.py:56
  14.3 0.7 all-gather.5.cloned.1.call-update
  15.0 0.2 fusion.35
  15.2 22.1 %all-gather.1 = bf16[32,1,16]{2,1,0:T(2,128)(2,1)S(1)} all-gather(bf16[1,1,16]{2,1,0:T(2,128)(2,1)S(1)} %bitcast.111), channel_id=1, replica_groups=mesh['dp'=4,'seq'=32] {'seq'}, dimensions={0}, use_global_device_ids=true | all-gather | bytes 1056 | tf_op jit(solution)/shard_map/all_gather | solution.py:10
  37.4 0.1 reshape.137
  37.5 0.1 copy.65
  37.6 51.6 %all-gather.7.cloned.1.call-done = bf16[512,128,128]{2,1,0:T(8,128)(2,1)} async-done(((bf16[16,128,128]{2,1,0:T(8,128)(2,1)}), bf16[512,128,128]{2,1,0:T(8,128)(2,1)}) %all-gather.7.cloned.1.call-update) | async-done | bytes 16777232 | tf_op jit(solution)/shard_map/all_gather | solution.py:10
  89.2 42.9 %while.14 = (s32[]{:T(128)}, f32[16,128,128]{2,1,0:T(8,128)S(1)}, s32[]{:T(128)}, bf16[32,16]{1,0:T(8,128)(2,1)S(1)}, bf16[32,16,128,128]{3,2,1,0:T(8,128)(2,1)}, /*index=5*/s32[]{:T(128)}, s32[]{:T(128)}) while((s32[]{:T(128)}, f32[16,128,128]{2,1,0:T(8,128)S(1)}, s32[]{:T(128)}, bf16[32,16]{1,0:T(8,128)(2,1)S(1)}, ...), condition=%wide.region_3.4_spmd.clone, body=%wide.region_2.3_spmd.clone.sunk | while | flops 1310740 | bytes 2621705 | solution.py:27
  89.3 1.3 fusion.54
  90.6 1.3 fusion.54
  91.9 1.3 fusion.54
  93.3 1.3 fusion.54
  94.6 1.3 fusion.54
  95.9 1.3 fusion.54
  97.3 1.3 fusion.54
  98.6 1.3 fusion.54
  99.9 1.3 fusion.54
  101.3 1.3 fusion.54
  102.7 1.3 fusion.54
  104.0 1.3 fusion.54
  105.3 1.3 fusion.54
  106.7 1.3 fusion.54
  108.0 1.3 fusion.54
  109.4 1.3 fusion.54
  110.7 1.3 fusion.54
  112.0 1.3 fusion.54
  113.4 1.3 fusion.54
  114.7 1.3 fusion.54
  116.0 1.3 fusion.54
  117.4 1.3 fusion.54
  118.7 1.3 fusion.54
  120.0 1.3 fusion.54
  121.4 1.4 fusion.54
  122.9 1.3 fusion.54
  124.2 1.3 fusion.54
  125.5 1.3 fusion.54
  126.9 1.3 fusion.54
  128.2 1.3 fusion.54
  129.5 1.3 fusion.54
  130.9 1.3 fusion.54
  132.2 2.8 fusion.18
  135.0 7.7 %multiply_reduce_fusion.1 = (f32[384,16]{0,1:T(8,128)S(1)}, f32[384,16,128]{0,2,1:T(8,128)}) fusion(f32[16,128,384]{2,1,0:T(8,128)} %fusion.18, f32[16,384]{1,0:T(8,128)S(1)} %get-tuple-element.145, pred[384,384]{1,0:T(8,128)(4,1)S(1)} %iota_compare_fusion, bf16[384,16,128]{0,2,1:T(8,128)(2,1)} %bitcast.106, bf16[384,2048]{1,0:T(8,128)(2,1)} %param.16, ...), kind=kOutput, calls=%fused_computation.23 | convolution fusion | flops 1224468480 | bytes 11206656 | tf_op jit(solution)/shard_map/hts,shd->thd/dot_general | solution.py:75
  142.7 2.3 multiply_convert_fusion.4
  145.1 6.0 %multiply_reduce_fusion = (f32[384]{0:T(512)S(1)}, f32[384,2048]{1,0:T(8,128)S(1)}) fusion(bf16[384,2048]{0,1:T(8,128)(2,1)S(1)} %bitcast.104, bf16[2048,2048]{1,0:T(8,128)(2,1)} %all-gather.5.cloned.1.call-done, bf16[384,2048]{1,0:T(8,128)(2,1)S(1)} %copy-done.3), kind=kOutput, calls=%fused_computation.20 | convolution fusion | flops 3225943552 | bytes 14681600 | tf_op jit(solution)/shard_map/dot_general | solution.py:92
  151.1 1.7 copy-done.2
  152.8 0.3 multiply_convert_fusion.3
  153.1 4.3 %gather_fusion = bf16[768,2048]{1,0:T(8,128)(2,1)} fusion(bf16[384,2048]{1,0:T(8,128)(2,1)S(1)} %multiply_convert_fusion.3, s32[1024]{0:T(1024)S(1)} %pad_clamp_fusion), kind=kCustom, calls=%fused_computation | custom fusion | bytes 6294528 | tf_op jit(solution)/shard_map/jit(_take)/gather | solution.py:103
  157.4 2.2 broadcast_select_fusion
  159.7 45.0 %all_to_all.10 = bf16[32,24,2048]{2,1,0:T(8,128)(2,1)S(1)} all-to-all(bf16[32,24,2048]{2,1,0:T(8,128)(2,1)S(1)} %broadcast_select_fusion), channel_id=1, replica_groups=mesh['dp'=4,'seq'=32] {'seq'}, dimensions={0} | all-to-all | bytes 6291456 | tf_op jit(solution)/shard_map/all_to_all | solution.py:104
  204.7 7.6 %fusion.3 = f32[32,24,1408]{2,1,0:T(8,128)S(1)} fusion(bf16[32,24,2048]{2,1,0:T(8,128)(2,1)S(1)} %all_to_all.10, bf16[1,2048,1408]{2,1,0:T(8,128)(2,1)} %param.24), kind=kOutput, calls=%fused_computation.9 | convolution fusion | flops 4429185024 | bytes 13238272 | tf_op jit(solution)/shard_map/snd,df->snf/dot_general | solution.py:106
  212.4 5.8 %multiply_convert_fusion.2 = bf16[32,24,1408]{2,1,0:T(8,128)(2,1)S(1)} fusion(f32[32,24,1408]{2,1,0:T(8,128)S(1)} %fusion.3, bf16[32,24,2048]{2,1,0:T(8,128)(2,1)S(1)} %all_to_all.10, bf16[1,2048,1408]{2,1,0:T(8,128)(2,1)S(1)} %bitcast.113), kind=kOutput, calls=%fused_computation.15 | convolution fusion | flops 4435673088 | bytes 15400960 | tf_op jit(solution)/shard_map/snd,df->snf/dot_general | solution.py:105
  218.2 6.5 %fusion.11 = bf16[32,24,2048]{2,1,0:T(8,128)(2,1)} fusion(bf16[32,24,1408]{2,1,0:T(8,128)(2,1)S(1)} %multiply_convert_fusion.2, bf16[1,1408,2048]{2,1,0:T(8,128)(2,1)S(1)} %bitcast.115), kind=kOutput, calls=%fused_computation.16 | convolution fusion | flops 4430757888 | bytes 11075584 | tf_op jit(solution)/shard_map/snf,fd->snd/dot_general | solution.py:108
  224.7 5.2 %all-to-all-start.1 = ((bf16[32,24,2048]{2,1,0:T(8,128)(2,1)}), bf16[32,24,2048]{2,1,0:T(8,128)(2,1)}, u32[]{:S(2)}, u32[]{:S(2)}) async-start(bf16[32,24,2048]{2,1,0:T(8,128)(2,1)} %fusion.11), calls=%async_computation.1 | async-start | bytes 6291456 | tf_op jit(solution)/shard_map/all_to_all | solution.py:111
  230.0 0.1 reshape.132
  230.1 41.5 %all-to-all-done.1 = bf16[32,24,2048]{2,1,0:T(8,128)(2,1)} async-done(((bf16[32,24,2048]{2,1,0:T(8,128)(2,1)}), bf16[32,24,2048]{2,1,0:T(8,128)(2,1)}, u32[]{:S(2)}, u32[]{:S(2)}) %all-to-all-start.1) | async-done | bytes 3145760 | tf_op jit(solution)/shard_map/all_to_all | solution.py:111
  271.7 5.0 %convert_multiply_fusion = f32[32,24,2048]{2,1,0:T(8,128)} fusion(bf16[32,24,2048]{2,1,0:T(8,128)(2,1)} %all-to-all-done.1, f32[32,24]{1,0:T(8,128)S(1)} %copy.67), kind=kLoop, calls=%fused_computation.6 | loop fusion | flops 3145728 | bytes 9440256 | tf_op jit(solution)/shard_map/mul | solution.py:112
  276.7 18.3 %scatter_fusion = f32[384,2048]{1,0:T(8,128)} fusion(f32[384,2048]{1,0:T(8,128)} %copy-done.2, s32[768]{0:T(1024)S(1)} %fusion.36, f32[768,2048]{1,0:T(8,128)} %bitcast.102), kind=kCustom, calls=%fused_computation.1 | custom fusion | flops 1572864 | bytes 18877440 | tf_op jit(solution)/shard_map/scatter-add | solution.py:113
  295.0 3.3 %convert_element_type.90 = bf16[384,2048]{1,0:T(8,128)(2,1)} convert(f32[384,2048]{1,0:T(8,128)} %scatter_fusion) | non-fusion elementwise | flops 786432 | bytes 4718592 | tf_op jit(solution)/shard_map/convert_element_type | solution.py:114
  (75 shorter events, 1.0 us)
Async XLA Ops:
  6.5 125.6 %copy-start = (bf16[384,2048]{1,0:T(8,128)(2,1)S(1)}, bf16[384,2048]{1,0:T(8,128)(2,1)}, u32[]{:S(2)}) copy-start(bf16[384,2048]{1,0:T(8,128)(2,1)} %param.14) | copy-start | bytes 4718596
  6.5 82.7 %all-gather.7.cloned.1.call-start = ((), (), s32[]{:S(2)}) async-start(), calls=%async_computation.3 | async-start | bytes 17301504 | tf_op jit(solution)/shard_map/all_gather | solution.py:10
  10.7 4.3 %copy-start.4 = (bf16[384,2048]{0,1:T(8,128)(2,1)}, bf16[384,2048]{0,1:T(8,128)(2,1)S(1)}, u32[]{:S(2)}) copy-start(bf16[384,2048]{0,1:T(8,128)(2,1)S(1)} %copy.70) | copy-start | bytes 4718596
  10.7 26.6 %copy-start.5 = (s32[32,24]{0,1:T(8,128)S(1)}, s32[32,24]{0,1:T(8,128)}, u32[]{:S(2)}) copy-start(s32[32,24]{0,1:T(8,128)} %param.19) | copy-start | bytes 9220
  14.2 130.9 %all-gather.5.cloned.1.call-start = ((), (), s32[]{:S(2)}) async-start(), calls=%async_computation.2 | async-start | bytes 8650752 | tf_op jit(solution)/shard_map/all_gather | solution.py:94
  142.7 2.4 copy-start.3
  145.1 7.7 %copy-start.7 = (f32[2048]{0:T(1024)S(1)}, f32[2048]{0:T(1024)}, u32[]{:S(2)}) copy-start(f32[2048]{0:T(1024)} %param.21) | copy-start | bytes 24580
  151.1 1.7 copy-start.2
  159.6 52.7 %slice-start = ((s8[5767168]{0:T(1024)(128)(4,1)}), s8[4194304]{0:T(1024)(128)(4,1)S(1)}, s32[]{:S(2)}) async-start(s8[5767168]{0:T(1024)(128)(4,1)} %bitcast.112), calls=%async_computation.4 | async-start | bytes 8388608
  204.7 7.7 %slice-start.1 = ((s8[5767168]{0:T(1024)(128)(4,1)}), s8[1572864]{0:T(1024)(128)(4,1)S(1)}, s32[]{:S(2)}) async-start(s8[5767168]{0:T(1024)(128)(4,1)} %bitcast.112), calls=%async_computation.5 | async-start | bytes 3145728
  204.7 13.5 %slice-start.2 = ((s8[5767168]{0:T(1024)(128)(4,1)}), s8[4194304]{0:T(1024)(128)(4,1)S(1)}, s32[]{:S(2)}) async-start(s8[5767168]{0:T(1024)(128)(4,1)} %bitcast.114), calls=%async_computation.6 | async-start | bytes 8388608
  212.4 5.8 %slice-start.3 = ((s8[5767168]{0:T(1024)(128)(4,1)}), s8[1572864]{0:T(1024)(128)(4,1)S(1)}, s32[]{:S(2)}) async-start(s8[5767168]{0:T(1024)(128)(4,1)} %bitcast.114), calls=%async_computation.7 | async-start | bytes 3145728
  224.7 5.3 %copy-start.6 = (f32[32,24]{0,1:T(8,128)S(1)}, f32[32,24]{0,1:T(8,128)}, u32[]{:S(2)}) copy-start(f32[32,24]{0,1:T(8,128)} %param.20) | copy-start | bytes 9220
  224.7 47.0 %all-to-all-start.1 = ((bf16[32,24,2048]{2,1,0:T(8,128)(2,1)}), bf16[32,24,2048]{2,1,0:T(8,128)(2,1)}, u32[]{:S(2)}, u32[]{:S(2)}) async-start(bf16[32,24,2048]{2,1,0:T(8,128)(2,1)} %fusion.11), calls=%async_computation.1 | async-start | bytes 6291456 | tf_op jit(solution)/shard_map/all_to_all | solution.py:111
  276.7 21.6 %copy-start.1 = (bf16[384,2048]{1,0:T(8,128)(2,1)S(1)}, bf16[384,2048]{1,0:T(8,128)(2,1)}, u32[]{:S(2)}) copy-start(bf16[384,2048]{1,0:T(8,128)(2,1)} %param.14) | copy-start | bytes 4718596
Sparse Core Ops, SparseCore 0:
  14.3 74.8 all-gather.6
  91.5 52.1 all-gather.4
where the time goes:
time: 307 us; the launch traced here: 305 us
  waiting for transfers between devices  93.9 us (31%)
  other arithmetic  74.6 us (24%)
  blocking collectives  67.1 us (22%)
  matrix products  39.9 us (13%)
  between operations  13.7 us (4%)
  local copies, waits for them, and re-layouts  9.74 us (3%)
  starting transfers between devices  5.22 us (2%)
    all_gather x1, waiting for transfers between devices, carried_in(): lax.all_gather(part.astype(kind), axis)  51.6 us
    all_to_all x1, blocking collectives, shards(): lax.all_to_all(picked, 'seq', split_axis=0, concat_axis=0, tiled=True)  45 us
    select_n x32, other arithmetic, turn(): return jax.tree.map(lambda a, b: jnp.where(reached, a, b), new, before)  41.6 us
    all_to_all x1, waiting for transfers between devices, shards(): lax.all_to_all(produced, 'seq', split_axis=0, concat_axis=0, tiled=True)  41.5 us
    all_gather x1, blocking collectives, carried_in(): lax.all_gather(part.astype(kind), axis)  22.1 us
    scatter-add x1, other arithmetic, shards(): total = widened.at[offsets.reshape(-1)].add(scaled.reshape(-1, model_width))  18.3 us
    dot_general x1, matrix products, shards(): jnp.einsum('hts,shd->thd', attend_weights, value_heads, preferred_element...  7.7 us
    dot_general x1, matrix products, shards(): jnp.einsum('snd,df->snf', arrived, up_weight[0], preferred_element_type=j...  7.64 us
  transfers between devices with their start and end apart: 3, of which 2 were waited for; matrix products, arithmetic and copies ran while one was open for 18% of the time, Pallas kernels for 0%

commit v1 on v0

--- a/solution.py
+++ b/solution.py
@@ -4,27 +4,31 @@
 from jax.sharding import PartitionSpec as P
 
 
-def carried_in(array, axis, combine, identity):
-    count, index = (lax.axis_size(axis), lax.axis_index(axis))
-    everything = jax.tree.map(
-        lambda part, kind: lax.all_gather(part.astype(kind), axis),
-        array,
-        (jnp.bfloat16, jnp.bfloat16),
-    )
-    start = jax.tree.map(
-        lambda part, zero: jnp.broadcast_to(jnp.asarray(zero, part.dtype), part.shape),
-        array,
-        identity,
-    )
+def carried_in(state, ending, axis):
+    count = lax.axis_size(axis)
 
-    def turn(k, before):
-        reached = k < index
-        new = combine(
-            before, jax.tree.map(lambda part, own: part[k].astype(own.dtype), everything, array)
-        )
-        return jax.tree.map(lambda a, b: jnp.where(reached, a, b), new, before)
+    def shifted(part, distance):
+        pairs = [(j, j + distance) for j in range(count - distance)]
+        return lax.ppermute(part, axis, pairs)
 
-    return lax.fori_loop(0, count, turn, start)
+    def combine(earlier, latter):
+        return (earlier[0] * jnp.exp(latter[1])[:, None, None] + latter[0], earlier[1] + latter[1])
+
+    def fetch(pair, distance):
+        low, wide = pair
+        return (shifted(low.astype(jnp.bfloat16), distance).astype(jnp.float32), shifted(wide, distance))
+
+    covered = (state, ending)
+    reach = 1
+    while 2 * reach < count:
+        covered = combine(fetch(covered, reach), covered)
+        reach *= 2
+    if count == 1:
+        return jnp.zeros_like(state)
+    near = fetch(covered, 1)
+    if reach + 1 < count:
+        near = combine(fetch(covered, reach + 1), near)
+    return near[0]
 
 
 def shards(
@@ -56,14 +60,7 @@
     local_state = jnp.einsum(
         "shd,she->hde", key_scaled, value_heads, preferred_element_type=jnp.float32
     )
-    zero_state = jnp.zeros_like(local_state)
-
-    def combine(earlier, latter):
-        return (earlier[0] * jnp.exp(latter[1])[:, None, None] + latter[0], earlier[1] + latter[1])
-
-    incoming, _ = carried_in(
-        (local_state, ending), "seq", combine, (zero_state, jnp.zeros_like(ending))
-    )
+    incoming = carried_in(local_state, ending, "seq")
     scores = (
         jnp.einsum("thd,shd->hts", query_heads, key_heads, preferred_element_type=jnp.float32)
         * scaling

time: 307 us -> 281 us (0.915)
  starting transfers between devices: 5.22 us -> 50 us
  other arithmetic: 74.6 us -> 34.4 us
  blocking collectives: 67.1 us -> 49.1 us
  waiting for transfers between devices: 93.9 us -> 83.4 us
    all_gather x1 -> x0, waiting for transfers between devices: 51.6 us -> none  [carried_in(): lax.all_gather(part.astype(kind), axis)]
    ppermute x0 -> x11, starting transfers between devices: none -> 44.8 us  [shifted(): return lax.ppermute(part, axis, pairs)]
    select_n x32 -> x0, other arithmetic: 41.6 us -> none  [turn(): return jax.tree.map(lambda a, b: jnp.where(reached, a, b), new, before)]
    ppermute x0 -> x11, waiting for transfers between devices: none -> 41.1 us  [shifted(): return lax.ppermute(part, axis, pairs)]
    all_gather x1 -> x0, blocking collectives: 22.1 us -> none  [carried_in(): lax.all_gather(part.astype(kind), axis)]
    all_to_all x1, blocking collectives: 45 us -> 49.1 us  [shards(): lax.all_to_all(picked, 'seq', split_axis=0, concat_axis=0, tiled=True)]
    convert_element_type x0 -> x4, other arithmetic: none -> 3.74 us  [fetch(): low.astype(jnp.bfloat16)]
  transfers between devices with their start and end apart: 3 -> 13, of which waited for: 2 -> 8; matrix products, arithmetic and copies ran while one was open for 18% -> 8% of each run, Pallas kernels for 0% -> 0%
where the time goes in v1:
time: 281 us; the launch traced here: 280 us
  waiting for transfers between devices  83.4 us (30%)
  starting transfers between devices  50 us (18%)
  blocking collectives  49.1 us (17%)
  matrix products  38.9 us (14%)
  other arithmetic  34.4 us (12%)
  between operations  13.8 us (5%)
  local copies, waits for them, and re-layouts  10.4 us (4%)
    all_to_all x1, blocking collectives, shards(): lax.all_to_all(picked, 'seq', split_axis=0, concat_axis=0, tiled=True)  49.1 us
    ppermute x11, starting transfers between devices, shifted(): return lax.ppermute(part, axis, pairs)  44.8 us
    all_to_all x1, waiting for transfers between devices, shards(): lax.all_to_all(produced, 'seq', split_axis=0, concat_axis=0, tiled=True)  41.5 us
    ppermute x11, waiting for transfers between devices, shifted(): return lax.ppermute(part, axis, pairs)  41.1 us
    scatter-add x1, other arithmetic, shards(): total = widened.at[offsets.reshape(-1)].add(scaled.reshape(-1, model_width))  18.3 us
    dot_general x1, matrix products, shards(): jnp.einsum('snd,df->snf', arrived, up_weight[0], preferred_element_type=j...  7.65 us
    dot_general x1, matrix products, shards(): jnp.einsum('hts,shd->thd', attend_weights, value_heads, preferred_element...  7.09 us
    dot_general x1, matrix products, shards(): jnp.einsum('snf,fd->snd', activated, down_weight[0], preferred_element_ty...  6.51 us
  transfers between devices with their start and end apart: 13, of which 8 were waited for; matrix products, arithmetic and copies ran while one was open for 8% of the time, Pallas kernels for 0%

profile of v1, /device:TPU:0, one launch (start us, length us, event | category | flops | bytes accessed | tf_op | source)
XLA Modules:
  0.0 280.0 jit_solution(10949357055601075202)
XLA Ops:
  6.5 0.7 all-gather.2.cloned.1.call-update
  7.3 0.7 copy_bitcast_fusion.1
  8.0 0.9 reduce-window.6
  8.9 0.2 slice_reduce_fusion
  9.0 1.9 copy.50
  10.9 0.0 copy-start.3
  10.9 0.1 fusion.35
  11.0 0.2 slice_reduce_fusion.1
  11.2 0.1 subtract_exponential_fusion
  11.3 2.2 fusion.40
  13.5 1.3 collective-permute-start
  14.9 4.2 %collective-permute-start.2 = (f32[16]{0:T(128)S(1)}, f32[16]{0:T(128)S(1)}, u32[]{:S(2)}, u32[]{:S(2)}) collective-permute-start(f32[16]{0:T(128)S(1)} %slice_reduce_fusion.1), channel_id=1, source_target_pairs={{0,1},{1,2},{2,3},{3,4},{4,5},{5,6},{6,7},{7,8},{8,9},{9,10},{10,1... | collective-permute-start | bytes 200 | tf_op jit(solution)/shard_map/ppermute | solution.py:12
  19.1 0.8 collective-permute-done.2
  19.9 0.0 collective-permute-done
  19.9 0.2 fusion.29
  20.1 8.8 %collective-permute-start.1 = (bf16[16,128,128]{2,1,0:T(8,128)(2,1)S(1)}, bf16[16,128,128]{2,1,0:T(8,128)(2,1)S(1)}, u32[]{:S(2)}, u32[]{:S(2)}) collective-permute-start(bf16[16,128,128]{2,1,0:T(8,128)(2,1)S(1)} %fusion.29), channel_id=1, source_target_pairs={{0,2},{1,3},{2,4},{3,5},{4,6},{5,7},{6,8},{7,9},{8,10},{9,11},{10,... | collective-permute-start | bytes 1572872 | tf_op jit(solution)/shard_map/ppermute | solution.py:12
  29.0 12.5 %collective-permute-done.1 = bf16[16,128,128]{2,1,0:T(8,128)(2,1)S(1)} collective-permute-done((bf16[16,128,128]{2,1,0:T(8,128)(2,1)S(1)}, bf16[16,128,128]{2,1,0:T(8,128)(2,1)S(1)}, u32[]{:S(2)}, u32[]{:S(2)}) %collective-permute-start.1) | collective-permute-done | bytes 524320 | tf_op jit(solution)/shard_map/ppermute | solution.py:12
  41.5 0.4 fusion.38
  41.9 4.9 %collective-permute-start.3 = (bf16[16,128,128]{2,1,0:T(8,128)(2,1)S(1)}, bf16[16,128,128]{2,1,0:T(8,128)(2,1)S(1)}, u32[]{:S(2)}, u32[]{:S(2)}) collective-permute-start(bf16[16,128,128]{2,1,0:T(8,128)(2,1)S(1)} %get-tuple-element.11), channel_id=1, source_target_pairs={{0,4},{1,5},{2,6},{3,7},{4,8},{5,9},{6,10},{7,11},{8,12},{9,13},{1... | collective-permute-start | bytes 1572872 | tf_op jit(solution)/shard_map/ppermute | solution.py:12
  46.8 3.2 %collective-permute-start.4 = (f32[16]{0:T(128)S(1)}, f32[16]{0:T(128)S(1)}, u32[]{:S(2)}, u32[]{:S(2)}) collective-permute-start(f32[16]{0:T(128)S(1)} %get-tuple-element.14), channel_id=1, source_target_pairs={{0,2},{1,3},{2,4},{3,5},{4,6},{5,7},{6,8},{7,9},{8,10},{9,11},{10,... | collective-permute-start | bytes 200 | tf_op jit(solution)/shard_map/ppermute | solution.py:12
  50.1 15.5 %collective-permute-done.4 = f32[16]{0:T(128)S(1)} collective-permute-done((f32[16]{0:T(128)S(1)}, f32[16]{0:T(128)S(1)}, u32[]{:S(2)}, u32[]{:S(2)}) %collective-permute-start.4) | collective-permute-done | bytes 96 | tf_op jit(solution)/shard_map/ppermute | solution.py:12
  65.6 0.0 collective-permute-done.3
  65.6 1.0 fusion.30
  66.6 8.8 %collective-permute-start.5 = (bf16[16,128,128]{2,1,0:T(8,128)(2,1)}, bf16[16,128,128]{2,1,0:T(8,128)(2,1)}, u32[]{:S(2)}, u32[]{:S(2)}) collective-permute-start(bf16[16,128,128]{2,1,0:T(8,128)(2,1)} %fusion.30), channel_id=1, source_target_pairs={{0,8},{1,9},{2,10},{3,11},{4,12},{5,13},{6,14},{7,15},{8,16},{9,17... | collective-permute-start | bytes 1572872 | tf_op jit(solution)/shard_map/ppermute | solution.py:12
  75.4 7.1 %fusion.6 = f32[16,384,128]{1,2,0:T(8,128)} fusion(f32[16,384]{1,0:T(8,128)S(1)} %get-tuple-element.18, pred[384,384]{1,0:T(8,128)(4,1)S(1)} %iota_compare_fusion, bf16[384,16,128]{0,2,1:T(8,128)(2,1)} %bitcast.89, bf16[384,2048]{1,0:T(8,128)(2,1)} %param.14, bf16[384,2048]{1,0:T(8,128)(2,1)S(1)} %copy-done), kind=kOutput, calls=%fused_computation.10 | convolution fusion | flops 1222115328 | bytes 8036352 | tf_op jit(solution)/shard_map/hts,shd->thd/dot_general | solution.py:72
  82.5 1.3 collective-permute-start.6
  83.8 1.3 collective-permute-done.6
  85.1 2.9 %collective-permute-done.5 = bf16[16,128,128]{2,1,0:T(8,128)(2,1)} collective-permute-done((bf16[16,128,128]{2,1,0:T(8,128)(2,1)}, bf16[16,128,128]{2,1,0:T(8,128)(2,1)}, u32[]{:S(2)}, u32[]{:S(2)}) %collective-permute-start.5) | collective-permute-done | bytes 524320 | tf_op jit(solution)/shard_map/ppermute | solution.py:12
  88.0 2.2 add_convert_fusion.2
  90.2 1.3 collective-permute-start.10
  91.5 6.9 %collective-permute-start.7 = (bf16[16,128,128]{2,1,0:T(8,128)(2,1)}, bf16[16,128,128]{2,1,0:T(8,128)(2,1)S(1)}, u32[]{:S(2)}, u32[]{:S(2)}) collective-permute-start(bf16[16,128,128]{2,1,0:T(8,128)(2,1)} %add_convert_fusion.2), channel_id=1, source_target_pairs={{0,17},{1,18},{2,19},{3,20},{4,21},{5,22},{6,23},{7,24},{8,25},{9,... | collective-permute-start | bytes 1572872 | tf_op jit(solution)/shard_map/ppermute | solution.py:12
  98.4 0.1 copy.47
  98.5 0.1 reshape.133
  98.5 2.7 collective-permute-start.8
  101.3 7.4 %collective-permute-done.8 = f32[16]{0:T(128)S(1)} collective-permute-done((f32[16]{0:T(128)S(1)}, f32[16]{0:T(128)S(1)}, u32[]{:S(2)}, u32[]{:S(2)}) %collective-permute-start.8) | collective-permute-done | bytes 96 | tf_op jit(solution)/shard_map/ppermute | solution.py:12
  108.7 1.3 collective-permute-start.9
  110.0 0.1 copy.46
  110.1 0.7 collective-permute-done.9
  110.8 0.0 collective-permute-done.10
  110.8 0.0 collective-permute-done.7
  110.8 3.7 %multiply_reduce_fusion.1 = (f32[384,16]{0,1:T(8,128)S(1)}, f32[384,16,128]{0,2,1:T(8,128)S(1)}) fusion(f32[384,16]{0,1:T(8,128)S(1)} %get-tuple-element.16, bf16[16,128,128]{2,1,0:T(8,128)(2,1)S(1)} %collective-permute-done.10, bf16[16,128,128]{2,1,0:T(8,128)(2,1)S(1)} %collective-permute-done.7, f32[16]{0:T(128)S(1)} %exp.38, f32[16,384,128]{1,2,0:T(8,128)} %fusion.6, ...), kind=kOutput, calls=%fused_computation.20 | convolution fusion | flops 207349760 | bytes 8962112 | tf_op jit(solution)/shard_map/thd,hde->the/dot_general | solution.py:78
  114.5 0.0 copy-start.4
  114.5 0.3 multiply_convert_fusion.4
  114.9 0.0 all-gather.2.cloned.1.call-done
  114.9 1.0 copy-done.4
  115.9 6.0 %multiply_reduce_fusion = (f32[384]{0:T(512)S(1)}, f32[384,2048]{1,0:T(8,128)S(1)}) fusion(bf16[384,2048]{0,1:T(8,128)(2,1)S(1)} %bitcast.87, bf16[2048,2048]{1,0:T(8,128)(2,1)} %all-gather.2.cloned.1.call-done, bf16[384,2048]{1,0:T(8,128)(2,1)S(1)} %copy-done.4), kind=kOutput, calls=%fused_computation.17 | convolution fusion | flops 3225943552 | bytes 14681600 | tf_op jit(solution)/shard_map/dot_general | solution.py:89
  121.9 1.7 copy-done.2
  123.6 0.3 multiply_convert_fusion.3
  123.9 4.2 %gather_fusion = bf16[768,2048]{1,0:T(8,128)(2,1)} fusion(bf16[384,2048]{1,0:T(8,128)(2,1)S(1)} %multiply_convert_fusion.3, s32[1024]{0:T(1024)S(1)} %pad_clamp_fusion), kind=kCustom, calls=%fused_computation | custom fusion | bytes 6294528 | tf_op jit(solution)/shard_map/jit(_take)/gather | solution.py:100
  128.2 2.2 broadcast_select_fusion
  130.4 0.0 slice-start
  130.4 49.1 %all_to_all.10 = bf16[32,24,2048]{2,1,0:T(8,128)(2,1)S(1)} all-to-all(bf16[32,24,2048]{2,1,0:T(8,128)(2,1)S(1)} %broadcast_select_fusion), channel_id=1, replica_groups=mesh['dp'=4,'seq'=32] {'seq'}, dimensions={0} | all-to-all | bytes 6291456 | tf_op jit(solution)/shard_map/all_to_all | solution.py:101
  179.6 7.6 %fusion.2 = f32[32,24,1408]{2,1,0:T(8,128)S(1)} fusion(bf16[32,24,2048]{2,1,0:T(8,128)(2,1)S(1)} %all_to_all.10, bf16[1,2048,1408]{2,1,0:T(8,128)(2,1)} %param.22), kind=kOutput, calls=%fused_computation.6 | convolution fusion | flops 4429185024 | bytes 13238272 | tf_op jit(solution)/shard_map/snd,df->snf/dot_general | solution.py:103
  187.2 0.0 slice-start.3
  187.2 5.8 %multiply_convert_fusion.2 = bf16[32,24,1408]{2,1,0:T(8,128)(2,1)S(1)} fusion(f32[32,24,1408]{2,1,0:T(8,128)S(1)} %fusion.2, bf16[32,24,2048]{2,1,0:T(8,128)(2,1)S(1)} %all_to_all.10, bf16[1,2048,1408]{2,1,0:T(8,128)(2,1)S(1)} %bitcast.93), kind=kOutput, calls=%fused_computation.12 | convolution fusion | flops 4435673088 | bytes 15400960 | tf_op jit(solution)/shard_map/snd,df->snf/dot_general | solution.py:102
  193.0 6.5 %fusion.10 = bf16[32,24,2048]{2,1,0:T(8,128)(2,1)} fusion(bf16[32,24,1408]{2,1,0:T(8,128)(2,1)S(1)} %multiply_convert_fusion.2, bf16[1,1408,2048]{2,1,0:T(8,128)(2,1)S(1)} %bitcast.95), kind=kOutput, calls=%fused_computation.13 | convolution fusion | flops 4430757888 | bytes 11075584 | tf_op jit(solution)/shard_map/snf,fd->snd/dot_general | solution.py:105
  199.6 5.2 %all-to-all-start.1 = ((bf16[32,24,2048]{2,1,0:T(8,128)(2,1)}), bf16[32,24,2048]{2,1,0:T(8,128)(2,1)}, u32[]{:S(2)}, u32[]{:S(2)}) async-start(bf16[32,24,2048]{2,1,0:T(8,128)(2,1)} %fusion.10), calls=%async_computation.1 | async-start | bytes 6291456 | tf_op jit(solution)/shard_map/all_to_all | solution.py:108
  204.7 0.1 copy.45
  204.8 0.1 copy.48
  204.9 0.1 reshape.129
  205.0 41.5 %all-to-all-done.1 = bf16[32,24,2048]{2,1,0:T(8,128)(2,1)} async-done(((bf16[32,24,2048]{2,1,0:T(8,128)(2,1)}), bf16[32,24,2048]{2,1,0:T(8,128)(2,1)}, u32[]{:S(2)}, u32[]{:S(2)}) %all-to-all-start.1) | async-done | bytes 3145760 | tf_op jit(solution)/shard_map/all_to_all | solution.py:108
  246.5 5.0 %convert_multiply_fusion = f32[32,24,2048]{2,1,0:T(8,128)} fusion(bf16[32,24,2048]{2,1,0:T(8,128)(2,1)} %all-to-all-done.1, f32[32,24]{1,0:T(8,128)S(1)} %copy.48), kind=kLoop, calls=%fused_computation.3 | loop fusion | flops 3145728 | bytes 9440256 | tf_op jit(solution)/shard_map/mul | solution.py:109
  251.5 18.3 %scatter_fusion = f32[384,2048]{1,0:T(8,128)} fusion(f32[384,2048]{1,0:T(8,128)} %copy-done.2, s32[768]{0:T(1024)S(1)} %fusion.32, f32[768,2048]{1,0:T(8,128)} %bitcast.85), kind=kCustom, calls=%fused_computation.1 | custom fusion | flops 1572864 | bytes 18877440 | tf_op jit(solution)/shard_map/scatter-add | solution.py:110
  269.9 3.3 %convert_element_type.104 = bf16[384,2048]{1,0:T(8,128)(2,1)} convert(f32[384,2048]{1,0:T(8,128)} %scatter_fusion) | non-fusion elementwise | flops 786432 | bytes 4718592 | tf_op jit(solution)/shard_map/convert_element_type | solution.py:111
  (34 shorter events, 0.2 us)
Async XLA Ops:
  6.5 68.9 %copy-start = (bf16[384,2048]{1,0:T(8,128)(2,1)S(1)}, bf16[384,2048]{1,0:T(8,128)(2,1)}, u32[]{:S(2)}) copy-start(bf16[384,2048]{1,0:T(8,128)(2,1)} %param.12) | copy-start | bytes 4718596
  6.5 108.3 %all-gather.2.cloned.1.call-start = ((), (), s32[]{:S(2)}) async-start(), calls=%async_computation.2 | async-start | bytes 8650752 | tf_op jit(solution)/shard_map/all_gather | solution.py:91
  10.9 9.2 %copy-start.3 = (bf16[384,2048]{0,1:T(8,128)(2,1)}, bf16[384,2048]{0,1:T(8,128)(2,1)S(1)}, u32[]{:S(2)}) copy-start(bf16[384,2048]{0,1:T(8,128)(2,1)S(1)} %copy.50) | copy-start | bytes 4718596
  13.5 6.4 %collective-permute-start = (bf16[16,128,128]{2,1,0:T(8,128)(2,1)S(1)}, bf16[16,128,128]{2,1,0:T(8,128)(2,1)S(1)}, u32[]{:S(2)}, u32[]{:S(2)}) collective-permute-start(bf16[16,128,128]{2,1,0:T(8,128)(2,1)S(1)} %get-tuple-element.20), channel_id=1, source_target_pairs={{0,1},{1,2},{2,3},{3,4},{4,5},{5,6},{6,7},{7,8},{8,9},{9,10},{10,1... | collective-permute-start | bytes 1572872 | tf_op jit(solution)/shard_map/ppermute | solution.py:12
  14.9 5.0 %collective-permute-start.2 = (f32[16]{0:T(128)S(1)}, f32[16]{0:T(128)S(1)}, u32[]{:S(2)}, u32[]{:S(2)}) collective-permute-start(f32[16]{0:T(128)S(1)} %slice_reduce_fusion.1), channel_id=1, source_target_pairs={{0,1},{1,2},{2,3},{3,4},{4,5},{5,6},{6,7},{7,8},{8,9},{9,10},{10,1... | collective-permute-start | bytes 200 | tf_op jit(solution)/shard_map/ppermute | solution.py:12
  20.1 21.4 %collective-permute-start.1 = (bf16[16,128,128]{2,1,0:T(8,128)(2,1)S(1)}, bf16[16,128,128]{2,1,0:T(8,128)(2,1)S(1)}, u32[]{:S(2)}, u32[]{:S(2)}) collective-permute-start(bf16[16,128,128]{2,1,0:T(8,128)(2,1)S(1)} %fusion.29), channel_id=1, source_target_pairs={{0,2},{1,3},{2,4},{3,5},{4,6},{5,7},{6,8},{7,9},{8,10},{9,11},{10,... | collective-permute-start | bytes 1572872 | tf_op jit(solution)/shard_map/ppermute | solution.py:12
  41.9 23.8 %collective-permute-start.3 = (bf16[16,128,128]{2,1,0:T(8,128)(2,1)S(1)}, bf16[16,128,128]{2,1,0:T(8,128)(2,1)S(1)}, u32[]{:S(2)}, u32[]{:S(2)}) collective-permute-start(bf16[16,128,128]{2,1,0:T(8,128)(2,1)S(1)} %get-tuple-element.11), channel_id=1, source_target_pairs={{0,4},{1,5},{2,6},{3,7},{4,8},{5,9},{6,10},{7,11},{8,12},{9,13},{1... | collective-permute-start | bytes 1572872 | tf_op jit(solution)/shard_map/ppermute | solution.py:12
  46.8 18.8 %collective-permute-start.4 = (f32[16]{0:T(128)S(1)}, f32[16]{0:T(128)S(1)}, u32[]{:S(2)}, u32[]{:S(2)}) collective-permute-start(f32[16]{0:T(128)S(1)} %get-tuple-element.14), channel_id=1, source_target_pairs={{0,2},{1,3},{2,4},{3,5},{4,6},{5,7},{6,8},{7,9},{8,10},{9,11},{10,... | collective-permute-start | bytes 200 | tf_op jit(solution)/shard_map/ppermute | solution.py:12
  66.6 21.4 %collective-permute-start.5 = (bf16[16,128,128]{2,1,0:T(8,128)(2,1)}, bf16[16,128,128]{2,1,0:T(8,128)(2,1)}, u32[]{:S(2)}, u32[]{:S(2)}) collective-permute-start(bf16[16,128,128]{2,1,0:T(8,128)(2,1)} %fusion.30), channel_id=1, source_target_pairs={{0,8},{1,9},{2,10},{3,11},{4,12},{5,13},{6,14},{7,15},{8,16},{9,17... | collective-permute-start | bytes 1572872 | tf_op jit(solution)/shard_map/ppermute | solution.py:12
  75.4 22.9 %copy-start.5 = (s32[32,24]{0,1:T(8,128)S(1)}, s32[32,24]{0,1:T(8,128)}, u32[]{:S(2)}) copy-start(s32[32,24]{0,1:T(8,128)} %param.17) | copy-start | bytes 9220
  82.5 2.6 collective-permute-start.6
  90.2 20.6 %collective-permute-start.10 = (bf16[16,128,128]{2,1,0:T(8,128)(2,1)}, bf16[16,128,128]{2,1,0:T(8,128)(2,1)S(1)}, u32[]{:S(2)}, u32[]{:S(2)}) collective-permute-start(bf16[16,128,128]{2,1,0:T(8,128)(2,1)} %add_convert_fusion.2), channel_id=1, source_target_pairs={{0,1},{1,2},{2,3},{3,4},{4,5},{5,6},{6,7},{7,8},{8,9},{9,10},{10,1... | collective-permute-start | bytes 1572872 | tf_op jit(solution)/shard_map/ppermute | solution.py:12
  91.5 19.3 %collective-permute-start.7 = (bf16[16,128,128]{2,1,0:T(8,128)(2,1)}, bf16[16,128,128]{2,1,0:T(8,128)(2,1)S(1)}, u32[]{:S(2)}, u32[]{:S(2)}) collective-permute-start(bf16[16,128,128]{2,1,0:T(8,128)(2,1)} %add_convert_fusion.2), channel_id=1, source_target_pairs={{0,17},{1,18},{2,19},{3,20},{4,21},{5,22},{6,23},{7,24},{8,25},{9,... | collective-permute-start | bytes 1572872 | tf_op jit(solution)/shard_map/ppermute | solution.py:12
  98.5 10.1 %collective-permute-start.8 = (f32[16]{0:T(128)S(1)}, f32[16]{0:T(128)S(1)}, u32[]{:S(2)}, u32[]{:S(2)}) collective-permute-start(f32[16]{0:T(128)S(1)} %get-tuple-element.8), channel_id=1, source_target_pairs={{0,8},{1,9},{2,10},{3,11},{4,12},{5,13},{6,14},{7,15},{8,16},{9,17... | collective-permute-start | bytes 200 | tf_op jit(solution)/shard_map/ppermute | solution.py:12
  108.7 2.1 collective-permute-start.9
  114.5 1.4 copy-start.4
  115.9 7.7 %copy-start.7 = (f32[2048]{0:T(1024)S(1)}, f32[2048]{0:T(1024)}, u32[]{:S(2)}) copy-start(f32[2048]{0:T(1024)} %param.19) | copy-start | bytes 24580
  121.9 1.7 copy-start.2
  130.4 56.8 %slice-start = ((s8[5767168]{0:T(1024)(128)(4,1)}), s8[4194304]{0:T(1024)(128)(4,1)S(1)}, s32[]{:S(2)}) async-start(s8[5767168]{0:T(1024)(128)(4,1)} %bitcast.92), calls=%async_computation.3 | async-start | bytes 8388608
  179.5 7.7 %slice-start.1 = ((s8[5767168]{0:T(1024)(128)(4,1)}), s8[1572864]{0:T(1024)(128)(4,1)S(1)}, s32[]{:S(2)}) async-start(s8[5767168]{0:T(1024)(128)(4,1)} %bitcast.92), calls=%async_computation.4 | async-start | bytes 3145728
  179.6 13.5 %slice-start.2 = ((s8[5767168]{0:T(1024)(128)(4,1)}), s8[4194304]{0:T(1024)(128)(4,1)S(1)}, s32[]{:S(2)}) async-start(s8[5767168]{0:T(1024)(128)(4,1)} %bitcast.94), calls=%async_computation.5 | async-start | bytes 8388608
  187.2 5.8 %slice-start.3 = ((s8[5767168]{0:T(1024)(128)(4,1)}), s8[1572864]{0:T(1024)(128)(4,1)S(1)}, s32[]{:S(2)}) async-start(s8[5767168]{0:T(1024)(128)(4,1)} %bitcast.94), calls=%async_computation.6 | async-start | bytes 3145728
  199.6 5.3 %copy-start.6 = (f32[32,24]{0,1:T(8,128)S(1)}, f32[32,24]{0,1:T(8,128)}, u32[]{:S(2)}) copy-start(f32[32,24]{0,1:T(8,128)} %param.18) | copy-start | bytes 9220
  199.6 47.0 %all-to-all-start.1 = ((bf16[32,24,2048]{2,1,0:T(8,128)(2,1)}), bf16[32,24,2048]{2,1,0:T(8,128)(2,1)}, u32[]{:S(2)}, u32[]{:S(2)}) async-start(bf16[32,24,2048]{2,1,0:T(8,128)(2,1)} %fusion.10), calls=%async_computation.1 | async-start | bytes 6291456 | tf_op jit(solution)/shard_map/all_to_all | solution.py:108
  251.5 21.6 %copy-start.1 = (bf16[384,2048]{1,0:T(8,128)(2,1)S(1)}, bf16[384,2048]{1,0:T(8,128)(2,1)}, u32[]{:S(2)}) copy-start(bf16[384,2048]{1,0:T(8,128)(2,1)} %param.12) | copy-start | bytes 4718596
Sparse Core Ops, SparseCore 0:
  9.6 73.6 all-gather.1

commit v2 on v1

--- a/solution.py
+++ b/solution.py
@@ -14,9 +14,26 @@
     def combine(earlier, latter):
         return (earlier[0] * jnp.exp(latter[1])[:, None, None] + latter[0], earlier[1] + latter[1])
 
+    heads, rows, width = state.shape
+
+    def pieces(wide):
+        parts = []
+        for _ in range(3):
+            part = wide.astype(jnp.bfloat16)
+            parts.append(part)
+            wide = wide - part.astype(jnp.float32)
+        block = jnp.stack(parts, axis=1)
+        return jnp.pad(block, ((0, 0), (0, width - 3)))
+
     def fetch(pair, distance):
         low, wide = pair
-        return (shifted(low.astype(jnp.bfloat16), distance).astype(jnp.float32), shifted(wide, distance))
+        message = jnp.concatenate(
+            [low.astype(jnp.bfloat16).reshape(heads * rows, width), pieces(wide)], axis=0
+        )
+        arrived = shifted(message, distance)
+        body = arrived[: heads * rows].reshape(heads, rows, width).astype(jnp.float32)
+        tail = arrived[heads * rows :, :3].astype(jnp.float32)
+        return (body, tail[:, 0] + tail[:, 1] + tail[:, 2])
 
     covered = (state, ending)
     reach = 1
@@ -96,8 +113,11 @@
     mixed_in = (
         widened * lax.rsqrt(jnp.mean(widened * widened, axis=1, keepdims=True) + 1e-06) * moe_gain
     ).astype(jnp.bfloat16)
-    offsets = token_index - device * length
-    picked = jnp.take(mixed_in, offsets, axis=0)
+    offsets = (token_index - device * length).reshape(-1)
+    positions = jnp.arange(length)
+    choose = (offsets[:, None] == positions[None, :]).astype(jnp.bfloat16)
+    picked = jnp.dot(choose, mixed_in, preferred_element_type=jnp.float32).astype(jnp.bfloat16)
+    picked = picked.reshape(token_index.shape + (model_width,))
     arrived = lax.all_to_all(picked, "seq", split_axis=0, concat_axis=0, tiled=True)
     gating = jnp.einsum("snd,df->snf", arrived, gate_weight[0], preferred_element_type=jnp.float32)
     upward = jnp.einsum("snd,df->snf", arrived, up_weight[0], preferred_element_type=jnp.float32)
@@ -106,8 +126,15 @@
         "snf,fd->snd", activated, down_weight[0], preferred_element_type=jnp.float32
     ).astype(jnp.bfloat16)
     returned = lax.all_to_all(produced, "seq", split_axis=0, concat_axis=0, tiled=True)
-    scaled = returned.astype(jnp.float32) * route_weight[:, :, None]
-    total = widened.at[offsets.reshape(-1)].add(scaled.reshape(-1, model_width))
+    spread_weight = jnp.where(
+        positions[:, None] == offsets[None, :], route_weight.reshape(-1)[None, :], 0.0
+    )
+    flat_returned = returned.reshape(-1, model_width)
+    total = widened
+    for _ in range(3):
+        part = spread_weight.astype(jnp.bfloat16)
+        total = total + jnp.dot(part, flat_returned, preferred_element_type=jnp.float32)
+        spread_weight = spread_weight - part.astype(jnp.float32)
     return total.astype(jnp.bfloat16)
 
 

time: 281 us -> 269 us (0.957)
  other arithmetic: 34.4 us -> 6.36 us
  matrix products: 38.9 us -> 53.2 us
  starting transfers between devices: 50 us -> 39.9 us
  local copies, waits for them, and re-layouts: 10.4 us -> 16.1 us
  blocking collectives: 49.1 us -> 52.4 us
  waiting for transfers between devices: 83.4 us -> 86.3 us
    scatter-add x1 -> x0, other arithmetic: 18.3 us -> none  [shards(): total = widened.at[offsets.reshape(-1)].add(scaled.reshape(-1, model_width))]
    dot_general x0 -> x4, matrix products: none -> 13.2 us  [the longest x3 11.3 us: shards(): jnp.dot(part, flat_returned, preferred_element_type=jnp.float32)]
    ppermute x11 -> x6, starting transfers between devices: 44.8 us -> 35 us  [shifted(): return lax.ppermute(part, axis, pairs)]
    slice x1 -> x11, local copies, waits for them, and re-layouts: 0.16 us -> 5.61 us  [the longest x6 5.45 us: fetch(): arrived[:heads * rows].reshape(heads, rows, width).astype(jnp.float32)]
    mul x1 -> x0, other arithmetic: 5.02 us -> none  [shards(): scaled = returned.astype(jnp.float32) * route_weight[:, :, None]]
    convert_element_type x6 -> x18, other arithmetic: 7.33 us -> 2.41 us  [the longest x4 2.33 us: fetch(): low.astype(jnp.bfloat16).reshape(heads * rows, width)]
    gather x1 -> x0, local copies, waits for them, and re-layouts: 4.25 us -> none  [shards(): picked = jnp.take(mixed_in, offsets, axis=0)]
    all_to_all x1, blocking collectives: 49.1 us -> 52.4 us  [shards(): lax.all_to_all(picked, 'seq', split_axis=0, concat_axis=0, tiled=True)]
  transfers between devices with their start and end apart: 13 -> 8, of which waited for: 8 -> 5; matrix products, arithmetic and copies ran while one was open for 8% -> 13% of each run, Pallas kernels for 0% -> 0%
where the time goes in v2:
time: 269 us; the launch traced here: 268 us
  waiting for transfers between devices  86.3 us (32%)
  matrix products  53.2 us (20%)
  blocking collectives  52.4 us (19%)
  starting transfers between devices  39.9 us (15%)
  local copies, waits for them, and re-layouts  16.1 us (6%)
  between operations  13.9 us (5%)
  other arithmetic  6.36 us (2%)
    all_to_all x1, blocking collectives, shards(): lax.all_to_all(picked, 'seq', split_axis=0, concat_axis=0, tiled=True)  52.4 us
    ppermute x6, waiting for transfers between devices, shifted(): return lax.ppermute(part, axis, pairs)  43.8 us
    all_to_all x1, waiting for transfers between devices, shards(): lax.all_to_all(produced, 'seq', split_axis=0, concat_axis=0, tiled=True)  41.8 us
    ppermute x6, starting transfers between devices, shifted(): return lax.ppermute(part, axis, pairs)  35 us
    dot_general x3, matrix products, shards(): jnp.dot(part, flat_returned, preferred_element_type=jnp.float32)  11.3 us
    dot_general x1, matrix products, shards(): jnp.dot(normed, lax.all_gather(out_weight, 'seq', axis=0, tiled=True), pr...  7.73 us
    dot_general x1, matrix products, shards(): jnp.einsum('hts,shd->thd', attend_weights, value_heads, preferred_element...  7.32 us
    dot_general x1, matrix products, shards(): jnp.einsum('snf,fd->snd', activated, down_weight[0], preferred_element_ty...  6.54 us
  transfers between devices with their start and end apart: 8, of which 5 were waited for; matrix products, arithmetic and copies ran while one was open for 13% of the time, Pallas kernels for 0%

profile of v2, /device:TPU:0, one launch (start us, length us, event | category | flops | bytes accessed | tf_op | source)
XLA Modules:
  0.0 268.1 jit_solution(8495160899724814217)
XLA Ops:
  6.5 0.7 all-gather.2.cloned.1.call-update
  7.3 0.7 copy_bitcast_fusion.1
  8.0 0.9 reduce-window.6
  8.9 0.2 slice_reduce_fusion
  9.0 0.1 copy_bitcast_fusion
  9.1 0.2 slice_reduce_fusion.1
  9.4 0.1 copy.119
  9.5 2.6 copy.124
  12.0 0.1 subtract_exponential_fusion
  12.1 2.5 fusion.91
  14.7 1.3 collective-permute-start
  16.0 1.5 collective-permute-done
  17.5 0.8 copy-done.6
  18.3 0.1 copy.115
  18.5 0.1 copy.120
  18.6 1.1 slice.118
  19.6 0.2 fusion.50
  19.9 12.7 %collective-permute-start.1 = (bf16[2064,128]{1,0:T(8,128)(2,1)S(1)}, bf16[2064,128]{1,0:T(8,128)(2,1)S(1)}, u32[]{:S(2)}, u32[]{:S(2)}) collective-permute-start(bf16[2064,128]{1,0:T(8,128)(2,1)S(1)} %fusion.63), channel_id=1, source_target_pairs={{0,2},{1,3},{2,4},{3,5},{4,6},{5,7},{6,8},{7,9},{8,10},{9,11},{10,... | collective-permute-start | bytes 1585160 | tf_op jit(solution)/shard_map/ppermute | solution.py:12
  32.6 11.5 %collective-permute-done.1 = bf16[2064,128]{1,0:T(8,128)(2,1)S(1)} collective-permute-done((bf16[2064,128]{1,0:T(8,128)(2,1)S(1)}, bf16[2064,128]{1,0:T(8,128)(2,1)S(1)}, u32[]{:S(2)}, u32[]{:S(2)}) %collective-permute-start.1) | collective-permute-done | bytes 528416 | tf_op jit(solution)/shard_map/ppermute | solution.py:12
  44.1 0.8 copy-done.5
  44.9 0.1 copy.116
  45.1 0.1 copy.121
  45.2 1.1 slice.120
  46.3 1.6 fusion.86
  47.9 5.2 %collective-permute-start.2 = (bf16[2064,128]{1,0:T(8,128)(2,1)S(1)}, bf16[2064,128]{1,0:T(8,128)(2,1)S(1)}, u32[]{:S(2)}, u32[]{:S(2)}) collective-permute-start(bf16[2064,128]{1,0:T(8,128)(2,1)S(1)} %fusion.64), channel_id=1, source_target_pairs={{0,4},{1,5},{2,6},{3,7},{4,8},{5,9},{6,10},{7,11},{8,12},{9,13},{1... | collective-permute-start | bytes 1585160 | tf_op jit(solution)/shard_map/ppermute | solution.py:12
  53.1 21.9 %collective-permute-done.2 = bf16[2064,128]{1,0:T(8,128)(2,1)S(1)} collective-permute-done((bf16[2064,128]{1,0:T(8,128)(2,1)S(1)}, bf16[2064,128]{1,0:T(8,128)(2,1)S(1)}, u32[]{:S(2)}, u32[]{:S(2)}) %collective-permute-start.2) | collective-permute-done | bytes 528416 | tf_op jit(solution)/shard_map/ppermute | solution.py:12
  75.0 0.8 copy-done.4
  75.9 0.1 copy.117
  76.0 0.1 copy.122
  76.1 1.1 slice.122
  77.2 0.2 fusion.51
  77.5 5.5 %collective-permute-start.3 = (bf16[2064,128]{1,0:T(8,128)(2,1)S(1)}, bf16[2064,128]{1,0:T(8,128)(2,1)S(1)}, u32[]{:S(2)}, u32[]{:S(2)}) collective-permute-start(bf16[2064,128]{1,0:T(8,128)(2,1)S(1)} %fusion.65), channel_id=1, source_target_pairs={{0,8},{1,9},{2,10},{3,11},{4,12},{5,13},{6,14},{7,15},{8,16},{9,17... | collective-permute-start | bytes 1585160 | tf_op jit(solution)/shard_map/ppermute | solution.py:12
  83.0 8.8 %collective-permute-done.3 = bf16[2064,128]{1,0:T(8,128)(2,1)S(1)} collective-permute-done((bf16[2064,128]{1,0:T(8,128)(2,1)S(1)}, bf16[2064,128]{1,0:T(8,128)(2,1)S(1)}, u32[]{:S(2)}, u32[]{:S(2)}) %collective-permute-start.3) | collective-permute-done | bytes 528416 | tf_op jit(solution)/shard_map/ppermute | solution.py:12
  91.8 0.8 copy-done.7
  92.7 0.1 copy.118
  92.8 0.1 copy.123
  92.9 1.1 slice.124
  94.0 0.3 fusion.45
  94.4 2.3 collective-permute-start.4
  96.7 7.9 %collective-permute-start.5 = (bf16[2064,128]{1,0:T(8,128)(2,1)S(1)}, bf16[2064,128]{1,0:T(8,128)(2,1)S(1)}, u32[]{:S(2)}, u32[]{:S(2)}) collective-permute-start(bf16[2064,128]{1,0:T(8,128)(2,1)S(1)} %fusion.66), channel_id=1, source_target_pairs={{0,1},{1,2},{2,3},{3,4},{4,5},{5,6},{6,7},{7,8},{8,9},{9,10},{10,1... | collective-permute-start | bytes 1585160 | tf_op jit(solution)/shard_map/ppermute | solution.py:12
  104.6 0.1 copy.113
  104.7 0.1 eq.29
  104.8 1.1 slice.126
  105.9 1.2 copy.110
  107.2 1.2 copy.111
  108.4 0.2 fusion.69
  108.6 5.0 %fusion.22 = f32[16,128,384]{2,1,0:T(8,128)} fusion(f32[384,16]{0,1:T(8,128)S(1)} %get-tuple-element.24, f32[16,128,128]{1,2,0:T(8,128)} %copy.111, f32[16,128,128]{1,2,0:T(8,128)} %copy.110, f32[16]{0:T(128)S(1)} %fusion.69, bf16[384,2048]{1,0:T(8,128)(2,1)S(1)} %copy-done), kind=kOutput, calls=%fused_computation.29 | convolution fusion | flops 204472320 | bytes 6840384 | tf_op jit(solution)/shard_map/thd,hde->the/dot_general | solution.py:95
  113.7 7.3 %multiply_reduce_fusion = (f32[384,16]{0,1:T(8,128)S(1)}, f32[384,16,128]{0,2,1:T(8,128)}) fusion(f32[16,128,384]{2,1,0:T(8,128)} %fusion.22, f32[16,384]{1,0:T(8,128)S(1)} %get-tuple-element.21, pred[384,384]{1,0:T(8,128)(4,1)S(1)} %iota_compare_fusion.4, bf16[384,16,128]{0,2,1:T(8,128)(2,1)S(1)} %bitcast.143, bf16[384,2048]{1,0:T(8,128)(2,1)} %param.14, ...), kind=kOutput, calls=%fused_computation.25 | convolution fusion | flops 1224468480 | bytes 11206656 | tf_op jit(solution)/shard_map/hts,shd->thd/dot_general | solution.py:89
  121.0 2.3 multiply_convert_fusion.3
  123.4 0.0 all-gather.2.cloned.1.call-done
  123.4 7.7 %fusion.15 = (f32[384]{0:T(512)S(1)}, bf16[384,2048]{1,0:T(8,128)(2,1)S(1)}) fusion(bf16[384,2048]{0,1:T(8,128)(2,1)S(1)} %bitcast.158, bf16[2048,2048]{1,0:T(8,128)(2,1)} %all-gather.2.cloned.1.call-done, bf16[384,2048]{1,0:T(8,128)(2,1)} %param.15), kind=kOutput, calls=%fused_computation.16 | convolution fusion | flops 3225943552 | bytes 13108736 | tf_op jit(solution)/shard_map/dot_general | solution.py:106
  131.2 1.9 convolution_convert_fusion
  133.1 52.4 %all_to_all.10 = bf16[32,24,2048]{2,1,0:T(8,128)(2,1)S(1)} all-to-all(bf16[32,24,2048]{2,1,0:T(8,128)(2,1)S(1)} %bitcast.148), channel_id=1, replica_groups=mesh['dp'=4,'seq'=32] {'seq'}, dimensions={0} | all-to-all | bytes 6291456 | tf_op jit(solution)/shard_map/all_to_all | solution.py:121
  185.5 5.1 %fusion.2 = f32[32,24,1408]{2,1,0:T(8,128)S(1)} fusion(bf16[32,24,2048]{2,1,0:T(8,128)(2,1)S(1)} %all_to_all.10, bf16[1,2048,1408]{2,1,0:T(8,128)(2,1)S(1)} %bitcast.162), kind=kOutput, calls=%fused_computation.3 | convolution fusion | flops 4429185024 | bytes 13238272 | tf_op jit(solution)/shard_map/snd,df->snf/dot_general | solution.py:123
  190.6 0.0 slice-start.5
  190.6 5.8 %multiply_convert_fusion.2 = bf16[32,24,1408]{2,1,0:T(8,128)(2,1)S(1)} fusion(f32[32,24,1408]{2,1,0:T(8,128)S(1)} %fusion.2, bf16[32,24,2048]{2,1,0:T(8,128)(2,1)S(1)} %all_to_all.10, bf16[1,2048,1408]{2,1,0:T(8,128)(2,1)S(1)} %bitcast.164), kind=kOutput, calls=%fused_computation.12 | convolution fusion | flops 4435673088 | bytes 15400960 | tf_op jit(solution)/shard_map/snd,df->snf/dot_general | solution.py:122
  196.4 6.5 %fusion.10 = bf16[32,24,2048]{2,1,0:T(8,128)(2,1)} fusion(bf16[32,24,1408]{2,1,0:T(8,128)(2,1)S(1)} %multiply_convert_fusion.2, bf16[1,1408,2048]{2,1,0:T(8,128)(2,1)S(1)} %bitcast.166), kind=kOutput, calls=%fused_computation.14 | convolution fusion | flops 4430757888 | bytes 11075584 | tf_op jit(solution)/shard_map/snf,fd->snd/dot_general | solution.py:125
  203.0 5.0 %all-to-all-start.1 = ((bf16[32,24,2048]{2,1,0:T(8,128)(2,1)}), bf16[32,24,2048]{2,1,0:T(8,128)(2,1)}, u32[]{:S(2)}, u32[]{:S(2)}) async-start(bf16[32,24,2048]{2,1,0:T(8,128)(2,1)} %fusion.10), calls=%async_computation.1 | async-start | bytes 6291456 | tf_op jit(solution)/shard_map/all_to_all | solution.py:128
  207.9 0.1 copy.114
  208.0 0.1 broadcast_in_dim.21
  208.1 41.8 %all-to-all-done.1 = bf16[32,24,2048]{2,1,0:T(8,128)(2,1)} async-done(((bf16[32,24,2048]{2,1,0:T(8,128)(2,1)}), bf16[32,24,2048]{2,1,0:T(8,128)(2,1)}, u32[]{:S(2)}, u32[]{:S(2)}) %all-to-all-start.1) | async-done | bytes 3145760 | tf_op jit(solution)/shard_map/all_to_all | solution.py:128
  249.9 3.3 %fusion.49 = f32[384,2048]{1,0:T(8,128)S(1)} fusion(bf16[768,2048]{1,0:T(8,128)(2,1)} %bitcast.26, f32[768]{0:T(1024)S(1)} %broadcast_in_dim.21, s32[768]{0:T(1024)S(1)} %eq.29), kind=kOutput, calls=%fused_computation.64 | convolution fusion | flops 1208549376 | bytes 6297600 | tf_op jit(solution)/shard_map/dot_general | solution.py:136
  253.2 3.4 %fusion.60 = f32[384,2048]{1,0:T(8,128)S(1)} fusion(bf16[768,2048]{1,0:T(8,128)(2,1)} %bitcast.26, f32[768]{0:T(1024)S(1)} %broadcast_in_dim.21, s32[768]{0:T(1024)S(1)} %eq.29), kind=kOutput, calls=%fused_computation.74 | convolution fusion | flops 1209729024 | bytes 6297600 | tf_op jit(solution)/shard_map/dot_general | solution.py:136
  256.6 4.7 %fusion.20 = bf16[384,2048]{1,0:T(8,128)(2,1)} fusion(f32[384,2048]{1,0:T(8,128)S(1)} %fusion.60, f32[384,2048]{1,0:T(8,128)S(1)} %fusion.49, bf16[384,2048]{1,0:T(8,128)(2,1)S(1)} %copy-done.12, bf16[768,2048]{1,0:T(8,128)(2,1)} %bitcast.26, f32[768]{0:T(1024)S(1)} %broadcast_in_dim.21, s32[768]{0:T(1024)S(1)} %eq.29), kind=kOutput, calls=%fused_computation.21 | convolution fusion | flops 1214545920 | bytes 12589056 | tf_op jit(solution)/shard_map/dot_general | solution.py:136
  (77 shorter events, 0.6 us)
Async XLA Ops:
  6.5 102.1 %copy-start = (bf16[384,2048]{1,0:T(8,128)(2,1)S(1)}, bf16[384,2048]{1,0:T(8,128)(2,1)}, u32[]{:S(2)}) copy-start(bf16[384,2048]{1,0:T(8,128)(2,1)} %param.12) | copy-start | bytes 4718596
  6.5 116.8 %all-gather.2.cloned.1.call-start = ((), (), s32[]{:S(2)}) async-start(), calls=%async_computation.2 | async-start | bytes 8650752 | tf_op jit(solution)/shard_map/all_gather | solution.py:108
  14.6 5.2 %copy-start.2 = (f32[16,128,128]{2,1,0:T(8,128)}, f32[16,128,128]{2,1,0:T(8,128)S(1)}, u32[]{:S(2)}) copy-start(f32[16,128,128]{2,1,0:T(8,128)S(1)} %get-tuple-element.38) | copy-start | bytes 3145732
  14.7 2.8 %collective-permute-start = (bf16[2064,128]{1,0:T(8,128)(2,1)S(1)}, bf16[2064,128]{1,0:T(8,128)(2,1)S(1)}, u32[]{:S(2)}, u32[]{:S(2)}) collective-permute-start(bf16[2064,128]{1,0:T(8,128)(2,1)S(1)} %fusion.62), channel_id=1, source_target_pairs={{0,1},{1,2},{2,3},{3,4},{4,5},{5,6},{6,7},{7,8},{8,9},{9,10},{10,1... | collective-permute-start | bytes 1585160 | tf_op jit(solution)/shard_map/ppermute | solution.py:12
  17.5 0.8 copy-start.6
  19.9 24.2 %collective-permute-start.1 = (bf16[2064,128]{1,0:T(8,128)(2,1)S(1)}, bf16[2064,128]{1,0:T(8,128)(2,1)S(1)}, u32[]{:S(2)}, u32[]{:S(2)}) collective-permute-start(bf16[2064,128]{1,0:T(8,128)(2,1)S(1)} %fusion.63), channel_id=1, source_target_pairs={{0,2},{1,3},{2,4},{3,5},{4,6},{5,7},{6,8},{7,9},{8,10},{9,11},{10,... | collective-permute-start | bytes 1585160 | tf_op jit(solution)/shard_map/ppermute | solution.py:12
  44.1 0.8 copy-start.5
  47.9 27.2 %collective-permute-start.2 = (bf16[2064,128]{1,0:T(8,128)(2,1)S(1)}, bf16[2064,128]{1,0:T(8,128)(2,1)S(1)}, u32[]{:S(2)}, u32[]{:S(2)}) collective-permute-start(bf16[2064,128]{1,0:T(8,128)(2,1)S(1)} %fusion.64), channel_id=1, source_target_pairs={{0,4},{1,5},{2,6},{3,7},{4,8},{5,9},{6,10},{7,11},{8,12},{9,13},{1... | collective-permute-start | bytes 1585160 | tf_op jit(solution)/shard_map/ppermute | solution.py:12
  75.0 0.8 copy-start.4
  77.5 14.3 %collective-permute-start.3 = (bf16[2064,128]{1,0:T(8,128)(2,1)S(1)}, bf16[2064,128]{1,0:T(8,128)(2,1)S(1)}, u32[]{:S(2)}, u32[]{:S(2)}) collective-permute-start(bf16[2064,128]{1,0:T(8,128)(2,1)S(1)} %fusion.65), channel_id=1, source_target_pairs={{0,8},{1,9},{2,10},{3,11},{4,12},{5,13},{6,14},{7,15},{8,16},{9,17... | collective-permute-start | bytes 1585160 | tf_op jit(solution)/shard_map/ppermute | solution.py:12
  91.8 0.8 copy-start.7
  92.9 11.7 %copy-start.9 = (s32[32,24]{0,1:T(8,128)S(1)}, s32[32,24]{0,1:T(8,128)}, u32[]{:S(2)}) copy-start(s32[32,24]{0,1:T(8,128)} %param.17) | copy-start | bytes 9220
  94.4 10.4 %collective-permute-start.4 = (bf16[2064,128]{1,0:T(8,128)(2,1)S(1)}, bf16[2064,128]{1,0:T(8,128)(2,1)}, u32[]{:S(2)}, u32[]{:S(2)}) collective-permute-start(bf16[2064,128]{1,0:T(8,128)(2,1)S(1)} %fusion.66), channel_id=1, source_target_pairs={{0,17},{1,18},{2,19},{3,20},{4,21},{5,22},{6,23},{7,24},{8,25},{9,... | collective-permute-start | bytes 1585160 | tf_op jit(solution)/shard_map/ppermute | solution.py:12
  96.7 10.4 %collective-permute-start.5 = (bf16[2064,128]{1,0:T(8,128)(2,1)S(1)}, bf16[2064,128]{1,0:T(8,128)(2,1)S(1)}, u32[]{:S(2)}, u32[]{:S(2)}) collective-permute-start(bf16[2064,128]{1,0:T(8,128)(2,1)S(1)} %fusion.66), channel_id=1, source_target_pairs={{0,1},{1,2},{2,3},{3,4},{4,5},{5,6},{6,7},{7,8},{8,9},{9,10},{10,1... | collective-permute-start | bytes 1585160 | tf_op jit(solution)/shard_map/ppermute | solution.py:12
  108.6 5.1 %copy-start.3 = (bf16[384,2048]{0,1:T(8,128)(2,1)S(1)}, bf16[384,2048]{0,1:T(8,128)(2,1)}, u32[]{:S(2)}) copy-start(bf16[384,2048]{0,1:T(8,128)(2,1)} %copy.124) | copy-start | bytes 4718596
  121.0 64.5 %slice-start = ((s8[5767168]{0:T(1024)(128)(4,1)}), s8[1572864]{0:T(1024)(128)(4,1)S(1)}, s32[]{:S(2)}) async-start(s8[5767168]{0:T(1024)(128)(4,1)} %bitcast.161), calls=%async_computation.3 | async-start | bytes 3145728
  123.4 7.8 %copy-start.10 = (f32[2048]{0:T(1024)S(1)}, f32[2048]{0:T(1024)}, u32[]{:S(2)}) copy-start(f32[2048]{0:T(1024)} %param.19) | copy-start | bytes 24580
  123.4 62.1 %slice-start.1 = ((s8[5767168]{0:T(1024)(128)(4,1)}), s8[4194304]{0:T(1024)(128)(4,1)S(1)}, s32[]{:S(2)}) async-start(s8[5767168]{0:T(1024)(128)(4,1)} %bitcast.161), calls=%async_computation.4 | async-start | bytes 8388608
  131.1 2.0 copy-start.11
  133.1 57.5 %slice-start.2 = ((s8[5767168]{0:T(1024)(128)(4,1)}), s8[4194304]{0:T(1024)(128)(4,1)S(1)}, s32[]{:S(2)}) async-start(s8[5767168]{0:T(1024)(128)(4,1)} %bitcast.163), calls=%async_computation.5 | async-start | bytes 8388608
  185.5 5.1 %slice-start.3 = ((s8[5767168]{0:T(1024)(128)(4,1)}), s8[1572864]{0:T(1024)(128)(4,1)S(1)}, s32[]{:S(2)}) async-start(s8[5767168]{0:T(1024)(128)(4,1)} %bitcast.163), calls=%async_computation.6 | async-start | bytes 3145728
  185.5 10.9 %slice-start.4 = ((s8[5767168]{0:T(1024)(128)(4,1)}), s8[4194304]{0:T(1024)(128)(4,1)S(1)}, s32[]{:S(2)}) async-start(s8[5767168]{0:T(1024)(128)(4,1)} %bitcast.165), calls=%async_computation.7 | async-start | bytes 8388608
  190.6 5.8 %slice-start.5 = ((s8[5767168]{0:T(1024)(128)(4,1)}), s8[1572864]{0:T(1024)(128)(4,1)S(1)}, s32[]{:S(2)}) async-start(s8[5767168]{0:T(1024)(128)(4,1)} %bitcast.165), calls=%async_computation.8 | async-start | bytes 3145728
  203.0 5.0 %copy-start.8 = (f32[32,24]{0,1:T(8,128)S(1)}, f32[32,24]{0,1:T(8,128)}, u32[]{:S(2)}) copy-start(f32[32,24]{0,1:T(8,128)} %param.18) | copy-start | bytes 9220
  203.0 47.0 %all-to-all-start.1 = ((bf16[32,24,2048]{2,1,0:T(8,128)(2,1)}), bf16[32,24,2048]{2,1,0:T(8,128)(2,1)}, u32[]{:S(2)}, u32[]{:S(2)}) async-start(bf16[32,24,2048]{2,1,0:T(8,128)(2,1)} %fusion.10), calls=%async_computation.1 | async-start | bytes 6291456 | tf_op jit(solution)/shard_map/all_to_all | solution.py:128
  253.2 3.4 %copy-start.12 = (bf16[384,2048]{1,0:T(8,128)(2,1)S(1)}, bf16[384,2048]{1,0:T(8,128)(2,1)}, u32[]{:S(2)}) copy-start(bf16[384,2048]{1,0:T(8,128)(2,1)} %copy-done.11) | copy-start | bytes 4718596
  256.6 4.7 %copy-start.1 = (bf16[384,2048]{1,0:T(8,128)(2,1)S(1)}, bf16[384,2048]{1,0:T(8,128)(2,1)}, u32[]{:S(2)}) copy-start(bf16[384,2048]{1,0:T(8,128)(2,1)} %param.12) | copy-start | bytes 4718596
Sparse Core Ops, SparseCore 0:
  9.6 73.8 all-gather.1

commit v3 on v2

--- a/solution.py
+++ b/solution.py
@@ -2,6 +2,10 @@
 import jax.numpy as jnp
 from jax import lax
 from jax.sharding import PartitionSpec as P
+
+SEQ = ("sy", "sx", "sc")
+CHIP_AXES = ("sy", "sx")
+CORE_AXIS = "sc"
 
 
 def carried_in(state, ending, axis):
@@ -19,9 +23,9 @@
     def pieces(wide):
         parts = []
         for _ in range(3):
-            part = wide.astype(jnp.bfloat16)
-            parts.append(part)
-            wide = wide - part.astype(jnp.float32)
+            part = lax.reduce_precision(wide, exponent_bits=8, mantissa_bits=7)
+            parts.append(part.astype(jnp.bfloat16))
+            wide = wide - part
         block = jnp.stack(parts, axis=1)
         return jnp.pad(block, ((0, 0), (0, width - 3)))
 
@@ -66,7 +70,7 @@
     head_count = log_decay.shape[1]
     head_size = model_width // head_count
     scaling = head_size ** (-0.5)
-    device = lax.axis_index("seq")
+    device = lax.axis_index(SEQ)
     query_heads = queries.reshape(length, head_count, head_size)
     key_heads = keys_in.reshape(length, head_count, head_size)
     value_heads = values.reshape(length, head_count, head_size)
@@ -77,7 +81,7 @@
     local_state = jnp.einsum(
         "shd,she->hde", key_scaled, value_heads, preferred_element_type=jnp.float32
     )
-    incoming = carried_in(local_state, ending, "seq")
+    incoming = carried_in(local_state, ending, SEQ)
     scores = (
         jnp.einsum("thd,shd->hts", query_heads, key_heads, preferred_element_type=jnp.float32)
         * scaling
@@ -103,9 +107,13 @@
     normed = (
         (unnormed * lax.rsqrt(spread + 1e-06)).astype(jnp.bfloat16).reshape(length, model_width)
     )
-    attended = jnp.dot(
-        normed,
-        lax.all_gather(out_weight, "seq", axis=0, tiled=True),
+    chips = lax.all_gather(out_weight, CHIP_AXES, axis=0, tiled=True)
+    gathered = lax.all_gather(chips, CORE_AXIS, axis=0)
+    cores = gathered.shape[0]
+    attended = jnp.einsum(
+        "tcbr,bcrd->td",
+        normed.reshape(length, -1, cores, out_weight.shape[0]),
+        gathered.reshape(cores, -1, out_weight.shape[0], model_width),
         preferred_element_type=jnp.float32,
     )
     residual = (stream.astype(jnp.float32) + attended).astype(jnp.bfloat16)
@@ -118,41 +126,47 @@
     choose = (offsets[:, None] == positions[None, :]).astype(jnp.bfloat16)
     picked = jnp.dot(choose, mixed_in, preferred_element_type=jnp.float32).astype(jnp.bfloat16)
     picked = picked.reshape(token_index.shape + (model_width,))
-    arrived = lax.all_to_all(picked, "seq", split_axis=0, concat_axis=0, tiled=True)
+    arrived = lax.all_to_all(picked, SEQ, split_axis=0, concat_axis=0, tiled=True)
     gating = jnp.einsum("snd,df->snf", arrived, gate_weight[0], preferred_element_type=jnp.float32)
     upward = jnp.einsum("snd,df->snf", arrived, up_weight[0], preferred_element_type=jnp.float32)
     activated = (jax.nn.silu(gating) * upward).astype(jnp.bfloat16)
     produced = jnp.einsum(
         "snf,fd->snd", activated, down_weight[0], preferred_element_type=jnp.float32
     ).astype(jnp.bfloat16)
-    returned = lax.all_to_all(produced, "seq", split_axis=0, concat_axis=0, tiled=True)
+    returned = lax.all_to_all(produced, SEQ, split_axis=0, concat_axis=0, tiled=True)
     spread_weight = jnp.where(
         positions[:, None] == offsets[None, :], route_weight.reshape(-1)[None, :], 0.0
     )
     flat_returned = returned.reshape(-1, model_width)
     total = widened
     for _ in range(3):
-        part = spread_weight.astype(jnp.bfloat16)
-        total = total + jnp.dot(part, flat_returned, preferred_element_type=jnp.float32)
-        spread_weight = spread_weight - part.astype(jnp.float32)
+        part = lax.reduce_precision(spread_weight, exponent_bits=8, mantissa_bits=7)
+        total = total + jnp.dot(
+            part.astype(jnp.bfloat16), flat_returned, preferred_element_type=jnp.float32
+        )
+        spread_weight = spread_weight - part
     return total.astype(jnp.bfloat16)
 
 
 def solution(mesh):
+    fine = jax.sharding.Mesh(
+        mesh.devices.reshape(mesh.shape["dp"], 4, -1, 2),
+        ("dp",) + SEQ,
+    )
     placed = (
-        P(("dp", "seq"), None),
-        P(("dp", "seq"), None),
-        P(("dp", "seq"), None),
-        P(("dp", "seq"), None),
-        P(("dp", "seq"), None),
-        P("dp", "seq"),
-        P("dp", "seq"),
+        P(("dp",) + SEQ, None),
+        P(("dp",) + SEQ, None),
+        P(("dp",) + SEQ, None),
+        P(("dp",) + SEQ, None),
+        P(("dp",) + SEQ, None),
+        P("dp", SEQ),
+        P("dp", SEQ),
         P(),
-        P("seq", None),
-        P("seq", None, None),
-        P("seq", None, None),
-        P("seq", None, None),
+        P(SEQ, None),
+        P(SEQ, None, None),
+        P(SEQ, None, None),
+        P(SEQ, None, None),
     )
     return jax.shard_map(
-        shards, mesh=mesh, in_specs=placed, out_specs=P(("dp", "seq"), None), check_vma=False
+        shards, mesh=fine, in_specs=placed, out_specs=P(("dp",) + SEQ, None), check_vma=False
     )

time: 269 us -> 281 us (1.045)
  waiting for transfers between devices: 86.3 us -> 98.8 us
    all_gather x1 -> x2, waiting for transfers between devices: 0.02 us -> 30.5 us  [the longest x1 30.5 us: shards(): chips = lax.all_gather(out_weight, CHIP_AXES, axis=0, tiled=True)]
    ppermute x6, waiting for transfers between devices: 43.8 us -> 25.8 us  [shifted(): return lax.ppermute(part, axis, pairs)]
  transfers between devices with their start and end apart: 8 -> 9, of which waited for: 5 -> 6; matrix products, arithmetic and copies ran while one was open for 13% -> 13% of each run, Pallas kernels for 0% -> 0%
where the time goes in v3:
time: 281 us; the launch traced here: 280 us
  waiting for transfers between devices  98.8 us (35%)
  matrix products  53 us (19%)
  blocking collectives  51.9 us (18%)
  starting transfers between devices  39 us (14%)
  local copies, waits for them, and re-layouts  16 us (6%)
  between operations  13.9 us (5%)
  other arithmetic  7.14 us (3%)
    all_to_all x1, blocking collectives, shards(): lax.all_to_all(picked, SEQ, split_axis=0, concat_axis=0, tiled=True)  51.9 us
    all_to_all x1, waiting for transfers between devices, shards(): lax.all_to_all(produced, SEQ, split_axis=0, concat_axis=0, tiled=True)  41.8 us
    ppermute x6, starting transfers between devices, shifted(): return lax.ppermute(part, axis, pairs)  34 us
    all_gather x1, waiting for transfers between devices, shards(): chips = lax.all_gather(out_weight, CHIP_AXES, axis=0, tiled=True)  30.5 us
    ppermute x6, waiting for transfers between devices, shifted(): return lax.ppermute(part, axis, pairs)  25.8 us
    dot_general x3, matrix products, shards(): jnp.dot(part.astype(jnp.bfloat16), flat_returned, preferred_element_type=...  11.4 us
    dot_general x1, matrix products, shards(): jnp.einsum('tcbr,bcrd->td', normed.reshape(length, -1, cores, out_weight....  7.73 us
    dot_general x1, matrix products, shards(): jnp.einsum('hts,shd->thd', attend_weights, value_heads, preferred_element...  7.33 us
  transfers between devices with their start and end apart: 9, of which 6 were waited for; matrix products, arithmetic and copies ran while one was open for 13% of the time, Pallas kernels for 0%

profile of v3, /device:TPU:0, one launch (start us, length us, event | category | flops | bytes accessed | tf_op | source)
XLA Modules:
  0.0 279.8 jit_solution(9768696481974259690)
XLA Ops:
  6.5 0.7 all-gather.4.cloned.1.call-update
  7.3 0.7 copy_bitcast_fusion.1
  8.0 0.9 reduce-window.6
  8.9 0.2 slice_reduce_fusion
  9.1 0.1 copy_bitcast_fusion
  9.2 0.2 slice_reduce_fusion.1
  9.4 0.1 copy.125
  9.5 2.6 copy.130
  12.1 0.1 subtract_exponential_fusion
  12.2 2.5 fusion.96
  14.7 1.3 collective-permute-start
  16.1 1.5 collective-permute-done
  17.6 0.8 copy-done.5
  18.4 0.1 copy.121
  18.5 0.1 copy.126
  18.6 1.1 slice.118
  19.7 0.2 fusion.52
  19.9 0.8 fusion.68
  20.7 13.5 %collective-permute-start.1 = (bf16[2064,128]{1,0:T(8,128)(2,1)}, bf16[2064,128]{1,0:T(8,128)(2,1)}, u32[]{:S(2)}, u32[]{:S(2)}) collective-permute-start(bf16[2064,128]{1,0:T(8,128)(2,1)} %fusion.68), channel_id=1, source_target_pairs={{0,2},{1,3},{2,4},{3,5},{4,6},{5,7},{6,8},{7,9},{8,10},{9,11},{10,... | collective-permute-start | bytes 1585160 | tf_op jit(solution)/shard_map/ppermute | solution.py:16
  34.2 30.5 %all-gather.4.cloned.1.call-done = bf16[1024,2048]{1,0:T(8,128)(2,1)} async-done(((bf16[64,2048]{1,0:T(8,128)(2,1)}), bf16[1024,2048]{1,0:T(8,128)(2,1)}) %all-gather.4.cloned.1.call-update) | async-done | bytes 4194320 | tf_op jit(solution)/shard_map/all_gather | solution.py:110
  64.7 0.7 slice.121
  65.4 0.1 copy.122
  65.5 0.1 copy.127
  65.6 1.1 slice.120
  66.7 1.6 fusion.94
  68.3 4.2 %collective-permute-start.2 = (bf16[2064,128]{1,0:T(8,128)(2,1)S(1)}, bf16[2064,128]{1,0:T(8,128)(2,1)S(1)}, u32[]{:S(2)}, u32[]{:S(2)}) collective-permute-start(bf16[2064,128]{1,0:T(8,128)(2,1)S(1)} %fusion.69), channel_id=1, source_target_pairs={{0,4},{1,5},{2,6},{3,7},{4,8},{5,9},{6,10},{7,11},{8,12},{9,13},{1... | collective-permute-start | bytes 1585160 | tf_op jit(solution)/shard_map/ppermute | solution.py:16
  72.5 11.1 %collective-permute-done.2 = bf16[2064,128]{1,0:T(8,128)(2,1)S(1)} collective-permute-done((bf16[2064,128]{1,0:T(8,128)(2,1)S(1)}, bf16[2064,128]{1,0:T(8,128)(2,1)S(1)}, u32[]{:S(2)}, u32[]{:S(2)}) %collective-permute-start.2) | collective-permute-done | bytes 528416 | tf_op jit(solution)/shard_map/ppermute | solution.py:16
  83.6 0.8 copy-done.4
  84.4 0.1 copy.123
  84.6 0.1 copy.128
  84.7 1.2 slice.122
  85.9 0.2 fusion.53
  86.2 6.2 %collective-permute-start.3 = (bf16[2064,128]{1,0:T(8,128)(2,1)S(1)}, bf16[2064,128]{1,0:T(8,128)(2,1)S(1)}, u32[]{:S(2)}, u32[]{:S(2)}) collective-permute-start(bf16[2064,128]{1,0:T(8,128)(2,1)S(1)} %fusion.70), channel_id=1, source_target_pairs={{0,8},{1,9},{2,10},{3,11},{4,12},{5,13},{6,14},{7,15},{8,16},{9,17... | collective-permute-start | bytes 1585160 | tf_op jit(solution)/shard_map/ppermute | solution.py:16
  92.4 10.4 %collective-permute-done.3 = bf16[2064,128]{1,0:T(8,128)(2,1)S(1)} collective-permute-done((bf16[2064,128]{1,0:T(8,128)(2,1)S(1)}, bf16[2064,128]{1,0:T(8,128)(2,1)S(1)}, u32[]{:S(2)}, u32[]{:S(2)}) %collective-permute-start.3) | collective-permute-done | bytes 528416 | tf_op jit(solution)/shard_map/ppermute | solution.py:16
  102.8 0.8 copy-done.6
  103.7 0.1 copy.124
  103.8 0.1 copy.129
  103.9 1.1 slice.124
  105.0 0.3 fusion.48
  105.4 4.8 %collective-permute-start.4 = (bf16[2064,128]{1,0:T(8,128)(2,1)S(1)}, bf16[2064,128]{1,0:T(8,128)(2,1)}, u32[]{:S(2)}, u32[]{:S(2)}) collective-permute-start(bf16[2064,128]{1,0:T(8,128)(2,1)S(1)} %fusion.71), channel_id=1, source_target_pairs={{0,17},{1,18},{2,19},{3,20},{4,21},{5,22},{6,23},{7,24},{8,25},{9,... | collective-permute-start | bytes 1585160 | tf_op jit(solution)/shard_map/ppermute | solution.py:16
  110.2 3.9 %collective-permute-start.5 = (bf16[2064,128]{1,0:T(8,128)(2,1)S(1)}, bf16[2064,128]{1,0:T(8,128)(2,1)S(1)}, u32[]{:S(2)}, u32[]{:S(2)}) collective-permute-start(bf16[2064,128]{1,0:T(8,128)(2,1)S(1)} %fusion.71), channel_id=1, source_target_pairs={{0,1},{1,2},{2,3},{3,4},{4,5},{5,6},{6,7},{7,8},{8,9},{9,10},{10,1... | collective-permute-start | bytes 1585160 | tf_op jit(solution)/shard_map/ppermute | solution.py:16
  114.2 0.1 copy.118
  114.2 0.1 eq.29
  114.4 2.8 %collective-permute-done.4 = bf16[2064,128]{1,0:T(8,128)(2,1)} collective-permute-done((bf16[2064,128]{1,0:T(8,128)(2,1)S(1)}, bf16[2064,128]{1,0:T(8,128)(2,1)}, u32[]{:S(2)}, u32[]{:S(2)}) %collective-permute-start.4) | collective-permute-done | bytes 528416 | tf_op jit(solution)/shard_map/ppermute | solution.py:16
  117.2 1.1 slice.126
  118.3 1.2 copy.114
  119.5 1.2 copy.115
  120.7 0.2 fusion.74
  120.9 4.9 %fusion.23 = f32[16,128,384]{2,1,0:T(8,128)} fusion(f32[384,16]{0,1:T(8,128)S(1)} %get-tuple-element.24, f32[16,128,128]{1,2,0:T(8,128)} %copy.115, f32[16,128,128]{1,2,0:T(8,128)} %copy.114, f32[16]{0:T(128)S(1)} %fusion.74, bf16[384,2048]{1,0:T(8,128)(2,1)S(1)} %copy-done), kind=kOutput, calls=%fused_computation.34 | convolution fusion | flops 204472320 | bytes 6840384 | tf_op jit(solution)/shard_map/thd,hde->the/dot_general | solution.py:99
  125.8 7.3 %multiply_reduce_fusion = (f32[384,16]{0,1:T(8,128)S(1)}, f32[384,16,128]{0,2,1:T(8,128)}) fusion(f32[16,128,384]{2,1,0:T(8,128)} %fusion.23, f32[16,384]{1,0:T(8,128)S(1)} %get-tuple-element.21, pred[384,384]{1,0:T(8,128)(4,1)S(1)} %iota_compare_fusion.4, bf16[384,16,128]{0,2,1:T(8,128)(2,1)S(1)} %bitcast.143, bf16[384,2048]{1,0:T(8,128)(2,1)} %param.14, ...), kind=kOutput, calls=%fused_computation.26 | convolution fusion | flops 1224468480 | bytes 11206656 | tf_op jit(solution)/shard_map/hts,shd->thd/dot_general | solution.py:93
  133.2 2.3 multiply_convert_fusion.3
  135.6 7.7 %fusion.15 = (f32[384]{0:T(512)S(1)}, bf16[384,2048]{1,0:T(8,128)(2,1)S(1)}) fusion(bf16[2,16,64,2048]{3,2,1,0:T(8,128)(2,1)} %bitcast.161, bf16[384,16,2,64]{0,3,2,1:T(8,128)(2,1)S(1)} %bitcast.158, bf16[384,2048]{1,0:T(8,128)(2,1)} %param.15), kind=kOutput, calls=%fused_computation.16 | convolution fusion | flops 3225943552 | bytes 13108736 | tf_op jit(solution)/shard_map/tcbr,bcrd->td/dot_general | solution.py:113
  143.3 1.9 convolution_convert_fusion
  145.3 51.9 %all_to_all.10 = bf16[32,24,2048]{2,1,0:T(8,128)(2,1)S(1)} all-to-all(bf16[32,24,2048]{2,1,0:T(8,128)(2,1)S(1)} %bitcast.148), channel_id=1, replica_groups=mesh['dp'=4,'sy'=4,'sx'=4,'sc'=2] {'sy','sx','sc'}, dimensions={0} | all-to-all | bytes 6291456 | tf_op jit(solution)/shard_map/all_to_all | solution.py:129
  197.2 5.1 %fusion.2 = f32[32,24,1408]{2,1,0:T(8,128)S(1)} fusion(bf16[32,24,2048]{2,1,0:T(8,128)(2,1)S(1)} %all_to_all.10, bf16[1,2048,1408]{2,1,0:T(8,128)(2,1)S(1)} %bitcast.163), kind=kOutput, calls=%fused_computation.3 | convolution fusion | flops 4429185024 | bytes 13238272 | tf_op jit(solution)/shard_map/snd,df->snf/dot_general | solution.py:131
  202.3 5.8 %multiply_convert_fusion.2 = bf16[32,24,1408]{2,1,0:T(8,128)(2,1)S(1)} fusion(f32[32,24,1408]{2,1,0:T(8,128)S(1)} %fusion.2, bf16[32,24,2048]{2,1,0:T(8,128)(2,1)S(1)} %all_to_all.10, bf16[1,2048,1408]{2,1,0:T(8,128)(2,1)S(1)} %bitcast.165), kind=kOutput, calls=%fused_computation.12 | convolution fusion | flops 4435673088 | bytes 15400960 | tf_op jit(solution)/shard_map/snd,df->snf/dot_general | solution.py:130
  208.1 6.5 %fusion.10 = bf16[32,24,2048]{2,1,0:T(8,128)(2,1)} fusion(bf16[32,24,1408]{2,1,0:T(8,128)(2,1)S(1)} %multiply_convert_fusion.2, bf16[1,1408,2048]{2,1,0:T(8,128)(2,1)S(1)} %bitcast.167), kind=kOutput, calls=%fused_computation.14 | convolution fusion | flops 4430757888 | bytes 11075584 | tf_op jit(solution)/shard_map/snf,fd->snd/dot_general | solution.py:133
  214.6 5.0 %all-to-all-start.1 = ((bf16[32,24,2048]{2,1,0:T(8,128)(2,1)}), bf16[32,24,2048]{2,1,0:T(8,128)(2,1)}, u32[]{:S(2)}, u32[]{:S(2)}) async-start(bf16[32,24,2048]{2,1,0:T(8,128)(2,1)} %fusion.10), calls=%async_computation.1 | async-start | bytes 6291456 | tf_op jit(solution)/shard_map/all_to_all | solution.py:136
  219.6 0.1 copy.119
  219.6 0.1 broadcast_in_dim.21
  219.7 41.8 %all-to-all-done.1 = bf16[32,24,2048]{2,1,0:T(8,128)(2,1)} async-done(((bf16[32,24,2048]{2,1,0:T(8,128)(2,1)}), bf16[32,24,2048]{2,1,0:T(8,128)(2,1)}, u32[]{:S(2)}, u32[]{:S(2)}) %all-to-all-start.1) | async-done | bytes 3145760 | tf_op jit(solution)/shard_map/all_to_all | solution.py:136
  261.5 3.3 %fusion.56 = f32[384,2048]{1,0:T(8,128)S(1)} fusion(bf16[768,2048]{1,0:T(8,128)(2,1)} %bitcast.29, f32[768]{0:T(1024)S(1)} %broadcast_in_dim.21, s32[768]{0:T(1024)S(1)} %eq.29), kind=kOutput, calls=%fused_computation.71 | convolution fusion | flops 1209139200 | bytes 6297600 | tf_op jit(solution)/shard_map/dot_general | solution.py:144
  264.8 3.4 %fusion.55 = f32[384,2048]{1,0:T(8,128)S(1)} fusion(bf16[768,2048]{1,0:T(8,128)(2,1)} %bitcast.29, f32[768]{0:T(1024)S(1)} %broadcast_in_dim.21, s32[768]{0:T(1024)S(1)} %eq.29), kind=kOutput, calls=%fused_computation.70 | convolution fusion | flops 1209729024 | bytes 6297600 | tf_op jit(solution)/shard_map/dot_general | solution.py:144
  268.3 4.7 %fusion.20 = bf16[384,2048]{1,0:T(8,128)(2,1)} fusion(f32[384,2048]{1,0:T(8,128)S(1)} %fusion.55, f32[384,2048]{1,0:T(8,128)S(1)} %fusion.56, bf16[384,2048]{1,0:T(8,128)(2,1)S(1)} %copy-done.11, bf16[768,2048]{1,0:T(8,128)(2,1)} %bitcast.29, f32[768]{0:T(1024)S(1)} %broadcast_in_dim.21, s32[768]{0:T(1024)S(1)} %eq.29), kind=kOutput, calls=%fused_computation.21 | convolution fusion | flops 1214251008 | bytes 12589056 | tf_op jit(solution)/shard_map/dot_general | solution.py:144
  (77 shorter events, 0.7 us)
Async XLA Ops:
  6.5 114.4 %copy-start = (bf16[384,2048]{1,0:T(8,128)(2,1)S(1)}, bf16[384,2048]{1,0:T(8,128)(2,1)}, u32[]{:S(2)}) copy-start(bf16[384,2048]{1,0:T(8,128)(2,1)} %param.12) | copy-start | bytes 4718596
  6.5 58.1 %all-gather.4.cloned.1.call-start = ((), (), s32[]{:S(2)}) async-start(), calls=%async_computation.2 | async-start | bytes 4456448 | tf_op jit(solution)/shard_map/all_gather | solution.py:110
  7.3 128.3 %all-gather.6.cloned.1.call-start = ((), (), s32[]{:S(2)}) async-start(), calls=%async_computation.3 | async-start | bytes 12582912 | tf_op jit(solution)/shard_map/all_gather | solution.py:111
  14.7 6.0 %copy-start.2 = (f32[16,128,128]{2,1,0:T(8,128)}, f32[16,128,128]{2,1,0:T(8,128)S(1)}, u32[]{:S(2)}) copy-start(f32[16,128,128]{2,1,0:T(8,128)S(1)} %get-tuple-element.38) | copy-start | bytes 3145732
  14.7 2.8 %collective-permute-start = (bf16[2064,128]{1,0:T(8,128)(2,1)S(1)}, bf16[2064,128]{1,0:T(8,128)(2,1)S(1)}, u32[]{:S(2)}, u32[]{:S(2)}) collective-permute-start(bf16[2064,128]{1,0:T(8,128)(2,1)S(1)} %fusion.67), channel_id=1, source_target_pairs={{0,1},{1,2},{2,3},{3,4},{4,5},{5,6},{6,7},{7,8},{8,9},{9,10},{10,1... | collective-permute-start | bytes 1585160 | tf_op jit(solution)/shard_map/ppermute | solution.py:16
  17.6 0.8 copy-start.5
  20.7 43.9 %collective-permute-start.1 = (bf16[2064,128]{1,0:T(8,128)(2,1)}, bf16[2064,128]{1,0:T(8,128)(2,1)}, u32[]{:S(2)}, u32[]{:S(2)}) collective-permute-start(bf16[2064,128]{1,0:T(8,128)(2,1)} %fusion.68), channel_id=1, source_target_pairs={{0,2},{1,3},{2,4},{3,5},{4,6},{5,7},{6,8},{7,9},{8,10},{9,11},{10,... | collective-permute-start | bytes 1585160 | tf_op jit(solution)/shard_map/ppermute | solution.py:16
  68.3 15.3 %collective-permute-start.2 = (bf16[2064,128]{1,0:T(8,128)(2,1)S(1)}, bf16[2064,128]{1,0:T(8,128)(2,1)S(1)}, u32[]{:S(2)}, u32[]{:S(2)}) collective-permute-start(bf16[2064,128]{1,0:T(8,128)(2,1)S(1)} %fusion.69), channel_id=1, source_target_pairs={{0,4},{1,5},{2,6},{3,7},{4,8},{5,9},{6,10},{7,11},{8,12},{9,13},{1... | collective-permute-start | bytes 1585160 | tf_op jit(solution)/shard_map/ppermute | solution.py:16
  83.6 0.8 copy-start.4
  86.2 16.6 %collective-permute-start.3 = (bf16[2064,128]{1,0:T(8,128)(2,1)S(1)}, bf16[2064,128]{1,0:T(8,128)(2,1)S(1)}, u32[]{:S(2)}, u32[]{:S(2)}) collective-permute-start(bf16[2064,128]{1,0:T(8,128)(2,1)S(1)} %fusion.70), channel_id=1, source_target_pairs={{0,8},{1,9},{2,10},{3,11},{4,12},{5,13},{6,14},{7,15},{8,16},{9,17... | collective-permute-start | bytes 1585160 | tf_op jit(solution)/shard_map/ppermute | solution.py:16
  102.8 0.8 copy-start.6
  103.9 10.3 %copy-start.8 = (s32[32,24]{0,1:T(8,128)S(1)}, s32[32,24]{0,1:T(8,128)}, u32[]{:S(2)}) copy-start(s32[32,24]{0,1:T(8,128)} %param.17) | copy-start | bytes 9220
  105.4 11.8 %collective-permute-start.4 = (bf16[2064,128]{1,0:T(8,128)(2,1)S(1)}, bf16[2064,128]{1,0:T(8,128)(2,1)}, u32[]{:S(2)}, u32[]{:S(2)}) collective-permute-start(bf16[2064,128]{1,0:T(8,128)(2,1)S(1)} %fusion.71), channel_id=1, source_target_pairs={{0,17},{1,18},{2,19},{3,20},{4,21},{5,22},{6,23},{7,24},{8,25},{9,... | collective-permute-start | bytes 1585160 | tf_op jit(solution)/shard_map/ppermute | solution.py:16
  110.2 9.3 %collective-permute-start.5 = (bf16[2064,128]{1,0:T(8,128)(2,1)S(1)}, bf16[2064,128]{1,0:T(8,128)(2,1)S(1)}, u32[]{:S(2)}, u32[]{:S(2)}) collective-permute-start(bf16[2064,128]{1,0:T(8,128)(2,1)S(1)} %fusion.71), channel_id=1, source_target_pairs={{0,1},{1,2},{2,3},{3,4},{4,5},{5,6},{6,7},{7,8},{8,9},{9,10},{10,1... | collective-permute-start | bytes 1585160 | tf_op jit(solution)/shard_map/ppermute | solution.py:16
  120.9 4.9 %copy-start.3 = (bf16[384,2048]{0,1:T(8,128)(2,1)S(1)}, bf16[384,2048]{0,1:T(8,128)(2,1)}, u32[]{:S(2)}) copy-start(bf16[384,2048]{0,1:T(8,128)(2,1)} %copy.130) | copy-start | bytes 4718596
  133.1 64.0 %slice-start = ((s8[5767168]{0:T(1024)(128)(4,1)}), s8[1572864]{0:T(1024)(128)(4,1)S(1)}, s32[]{:S(2)}) async-start(s8[5767168]{0:T(1024)(128)(4,1)} %bitcast.162), calls=%async_computation.4 | async-start | bytes 3145728
  135.5 7.8 %copy-start.9 = (f32[2048]{0:T(1024)S(1)}, f32[2048]{0:T(1024)}, u32[]{:S(2)}) copy-start(f32[2048]{0:T(1024)} %param.19) | copy-start | bytes 24580
  135.5 61.6 %slice-start.1 = ((s8[5767168]{0:T(1024)(128)(4,1)}), s8[4194304]{0:T(1024)(128)(4,1)S(1)}, s32[]{:S(2)}) async-start(s8[5767168]{0:T(1024)(128)(4,1)} %bitcast.162), calls=%async_computation.5 | async-start | bytes 8388608
  143.3 1.9 copy-start.10
  145.2 57.0 %slice-start.2 = ((s8[5767168]{0:T(1024)(128)(4,1)}), s8[4194304]{0:T(1024)(128)(4,1)S(1)}, s32[]{:S(2)}) async-start(s8[5767168]{0:T(1024)(128)(4,1)} %bitcast.164), calls=%async_computation.6 | async-start | bytes 8388608
  197.2 5.1 %slice-start.3 = ((s8[5767168]{0:T(1024)(128)(4,1)}), s8[1572864]{0:T(1024)(128)(4,1)S(1)}, s32[]{:S(2)}) async-start(s8[5767168]{0:T(1024)(128)(4,1)} %bitcast.164), calls=%async_computation.7 | async-start | bytes 3145728
  197.2 10.9 %slice-start.4 = ((s8[5767168]{0:T(1024)(128)(4,1)}), s8[4194304]{0:T(1024)(128)(4,1)S(1)}, s32[]{:S(2)}) async-start(s8[5767168]{0:T(1024)(128)(4,1)} %bitcast.166), calls=%async_computation.8 | async-start | bytes 8388608
  202.3 5.8 %slice-start.5 = ((s8[5767168]{0:T(1024)(128)(4,1)}), s8[1572864]{0:T(1024)(128)(4,1)S(1)}, s32[]{:S(2)}) async-start(s8[5767168]{0:T(1024)(128)(4,1)} %bitcast.166), calls=%async_computation.9 | async-start | bytes 3145728
  214.6 5.0 %copy-start.7 = (f32[32,24]{0,1:T(8,128)S(1)}, f32[32,24]{0,1:T(8,128)}, u32[]{:S(2)}) copy-start(f32[32,24]{0,1:T(8,128)} %param.18) | copy-start | bytes 9220
  214.6 47.0 %all-to-all-start.1 = ((bf16[32,24,2048]{2,1,0:T(8,128)(2,1)}), bf16[32,24,2048]{2,1,0:T(8,128)(2,1)}, u32[]{:S(2)}, u32[]{:S(2)}) async-start(bf16[32,24,2048]{2,1,0:T(8,128)(2,1)} %fusion.10), calls=%async_computation.1 | async-start | bytes 6291456 | tf_op jit(solution)/shard_map/all_to_all | solution.py:136
  264.8 3.4 %copy-start.11 = (bf16[384,2048]{1,0:T(8,128)(2,1)S(1)}, bf16[384,2048]{1,0:T(8,128)(2,1)}, u32[]{:S(2)}) copy-start(bf16[384,2048]{1,0:T(8,128)(2,1)} %copy-done.10) | copy-start | bytes 4718596
  268.2 4.7 %copy-start.1 = (bf16[384,2048]{1,0:T(8,128)(2,1)S(1)}, bf16[384,2048]{1,0:T(8,128)(2,1)}, u32[]{:S(2)}) copy-start(bf16[384,2048]{1,0:T(8,128)(2,1)} %param.12) | copy-start | bytes 4718596
Sparse Core Ops, SparseCore 0:
  9.5 55.1 all-gather.3
  66.3 24.6 all-gather.5

commit v4 on v3

--- a/solution.py
+++ b/solution.py
@@ -6,6 +6,7 @@
 SEQ = ("sy", "sx", "sc")
 CHIP_AXES = ("sy", "sx")
 CORE_AXIS = "sc"
+CHUNKS = 2
 
 
 def carried_in(state, ending, axis):
@@ -107,13 +108,9 @@
     normed = (
         (unnormed * lax.rsqrt(spread + 1e-06)).astype(jnp.bfloat16).reshape(length, model_width)
     )
-    chips = lax.all_gather(out_weight, CHIP_AXES, axis=0, tiled=True)
-    gathered = lax.all_gather(chips, CORE_AXIS, axis=0)
-    cores = gathered.shape[0]
-    attended = jnp.einsum(
-        "tcbr,bcrd->td",
-        normed.reshape(length, -1, cores, out_weight.shape[0]),
-        gathered.reshape(cores, -1, out_weight.shape[0], model_width),
+    attended = jnp.dot(
+        normed,
+        lax.all_gather(out_weight, SEQ, axis=0, tiled=True),
         preferred_element_type=jnp.float32,
     )
     residual = (stream.astype(jnp.float32) + attended).astype(jnp.bfloat16)
@@ -126,25 +123,32 @@
     choose = (offsets[:, None] == positions[None, :]).astype(jnp.bfloat16)
     picked = jnp.dot(choose, mixed_in, preferred_element_type=jnp.float32).astype(jnp.bfloat16)
     picked = picked.reshape(token_index.shape + (model_width,))
-    arrived = lax.all_to_all(picked, SEQ, split_axis=0, concat_axis=0, tiled=True)
-    gating = jnp.einsum("snd,df->snf", arrived, gate_weight[0], preferred_element_type=jnp.float32)
-    upward = jnp.einsum("snd,df->snf", arrived, up_weight[0], preferred_element_type=jnp.float32)
-    activated = (jax.nn.silu(gating) * upward).astype(jnp.bfloat16)
-    produced = jnp.einsum(
-        "snf,fd->snd", activated, down_weight[0], preferred_element_type=jnp.float32
-    ).astype(jnp.bfloat16)
-    returned = lax.all_to_all(produced, SEQ, split_axis=0, concat_axis=0, tiled=True)
     spread_weight = jnp.where(
         positions[:, None] == offsets[None, :], route_weight.reshape(-1)[None, :], 0.0
-    )
-    flat_returned = returned.reshape(-1, model_width)
+    ).reshape((length,) + token_index.shape)
+    slots = token_index.shape[1]
+    step = slots // CHUNKS
     total = widened
-    for _ in range(3):
-        part = lax.reduce_precision(spread_weight, exponent_bits=8, mantissa_bits=7)
-        total = total + jnp.dot(
-            part.astype(jnp.bfloat16), flat_returned, preferred_element_type=jnp.float32
+    for chunk in range(CHUNKS):
+        window = slice(chunk * step, (chunk + 1) * step)
+        arrived = lax.all_to_all(picked[:, window], SEQ, split_axis=0, concat_axis=0, tiled=True)
+        gating = jnp.einsum(
+            "snd,df->snf", arrived, gate_weight[0], preferred_element_type=jnp.float32
         )
-        spread_weight = spread_weight - part
+        upward = jnp.einsum("snd,df->snf", arrived, up_weight[0], preferred_element_type=jnp.float32)
+        activated = (jax.nn.silu(gating) * upward).astype(jnp.bfloat16)
+        produced = jnp.einsum(
+            "snf,fd->snd", activated, down_weight[0], preferred_element_type=jnp.float32
+        ).astype(jnp.bfloat16)
+        returned = lax.all_to_all(produced, SEQ, split_axis=0, concat_axis=0, tiled=True)
+        flat_returned = returned.reshape(-1, model_width)
+        remaining = spread_weight[:, :, window].reshape(length, -1)
+        for _ in range(3):
+            part = lax.reduce_precision(remaining, exponent_bits=8, mantissa_bits=7)
+            total = total + jnp.dot(
+                part.astype(jnp.bfloat16), flat_returned, preferred_element_type=jnp.float32
+            )
+            remaining = remaining - part
     return total.astype(jnp.bfloat16)
 
 

time: 281 us -> 310 us (1.10); the launches traced: 280 us -> 305 us
  blocking collectives: 51.9 us -> 0 us
  matrix products: 53 us -> 86 us
  starting transfers between devices: 39 us -> 60 us
  waiting for transfers between devices: 98.8 us -> 115 us
  local copies, waits for them, and re-layouts: 16 us -> 23.3 us
    all_to_all x1 -> x0, blocking collectives: 51.9 us -> none  [shards(): lax.all_to_all(picked, SEQ, split_axis=0, concat_axis=0, tiled=True)]
    all_to_all x0 -> x2, waiting for transfers between devices: none -> 39.1 us  [shards(): lax.all_to_all(picked[:, window], SEQ, split_axis=0, concat_axis=0, tiled...]
    all_gather x2 -> x1, waiting for transfers between devices: 30.5 us -> 0.02 us  [shards(): lax.all_gather(out_weight, SEQ, axis=0, tiled=True)]
    ppermute x6, waiting for transfers between devices: 25.8 us -> 49.8 us  [shifted(): return lax.ppermute(part, axis, pairs)]
    all_to_all x1 -> x2, waiting for transfers between devices: 41.8 us -> 25.5 us  [shards(): lax.all_to_all(produced, SEQ, split_axis=0, concat_axis=0, tiled=True)]
    dot_general x1 -> x2, matrix products: 6.51 us -> 21.8 us  [shards(): jnp.einsum('snf,fd->snd', activated, down_weight[0], preferred_element_ty...]
    all_to_all x0 -> x2, starting transfers between devices: none -> 14.4 us  [shards(): lax.all_to_all(picked[:, window], SEQ, split_axis=0, concat_axis=0, tiled...]
    dot_general x3 -> x6, matrix products: 11.4 us -> 25.3 us  [shards(): jnp.dot(part.astype(jnp.bfloat16), flat_returned, preferred_element_type=...]
  transfers between devices with their start and end apart: 9 -> 11, of which waited for: 6 -> 9; matrix products, arithmetic and copies ran while one was open for 13% -> 29% of each run, Pallas kernels for 0% -> 0%
where the time goes in v4:
time: 310 us; the launch traced here: 305 us
  waiting for transfers between devices  115 us (37%)
  matrix products  86 us (28%)
  starting transfers between devices  60 us (19%)
  local copies, waits for them, and re-layouts  23.3 us (8%)
  between operations  14.2 us (5%)
  other arithmetic  6.63 us (2%)
    ppermute x6, waiting for transfers between devices, shifted(): return lax.ppermute(part, axis, pairs)  49.8 us
    all_to_all x2, waiting for transfers between devices, shards(): lax.all_to_all(picked[:, window], SEQ, split_axis=0, concat_axis=0, tiled...  39.1 us
    ppermute x6, starting transfers between devices, shifted(): return lax.ppermute(part, axis, pairs)  35.5 us
    all_to_all x2, waiting for transfers between devices, shards(): lax.all_to_all(produced, SEQ, split_axis=0, concat_axis=0, tiled=True)  25.5 us
    dot_general x6, matrix products, shards(): jnp.dot(part.astype(jnp.bfloat16), flat_returned, preferred_element_type=...  25.3 us
    dot_general x2, matrix products, shards(): jnp.einsum('snf,fd->snd', activated, down_weight[0], preferred_element_ty...  21.8 us
    dot_general x2, matrix products, shards(): jnp.einsum('snd,df->snf', arrived, gate_weight[0], preferred_element_type...  15 us
    all_to_all x2, starting transfers between devices, shards(): lax.all_to_all(picked[:, window], SEQ, split_axis=0, concat_axis=0, tiled...  14.4 us
  transfers between devices with their start and end apart: 11, of which 9 were waited for; matrix products, arithmetic and copies ran while one was open for 29% of the time, Pallas kernels for 0%

profile of v4, /device:TPU:0, one launch (start us, length us, event | category | flops | bytes accessed | tf_op | source)
XLA Modules:
  0.0 305.1 jit_solution(12988099493214784519)
XLA Ops:
  6.5 0.7 all-gather.2.cloned.1.call-update
  7.3 0.7 copy_bitcast_fusion.1
  8.0 0.9 reduce-window.6
  8.9 0.2 slice_reduce_fusion
  9.1 0.2 slice_reduce_fusion.1
  9.4 2.6 copy.150
  12.1 2.5 fusion.134
  14.7 1.3 collective-permute-start
  16.0 1.5 collective-permute-done
  17.5 0.8 copy-done.5
  18.3 0.1 copy.141
  18.6 1.1 slice.134
  19.6 0.2 fusion.96
  19.9 12.7 %collective-permute-start.1 = (bf16[2064,128]{1,0:T(8,128)(2,1)S(1)}, bf16[2064,128]{1,0:T(8,128)(2,1)S(1)}, u32[]{:S(2)}, u32[]{:S(2)}) collective-permute-start(bf16[2064,128]{1,0:T(8,128)(2,1)S(1)} %fusion.104), channel_id=1, source_target_pairs={{0,2},{1,3},{2,4},{3,5},{4,6},{5,7},{6,8},{7,9},{8,10},{9,11},{10,... | collective-permute-start | bytes 1585160 | tf_op jit(solution)/shard_map/ppermute | solution.py:17
  32.6 11.6 %collective-permute-done.1 = bf16[2064,128]{1,0:T(8,128)(2,1)S(1)} collective-permute-done((bf16[2064,128]{1,0:T(8,128)(2,1)S(1)}, bf16[2064,128]{1,0:T(8,128)(2,1)S(1)}, u32[]{:S(2)}, u32[]{:S(2)}) %collective-permute-start.1) | collective-permute-done | bytes 528416 | tf_op jit(solution)/shard_map/ppermute | solution.py:17
  44.2 0.1 copy.142
  44.4 1.6 fusion.131
  46.1 5.2 %collective-permute-start.2 = (bf16[2064,128]{1,0:T(8,128)(2,1)S(1)}, bf16[2064,128]{1,0:T(8,128)(2,1)S(1)}, u32[]{:S(2)}, u32[]{:S(2)}) collective-permute-start(bf16[2064,128]{1,0:T(8,128)(2,1)S(1)} %fusion.105), channel_id=1, source_target_pairs={{0,4},{1,5},{2,6},{3,7},{4,8},{5,9},{6,10},{7,11},{8,12},{9,13},{1... | collective-permute-start | bytes 1585160 | tf_op jit(solution)/shard_map/ppermute | solution.py:17
  51.3 20.6 %collective-permute-done.2 = bf16[2064,128]{1,0:T(8,128)(2,1)S(1)} collective-permute-done((bf16[2064,128]{1,0:T(8,128)(2,1)S(1)}, bf16[2064,128]{1,0:T(8,128)(2,1)S(1)}, u32[]{:S(2)}, u32[]{:S(2)}) %collective-permute-start.2) | collective-permute-done | bytes 528416 | tf_op jit(solution)/shard_map/ppermute | solution.py:17
  71.9 0.9 copy-done.4
  73.0 1.1 slice.138
  74.1 0.2 fusion.97
  74.4 5.6 %collective-permute-start.3 = (bf16[2064,128]{1,0:T(8,128)(2,1)S(1)}, bf16[2064,128]{1,0:T(8,128)(2,1)S(1)}, u32[]{:S(2)}, u32[]{:S(2)}) collective-permute-start(bf16[2064,128]{1,0:T(8,128)(2,1)S(1)} %fusion.106), channel_id=1, source_target_pairs={{0,8},{1,9},{2,10},{3,11},{4,12},{5,13},{6,14},{7,15},{8,16},{9,17... | collective-permute-start | bytes 1585160 | tf_op jit(solution)/shard_map/ppermute | solution.py:17
  80.0 10.0 %collective-permute-done.3 = bf16[2064,128]{1,0:T(8,128)(2,1)S(1)} collective-permute-done((bf16[2064,128]{1,0:T(8,128)(2,1)S(1)}, bf16[2064,128]{1,0:T(8,128)(2,1)S(1)}, u32[]{:S(2)}, u32[]{:S(2)}) %collective-permute-start.3) | collective-permute-done | bytes 528416 | tf_op jit(solution)/shard_map/ppermute | solution.py:17
  90.0 0.9 copy-done.6
  91.0 0.1 copy.149
  91.1 1.1 slice.140
  92.2 0.3 fusion.81
  92.6 1.3 collective-permute-start.5
  94.0 9.3 %collective-permute-start.4 = (bf16[2064,128]{1,0:T(8,128)(2,1)S(1)}, bf16[2064,128]{1,0:T(8,128)(2,1)}, u32[]{:S(2)}, u32[]{:S(2)}) collective-permute-start(bf16[2064,128]{1,0:T(8,128)(2,1)S(1)} %fusion.107), channel_id=1, source_target_pairs={{0,17},{1,18},{2,19},{3,20},{4,21},{5,22},{6,23},{7,24},{8,25},{9,... | collective-permute-start | bytes 1585160 | tf_op jit(solution)/shard_map/ppermute | solution.py:17
  103.6 1.2 copy.126
  104.8 6.1 %collective-permute-done.4 = bf16[2064,128]{1,0:T(8,128)(2,1)} collective-permute-done((bf16[2064,128]{1,0:T(8,128)(2,1)S(1)}, bf16[2064,128]{1,0:T(8,128)(2,1)}, u32[]{:S(2)}, u32[]{:S(2)}) %collective-permute-start.4) | collective-permute-done | bytes 528416 | tf_op jit(solution)/shard_map/ppermute | solution.py:17
  110.9 1.1 slice.142
  112.0 1.2 copy.125
  113.2 0.2 fusion.112
  113.4 5.1 %fusion.44 = f32[16,128,384]{2,1,0:T(8,128)} fusion(f32[384,16]{0,1:T(8,128)S(1)} %get-tuple-element.26, f32[16,128,128]{1,2,0:T(8,128)} %copy.126, f32[16,128,128]{1,2,0:T(8,128)} %copy.125, f32[16]{0:T(128)S(1)} %fusion.112, bf16[384,2048]{1,0:T(8,128)(2,1)S(1)} %copy-done), kind=kOutput, calls=%fused_computation.42 | convolution fusion | flops 204472320 | bytes 6840384 | tf_op jit(solution)/shard_map/thd,hde->the/dot_general | solution.py:100
  118.5 7.3 %multiply_reduce_fusion = (f32[384,16]{0,1:T(8,128)S(1)}, f32[384,16,128]{0,2,1:T(8,128)}) fusion(f32[16,128,384]{2,1,0:T(8,128)} %fusion.44, f32[16,384]{1,0:T(8,128)S(1)} %get-tuple-element.23, pred[384,384]{1,0:T(8,128)(4,1)S(1)} %iota_compare_fusion.4, bf16[384,16,128]{0,2,1:T(8,128)(2,1)S(1)} %bitcast.160, bf16[384,2048]{1,0:T(8,128)(2,1)} %param.14, ...), kind=kOutput, calls=%fused_computation.32 | convolution fusion | flops 1224468480 | bytes 11206656 | tf_op jit(solution)/shard_map/hts,shd->thd/dot_general | solution.py:94
  125.8 2.3 multiply_convert_fusion.2
  128.3 7.2 %fusion.16 = (f32[384]{0:T(512)S(1)}, bf16[384,2048]{1,0:T(8,128)(2,1)S(1)}) fusion(bf16[384,2048]{0,1:T(8,128)(2,1)S(1)} %bitcast.175, bf16[2048,2048]{1,0:T(8,128)(2,1)} %all-gather.2.cloned.1.call-done, bf16[384,2048]{1,0:T(8,128)(2,1)S(1)} %copy-done.9), kind=kOutput, calls=%fused_computation.20 | convolution fusion | flops 3225943552 | bytes 13108736 | tf_op jit(solution)/shard_map/dot_general | solution.py:111
  135.4 1.9 convolution_convert_fusion
  137.4 3.0 fusion.133
  140.4 9.5 %all-to-all-start = ((bf16[32,12,2048]{2,1,0:T(8,128)(2,1)}), bf16[32,12,2048]{2,1,0:T(8,128)(2,1)}, u32[]{:S(2)}, u32[]{:S(2)}) async-start(bf16[32,12,2048]{2,1,0:T(8,128)(2,1)} %get-tuple-element.21), calls=%async_computation | async-start | bytes 4194304 | tf_op jit(solution)/shard_map/all_to_all | solution.py:134
  149.9 0.3 fusion.60
  150.2 29.8 %all-to-all-done = bf16[32,12,2048]{2,1,0:T(8,128)(2,1)} async-done(((bf16[32,12,2048]{2,1,0:T(8,128)(2,1)}), bf16[32,12,2048]{2,1,0:T(8,128)(2,1)}, u32[]{:S(2)}, u32[]{:S(2)}) %all-to-all-start) | async-done | bytes 1572896 | tf_op jit(solution)/shard_map/all_to_all | solution.py:134
  179.9 4.9 %all-to-all-start.2 = ((bf16[32,12,2048]{2,1,0:T(8,128)(2,1)}), bf16[32,12,2048]{2,1,0:T(8,128)(2,1)}, u32[]{:S(2)}, u32[]{:S(2)}) async-start(bf16[32,12,2048]{2,1,0:T(8,128)(2,1)} %get-tuple-element.22), calls=%async_computation.2 | async-start | bytes 4194304 | tf_op jit(solution)/shard_map/all_to_all | solution.py:134
  184.8 7.5 %fusion.10 = f32[32,12,1408]{2,0,1:T(8,128)} fusion(bf16[1,2048,1408]{2,1,0:T(8,128)(2,1)} %param.21, bf16[32,12,2048]{2,1,0:T(8,128)(2,1)} %all-to-all-done), kind=kOutput, calls=%fused_computation.11 | convolution fusion | flops 2214592512 | bytes 9502720 | tf_op jit(solution)/shard_map/snd,df->snf/dot_general | solution.py:135
  192.3 10.9 %fusion.37 = bf16[32,12,2048]{2,0,1:T(8,128)(2,1)S(1)} fusion(bf16[1,1408,2048]{2,1,0:T(8,128)(2,1)} %param.23, bf16[1,2048,1408]{2,1,0:T(8,128)(2,1)} %param.22, f32[32,12,1408]{2,0,1:T(8,128)} %fusion.10, bf16[32,12,2048]{2,1,0:T(8,128)(2,1)} %all-to-all-done), kind=kOutput, calls=%fused_computation.39 | convolution fusion | flops 4433215488 | bytes 16842752 | tf_op jit(solution)/shard_map/snf,fd->snd/dot_general | solution.py:140
  203.2 2.3 copy.131
  205.5 9.4 %all-to-all-done.2 = bf16[32,12,2048]{2,1,0:T(8,128)(2,1)} async-done(((bf16[32,12,2048]{2,1,0:T(8,128)(2,1)}), bf16[32,12,2048]{2,1,0:T(8,128)(2,1)}, u32[]{:S(2)}, u32[]{:S(2)}) %all-to-all-start.2) | async-done | bytes 1572896 | tf_op jit(solution)/shard_map/all_to_all | solution.py:134
  214.9 5.0 %all-to-all-start.1 = ((bf16[32,12,2048]{2,1,0:T(8,128)(2,1)}), bf16[32,12,2048]{2,1,0:T(8,128)(2,1)}, u32[]{:S(2)}, u32[]{:S(2)}) async-start(bf16[32,12,2048]{2,1,0:T(8,128)(2,1)} %copy.131), calls=%async_computation.1 | async-start | bytes 4194304 | tf_op jit(solution)/shard_map/all_to_all | solution.py:143
  219.9 7.5 %fusion.8 = f32[32,12,1408]{2,0,1:T(8,128)} fusion(bf16[1,2048,1408]{2,1,0:T(8,128)(2,1)} %param.21, bf16[32,12,2048]{2,1,0:T(8,128)(2,1)} %all-to-all-done.2), kind=kOutput, calls=%fused_computation.9 | convolution fusion | flops 2214592512 | bytes 9502720 | tf_op jit(solution)/shard_map/snd,df->snf/dot_general | solution.py:135
  227.3 10.9 %fusion.40 = bf16[32,12,2048]{2,0,1:T(8,128)(2,1)S(1)} fusion(bf16[1,1408,2048]{2,1,0:T(8,128)(2,1)} %param.23, bf16[1,2048,1408]{2,1,0:T(8,128)(2,1)} %param.22, f32[32,12,1408]{2,0,1:T(8,128)} %fusion.8, bf16[32,12,2048]{2,1,0:T(8,128)(2,1)} %all-to-all-done.2), kind=kOutput, calls=%fused_computation.40 | convolution fusion | flops 4433215488 | bytes 16842752 | tf_op jit(solution)/shard_map/snf,fd->snd/dot_general | solution.py:140
  238.2 2.2 copy.137
  240.5 9.4 %all-to-all-done.1 = bf16[32,12,2048]{2,1,0:T(8,128)(2,1)} async-done(((bf16[32,12,2048]{2,1,0:T(8,128)(2,1)}), bf16[32,12,2048]{2,1,0:T(8,128)(2,1)}, u32[]{:S(2)}, u32[]{:S(2)}) %all-to-all-start.1) | async-done | bytes 1572896 | tf_op jit(solution)/shard_map/all_to_all | solution.py:143
  249.9 5.0 %all-to-all-start.3 = ((bf16[32,12,2048]{2,1,0:T(8,128)(2,1)}), bf16[32,12,2048]{2,1,0:T(8,128)(2,1)}, u32[]{:S(2)}, u32[]{:S(2)}) async-start(bf16[32,12,2048]{2,1,0:T(8,128)(2,1)} %copy.137), calls=%async_computation.3 | async-start | bytes 4194304 | tf_op jit(solution)/shard_map/all_to_all | solution.py:143
  254.9 4.7 %fusion.94 = f32[384,2048,1]{1,0,2:T(8,128)} fusion(bf16[32,12,2048]{2,1,0:T(8,128)(2,1)} %all-to-all-done.1, f32[384,32,24]{0,1,2:T(8,128)S(1)} %fusion.60), kind=kOutput, calls=%fused_computation.97 | convolution fusion | flops 604274688 | bytes 5308416 | tf_op jit(solution)/shard_map/dot_general | solution.py:148
  259.6 4.7 %fusion.92 = f32[384,2048,1]{1,0,2:T(8,128)} fusion(bf16[32,12,2048]{2,1,0:T(8,128)(2,1)} %all-to-all-done.1, f32[384,32,24]{0,1,2:T(8,128)S(1)} %fusion.60), kind=kOutput, calls=%fused_computation.95 | convolution fusion | flops 604569600 | bytes 5308416 | tf_op jit(solution)/shard_map/dot_general | solution.py:148
  264.3 4.6 %fusion.90 = f32[384,2048,1]{1,0,2:T(8,128)} fusion(bf16[32,12,2048]{2,1,0:T(8,128)(2,1)} %all-to-all-done.1, f32[384,32,24]{0,1,2:T(8,128)S(1)} %fusion.60), kind=kOutput, calls=%fused_computation.93 | convolution fusion | flops 604864512 | bytes 5308416 | tf_op jit(solution)/shard_map/dot_general | solution.py:148
  268.9 16.1 %all-to-all-done.3 = bf16[32,12,2048]{2,1,0:T(8,128)(2,1)} async-done(((bf16[32,12,2048]{2,1,0:T(8,128)(2,1)}), bf16[32,12,2048]{2,1,0:T(8,128)(2,1)}, u32[]{:S(2)}, u32[]{:S(2)}) %all-to-all-start.3) | async-done | bytes 1572896 | tf_op jit(solution)/shard_map/all_to_all | solution.py:143
  285.0 3.0 fusion.86
  288.0 3.1 %fusion.88 = f32[384,2048,1]{1,0,2:T(8,128)S(1)} fusion(bf16[32,12,2048]{2,1,0:T(8,128)(2,1)} %all-to-all-done.3, f32[384,32,24]{0,1,2:T(8,128)S(1)} %fusion.60), kind=kOutput, calls=%fused_computation.91 | convolution fusion | flops 604274688 | bytes 5308416 | tf_op jit(solution)/shard_map/dot_general | solution.py:148
  291.1 0.8 copy-done.14
  291.9 0.9 copy-done.15
  292.8 5.2 %fusion.24 = bf16[384,2048]{1,0:T(8,128)(2,1)} fusion(bf16[384,2048]{1,0:T(8,128)(2,1)S(1)} %copy-done.12, f32[384,2048,1]{1,0,2:T(8,128)S(1)} %fusion.86, f32[384,2048,1]{1,0,2:T(8,128)S(1)} %fusion.88, f32[384,2048,1]{1,0,2:T(8,128)S(1)} %copy-done.15, f32[384,2048,1]{1,0,2:T(8,128)S(1)} %copy-done.14, f32[384,2048,1]{1,0,2:T(8,128)S(1)} %copy-done.13, ...), kind=kOutput, calls=%fused_computation.28 | convolution fusion | flops 611155968 | bytes 21037056 | tf_op jit(solution)/shard_map/dot_general | solution.py:148
  (78 shorter events, 1.5 us)
Async XLA Ops:
  6.5 106.9 %copy-start = (bf16[384,2048]{1,0:T(8,128)(2,1)S(1)}, bf16[384,2048]{1,0:T(8,128)(2,1)}, u32[]{:S(2)}) copy-start(bf16[384,2048]{1,0:T(8,128)(2,1)} %param.12) | copy-start | bytes 4718596
  6.5 121.7 %all-gather.2.cloned.1.call-start = ((), (), s32[]{:S(2)}) async-start(), calls=%async_computation.4 | async-start | bytes 8650752 | tf_op jit(solution)/shard_map/all_gather | solution.py:113
  14.6 5.2 %copy-start.2 = (f32[16,128,128]{2,1,0:T(8,128)}, f32[16,128,128]{2,1,0:T(8,128)S(1)}, u32[]{:S(2)}) copy-start(f32[16,128,128]{2,1,0:T(8,128)S(1)} %get-tuple-element.40) | copy-start | bytes 3145732
  14.7 2.8 collective-permute-start
  17.5 0.8 copy-start.5
  19.9 24.2 %collective-permute-start.1 = (bf16[2064,128]{1,0:T(8,128)(2,1)S(1)}, bf16[2064,128]{1,0:T(8,128)(2,1)S(1)}, u32[]{:S(2)}, u32[]{:S(2)}) collective-permute-start(bf16[2064,128]{1,0:T(8,128)(2,1)S(1)} %fusion.104), channel_id=1, source_target_pairs={{0,2},{1,3},{2,4},{3,5},{4,6},{5,7},{6,8},{7,9},{8,10},{9,11},{10,... | collective-permute-start | bytes 1585160 | tf_op jit(solution)/shard_map/ppermute | solution.py:17
  46.1 25.8 %collective-permute-start.2 = (bf16[2064,128]{1,0:T(8,128)(2,1)S(1)}, bf16[2064,128]{1,0:T(8,128)(2,1)S(1)}, u32[]{:S(2)}, u32[]{:S(2)}) collective-permute-start(bf16[2064,128]{1,0:T(8,128)(2,1)S(1)} %fusion.105), channel_id=1, source_target_pairs={{0,4},{1,5},{2,6},{3,7},{4,8},{5,9},{6,10},{7,11},{8,12},{9,13},{1... | collective-permute-start | bytes 1585160 | tf_op jit(solution)/shard_map/ppermute | solution.py:17
  71.9 0.9 copy-start.4
  74.4 15.7 %collective-permute-start.3 = (bf16[2064,128]{1,0:T(8,128)(2,1)S(1)}, bf16[2064,128]{1,0:T(8,128)(2,1)S(1)}, u32[]{:S(2)}, u32[]{:S(2)}) collective-permute-start(bf16[2064,128]{1,0:T(8,128)(2,1)S(1)} %fusion.106), channel_id=1, source_target_pairs={{0,8},{1,9},{2,10},{3,11},{4,12},{5,13},{6,14},{7,15},{8,16},{9,17... | collective-permute-start | bytes 1585160 | tf_op jit(solution)/shard_map/ppermute | solution.py:17
  90.0 0.9 copy-start.6
  92.2 11.1 %copy-start.8 = (s32[32,24]{0,1:T(8,128)S(1)}, s32[32,24]{0,1:T(8,128)}, u32[]{:S(2)}) copy-start(s32[32,24]{0,1:T(8,128)} %param.17) | copy-start | bytes 9220
  92.6 10.9 %collective-permute-start.5 = (bf16[2064,128]{1,0:T(8,128)(2,1)S(1)}, bf16[2064,128]{1,0:T(8,128)(2,1)S(1)}, u32[]{:S(2)}, u32[]{:S(2)}) collective-permute-start(bf16[2064,128]{1,0:T(8,128)(2,1)S(1)} %fusion.107), channel_id=1, source_target_pairs={{0,1},{1,2},{2,3},{3,4},{4,5},{5,6},{6,7},{7,8},{8,9},{9,10},{10,1... | collective-permute-start | bytes 1585160 | tf_op jit(solution)/shard_map/ppermute | solution.py:17
  94.0 17.0 %collective-permute-start.4 = (bf16[2064,128]{1,0:T(8,128)(2,1)S(1)}, bf16[2064,128]{1,0:T(8,128)(2,1)}, u32[]{:S(2)}, u32[]{:S(2)}) collective-permute-start(bf16[2064,128]{1,0:T(8,128)(2,1)S(1)} %fusion.107), channel_id=1, source_target_pairs={{0,17},{1,18},{2,19},{3,20},{4,21},{5,22},{6,23},{7,24},{8,25},{9,... | collective-permute-start | bytes 1585160 | tf_op jit(solution)/shard_map/ppermute | solution.py:17
  113.4 5.1 %copy-start.3 = (bf16[384,2048]{0,1:T(8,128)(2,1)S(1)}, bf16[384,2048]{0,1:T(8,128)(2,1)}, u32[]{:S(2)}) copy-start(bf16[384,2048]{0,1:T(8,128)(2,1)} %copy.150) | copy-start | bytes 4718596
  125.8 2.4 copy-start.9
  128.2 7.2 %copy-start.10 = (f32[2048]{0:T(1024)S(1)}, f32[2048]{0:T(1024)}, u32[]{:S(2)}) copy-start(f32[2048]{0:T(1024)} %param.19) | copy-start | bytes 24580
  135.4 2.0 copy-start.11
  140.4 9.5 %copy-start.7 = (f32[32,24]{0,1:T(8,128)S(1)}, f32[32,24]{0,1:T(8,128)}, u32[]{:S(2)}) copy-start(f32[32,24]{0,1:T(8,128)} %param.18) | copy-start | bytes 9220
  140.4 39.5 %all-to-all-start = ((bf16[32,12,2048]{2,1,0:T(8,128)(2,1)}), bf16[32,12,2048]{2,1,0:T(8,128)(2,1)}, u32[]{:S(2)}, u32[]{:S(2)}) async-start(bf16[32,12,2048]{2,1,0:T(8,128)(2,1)} %get-tuple-element.21), calls=%async_computation | async-start | bytes 4194304 | tf_op jit(solution)/shard_map/all_to_all | solution.py:134
  179.9 35.0 %all-to-all-start.2 = ((bf16[32,12,2048]{2,1,0:T(8,128)(2,1)}), bf16[32,12,2048]{2,1,0:T(8,128)(2,1)}, u32[]{:S(2)}, u32[]{:S(2)}) async-start(bf16[32,12,2048]{2,1,0:T(8,128)(2,1)} %get-tuple-element.22), calls=%async_computation.2 | async-start | bytes 4194304 | tf_op jit(solution)/shard_map/all_to_all | solution.py:134
  214.9 35.0 %all-to-all-start.1 = ((bf16[32,12,2048]{2,1,0:T(8,128)(2,1)}), bf16[32,12,2048]{2,1,0:T(8,128)(2,1)}, u32[]{:S(2)}, u32[]{:S(2)}) async-start(bf16[32,12,2048]{2,1,0:T(8,128)(2,1)} %copy.131), calls=%async_computation.1 | async-start | bytes 4194304 | tf_op jit(solution)/shard_map/all_to_all | solution.py:143
  249.9 35.1 %all-to-all-start.3 = ((bf16[32,12,2048]{2,1,0:T(8,128)(2,1)}), bf16[32,12,2048]{2,1,0:T(8,128)(2,1)}, u32[]{:S(2)}, u32[]{:S(2)}) async-start(bf16[32,12,2048]{2,1,0:T(8,128)(2,1)} %copy.137), calls=%async_computation.3 | async-start | bytes 4194304 | tf_op jit(solution)/shard_map/all_to_all | solution.py:143
  287.9 3.2 %copy-start.12 = (bf16[384,2048]{1,0:T(8,128)(2,1)S(1)}, bf16[384,2048]{1,0:T(8,128)(2,1)}, u32[]{:S(2)}) copy-start(bf16[384,2048]{1,0:T(8,128)(2,1)} %copy-done.11) | copy-start | bytes 4718596
  288.0 3.2 %copy-start.13 = (f32[384,2048,1]{1,0,2:T(8,128)S(1)}, f32[384,2048,1]{1,0,2:T(8,128)}, u32[]{:S(2)}) copy-start(f32[384,2048,1]{1,0,2:T(8,128)} %fusion.94) | copy-start | bytes 9437188
  288.0 3.9 %copy-start.14 = (f32[384,2048,1]{1,0,2:T(8,128)S(1)}, f32[384,2048,1]{1,0,2:T(8,128)}, u32[]{:S(2)}) copy-start(f32[384,2048,1]{1,0,2:T(8,128)} %fusion.92) | copy-start | bytes 9437188
  288.0 4.8 %copy-start.15 = (f32[384,2048,1]{1,0,2:T(8,128)S(1)}, f32[384,2048,1]{1,0,2:T(8,128)}, u32[]{:S(2)}) copy-start(f32[384,2048,1]{1,0,2:T(8,128)} %fusion.90) | copy-start | bytes 9437188
  292.8 5.2 %copy-start.1 = (bf16[384,2048]{1,0:T(8,128)(2,1)S(1)}, bf16[384,2048]{1,0:T(8,128)(2,1)}, u32[]{:S(2)}) copy-start(bf16[384,2048]{1,0:T(8,128)(2,1)} %param.12) | copy-start | bytes 4718596
Sparse Core Ops, SparseCore 0:
  9.6 74.2 all-gather.1

commit v5 on v4

--- a/solution.py
+++ b/solution.py
@@ -6,7 +6,7 @@
 SEQ = ("sy", "sx", "sc")
 CHIP_AXES = ("sy", "sx")
 CORE_AXIS = "sc"
-CHUNKS = 2
+CHUNKS = 1
 
 
 def carried_in(state, ending, axis):
@@ -72,33 +72,34 @@
     head_size = model_width // head_count
     scaling = head_size ** (-0.5)
     device = lax.axis_index(SEQ)
-    query_heads = queries.reshape(length, head_count, head_size)
-    key_heads = keys_in.reshape(length, head_count, head_size)
-    value_heads = values.reshape(length, head_count, head_size)
-    running = jnp.cumsum(log_decay, axis=0)
-    ending = running[-1]
-    shrink = jnp.exp(ending[None, :] - running)
+    query_heads = queries.reshape(length, head_count, head_size).transpose(1, 0, 2)
+    key_heads = keys_in.reshape(length, head_count, head_size).transpose(1, 0, 2)
+    value_heads = values.reshape(length, head_count, head_size).transpose(1, 0, 2)
+    running = jnp.cumsum(log_decay, axis=0).T
+    ending = running[:, -1]
+    shrink = jnp.exp(ending[:, None] - running)
     key_scaled = (key_heads.astype(jnp.float32) * shrink[:, :, None]).astype(jnp.bfloat16)
     local_state = jnp.einsum(
-        "shd,she->hde", key_scaled, value_heads, preferred_element_type=jnp.float32
+        "hsd,hse->hde", key_scaled, value_heads, preferred_element_type=jnp.float32
     )
     incoming = carried_in(local_state, ending, SEQ)
     scores = (
-        jnp.einsum("thd,shd->hts", query_heads, key_heads, preferred_element_type=jnp.float32)
+        jnp.einsum("htd,hsd->hts", query_heads, key_heads, preferred_element_type=jnp.float32)
         * scaling
     )
-    spacing = running.T[:, :, None] - running.T[:, None, :]
+    spacing = running[:, :, None] - running[:, None, :]
     causal = jnp.arange(length)[:, None] >= jnp.arange(length)[None, :]
     decay_mask = jnp.where(causal[None], jnp.exp(jnp.minimum(spacing, 0.0)), 0.0)
     attend_weights = (scores * decay_mask).astype(jnp.bfloat16)
     within = jnp.einsum(
-        "hts,shd->thd", attend_weights, value_heads, preferred_element_type=jnp.float32
+        "hts,hsd->htd", attend_weights, value_heads, preferred_element_type=jnp.float32
     )
     query_scaled = (
         query_heads.astype(jnp.float32) * (jnp.exp(running) * scaling)[:, :, None]
     ).astype(jnp.bfloat16)
+    within, query_scaled = lax.optimization_barrier((within, query_scaled))
     across = jnp.einsum(
-        "thd,hde->the",
+        "htd,hde->hte",
         query_scaled,
         incoming.astype(jnp.bfloat16),
         preferred_element_type=jnp.float32,
@@ -106,7 +107,10 @@
     unnormed = within + across
     spread = jnp.mean(unnormed * unnormed, axis=2, keepdims=True)
     normed = (
-        (unnormed * lax.rsqrt(spread + 1e-06)).astype(jnp.bfloat16).reshape(length, model_width)
+        (unnormed * lax.rsqrt(spread + 1e-06))
+        .astype(jnp.bfloat16)
+        .transpose(1, 0, 2)
+        .reshape(length, model_width)
     )
     attended = jnp.dot(
         normed,

time: 310 us -> 263 us (0.85); the launches traced: 305 us -> 262 us
  blocking collectives: 0 us -> 52.1 us
  waiting for transfers between devices: 115 us -> 77.2 us
  matrix products: 86 us -> 53.4 us
  starting transfers between devices: 60 us -> 42.3 us
  local copies, waits for them, and re-layouts: 23.3 us -> 16 us
    all_to_all x0 -> x1, blocking collectives: none -> 52.1 us  [shards(): lax.all_to_all(picked[:, window], SEQ, split_axis=0, concat_axis=0, tiled...]
    all_to_all x2 -> x0, waiting for transfers between devices: 39.1 us -> none  [shards(): lax.all_to_all(picked[:, window], SEQ, split_axis=0, concat_axis=0, tiled...]
    all_to_all x2 -> x1, waiting for transfers between devices: 25.5 us -> 41.8 us  [shards(): lax.all_to_all(produced, SEQ, split_axis=0, concat_axis=0, tiled=True)]
    dot_general x2 -> x1, matrix products: 21.8 us -> 6.55 us  [shards(): jnp.einsum('snf,fd->snd', activated, down_weight[0], preferred_element_ty...]
    ppermute x6, waiting for transfers between devices: 49.8 us -> 34.7 us  [shifted(): return lax.ppermute(part, axis, pairs)]
    all_to_all x2 -> x0, starting transfers between devices: 14.4 us -> none  [shards(): lax.all_to_all(picked[:, window], SEQ, split_axis=0, concat_axis=0, tiled...]
    dot_general x6 -> x3, matrix products: 25.3 us -> 11.3 us  [shards(): jnp.dot(part.astype(jnp.bfloat16), flat_returned, preferred_element_type=...]
    dot_general x2 -> x1, matrix products: 15 us -> 5.76 us  [shards(): jnp.einsum('snd,df->snf', arrived, gate_weight[0], preferred_element_type...]
  transfers between devices with their start and end apart: 11 -> 8, of which waited for: 9 -> 5; matrix products, arithmetic and copies ran while one was open for 29% -> 13% of each run, Pallas kernels for 0% -> 0%
where the time goes in v5:
time: 263 us; the launch traced here: 262 us
  waiting for transfers between devices  77.2 us (29%)
  matrix products  53.4 us (20%)
  blocking collectives  52.1 us (20%)
  starting transfers between devices  42.3 us (16%)
  local copies, waits for them, and re-layouts  16 us (6%)
  between operations  13.9 us (5%)
  other arithmetic  7.01 us (3%)
    all_to_all x1, blocking collectives, shards(): lax.all_to_all(picked[:, window], SEQ, split_axis=0, concat_axis=0, tiled...  52.1 us
    all_to_all x1, waiting for transfers between devices, shards(): lax.all_to_all(produced, SEQ, split_axis=0, concat_axis=0, tiled=True)  41.8 us
    ppermute x6, starting transfers between devices, shifted(): return lax.ppermute(part, axis, pairs)  37.4 us
    ppermute x6, waiting for transfers between devices, shifted(): return lax.ppermute(part, axis, pairs)  34.7 us
    dot_general x3, matrix products, shards(): jnp.dot(part.astype(jnp.bfloat16), flat_returned, preferred_element_type=...  11.3 us
    dot_general x1, matrix products, shards(): jnp.einsum('snd,df->snf', arrived, up_weight[0], preferred_element_type=j...  7.64 us
    dot_general x1, matrix products, shards(): jnp.dot(normed, lax.all_gather(out_weight, SEQ, axis=0, tiled=True), pref...  7.59 us
    dot_general x1, matrix products, shards(): jnp.einsum('hts,hsd->htd', attend_weights, value_heads, preferred_element...  6.77 us
  transfers between devices with their start and end apart: 8, of which 5 were waited for; matrix products, arithmetic and copies ran while one was open for 13% of the time, Pallas kernels for 0%

profile of v5, /device:TPU:0, one launch (start us, length us, event | category | flops | bytes accessed | tf_op | source)
XLA Modules:
  0.0 261.9 jit_solution(8548056490432193947)
XLA Ops:
  6.5 0.7 all-gather.2.cloned.1.call-update
  7.3 0.7 copy_bitcast_fusion.1
  8.0 0.9 reduce-window.6
  8.9 0.2 slice_reduce_fusion
  9.2 0.1 copy.183
  9.3 0.1 copy.188
  9.4 2.6 copy.182
  12.0 0.1 subtract_exponential_fusion
  12.1 2.5 fusion.86
  14.7 1.3 collective-permute-start
  16.0 1.5 collective-permute-done
  17.5 0.8 copy-done.4
  18.3 0.1 copy.184
  18.4 0.1 copy.189
  18.5 1.1 slice.121
  19.6 0.2 fusion.43
  19.9 12.7 %collective-permute-start.1 = (bf16[2064,128]{1,0:T(8,128)(2,1)S(1)}, bf16[2064,128]{1,0:T(8,128)(2,1)S(1)}, u32[]{:S(2)}, u32[]{:S(2)}) collective-permute-start(bf16[2064,128]{1,0:T(8,128)(2,1)S(1)} %fusion.59), channel_id=1, source_target_pairs={{0,2},{1,3},{2,4},{3,5},{4,6},{5,7},{6,8},{7,9},{8,10},{9,11},{10,... | collective-permute-start | bytes 1585160 | tf_op jit(solution)/shard_map/ppermute | solution.py:17
  32.6 11.5 %collective-permute-done.1 = bf16[2064,128]{1,0:T(8,128)(2,1)S(1)} collective-permute-done((bf16[2064,128]{1,0:T(8,128)(2,1)S(1)}, bf16[2064,128]{1,0:T(8,128)(2,1)S(1)}, u32[]{:S(2)}, u32[]{:S(2)}) %collective-permute-start.1) | collective-permute-done | bytes 528416 | tf_op jit(solution)/shard_map/ppermute | solution.py:17
  44.1 0.1 copy.185
  44.3 0.1 copy.190
  44.4 1.2 copy-done.3
  45.6 0.3 fusion.84
  46.0 6.1 %collective-permute-start.2 = (bf16[2064,128]{1,0:T(8,128)(2,1)S(1)}, bf16[2064,128]{1,0:T(8,128)(2,1)}, u32[]{:S(2)}, u32[]{:S(2)}) collective-permute-start(bf16[2064,128]{1,0:T(8,128)(2,1)S(1)} %fusion.60), channel_id=1, source_target_pairs={{0,4},{1,5},{2,6},{3,7},{4,8},{5,9},{6,10},{7,11},{8,12},{9,13},{1... | collective-permute-start | bytes 1585160 | tf_op jit(solution)/shard_map/ppermute | solution.py:17
  52.2 19.7 %collective-permute-done.2 = bf16[2064,128]{1,0:T(8,128)(2,1)} collective-permute-done((bf16[2064,128]{1,0:T(8,128)(2,1)S(1)}, bf16[2064,128]{1,0:T(8,128)(2,1)}, u32[]{:S(2)}, u32[]{:S(2)}) %collective-permute-start.2) | collective-permute-done | bytes 528416 | tf_op jit(solution)/shard_map/ppermute | solution.py:17
  71.8 0.7 slice.126
  72.5 0.1 copy.186
  72.6 0.1 copy.191
  72.7 1.2 slice.125
  73.9 0.2 fusion.44
  74.1 0.8 fusion.61
  74.9 6.4 %collective-permute-start.3 = (bf16[2064,128]{1,0:T(8,128)(2,1)}, bf16[2064,128]{1,0:T(8,128)(2,1)}, u32[]{:S(2)}, u32[]{:S(2)}) collective-permute-start(bf16[2064,128]{1,0:T(8,128)(2,1)} %fusion.61), channel_id=1, source_target_pairs={{0,8},{1,9},{2,10},{3,11},{4,12},{5,13},{6,14},{7,15},{8,16},{9,17... | collective-permute-start | bytes 1585160 | tf_op jit(solution)/shard_map/ppermute | solution.py:17
  81.4 6.8 %fusion.6 = f32[16,384,128]{2,1,0:T(8,128)} fusion(f32[16,384]{1,0:T(8,128)S(1)} %copy_bitcast_fusion, pred[384,384]{1,0:T(8,128)(4,1)S(1)} %iota_compare_fusion.4, bf16[16,384,128]{1,2,0:T(8,128)(2,1)} %bitcast.135, bf16[384,2048]{1,0:T(8,128)(2,1)} %param.14, bf16[384,2048]{1,0:T(8,128)(2,1)S(1)} %copy-done), kind=kOutput, calls=%fused_computation.10 | convolution fusion | flops 1222115328 | bytes 8036352 | tf_op jit(solution)/shard_map/hts,hsd->htd/dot_general | solution.py:94
  88.1 2.0 collective-permute-done.3
  90.1 0.7 slice.128
  90.8 0.1 copy.187
  90.9 0.1 copy.192
  91.0 1.1 slice.127
  92.1 0.3 fusion.39
  92.5 0.8 fusion.62
  93.3 2.2 collective-permute-start.4
  95.5 8.6 %collective-permute-start.5 = (bf16[2064,128]{1,0:T(8,128)(2,1)}, bf16[2064,128]{1,0:T(8,128)(2,1)}, u32[]{:S(2)}, u32[]{:S(2)}) collective-permute-start(bf16[2064,128]{1,0:T(8,128)(2,1)} %fusion.62), channel_id=1, source_target_pairs={{0,1},{1,2},{2,3},{3,4},{4,5},{5,6},{6,7},{7,8},{8,9},{9,10},{10,1... | collective-permute-start | bytes 1585160 | tf_op jit(solution)/shard_map/ppermute | solution.py:17
  104.1 1.0 multiply_convert_fusion.5
  105.2 0.1 eq.29
  105.3 1.1 slice.129
  106.3 0.2 copy.174
  106.6 1.1 slice.134
  107.7 1.2 copy.175
  108.8 0.7 slice_convert_fusion
  109.5 0.2 fusion.65
  109.7 3.4 %multiply_reduce_fusion = (f32[16,384]{1,0:T(8,128)S(1)}, f32[16,384,128]{2,1,0:T(8,128)S(1)}) fusion(f32[16,384,128]{2,1,0:T(8,128)} %fusion.6, bf16[16,384,128]{2,1,0:T(8,128)(2,1)S(1)} %multiply_convert_fusion.5, f32[16,128,128]{1,2,0:T(8,128)} %copy.175, f32[16,128,128]{1,2,0:T(8,128)S(1)} %copy.174, f32[16]{0:T(128)S(1)} %fusion.65), kind=kOutput, calls=%fused_computation.24 | convolution fusion | flops 204466176 | bytes 9986112 | tf_op jit(solution)/shard_map/htd,hde->hte/dot_general | solution.py:101
  113.1 1.0 fusion.22
  114.1 0.9 copy.177
  115.0 7.6 %fusion.15 = (f32[384]{0:T(512)S(1)}, bf16[384,2048]{1,0:T(8,128)(2,1)S(1)}) fusion(bf16[384,2048]{0,1:T(8,128)(2,1)S(1)} %bitcast.150, bf16[2048,2048]{1,0:T(8,128)(2,1)} %all-gather.2.cloned.1.call-done, bf16[384,2048]{1,0:T(8,128)(2,1)} %param.15), kind=kOutput, calls=%fused_computation.16 | convolution fusion | flops 3225943552 | bytes 13108736 | tf_op jit(solution)/shard_map/dot_general | solution.py:115
  122.6 1.9 convolution_convert_fusion
  124.6 52.1 %all_to_all.10 = bf16[32,24,2048]{2,1,0:T(8,128)(2,1)S(1)} all-to-all(bf16[32,24,2048]{2,1,0:T(8,128)(2,1)S(1)} %bitcast.140), channel_id=1, replica_groups=mesh['dp'=4,'sy'=4,'sx'=4,'sc'=2] {'sy','sx','sc'}, dimensions={0} | all-to-all | bytes 6291456 | tf_op jit(solution)/shard_map/all_to_all | solution.py:138
  176.7 7.6 %fusion.2 = f32[32,24,1408]{2,1,0:T(8,128)S(1)} fusion(bf16[32,24,2048]{2,1,0:T(8,128)(2,1)S(1)} %all_to_all.10, bf16[1,2048,1408]{2,1,0:T(8,128)(2,1)} %param.22), kind=kOutput, calls=%fused_computation.3 | convolution fusion | flops 4429185024 | bytes 13238272 | tf_op jit(solution)/shard_map/snd,df->snf/dot_general | solution.py:142
  184.4 5.8 %multiply_convert_fusion.2 = bf16[32,24,1408]{2,1,0:T(8,128)(2,1)S(1)} fusion(f32[32,24,1408]{2,1,0:T(8,128)S(1)} %fusion.2, bf16[32,24,2048]{2,1,0:T(8,128)(2,1)S(1)} %all_to_all.10, bf16[1,2048,1408]{2,1,0:T(8,128)(2,1)S(1)} %bitcast.155), kind=kOutput, calls=%fused_computation.12 | convolution fusion | flops 4435673088 | bytes 15400960 | tf_op jit(solution)/shard_map/snd,df->snf/dot_general | solution.py:139
  190.2 6.6 %fusion.10 = bf16[32,24,2048]{2,1,0:T(8,128)(2,1)} fusion(bf16[32,24,1408]{2,1,0:T(8,128)(2,1)S(1)} %multiply_convert_fusion.2, bf16[1,1408,2048]{2,1,0:T(8,128)(2,1)S(1)} %bitcast.157), kind=kOutput, calls=%fused_computation.14 | convolution fusion | flops 4430757888 | bytes 11075584 | tf_op jit(solution)/shard_map/snf,fd->snd/dot_general | solution.py:144
  196.7 5.0 %all-to-all-start.1 = ((bf16[32,24,2048]{2,1,0:T(8,128)(2,1)}), bf16[32,24,2048]{2,1,0:T(8,128)(2,1)}, u32[]{:S(2)}, u32[]{:S(2)}) async-start(bf16[32,24,2048]{2,1,0:T(8,128)(2,1)} %fusion.10), calls=%async_computation.1 | async-start | bytes 6291456 | tf_op jit(solution)/shard_map/all_to_all | solution.py:147
  201.8 0.1 broadcast_in_dim.21
  201.9 41.8 %all-to-all-done.1 = bf16[32,24,2048]{2,1,0:T(8,128)(2,1)} async-done(((bf16[32,24,2048]{2,1,0:T(8,128)(2,1)}), bf16[32,24,2048]{2,1,0:T(8,128)(2,1)}, u32[]{:S(2)}, u32[]{:S(2)}) %all-to-all-start.1) | async-done | bytes 3145760 | tf_op jit(solution)/shard_map/all_to_all | solution.py:147
  243.7 3.3 %fusion.47 = f32[384,2048]{1,0:T(8,128)S(1)} fusion(bf16[768,2048]{1,0:T(8,128)(2,1)} %bitcast.30, f32[768]{0:T(1024)S(1)} %broadcast_in_dim.21, s32[768]{0:T(1024)S(1)} %eq.29), kind=kOutput, calls=%fused_computation.65 | convolution fusion | flops 1209139200 | bytes 6297600 | tf_op jit(solution)/shard_map/dot_general | solution.py:152
  247.0 3.4 %fusion.46 = f32[384,2048]{1,0:T(8,128)S(1)} fusion(bf16[768,2048]{1,0:T(8,128)(2,1)} %bitcast.30, f32[768]{0:T(1024)S(1)} %broadcast_in_dim.21, s32[768]{0:T(1024)S(1)} %eq.29), kind=kOutput, calls=%fused_computation.64 | convolution fusion | flops 1209729024 | bytes 6297600 | tf_op jit(solution)/shard_map/dot_general | solution.py:152
  250.4 4.6 %fusion.20 = bf16[384,2048]{1,0:T(8,128)(2,1)} fusion(f32[384,2048]{1,0:T(8,128)S(1)} %fusion.46, f32[384,2048]{1,0:T(8,128)S(1)} %fusion.47, bf16[384,2048]{1,0:T(8,128)(2,1)S(1)} %copy-done.9, bf16[768,2048]{1,0:T(8,128)(2,1)} %bitcast.30, f32[768]{0:T(1024)S(1)} %broadcast_in_dim.21, s32[768]{0:T(1024)S(1)} %eq.29), kind=kOutput, calls=%fused_computation.21 | convolution fusion | flops 1214251008 | bytes 12589056 | tf_op jit(solution)/shard_map/dot_general | solution.py:152
  (68 shorter events, 0.8 us)
Async XLA Ops:
  6.5 74.8 %copy-start = (bf16[384,2048]{1,0:T(8,128)(2,1)S(1)}, bf16[384,2048]{1,0:T(8,128)(2,1)}, u32[]{:S(2)}) copy-start(bf16[384,2048]{1,0:T(8,128)(2,1)} %param.12) | copy-start | bytes 4718596
  6.5 108.4 %all-gather.2.cloned.1.call-start = ((), (), s32[]{:S(2)}) async-start(), calls=%async_computation.2 | async-start | bytes 8650752 | tf_op jit(solution)/shard_map/all_gather | solution.py:117
  14.6 5.2 %copy-start.2 = (f32[16,128,128]{2,1,0:T(8,128)}, f32[16,128,128]{2,1,0:T(8,128)S(1)}, u32[]{:S(2)}) copy-start(f32[16,128,128]{2,1,0:T(8,128)S(1)} %get-tuple-element.40) | copy-start | bytes 3145732
  14.7 2.8 %collective-permute-start = (bf16[2064,128]{1,0:T(8,128)(2,1)S(1)}, bf16[2064,128]{1,0:T(8,128)(2,1)S(1)}, u32[]{:S(2)}, u32[]{:S(2)}) collective-permute-start(bf16[2064,128]{1,0:T(8,128)(2,1)S(1)} %fusion.58), channel_id=1, source_target_pairs={{0,1},{1,2},{2,3},{3,4},{4,5},{5,6},{6,7},{7,8},{8,9},{9,10},{10,1... | collective-permute-start | bytes 1585160 | tf_op jit(solution)/shard_map/ppermute | solution.py:17
  17.5 0.8 copy-start.4
  19.9 24.2 %collective-permute-start.1 = (bf16[2064,128]{1,0:T(8,128)(2,1)S(1)}, bf16[2064,128]{1,0:T(8,128)(2,1)S(1)}, u32[]{:S(2)}, u32[]{:S(2)}) collective-permute-start(bf16[2064,128]{1,0:T(8,128)(2,1)S(1)} %fusion.59), channel_id=1, source_target_pairs={{0,2},{1,3},{2,4},{3,5},{4,6},{5,7},{6,8},{7,9},{8,10},{9,11},{10,... | collective-permute-start | bytes 1585160 | tf_op jit(solution)/shard_map/ppermute | solution.py:17
  44.4 1.2 copy-start.3
  46.0 25.8 %collective-permute-start.2 = (bf16[2064,128]{1,0:T(8,128)(2,1)S(1)}, bf16[2064,128]{1,0:T(8,128)(2,1)}, u32[]{:S(2)}, u32[]{:S(2)}) collective-permute-start(bf16[2064,128]{1,0:T(8,128)(2,1)S(1)} %fusion.60), channel_id=1, source_target_pairs={{0,4},{1,5},{2,6},{3,7},{4,8},{5,9},{6,10},{7,11},{8,12},{9,13},{1... | collective-permute-start | bytes 1585160 | tf_op jit(solution)/shard_map/ppermute | solution.py:17
  74.9 15.2 %collective-permute-start.3 = (bf16[2064,128]{1,0:T(8,128)(2,1)}, bf16[2064,128]{1,0:T(8,128)(2,1)}, u32[]{:S(2)}, u32[]{:S(2)}) collective-permute-start(bf16[2064,128]{1,0:T(8,128)(2,1)} %fusion.61), channel_id=1, source_target_pairs={{0,8},{1,9},{2,10},{3,11},{4,12},{5,13},{6,14},{7,15},{8,16},{9,17... | collective-permute-start | bytes 1585160 | tf_op jit(solution)/shard_map/ppermute | solution.py:17
  93.3 12.0 %collective-permute-start.4 = (bf16[2064,128]{1,0:T(8,128)(2,1)}, bf16[2064,128]{1,0:T(8,128)(2,1)}, u32[]{:S(2)}, u32[]{:S(2)}) collective-permute-start(bf16[2064,128]{1,0:T(8,128)(2,1)} %fusion.62), channel_id=1, source_target_pairs={{0,17},{1,18},{2,19},{3,20},{4,21},{5,22},{6,23},{7,24},{8,25},{9,... | collective-permute-start | bytes 1585160 | tf_op jit(solution)/shard_map/ppermute | solution.py:17
  95.5 11.1 %collective-permute-start.5 = (bf16[2064,128]{1,0:T(8,128)(2,1)}, bf16[2064,128]{1,0:T(8,128)(2,1)}, u32[]{:S(2)}, u32[]{:S(2)}) collective-permute-start(bf16[2064,128]{1,0:T(8,128)(2,1)} %fusion.62), channel_id=1, source_target_pairs={{0,1},{1,2},{2,3},{3,4},{4,5},{5,6},{6,7},{7,8},{8,9},{9,10},{10,1... | collective-permute-start | bytes 1585160 | tf_op jit(solution)/shard_map/ppermute | solution.py:17
  104.1 1.0 copy-start.6
  115.0 7.6 %copy-start.7 = (f32[2048]{0:T(1024)S(1)}, f32[2048]{0:T(1024)}, u32[]{:S(2)}) copy-start(f32[2048]{0:T(1024)} %param.19) | copy-start | bytes 24580
  122.6 2.0 copy-start.8
  124.6 59.8 %slice-start = ((s8[5767168]{0:T(1024)(128)(4,1)}), s8[4194304]{0:T(1024)(128)(4,1)S(1)}, s32[]{:S(2)}) async-start(s8[5767168]{0:T(1024)(128)(4,1)} %bitcast.154), calls=%async_computation.3 | async-start | bytes 8388608
  176.7 7.7 %slice-start.1 = ((s8[5767168]{0:T(1024)(128)(4,1)}), s8[1572864]{0:T(1024)(128)(4,1)S(1)}, s32[]{:S(2)}) async-start(s8[5767168]{0:T(1024)(128)(4,1)} %bitcast.154), calls=%async_computation.4 | async-start | bytes 3145728
  176.7 13.5 %slice-start.2 = ((s8[5767168]{0:T(1024)(128)(4,1)}), s8[4194304]{0:T(1024)(128)(4,1)S(1)}, s32[]{:S(2)}) async-start(s8[5767168]{0:T(1024)(128)(4,1)} %bitcast.156), calls=%async_computation.5 | async-start | bytes 8388608
  184.4 5.8 %slice-start.3 = ((s8[5767168]{0:T(1024)(128)(4,1)}), s8[1572864]{0:T(1024)(128)(4,1)S(1)}, s32[]{:S(2)}) async-start(s8[5767168]{0:T(1024)(128)(4,1)} %bitcast.156), calls=%async_computation.6 | async-start | bytes 3145728
  196.7 5.0 %copy-start.5 = (f32[32,24]{0,1:T(8,128)S(1)}, f32[32,24]{0,1:T(8,128)}, u32[]{:S(2)}) copy-start(f32[32,24]{0,1:T(8,128)} %param.18) | copy-start | bytes 9220
  196.7 47.0 %all-to-all-start.1 = ((bf16[32,24,2048]{2,1,0:T(8,128)(2,1)}), bf16[32,24,2048]{2,1,0:T(8,128)(2,1)}, u32[]{:S(2)}, u32[]{:S(2)}) async-start(bf16[32,24,2048]{2,1,0:T(8,128)(2,1)} %fusion.10), calls=%async_computation.1 | async-start | bytes 6291456 | tf_op jit(solution)/shard_map/all_to_all | solution.py:147
  247.0 3.4 %copy-start.9 = (bf16[384,2048]{1,0:T(8,128)(2,1)S(1)}, bf16[384,2048]{1,0:T(8,128)(2,1)}, u32[]{:S(2)}) copy-start(bf16[384,2048]{1,0:T(8,128)(2,1)} %copy-done.8) | copy-start | bytes 4718596
  250.4 4.6 %copy-start.1 = (bf16[384,2048]{1,0:T(8,128)(2,1)S(1)}, bf16[384,2048]{1,0:T(8,128)(2,1)}, u32[]{:S(2)}) copy-start(bf16[384,2048]{1,0:T(8,128)(2,1)} %param.12) | copy-start | bytes 4718596
Sparse Core Ops, SparseCore 0:
  9.6 73.6 all-gather.1

commit v6 on v5

--- a/solution.py
+++ b/solution.py
@@ -7,9 +7,10 @@
 CHIP_AXES = ("sy", "sx")
 CORE_AXIS = "sc"
 CHUNKS = 1
+TIE_REACH = 8
 
 
-def carried_in(state, ending, axis):
+def carried_in(state, ending, axis, rider):
     count = lax.axis_size(axis)
 
     def shifted(part, distance):
@@ -45,12 +46,14 @@
     while 2 * reach < count:
         covered = combine(fetch(covered, reach), covered)
         reach *= 2
+        if reach == TIE_REACH:
+            covered, rider = lax.optimization_barrier((covered, rider))
     if count == 1:
         return jnp.zeros_like(state)
     near = fetch(covered, 1)
     if reach + 1 < count:
         near = combine(fetch(covered, reach + 1), near)
-    return near[0]
+    return near[0], rider
 
 
 def shards(
@@ -82,7 +85,9 @@
     local_state = jnp.einsum(
         "hsd,hse->hde", key_scaled, value_heads, preferred_element_type=jnp.float32
     )
-    incoming = carried_in(local_state, ending, SEQ)
+    chips = lax.all_gather(out_weight, CHIP_AXES, axis=0, tiled=True)
+    incoming, chips = carried_in(local_state, ending, SEQ, chips)
+    other = lax.ppermute(chips, CORE_AXIS, [(0, 1), (1, 0)])
     scores = (
         jnp.einsum("htd,hsd->hts", query_heads, key_heads, preferred_element_type=jnp.float32)
         * scaling
@@ -112,9 +117,18 @@
         .transpose(1, 0, 2)
         .reshape(length, model_width)
     )
-    attended = jnp.dot(
-        normed,
-        lax.all_gather(out_weight, SEQ, axis=0, tiled=True),
+    core = lax.axis_index(CORE_AXIS)
+    split = normed.reshape(length, -1, 2, out_weight.shape[0])
+    shaped = (-1, out_weight.shape[0], model_width)
+    attended = jnp.einsum(
+        "tbr,brd->td",
+        lax.dynamic_index_in_dim(split, core, axis=2, keepdims=False),
+        chips.reshape(shaped),
+        preferred_element_type=jnp.float32,
+    ) + jnp.einsum(
+        "tbr,brd->td",
+        lax.dynamic_index_in_dim(split, 1 - core, axis=2, keepdims=False),
+        other.reshape(shaped),
         preferred_element_type=jnp.float32,
     )
     residual = (stream.astype(jnp.float32) + attended).astype(jnp.bfloat16)
@@ -147,7 +161,7 @@
         returned = lax.all_to_all(produced, SEQ, split_axis=0, concat_axis=0, tiled=True)
         flat_returned = returned.reshape(-1, model_width)
         remaining = spread_weight[:, :, window].reshape(length, -1)
-        for _ in range(3):
+        for _ in range(2):
             part = lax.reduce_precision(remaining, exponent_bits=8, mantissa_bits=7)
             total = total + jnp.dot(
                 part.astype(jnp.bfloat16), flat_returned, preferred_element_type=jnp.float32

time: 263 us -> 265 us (level)
  waiting for transfers between devices: 77.2 us -> 89.3 us
  matrix products: 53.4 us -> 48.5 us
  starting transfers between devices: 42.3 us -> 38.5 us
  local copies, waits for them, and re-layouts: 16 us -> 12.9 us
  other arithmetic: 7.01 us -> 9.81 us
    ppermute x6, waiting for transfers between devices: 34.7 us -> 41.8 us  [shifted(): return lax.ppermute(part, axis, pairs)]
    all_gather x1, waiting for transfers between devices: 0.02 us -> 4.97 us  [shards(): chips = lax.all_gather(out_weight, CHIP_AXES, axis=0, tiled=True)]
    ppermute x6, starting transfers between devices: 37.4 us -> 33.5 us  [shifted(): return lax.ppermute(part, axis, pairs)]
    dot_general x3 -> x2, matrix products: 11.3 us -> 7.89 us  [shards(): jnp.dot(part.astype(jnp.bfloat16), flat_returned, preferred_element_type=...]
    dot_general x1 -> x2, matrix products: 7.59 us -> 8.75 us  [the longest x1 4.62 us: shards(): jnp.einsum('tbr,brd->td', lax.dynamic_index_in_dim(split, 1 - core, axis=...]
  transfers between devices with their start and end apart: 8 -> 9, of which waited for: 5 -> 7; matrix products, arithmetic and copies ran while one was open for 13% -> 13% of each run, Pallas kernels for 0% -> 0%
where the time goes in v6:
time: 265 us; the launch traced here: 264 us
  waiting for transfers between devices  89.3 us (34%)
  blocking collectives  51 us (19%)
  matrix products  48.5 us (18%)
  starting transfers between devices  38.5 us (15%)
  between operations  13.9 us (5%)
  local copies, waits for them, and re-layouts  12.9 us (5%)
  other arithmetic  9.81 us (4%)
    all_to_all x1, blocking collectives, shards(): lax.all_to_all(picked[:, window], SEQ, split_axis=0, concat_axis=0, tiled...  51 us
    all_to_all x1, waiting for transfers between devices, shards(): lax.all_to_all(produced, SEQ, split_axis=0, concat_axis=0, tiled=True)  41.8 us
    ppermute x6, waiting for transfers between devices, shifted(): return lax.ppermute(part, axis, pairs)  41.8 us
    ppermute x6, starting transfers between devices, shifted(): return lax.ppermute(part, axis, pairs)  33.5 us
    dot_general x2, matrix products, shards(): jnp.dot(part.astype(jnp.bfloat16), flat_returned, preferred_element_type=...  7.89 us
    dot_general x1, matrix products, shards(): jnp.einsum('hts,hsd->htd', attend_weights, value_heads, preferred_element...  6.69 us
    dot_general x1, matrix products, shards(): jnp.einsum('snf,fd->snd', activated, down_weight[0], preferred_element_ty...  6.55 us
    dot_general x1, matrix products, shards(): jnp.einsum('snd,df->snf', arrived, gate_weight[0], preferred_element_type...  5.76 us
  transfers between devices with their start and end apart: 9, of which 7 were waited for; matrix products, arithmetic and copies ran while one was open for 13% of the time, Pallas kernels for 0%

profile of v6, /device:TPU:0, one launch (start us, length us, event | category | flops | bytes accessed | tf_op | source)
XLA Modules:
  0.0 264.0 jit_solution(10114786583587270929)
XLA Ops:
  6.5 0.7 all-gather.2.cloned.1.call-update
  7.3 0.7 copy_bitcast_fusion.1
  8.0 0.9 reduce-window.6
  8.9 0.2 slice_reduce_fusion
  9.3 0.1 copy.182
  9.4 2.6 copy.178
  12.0 0.1 exponential_multiply_fusion
  12.1 2.5 fusion.96
  14.7 1.3 collective-permute-start
  16.0 1.5 collective-permute-done
  17.5 0.8 copy-done.4
  18.3 0.1 copy.180
  18.4 0.1 copy.183
  18.5 1.1 slice.121
  19.6 0.2 fusion.49
  19.9 12.7 %collective-permute-start.1 = (bf16[2064,128]{1,0:T(8,128)(2,1)S(1)}, bf16[2064,128]{1,0:T(8,128)(2,1)S(1)}, u32[]{:S(2)}, u32[]{:S(2)}) collective-permute-start(bf16[2064,128]{1,0:T(8,128)(2,1)S(1)} %fusion.60), channel_id=1, source_target_pairs={{0,2},{1,3},{2,4},{3,5},{4,6},{5,7},{6,8},{7,9},{8,10},{9,11},{10,... | collective-permute-start | bytes 1585160 | tf_op jit(solution)/shard_map/ppermute | solution.py:18
  32.6 11.8 %collective-permute-done.1 = bf16[2064,128]{1,0:T(8,128)(2,1)S(1)} collective-permute-done((bf16[2064,128]{1,0:T(8,128)(2,1)S(1)}, bf16[2064,128]{1,0:T(8,128)(2,1)S(1)}, u32[]{:S(2)}, u32[]{:S(2)}) %collective-permute-start.1) | collective-permute-done | bytes 528416 | tf_op jit(solution)/shard_map/ppermute | solution.py:18
  44.3 0.8 copy-done.5
  45.1 0.1 copy.181
  45.3 0.1 copy.184
  45.4 1.1 slice.123
  46.5 0.3 fusion.94
  46.8 4.9 %collective-permute-start.2 = (bf16[2064,128]{1,0:T(8,128)(2,1)S(1)}, bf16[2064,128]{1,0:T(8,128)(2,1)S(1)}, u32[]{:S(2)}, u32[]{:S(2)}) collective-permute-start(bf16[2064,128]{1,0:T(8,128)(2,1)S(1)} %fusion.61), channel_id=1, source_target_pairs={{0,4},{1,5},{2,6},{3,7},{4,8},{5,9},{6,10},{7,11},{8,12},{9,13},{1... | collective-permute-start | bytes 1585160 | tf_op jit(solution)/shard_map/ppermute | solution.py:18
  51.8 22.2 %collective-permute-done.2 = bf16[2064,128]{1,0:T(8,128)(2,1)S(1)} collective-permute-done((bf16[2064,128]{1,0:T(8,128)(2,1)S(1)}, bf16[2064,128]{1,0:T(8,128)(2,1)S(1)}, u32[]{:S(2)}, u32[]{:S(2)}) %collective-permute-start.2) | collective-permute-done | bytes 528416 | tf_op jit(solution)/shard_map/ppermute | solution.py:18
  74.1 0.2 fusion.68
  74.2 1.4 fusion.41
  75.7 5.0 %all-gather.2.cloned.1.call-done = bf16[1024,2048]{1,0:T(8,128)(2,1)} async-done(((bf16[64,2048]{1,0:T(8,128)(2,1)}), bf16[1024,2048]{1,0:T(8,128)(2,1)}) %all-gather.2.cloned.1.call-update) | async-done | bytes 4194320 | tf_op jit(solution)/shard_map/all_gather | solution.py:88
  80.7 0.1 copy.185
  80.8 1.3 convert_element_type.210
  82.1 0.9 fusion.62
  83.0 3.7 %collective-permute-start.3 = (bf16[2064,128]{1,0:T(8,128)(2,1)}, bf16[2064,128]{1,0:T(8,128)(2,1)S(1)}, u32[]{:S(2)}, u32[]{:S(2)}) collective-permute-start(bf16[2064,128]{1,0:T(8,128)(2,1)} %fusion.62), channel_id=1, source_target_pairs={{0,8},{1,9},{2,10},{3,11},{4,12},{5,13},{6,14},{7,15},{8,16},{9,17... | collective-permute-start | bytes 1585160 | tf_op jit(solution)/shard_map/ppermute | solution.py:18
  86.7 0.1 collective-permute-start.6
  86.8 6.7 %fusion.6 = f32[16,384,128]{2,1,0:T(8,128)} fusion(f32[16,384]{1,0:T(8,128)S(1)} %copy_bitcast_fusion, pred[384,384]{1,0:T(8,128)(4,1)S(1)} %iota_compare_fusion.4, bf16[16,384,128]{1,2,0:T(8,128)(2,1)} %bitcast.166, bf16[384,2048]{1,0:T(8,128)(2,1)} %param.14, bf16[384,2048]{1,0:T(8,128)(2,1)S(1)} %copy-done), kind=kOutput, calls=%fused_computation.10 | convolution fusion | flops 1222115328 | bytes 8036352 | tf_op jit(solution)/shard_map/hts,hsd->htd/dot_general | solution.py:99
  93.5 4.8 %collective-permute-done.3 = bf16[2064,128]{1,0:T(8,128)(2,1)S(1)} collective-permute-done((bf16[2064,128]{1,0:T(8,128)(2,1)}, bf16[2064,128]{1,0:T(8,128)(2,1)S(1)}, u32[]{:S(2)}, u32[]{:S(2)}) %collective-permute-start.3) | collective-permute-done | bytes 528416 | tf_op jit(solution)/shard_map/ppermute | solution.py:18
  98.3 0.2 fusion.67
  98.5 0.1 copy.186
  98.7 0.2 fusion.40
  98.9 0.8 fusion.63
  99.7 4.8 %collective-permute-start.4 = (bf16[2064,128]{1,0:T(8,128)(2,1)}, bf16[2064,128]{1,0:T(8,128)(2,1)}, u32[]{:S(2)}, u32[]{:S(2)}) collective-permute-start(bf16[2064,128]{1,0:T(8,128)(2,1)} %fusion.63), channel_id=1, source_target_pairs={{0,17},{1,18},{2,19},{3,20},{4,21},{5,22},{6,23},{7,24},{8,25},{9,... | collective-permute-start | bytes 1585160 | tf_op jit(solution)/shard_map/ppermute | solution.py:18
  104.6 6.0 %collective-permute-start.5 = (bf16[2064,128]{1,0:T(8,128)(2,1)}, bf16[2064,128]{1,0:T(8,128)(2,1)}, u32[]{:S(2)}, u32[]{:S(2)}) collective-permute-start(bf16[2064,128]{1,0:T(8,128)(2,1)} %fusion.63), channel_id=1, source_target_pairs={{0,1},{1,2},{2,3},{3,4},{4,5},{5,6},{6,7},{7,8},{8,9},{9,10},{10,1... | collective-permute-start | bytes 1585160 | tf_op jit(solution)/shard_map/ppermute | solution.py:18
  110.5 1.0 multiply_convert_fusion.5
  111.6 0.1 eq.29
  111.7 1.6 collective-permute-done.4
  113.3 1.1 slice.135
  114.4 0.2 copy.170
  114.6 1.1 slice.140
  115.7 1.2 copy.171
  116.9 0.7 slice_convert_fusion
  117.5 0.2 fusion.66
  117.7 3.4 %multiply_reduce_fusion = (f32[16,384]{1,0:T(8,128)S(1)}, f32[16,384,128]{2,1,0:T(8,128)S(1)}) fusion(f32[16,384,128]{2,1,0:T(8,128)} %fusion.6, bf16[16,384,128]{2,1,0:T(8,128)(2,1)S(1)} %multiply_convert_fusion.5, f32[16,128,128]{1,2,0:T(8,128)} %copy.171, f32[16,128,128]{1,2,0:T(8,128)S(1)} %copy.170, f32[16]{0:T(128)S(1)} %fusion.66), kind=kOutput, calls=%fused_computation.25 | convolution fusion | flops 204466176 | bytes 9986112 | tf_op jit(solution)/shard_map/htd,hde->hte/dot_general | solution.py:106
  121.1 1.0 fusion.23
  122.1 0.9 copy.173
  123.0 4.1 %fusion.45 = f32[384,2048,1]{1,0,2:T(8,128)S(1)} fusion(bf16[16,64,2048]{2,1,0:T(8,128)(2,1)} %bitcast.159, bf16[384,16,2,64]{0,3,2,1:T(8,128)(2,1)S(1)} %bitcast.163, s32[]{:T(128)S(6)} %select_n.16), kind=kOutput, calls=%fused_computation.62 | convolution fusion | flops 1610612736 | bytes 8126468 | tf_op jit(solution)/shard_map/tbr,brd->td/dot_general | solution.py:123
  127.2 4.6 %fusion.15 = (f32[384]{0:T(512)S(1)}, bf16[384,2048]{1,0:T(8,128)(2,1)S(1)}) fusion(bf16[16,64,2048]{2,1,0:T(8,128)(2,1)} %bitcast.32, bf16[384,16,2,64]{0,3,2,1:T(8,128)(2,1)S(1)} %bitcast.164, s32[]{:T(128)S(6)} %select_n.17, f32[384,2048,1]{1,0,2:T(8,128)S(1)} %fusion.45, bf16[384,2048]{1,0:T(8,128)(2,1)S(1)} %copy-done.3), kind=kOutput, calls=%fused_computation.16 | convolution fusion | flops 1616117376 | bytes 11273732 | tf_op jit(solution)/shard_map/tbr,brd->td/dot_general | solution.py:128
  131.8 1.9 convolution_convert_fusion
  133.8 51.0 %all_to_all.10 = bf16[32,24,2048]{2,1,0:T(8,128)(2,1)S(1)} all-to-all(bf16[32,24,2048]{2,1,0:T(8,128)(2,1)S(1)} %bitcast.169), channel_id=1, replica_groups=mesh['dp'=4,'sy'=4,'sx'=4,'sc'=2] {'sy','sx','sc'}, dimensions={0} | all-to-all | bytes 6291456 | tf_op jit(solution)/shard_map/all_to_all | solution.py:152
  184.8 5.1 %fusion.2 = f32[32,24,1408]{2,1,0:T(8,128)S(1)} fusion(bf16[32,24,2048]{2,1,0:T(8,128)(2,1)S(1)} %all_to_all.10, bf16[1,2048,1408]{2,1,0:T(8,128)(2,1)S(1)} %bitcast.183), kind=kOutput, calls=%fused_computation.3 | convolution fusion | flops 4429185024 | bytes 13238272 | tf_op jit(solution)/shard_map/snd,df->snf/dot_general | solution.py:156
  189.9 5.8 %multiply_convert_fusion.2 = bf16[32,24,1408]{2,1,0:T(8,128)(2,1)S(1)} fusion(f32[32,24,1408]{2,1,0:T(8,128)S(1)} %fusion.2, bf16[32,24,2048]{2,1,0:T(8,128)(2,1)S(1)} %all_to_all.10, bf16[1,2048,1408]{2,1,0:T(8,128)(2,1)S(1)} %bitcast.185), kind=kOutput, calls=%fused_computation.12 | convolution fusion | flops 4435673088 | bytes 15400960 | tf_op jit(solution)/shard_map/snd,df->snf/dot_general | solution.py:153
  195.7 6.6 %fusion.10 = bf16[32,24,2048]{2,1,0:T(8,128)(2,1)} fusion(bf16[32,24,1408]{2,1,0:T(8,128)(2,1)S(1)} %multiply_convert_fusion.2, bf16[1,1408,2048]{2,1,0:T(8,128)(2,1)S(1)} %bitcast.187), kind=kOutput, calls=%fused_computation.14 | convolution fusion | flops 4430757888 | bytes 11075584 | tf_op jit(solution)/shard_map/snf,fd->snd/dot_general | solution.py:158
  202.3 5.0 %all-to-all-start.1 = ((bf16[32,24,2048]{2,1,0:T(8,128)(2,1)}), bf16[32,24,2048]{2,1,0:T(8,128)(2,1)}, u32[]{:S(2)}, u32[]{:S(2)}) async-start(bf16[32,24,2048]{2,1,0:T(8,128)(2,1)} %fusion.10), calls=%async_computation.1 | async-start | bytes 6291456 | tf_op jit(solution)/shard_map/all_to_all | solution.py:161
  207.3 0.1 broadcast_in_dim.21
  207.4 41.8 %all-to-all-done.1 = bf16[32,24,2048]{2,1,0:T(8,128)(2,1)} async-done(((bf16[32,24,2048]{2,1,0:T(8,128)(2,1)}), bf16[32,24,2048]{2,1,0:T(8,128)(2,1)}, u32[]{:S(2)}, u32[]{:S(2)}) %all-to-all-start.1) | async-done | bytes 3145760 | tf_op jit(solution)/shard_map/all_to_all | solution.py:161
  249.2 3.3 %fusion.51 = f32[384,2048]{1,0:T(8,128)S(1)} fusion(bf16[768,2048]{1,0:T(8,128)(2,1)} %bitcast.41, f32[768]{0:T(1024)S(1)} %broadcast_in_dim.21, s32[768]{0:T(1024)S(1)} %eq.29), kind=kOutput, calls=%fused_computation.67 | convolution fusion | flops 1209139200 | bytes 6297600 | tf_op jit(solution)/shard_map/dot_general | solution.py:166
  252.5 4.6 %fusion.19 = bf16[384,2048]{1,0:T(8,128)(2,1)} fusion(f32[384,2048]{1,0:T(8,128)S(1)} %fusion.51, bf16[384,2048]{1,0:T(8,128)(2,1)S(1)} %get-tuple-element.44, bf16[768,2048]{1,0:T(8,128)(2,1)} %bitcast.41, f32[768]{0:T(1024)S(1)} %broadcast_in_dim.21, s32[768]{0:T(1024)S(1)} %eq.29), kind=kOutput, calls=%fused_computation.20 | convolution fusion | flops 1212874752 | bytes 9443328 | tf_op jit(solution)/shard_map/dot_general | solution.py:166
  (69 shorter events, 0.9 us)
Async XLA Ops:
  6.5 80.3 %copy-start = (bf16[384,2048]{1,0:T(8,128)(2,1)S(1)}, bf16[384,2048]{1,0:T(8,128)(2,1)}, u32[]{:S(2)}) copy-start(bf16[384,2048]{1,0:T(8,128)(2,1)} %param.12) | copy-start | bytes 4718596
  6.5 74.1 %all-gather.2.cloned.1.call-start = ((), (), s32[]{:S(2)}) async-start(), calls=%async_computation.2 | async-start | bytes 4456448 | tf_op jit(solution)/shard_map/all_gather | solution.py:88
  14.7 2.8 %collective-permute-start = (bf16[2064,128]{1,0:T(8,128)(2,1)S(1)}, bf16[2064,128]{1,0:T(8,128)(2,1)S(1)}, u32[]{:S(2)}, u32[]{:S(2)}) collective-permute-start(bf16[2064,128]{1,0:T(8,128)(2,1)S(1)} %fusion.59), channel_id=1, source_target_pairs={{0,1},{1,2},{2,3},{3,4},{4,5},{5,6},{6,7},{7,8},{8,9},{9,10},{10,1... | collective-permute-start | bytes 1585160 | tf_op jit(solution)/shard_map/ppermute | solution.py:18
  17.5 0.8 copy-start.4
  19.9 24.5 %collective-permute-start.1 = (bf16[2064,128]{1,0:T(8,128)(2,1)S(1)}, bf16[2064,128]{1,0:T(8,128)(2,1)S(1)}, u32[]{:S(2)}, u32[]{:S(2)}) collective-permute-start(bf16[2064,128]{1,0:T(8,128)(2,1)S(1)} %fusion.60), channel_id=1, source_target_pairs={{0,2},{1,3},{2,4},{3,5},{4,6},{5,7},{6,8},{7,9},{8,10},{9,11},{10,... | collective-permute-start | bytes 1585160 | tf_op jit(solution)/shard_map/ppermute | solution.py:18
  44.3 0.8 copy-start.5
  46.8 27.2 %collective-permute-start.2 = (bf16[2064,128]{1,0:T(8,128)(2,1)S(1)}, bf16[2064,128]{1,0:T(8,128)(2,1)S(1)}, u32[]{:S(2)}, u32[]{:S(2)}) collective-permute-start(bf16[2064,128]{1,0:T(8,128)(2,1)S(1)} %fusion.61), channel_id=1, source_target_pairs={{0,4},{1,5},{2,6},{3,7},{4,8},{5,9},{6,10},{7,11},{8,12},{9,13},{1... | collective-permute-start | bytes 1585160 | tf_op jit(solution)/shard_map/ppermute | solution.py:18
  83.0 15.7 %copy-start.2 = (f32[16,128,128]{2,1,0:T(8,128)S(1)}, f32[16,128,128]{2,1,0:T(8,128)}, u32[]{:S(2)}) copy-start(f32[16,128,128]{2,1,0:T(8,128)} %fusion.41) | copy-start | bytes 3145732
  83.0 15.3 %collective-permute-start.3 = (bf16[2064,128]{1,0:T(8,128)(2,1)}, bf16[2064,128]{1,0:T(8,128)(2,1)S(1)}, u32[]{:S(2)}, u32[]{:S(2)}) collective-permute-start(bf16[2064,128]{1,0:T(8,128)(2,1)} %fusion.62), channel_id=1, source_target_pairs={{0,8},{1,9},{2,10},{3,11},{4,12},{5,13},{6,14},{7,15},{8,16},{9,17... | collective-permute-start | bytes 1585160 | tf_op jit(solution)/shard_map/ppermute | solution.py:18
  86.7 40.4 %collective-permute-start.6 = (bf16[1024,2048]{1,0:T(8,128)(2,1)}, bf16[1024,2048]{1,0:T(8,128)(2,1)}, u32[]{:S(2)}, u32[]{:S(2)}) collective-permute-start(bf16[1024,2048]{1,0:T(8,128)(2,1)} %all-gather.2.cloned.1.call-done), channel_id=1, source_target_pairs={{0,1},{1,0},{2,3},{3,2},{4,5},{5,4},{6,7},{7,6},{8,9},{9,8},{10,11... | collective-permute-start | bytes 12582920 | tf_op jit(solution)/shard_map/ppermute | solution.py:90
  98.9 12.6 %copy-start.7 = (s32[32,24]{0,1:T(8,128)S(1)}, s32[32,24]{0,1:T(8,128)}, u32[]{:S(2)}) copy-start(s32[32,24]{0,1:T(8,128)} %param.17) | copy-start | bytes 9220
  99.7 13.6 %collective-permute-start.4 = (bf16[2064,128]{1,0:T(8,128)(2,1)}, bf16[2064,128]{1,0:T(8,128)(2,1)}, u32[]{:S(2)}, u32[]{:S(2)}) collective-permute-start(bf16[2064,128]{1,0:T(8,128)(2,1)} %fusion.63), channel_id=1, source_target_pairs={{0,17},{1,18},{2,19},{3,20},{4,21},{5,22},{6,23},{7,24},{8,25},{9,... | collective-permute-start | bytes 1585160 | tf_op jit(solution)/shard_map/ppermute | solution.py:18
  104.6 10.0 %collective-permute-start.5 = (bf16[2064,128]{1,0:T(8,128)(2,1)}, bf16[2064,128]{1,0:T(8,128)(2,1)}, u32[]{:S(2)}, u32[]{:S(2)}) collective-permute-start(bf16[2064,128]{1,0:T(8,128)(2,1)} %fusion.63), channel_id=1, source_target_pairs={{0,1},{1,2},{2,3},{3,4},{4,5},{5,6},{6,7},{7,8},{8,9},{9,10},{10,1... | collective-permute-start | bytes 1585160 | tf_op jit(solution)/shard_map/ppermute | solution.py:18
  123.0 4.2 %copy-start.3 = (bf16[384,2048]{1,0:T(8,128)(2,1)S(1)}, bf16[384,2048]{1,0:T(8,128)(2,1)}, u32[]{:S(2)}) copy-start(bf16[384,2048]{1,0:T(8,128)(2,1)} %param.15) | copy-start | bytes 4718596
  127.1 4.7 %copy-start.8 = (f32[2048]{0:T(1024)S(1)}, f32[2048]{0:T(1024)}, u32[]{:S(2)}) copy-start(f32[2048]{0:T(1024)} %param.19) | copy-start | bytes 24580
  127.2 57.6 %slice-start = ((s8[5767168]{0:T(1024)(128)(4,1)}), s8[4194304]{0:T(1024)(128)(4,1)S(1)}, s32[]{:S(2)}) async-start(s8[5767168]{0:T(1024)(128)(4,1)} %bitcast.182), calls=%async_computation.3 | async-start | bytes 8388608
  131.8 53.0 %slice-start.1 = ((s8[5767168]{0:T(1024)(128)(4,1)}), s8[1572864]{0:T(1024)(128)(4,1)S(1)}, s32[]{:S(2)}) async-start(s8[5767168]{0:T(1024)(128)(4,1)} %bitcast.182), calls=%async_computation.4 | async-start | bytes 3145728
  133.7 56.1 %slice-start.2 = ((s8[5767168]{0:T(1024)(128)(4,1)}), s8[4194304]{0:T(1024)(128)(4,1)S(1)}, s32[]{:S(2)}) async-start(s8[5767168]{0:T(1024)(128)(4,1)} %bitcast.184), calls=%async_computation.5 | async-start | bytes 8388608
  184.8 5.1 %slice-start.3 = ((s8[5767168]{0:T(1024)(128)(4,1)}), s8[1572864]{0:T(1024)(128)(4,1)S(1)}, s32[]{:S(2)}) async-start(s8[5767168]{0:T(1024)(128)(4,1)} %bitcast.184), calls=%async_computation.6 | async-start | bytes 3145728
  184.8 10.9 %slice-start.4 = ((s8[5767168]{0:T(1024)(128)(4,1)}), s8[4194304]{0:T(1024)(128)(4,1)S(1)}, s32[]{:S(2)}) async-start(s8[5767168]{0:T(1024)(128)(4,1)} %bitcast.186), calls=%async_computation.7 | async-start | bytes 8388608
  189.9 5.8 %slice-start.5 = ((s8[5767168]{0:T(1024)(128)(4,1)}), s8[1572864]{0:T(1024)(128)(4,1)S(1)}, s32[]{:S(2)}) async-start(s8[5767168]{0:T(1024)(128)(4,1)} %bitcast.186), calls=%async_computation.8 | async-start | bytes 3145728
  202.3 5.0 %copy-start.6 = (f32[32,24]{0,1:T(8,128)S(1)}, f32[32,24]{0,1:T(8,128)}, u32[]{:S(2)}) copy-start(f32[32,24]{0,1:T(8,128)} %param.18) | copy-start | bytes 9220
  202.3 47.0 %all-to-all-start.1 = ((bf16[32,24,2048]{2,1,0:T(8,128)(2,1)}), bf16[32,24,2048]{2,1,0:T(8,128)(2,1)}, u32[]{:S(2)}, u32[]{:S(2)}) async-start(bf16[32,24,2048]{2,1,0:T(8,128)(2,1)} %fusion.10), calls=%async_computation.1 | async-start | bytes 6291456 | tf_op jit(solution)/shard_map/all_to_all | solution.py:161
  252.5 4.6 %copy-start.1 = (bf16[384,2048]{1,0:T(8,128)(2,1)S(1)}, bf16[384,2048]{1,0:T(8,128)(2,1)}, u32[]{:S(2)}) copy-start(bf16[384,2048]{1,0:T(8,128)(2,1)} %param.12) | copy-start | bytes 4718596
Sparse Core Ops, SparseCore 0:
  9.5 71.1 all-gather.1

commit v7 on v5

--- a/solution.py
+++ b/solution.py
@@ -9,36 +9,37 @@
 CHUNKS = 1
 
 
-def carried_in(state, ending, axis):
+def pack(state, ending):
+    heads, rows, width = state.shape
+    wide, parts = ending, []
+    for _ in range(3):
+        part = lax.reduce_precision(wide, exponent_bits=8, mantissa_bits=7)
+        parts.append(part.astype(jnp.bfloat16))
+        wide = wide - part
+    block = jnp.pad(jnp.stack(parts, axis=1), ((0, 0), (0, width - 3)))
+    return jnp.concatenate(
+        [state.astype(jnp.bfloat16).reshape(heads * rows, width), block], axis=0
+    )
+
+
+def unpack(message, heads):
+    width = message.shape[1]
+    body = message[: heads * width].reshape(heads, width, width).astype(jnp.float32)
+    tail = message[heads * width :, :3].astype(jnp.float32)
+    return body, tail[:, 0] + tail[:, 1] + tail[:, 2]
+
+
+def combine(earlier, latter):
+    return (earlier[0] * jnp.exp(latter[1])[:, None, None] + latter[0], earlier[1] + latter[1])
+
+
+def exclusive_scan(state, ending, axis):
     count = lax.axis_size(axis)
-
-    def shifted(part, distance):
+    heads = state.shape[0]
+
+    def fetch(pair, distance):
         pairs = [(j, j + distance) for j in range(count - distance)]
-        return lax.ppermute(part, axis, pairs)
-
-    def combine(earlier, latter):
-        return (earlier[0] * jnp.exp(latter[1])[:, None, None] + latter[0], earlier[1] + latter[1])
-
-    heads, rows, width = state.shape
-
-    def pieces(wide):
-        parts = []
-        for _ in range(3):
-            part = lax.reduce_precision(wide, exponent_bits=8, mantissa_bits=7)
-            parts.append(part.astype(jnp.bfloat16))
-            wide = wide - part
-        block = jnp.stack(parts, axis=1)
-        return jnp.pad(block, ((0, 0), (0, width - 3)))
-
-    def fetch(pair, distance):
-        low, wide = pair
-        message = jnp.concatenate(
-            [low.astype(jnp.bfloat16).reshape(heads * rows, width), pieces(wide)], axis=0
-        )
-        arrived = shifted(message, distance)
-        body = arrived[: heads * rows].reshape(heads, rows, width).astype(jnp.float32)
-        tail = arrived[heads * rows :, :3].astype(jnp.float32)
-        return (body, tail[:, 0] + tail[:, 1] + tail[:, 2])
+        return unpack(lax.ppermute(pack(*pair), axis, pairs), heads)
 
     covered = (state, ending)
     reach = 1
@@ -51,6 +52,28 @@
     if reach + 1 < count:
         near = combine(fetch(covered, reach + 1), near)
     return near[0]
+
+
+def carried_in(state, ending):
+    heads = state.shape[0]
+    half = heads // 2
+    swap = [(0, 1), (1, 0)]
+    core = lax.axis_index(CORE_AXIS)
+    first = core == 0
+    other_state, other_ending = unpack(lax.ppermute(pack(state, ending), CORE_AXIS, swap), heads)
+    lower = (jnp.where(first, state, other_state), jnp.where(first, ending, other_ending))
+    upper = (jnp.where(first, other_state, state), jnp.where(first, other_ending, ending))
+    chip_state, chip_ending = combine(lower, upper)
+    mine = exclusive_scan(
+        lax.dynamic_slice_in_dim(chip_state, core * half, half, axis=0),
+        lax.dynamic_slice_in_dim(chip_ending, core * half, half, axis=0),
+        CHIP_AXES,
+    )
+    theirs = lax.ppermute(mine.astype(jnp.bfloat16), CORE_AXIS, swap).astype(jnp.float32)
+    before = jnp.where(
+        first, jnp.concatenate([mine, theirs], axis=0), jnp.concatenate([theirs, mine], axis=0)
+    )
+    return jnp.where(first, before, combine((before, 0.0), lower)[0])
 
 
 def shards(
@@ -82,7 +105,7 @@
     local_state = jnp.einsum(
         "hsd,hse->hde", key_scaled, value_heads, preferred_element_type=jnp.float32
     )
-    incoming = carried_in(local_state, ending, SEQ)
+    incoming = carried_in(local_state, ending)
     scores = (
         jnp.einsum("htd,hsd->hts", query_heads, key_heads, preferred_element_type=jnp.float32)
         * scaling
@@ -147,7 +170,7 @@
         returned = lax.all_to_all(produced, SEQ, split_axis=0, concat_axis=0, tiled=True)
         flat_returned = returned.reshape(-1, model_width)
         remaining = spread_weight[:, :, window].reshape(length, -1)
-        for _ in range(3):
+        for _ in range(2):
             part = lax.reduce_precision(remaining, exponent_bits=8, mantissa_bits=7)
             total = total + jnp.dot(
                 part.astype(jnp.bfloat16), flat_returned, preferred_element_type=jnp.float32

time: 263 us -> 253 us (0.962)
  other arithmetic: 7.01 us -> 21.1 us
  starting transfers between devices: 42.3 us -> 31.7 us
  waiting for transfers between devices: 77.2 us -> 70.2 us
  blocking collectives: 52.1 us -> 45.8 us
    convert_element_type x18, other arithmetic: 1.88 us -> 14 us  [the longest x6 4.72 us: unpack(): message[:heads * width].reshape(heads, width, width).astype(jnp.float32)]
    ppermute x6 -> x7, starting transfers between devices: 37.4 us -> 26.7 us  [the longest x5 26.6 us: fetch(): return unpack(lax.ppermute(pack(*pair), axis, pairs), heads)]
    ppermute x6 -> x7, waiting for transfers between devices: 34.7 us -> 27.7 us  [the longest x5 25.8 us: fetch(): return unpack(lax.ppermute(pack(*pair), axis, pairs), heads)]
    slice x11 -> x2, local copies, waits for them, and re-layouts: 7 us -> 0.19 us  [the longest x6 5.5 us: fetch(): arrived[:heads * rows].reshape(heads, rows, width).astype(jnp.float32)]
    all_to_all x1, blocking collectives: 52.1 us -> 45.8 us  [shards(): lax.all_to_all(picked[:, window], SEQ, split_axis=0, concat_axis=0, tiled...]
    convert_element_type x2 -> x5, local copies, waits for them, and re-layouts: 1.4 us -> 7.41 us  [unpack(): message[:heads * width].reshape(heads, width, width).astype(jnp.float32)]
    dot_general x3 -> x2, matrix products: 11.3 us -> 8 us  [shards(): jnp.dot(part.astype(jnp.bfloat16), flat_returned, preferred_element_type=...]
  transfers between devices with their start and end apart: 8 -> 9, of which waited for: 5 -> 5; matrix products, arithmetic and copies ran while one was open for 13% -> 20% of each run, Pallas kernels for 0% -> 0%
where the time goes in v7:
time: 253 us; the launch traced here: 252 us
  waiting for transfers between devices  70.2 us (28%)
  matrix products  51.7 us (20%)
  blocking collectives  45.8 us (18%)
  starting transfers between devices  31.7 us (13%)
  other arithmetic  21.1 us (8%)
  local copies, waits for them, and re-layouts  17.5 us (7%)
  between operations  13.8 us (5%)
    all_to_all x1, blocking collectives, shards(): lax.all_to_all(picked[:, window], SEQ, split_axis=0, concat_axis=0, tiled...  45.8 us
    all_to_all x1, waiting for transfers between devices, shards(): lax.all_to_all(produced, SEQ, split_axis=0, concat_axis=0, tiled=True)  41.8 us
    ppermute x5, starting transfers between devices, fetch(): return unpack(lax.ppermute(pack(*pair), axis, pairs), heads)  26.6 us
    ppermute x5, waiting for transfers between devices, fetch(): return unpack(lax.ppermute(pack(*pair), axis, pairs), heads)  25.8 us
    dot_general x1, matrix products, shards(): jnp.dot(normed, lax.all_gather(out_weight, SEQ, axis=0, tiled=True), pref...  8.04 us
    dot_general x2, matrix products, shards(): jnp.dot(part.astype(jnp.bfloat16), flat_returned, preferred_element_type=...  8 us
    dot_general x1, matrix products, shards(): jnp.einsum('snd,df->snf', arrived, up_weight[0], preferred_element_type=j...  7.64 us
    convert_element_type x5, local copies, waits for them, and re-layouts, unpack(): message[:heads * width].reshape(heads, width, width).astype(jnp.float32)  7.41 us
  transfers between devices with their start and end apart: 9, of which 5 were waited for; matrix products, arithmetic and copies ran while one was open for 20% of the time, Pallas kernels for 0%

profile of v7, /device:TPU:0, one launch (start us, length us, event | category | flops | bytes accessed | tf_op | source)
XLA Modules:
  0.0 251.8 jit_solution(3468067414582376797)
XLA Ops:
  6.5 0.7 all-gather.2.cloned.1.call-update
  7.3 0.7 copy_bitcast_fusion.1
  8.0 0.9 reduce-window.6
  8.9 0.2 slice_reduce_fusion
  9.3 0.1 copy.174
  9.4 2.6 %copy.172 = bf16[384,2048]{0,1:T(8,128)(2,1)} copy(bf16[384,2048]{1,0:T(8,128)(2,1)} %param.13) | data formatting | bytes 3145728 | tf_op jit(solution)/shard_map/reshape | solution.py:99
  12.1 3.6 %fusion.105 = (bf16[16,128,128]{2,1,0:T(8,128)(2,1)S(1)}, f32[16,128,128]{2,1,0:T(8,128)}) fusion(bf16[16,384,128]{1,2,0:T(8,128)(2,1)} %bitcast.146, f32[16,384]{1,0:T(8,128)S(1)} %get-tuple-element.23, bf16[384,2048]{1,0:T(8,128)(2,1)} %param.14), kind=kOutput, calls=%fused_computation.178 | convolution fusion | flops 203948032 | bytes 4743168 | tf_op jit(solution)/shard_map/hsd,hse->hde/dot_general | solution.py:105
  15.7 0.1 collective-permute-start
  15.8 1.9 collective-permute-done
  17.7 0.1 convert.6
  17.9 0.2 fusion.67
  18.1 0.1 broadcast_select_fusion
  18.2 0.1 fusion.103
  18.4 0.9 copy.155
  19.4 1.0 pad_maximum_fusion
  20.4 3.5 %collective-permute-start.1 = (bf16[1032,128]{0,1:T(8,128)(2,1)S(1)}, bf16[1032,128]{0,1:T(8,128)(2,1)S(1)}, u32[]{:S(2)}, u32[]{:S(2)}) collective-permute-start(bf16[1032,128]{0,1:T(8,128)(2,1)S(1)} %pad_maximum_fusion), channel_id=1, source_target_pairs={{0,2},{2,4},{4,6},{6,8},{8,10},{10,12},{12,14},{14,16},{16,18},{18... | collective-permute-start | bytes 792584 | tf_op jit(solution)/shard_map/ppermute | solution.py:42
  23.9 8.8 %collective-permute-done.1 = bf16[1032,128]{0,1:T(8,128)(2,1)S(1)} collective-permute-done((bf16[1032,128]{0,1:T(8,128)(2,1)S(1)}, bf16[1032,128]{0,1:T(8,128)(2,1)S(1)}, u32[]{:S(2)}, u32[]{:S(2)}) %collective-permute-start.1) | collective-permute-done | bytes 264224 | tf_op jit(solution)/shard_map/ppermute | solution.py:42
  32.7 0.7 copy-done.5
  33.4 0.8 slice_convert_fusion.4
  34.2 2.1 copy.156
  36.4 1.2 fusion.46
  37.5 0.9 copy.157
  38.4 0.6 slice_convert_fusion.9
  39.0 1.0 pad_maximum_fusion.1
  40.0 6.6 %collective-permute-start.2 = (bf16[1032,128]{0,1:T(8,128)(2,1)S(1)}, bf16[1032,128]{0,1:T(8,128)(2,1)S(1)}, u32[]{:S(2)}, u32[]{:S(2)}) collective-permute-start(bf16[1032,128]{0,1:T(8,128)(2,1)S(1)} %pad_maximum_fusion.1), channel_id=1, source_target_pairs={{0,4},{2,6},{4,8},{6,10},{8,12},{10,14},{12,16},{14,18},{16,20},{1... | collective-permute-start | bytes 792584 | tf_op jit(solution)/shard_map/ppermute | solution.py:42
  46.6 13.2 %collective-permute-done.2 = bf16[1032,128]{0,1:T(8,128)(2,1)S(1)} collective-permute-done((bf16[1032,128]{0,1:T(8,128)(2,1)S(1)}, bf16[1032,128]{0,1:T(8,128)(2,1)S(1)}, u32[]{:S(2)}, u32[]{:S(2)}) %collective-permute-start.2) | collective-permute-done | bytes 264224 | tf_op jit(solution)/shard_map/ppermute | solution.py:42
  59.8 0.7 copy-done.3
  60.5 0.8 slice_convert_fusion.3
  61.4 2.0 copy.158
  63.4 2.2 fusion.100
  65.6 0.1 copy.159
  65.7 0.7 slice_convert_fusion.8
  66.5 7.4 %collective-permute-start.3 = (bf16[1032,128]{0,1:T(8,128)(2,1)S(1)}, bf16[1032,128]{0,1:T(8,128)(2,1)S(1)}, u32[]{:S(2)}, u32[]{:S(2)}) collective-permute-start(bf16[1032,128]{0,1:T(8,128)(2,1)S(1)} %pad_maximum_fusion.2), channel_id=1, source_target_pairs={{0,8},{2,10},{4,12},{6,14},{8,16},{10,18},{12,20},{14,22},{16,24},... | collective-permute-start | bytes 792584 | tf_op jit(solution)/shard_map/ppermute | solution.py:42
  73.9 0.7 iota_compare_fusion.4
  74.6 3.8 %collective-permute-done.3 = bf16[1032,128]{0,1:T(8,128)(2,1)S(1)} collective-permute-done((bf16[1032,128]{0,1:T(8,128)(2,1)S(1)}, bf16[1032,128]{0,1:T(8,128)(2,1)S(1)}, u32[]{:S(2)}, u32[]{:S(2)}) %collective-permute-start.3) | collective-permute-done | bytes 264224 | tf_op jit(solution)/shard_map/ppermute | solution.py:42
  78.4 0.7 copy-done.4
  79.1 0.9 slice_convert_fusion.2
  80.1 1.2 copy.160
  81.3 1.2 add_convert_fusion.1
  82.5 0.1 copy.161
  82.6 0.6 slice_convert_fusion.7
  83.3 5.3 %collective-permute-start.4 = (bf16[1032,128]{0,1:T(8,128)(2,1)S(1)}, bf16[1032,128]{0,1:T(8,128)(2,1)}, u32[]{:S(2)}, u32[]{:S(2)}) collective-permute-start(bf16[1032,128]{0,1:T(8,128)(2,1)S(1)} %pad_maximum_fusion.3), channel_id=1, source_target_pairs={{0,18},{2,20},{4,22},{6,24},{8,26},{10,28},{12,30},{1,19},{3,21},{... | collective-permute-start | bytes 792584 | tf_op jit(solution)/shard_map/ppermute | solution.py:42
  88.6 3.8 %collective-permute-start.5 = (bf16[1032,128]{0,1:T(8,128)(2,1)S(1)}, bf16[1032,128]{0,1:T(8,128)(2,1)}, u32[]{:S(2)}, u32[]{:S(2)}) collective-permute-start(bf16[1032,128]{0,1:T(8,128)(2,1)S(1)} %pad_maximum_fusion.3), channel_id=1, source_target_pairs={{0,2},{2,4},{4,6},{6,8},{8,10},{10,12},{12,14},{14,16},{16,18},{18... | collective-permute-start | bytes 792584 | tf_op jit(solution)/shard_map/ppermute | solution.py:42
  92.4 6.7 %fusion.6 = f32[16,384,128]{2,1,0:T(8,128)} fusion(f32[16,384]{1,0:T(8,128)S(1)} %copy_bitcast_fusion, pred[384,384]{1,0:T(8,128)(4,1)} %iota_compare_fusion.4, bf16[16,384,128]{1,2,0:T(8,128)(2,1)} %bitcast.147, bf16[384,2048]{1,0:T(8,128)(2,1)S(1)} %copy-done, bf16[384,2048]{1,0:T(8,128)(2,1)} %param.14), kind=kOutput, calls=%fused_computation.10 | convolution fusion | flops 1222115328 | bytes 8036352 | tf_op jit(solution)/shard_map/hts,hsd->htd/dot_general | solution.py:117
  99.1 1.0 slice_convert_fusion.1
  100.1 1.0 copy.162
  101.2 1.0 slice_convert_fusion
  102.2 1.0 copy.163
  103.2 0.7 slice_convert_fusion.6
  103.8 2.0 fusion.98
  105.9 1.8 multiply_convert_fusion.5
  108.0 3.5 %multiply_reduce_fusion = (f32[16,384]{1,0:T(8,128)S(1)}, f32[16,384,128]{2,1,0:T(8,128)S(1)}) fusion(f32[16,384,128]{2,1,0:T(8,128)} %fusion.6, bf16[16,384,128]{2,1,0:T(8,128)(2,1)} %multiply_convert_fusion.5, f32[16,128,128]{2,1,0:T(8,128)S(1)} %broadcast_select_fusion, f32[8,128,128]{2,1,0:T(8,128)S(1)} %get-tuple-element.10, ...), kind=kOutput, calls=%fused_computation.23 | convolution fusion | flops 205514752 | bytes 9986113 | tf_op jit(solution)/shard_map/htd,hde->hte/dot_general | solution.py:124
  111.5 1.0 fusion.21
  112.5 1.6 copy.166
  114.0 8.0 %fusion.15 = (f32[384]{0:T(512)S(1)}, bf16[384,2048]{1,0:T(8,128)(2,1)S(1)}) fusion(bf16[384,2048]{0,1:T(8,128)(2,1)} %bitcast.158, bf16[2048,2048]{1,0:T(8,128)(2,1)} %all-gather.2.cloned.1.call-done, bf16[384,2048]{1,0:T(8,128)(2,1)} %param.15), kind=kOutput, calls=%fused_computation.16 | convolution fusion | flops 3225943552 | bytes 13108736 | tf_op jit(solution)/shard_map/dot_general | solution.py:138
  122.1 1.9 convolution_convert_fusion
  124.1 45.8 %all_to_all.10 = bf16[32,24,2048]{2,1,0:T(8,128)(2,1)S(1)} all-to-all(bf16[32,24,2048]{2,1,0:T(8,128)(2,1)S(1)} %bitcast.152), channel_id=1, replica_groups=mesh['dp'=4,'sy'=4,'sx'=4,'sc'=2] {'sy','sx','sc'}, dimensions={0} | all-to-all | bytes 6291456 | tf_op jit(solution)/shard_map/all_to_all | solution.py:161
  169.9 7.6 %fusion.2 = f32[32,24,1408]{2,1,0:T(8,128)S(1)} fusion(bf16[32,24,2048]{2,1,0:T(8,128)(2,1)S(1)} %all_to_all.10, bf16[1,2048,1408]{2,1,0:T(8,128)(2,1)} %param.22), kind=kOutput, calls=%fused_computation.3 | convolution fusion | flops 4429185024 | bytes 13238272 | tf_op jit(solution)/shard_map/snd,df->snf/dot_general | solution.py:165
  177.6 5.8 %multiply_convert_fusion.2 = bf16[32,24,1408]{2,1,0:T(8,128)(2,1)S(1)} fusion(f32[32,24,1408]{2,1,0:T(8,128)S(1)} %fusion.2, bf16[32,24,2048]{2,1,0:T(8,128)(2,1)S(1)} %all_to_all.10, bf16[1,2048,1408]{2,1,0:T(8,128)(2,1)S(1)} %bitcast.167), kind=kOutput, calls=%fused_computation.12 | convolution fusion | flops 4435673088 | bytes 15400960 | tf_op jit(solution)/shard_map/snd,df->snf/dot_general | solution.py:162
  183.4 6.5 %fusion.10 = bf16[32,24,2048]{2,1,0:T(8,128)(2,1)} fusion(bf16[32,24,1408]{2,1,0:T(8,128)(2,1)S(1)} %multiply_convert_fusion.2, bf16[1,1408,2048]{2,1,0:T(8,128)(2,1)S(1)} %bitcast.169), kind=kOutput, calls=%fused_computation.14 | convolution fusion | flops 4430757888 | bytes 11075584 | tf_op jit(solution)/shard_map/snf,fd->snd/dot_general | solution.py:167
  189.9 5.0 %all-to-all-start.1 = ((bf16[32,24,2048]{2,1,0:T(8,128)(2,1)}), bf16[32,24,2048]{2,1,0:T(8,128)(2,1)}, u32[]{:S(2)}, u32[]{:S(2)}) async-start(bf16[32,24,2048]{2,1,0:T(8,128)(2,1)} %fusion.10), calls=%async_computation.1 | async-start | bytes 6291456 | tf_op jit(solution)/shard_map/all_to_all | solution.py:170
  195.1 41.8 %all-to-all-done.1 = bf16[32,24,2048]{2,1,0:T(8,128)(2,1)} async-done(((bf16[32,24,2048]{2,1,0:T(8,128)(2,1)}), bf16[32,24,2048]{2,1,0:T(8,128)(2,1)}, u32[]{:S(2)}, u32[]{:S(2)}) %all-to-all-start.1) | async-done | bytes 3145760 | tf_op jit(solution)/shard_map/all_to_all | solution.py:170
  236.9 3.4 %fusion.34 = f32[384,2048]{1,0:T(8,128)S(1)} fusion(bf16[768,2048]{1,0:T(8,128)(2,1)} %bitcast.44, f32[768]{0:T(1024)S(1)} %broadcast_in_dim.21, s32[768]{0:T(1024)S(1)} %eq.33), kind=kOutput, calls=%fused_computation.47 | convolution fusion | flops 1209139200 | bytes 6297600 | tf_op jit(solution)/shard_map/dot_general | solution.py:175
  240.3 4.6 %fusion.19 = bf16[384,2048]{1,0:T(8,128)(2,1)} fusion(f32[384,2048]{1,0:T(8,128)S(1)} %fusion.34, bf16[384,2048]{1,0:T(8,128)(2,1)S(1)} %copy-done.10, bf16[768,2048]{1,0:T(8,128)(2,1)} %bitcast.44, f32[768]{0:T(1024)S(1)} %broadcast_in_dim.21, s32[768]{0:T(1024)S(1)} %eq.33), kind=kOutput, calls=%fused_computation.20 | convolution fusion | flops 1212874752 | bytes 9443328 | tf_op jit(solution)/shard_map/dot_general | solution.py:175
  (70 shorter events, 1.3 us)
Async XLA Ops:
  6.5 85.9 %copy-start = (bf16[384,2048]{1,0:T(8,128)(2,1)S(1)}, bf16[384,2048]{1,0:T(8,128)(2,1)}, u32[]{:S(2)}) copy-start(bf16[384,2048]{1,0:T(8,128)(2,1)} %param.12) | copy-start | bytes 4718596
  6.5 107.5 %all-gather.2.cloned.1.call-start = ((), (), s32[]{:S(2)}) async-start(), calls=%async_computation.2 | async-start | bytes 8650752 | tf_op jit(solution)/shard_map/all_gather | solution.py:140
  15.7 2.0 collective-permute-start
  15.8 2.3 copy-start.2
  20.4 12.3 %collective-permute-start.1 = (bf16[1032,128]{0,1:T(8,128)(2,1)S(1)}, bf16[1032,128]{0,1:T(8,128)(2,1)S(1)}, u32[]{:S(2)}, u32[]{:S(2)}) collective-permute-start(bf16[1032,128]{0,1:T(8,128)(2,1)S(1)} %pad_maximum_fusion), channel_id=1, source_target_pairs={{0,2},{2,4},{4,6},{6,8},{8,10},{10,12},{12,14},{14,16},{16,18},{18... | collective-permute-start | bytes 792584 | tf_op jit(solution)/shard_map/ppermute | solution.py:42
  32.7 0.7 copy-start.5
  40.0 19.8 %collective-permute-start.2 = (bf16[1032,128]{0,1:T(8,128)(2,1)S(1)}, bf16[1032,128]{0,1:T(8,128)(2,1)S(1)}, u32[]{:S(2)}, u32[]{:S(2)}) collective-permute-start(bf16[1032,128]{0,1:T(8,128)(2,1)S(1)} %pad_maximum_fusion.1), channel_id=1, source_target_pairs={{0,4},{2,6},{4,8},{6,10},{8,12},{10,14},{12,16},{14,18},{16,20},{1... | collective-permute-start | bytes 792584 | tf_op jit(solution)/shard_map/ppermute | solution.py:42
  59.8 0.8 copy-start.3
  66.5 11.9 %collective-permute-start.3 = (bf16[1032,128]{0,1:T(8,128)(2,1)S(1)}, bf16[1032,128]{0,1:T(8,128)(2,1)S(1)}, u32[]{:S(2)}, u32[]{:S(2)}) collective-permute-start(bf16[1032,128]{0,1:T(8,128)(2,1)S(1)} %pad_maximum_fusion.2), channel_id=1, source_target_pairs={{0,8},{2,10},{4,12},{6,14},{8,16},{10,18},{12,20},{14,22},{16,24},... | collective-permute-start | bytes 792584 | tf_op jit(solution)/shard_map/ppermute | solution.py:42
  78.4 0.7 copy-start.4
  83.3 15.8 %collective-permute-start.4 = (bf16[1032,128]{0,1:T(8,128)(2,1)S(1)}, bf16[1032,128]{0,1:T(8,128)(2,1)}, u32[]{:S(2)}, u32[]{:S(2)}) collective-permute-start(bf16[1032,128]{0,1:T(8,128)(2,1)S(1)} %pad_maximum_fusion.3), channel_id=1, source_target_pairs={{0,18},{2,20},{4,22},{6,24},{8,26},{10,28},{12,30},{1,19},{3,21},{... | collective-permute-start | bytes 792584 | tf_op jit(solution)/shard_map/ppermute | solution.py:42
  88.6 12.6 %collective-permute-start.5 = (bf16[1032,128]{0,1:T(8,128)(2,1)S(1)}, bf16[1032,128]{0,1:T(8,128)(2,1)}, u32[]{:S(2)}, u32[]{:S(2)}) collective-permute-start(bf16[1032,128]{0,1:T(8,128)(2,1)S(1)} %pad_maximum_fusion.3), channel_id=1, source_target_pairs={{0,2},{2,4},{4,6},{6,8},{8,10},{10,12},{12,14},{14,16},{16,18},{18... | collective-permute-start | bytes 792584 | tf_op jit(solution)/shard_map/ppermute | solution.py:42
  102.2 5.6 %copy-start.7 = (s32[32,24]{0,1:T(8,128)S(1)}, s32[32,24]{0,1:T(8,128)}, u32[]{:S(2)}) copy-start(s32[32,24]{0,1:T(8,128)} %param.17) | copy-start | bytes 9220
  105.9 2.0 collective-permute-start.6
  114.0 8.1 %copy-start.8 = (f32[2048]{0:T(1024)S(1)}, f32[2048]{0:T(1024)}, u32[]{:S(2)}) copy-start(f32[2048]{0:T(1024)} %param.19) | copy-start | bytes 24580
  122.1 2.0 copy-start.9
  124.0 53.5 %slice-start = ((s8[5767168]{0:T(1024)(128)(4,1)}), s8[4194304]{0:T(1024)(128)(4,1)S(1)}, s32[]{:S(2)}) async-start(s8[5767168]{0:T(1024)(128)(4,1)} %bitcast.166), calls=%async_computation.3 | async-start | bytes 8388608
  169.9 7.7 %slice-start.1 = ((s8[5767168]{0:T(1024)(128)(4,1)}), s8[1572864]{0:T(1024)(128)(4,1)S(1)}, s32[]{:S(2)}) async-start(s8[5767168]{0:T(1024)(128)(4,1)} %bitcast.166), calls=%async_computation.4 | async-start | bytes 3145728
  169.9 13.5 %slice-start.2 = ((s8[5767168]{0:T(1024)(128)(4,1)}), s8[4194304]{0:T(1024)(128)(4,1)S(1)}, s32[]{:S(2)}) async-start(s8[5767168]{0:T(1024)(128)(4,1)} %bitcast.168), calls=%async_computation.5 | async-start | bytes 8388608
  177.6 5.8 %slice-start.3 = ((s8[5767168]{0:T(1024)(128)(4,1)}), s8[1572864]{0:T(1024)(128)(4,1)S(1)}, s32[]{:S(2)}) async-start(s8[5767168]{0:T(1024)(128)(4,1)} %bitcast.168), calls=%async_computation.6 | async-start | bytes 3145728
  189.9 5.0 %copy-start.6 = (f32[32,24]{0,1:T(8,128)S(1)}, f32[32,24]{0,1:T(8,128)}, u32[]{:S(2)}) copy-start(f32[32,24]{0,1:T(8,128)} %param.18) | copy-start | bytes 9220
  189.9 47.0 %all-to-all-start.1 = ((bf16[32,24,2048]{2,1,0:T(8,128)(2,1)}), bf16[32,24,2048]{2,1,0:T(8,128)(2,1)}, u32[]{:S(2)}, u32[]{:S(2)}) async-start(bf16[32,24,2048]{2,1,0:T(8,128)(2,1)} %fusion.10), calls=%async_computation.1 | async-start | bytes 6291456 | tf_op jit(solution)/shard_map/all_to_all | solution.py:170
  236.9 3.4 %copy-start.10 = (bf16[384,2048]{1,0:T(8,128)(2,1)S(1)}, bf16[384,2048]{1,0:T(8,128)(2,1)}, u32[]{:S(2)}) copy-start(bf16[384,2048]{1,0:T(8,128)(2,1)} %copy-done.9) | copy-start | bytes 4718596
  240.3 4.6 %copy-start.1 = (bf16[384,2048]{1,0:T(8,128)(2,1)S(1)}, bf16[384,2048]{1,0:T(8,128)(2,1)}, u32[]{:S(2)}) copy-start(bf16[384,2048]{1,0:T(8,128)(2,1)} %param.12) | copy-start | bytes 4718596
Sparse Core Ops, SparseCore 0:
  9.6 62.8 all-gather.1

commit v8 on v7

--- a/solution.py
+++ b/solution.py
@@ -7,6 +7,7 @@
 CHIP_AXES = ("sy", "sx")
 CORE_AXIS = "sc"
 CHUNKS = 1
+RADIX = 4
 
 
 def pack(state, ending):
@@ -43,14 +44,19 @@
 
     covered = (state, ending)
     reach = 1
-    while 2 * reach < count:
-        covered = combine(fetch(covered, reach), covered)
-        reach *= 2
+    while reach * RADIX < count:
+        gathered = covered
+        for multiple in range(1, RADIX):
+            gathered = combine(fetch(covered, multiple * reach), gathered)
+        covered = gathered
+        reach *= RADIX
     if count == 1:
         return jnp.zeros_like(state)
     near = fetch(covered, 1)
-    if reach + 1 < count:
-        near = combine(fetch(covered, reach + 1), near)
+    distance = 1 + reach
+    while distance < count:
+        near = combine(fetch(covered, distance), near)
+        distance += reach
     return near[0]
 
 

time: 253 us -> 255 us (level)
  waiting for transfers between devices: 70.2 us -> 58.5 us
  starting transfers between devices: 31.7 us -> 39.7 us
  other arithmetic: 21.1 us -> 25.3 us
    ppermute x5 -> x7, waiting for transfers between devices: 25.8 us -> 13.7 us  [fetch(): return unpack(lax.ppermute(pack(*pair), axis, pairs), heads)]
    ppermute x5 -> x7, starting transfers between devices: 26.6 us -> 34.5 us  [fetch(): return unpack(lax.ppermute(pack(*pair), axis, pairs), heads)]
    convert_element_type x6 -> x8, other arithmetic: 4.72 us -> 9.36 us  [unpack(): message[:heads * width].reshape(heads, width, width).astype(jnp.float32)]
    convert_element_type x5 -> x7, local copies, waits for them, and re-layouts: 7.41 us -> 11.3 us  [unpack(): message[:heads * width].reshape(heads, width, width).astype(jnp.float32)]
    convert_element_type x4 -> x2, other arithmetic: 4.67 us -> 1.72 us  [pack(): state.astype(jnp.bfloat16).reshape(heads * rows, width)]
  transfers between devices with their start and end apart: 9 -> 11, of which waited for: 5 -> 6; matrix products, arithmetic and copies ran while one was open for 20% -> 22% of each run, Pallas kernels for 0% -> 0%
where the time goes in v8:
time: 255 us; the launch traced here: 254 us
  waiting for transfers between devices  58.5 us (23%)
  matrix products  51.4 us (20%)
  blocking collectives  46.7 us (18%)
  starting transfers between devices  39.7 us (16%)
  other arithmetic  25.3 us (10%)
  local copies, waits for them, and re-layouts  18.5 us (7%)
  between operations  13.8 us (5%)
    all_to_all x1, blocking collectives, shards(): lax.all_to_all(picked[:, window], SEQ, split_axis=0, concat_axis=0, tiled...  46.7 us
    all_to_all x1, waiting for transfers between devices, shards(): lax.all_to_all(produced, SEQ, split_axis=0, concat_axis=0, tiled=True)  41.8 us
    ppermute x7, starting transfers between devices, fetch(): return unpack(lax.ppermute(pack(*pair), axis, pairs), heads)  34.5 us
    ppermute x7, waiting for transfers between devices, fetch(): return unpack(lax.ppermute(pack(*pair), axis, pairs), heads)  13.7 us
    convert_element_type x7, local copies, waits for them, and re-layouts, unpack(): message[:heads * width].reshape(heads, width, width).astype(jnp.float32)  11.3 us
    convert_element_type x8, other arithmetic, unpack(): message[:heads * width].reshape(heads, width, width).astype(jnp.float32)  9.36 us
    dot_general x2, matrix products, shards(): jnp.dot(part.astype(jnp.bfloat16), flat_returned, preferred_element_type=...  8 us
    dot_general x1, matrix products, shards(): jnp.einsum('snd,df->snf', arrived, up_weight[0], preferred_element_type=j...  7.64 us
  transfers between devices with their start and end apart: 11, of which 6 were waited for; matrix products, arithmetic and copies ran while one was open for 22% of the time, Pallas kernels for 0%

profile of v8, /device:TPU:0, one launch (start us, length us, event | category | flops | bytes accessed | tf_op | source)
XLA Modules:
  0.0 253.9 jit_solution(8255521493144821072)
XLA Ops:
  6.5 0.7 all-gather.2.cloned.1.call-update
  7.3 0.7 copy_bitcast_fusion.1
  8.0 0.9 reduce-window.6
  9.4 1.9 copy.172
  11.4 3.6 %fusion.82 = (bf16[16,128,128]{2,1,0:T(8,128)(2,1)S(1)}, f32[16,128,128]{2,1,0:T(8,128)}) fusion(bf16[16,384,128]{1,2,0:T(8,128)(2,1)S(1)} %bitcast.138, f32[16,384]{1,0:T(8,128)S(1)} %get-tuple-element.23, bf16[384,2048]{1,0:T(8,128)(2,1)} %param.14), kind=kOutput, calls=%fused_computation.151 | convolution fusion | flops 203948032 | bytes 4743168 | tf_op jit(solution)/shard_map/hsd,hse->hde/dot_general | solution.py:111
  15.0 0.8 fusion.42
  15.8 2.3 collective-permute-done
  18.1 1.1 slice.161
  19.3 0.7 slice_convert_fusion.7
  20.0 0.2 fusion.56
  20.5 0.9 copy.155
  21.5 1.0 pad_maximum_fusion
  22.5 4.8 %collective-permute-start.1 = (bf16[1032,128]{0,1:T(8,128)(2,1)S(1)}, bf16[1032,128]{0,1:T(8,128)(2,1)S(1)}, u32[]{:S(2)}, u32[]{:S(2)}) collective-permute-start(bf16[1032,128]{0,1:T(8,128)(2,1)S(1)} %pad_maximum_fusion), channel_id=1, source_target_pairs={{0,6},{2,8},{4,10},{6,12},{8,14},{10,16},{12,18},{14,20},{16,22},{... | collective-permute-start | bytes 792584 | tf_op jit(solution)/shard_map/ppermute | solution.py:43
  27.3 4.4 %collective-permute-start.2 = (bf16[1032,128]{0,1:T(8,128)(2,1)S(1)}, bf16[1032,128]{0,1:T(8,128)(2,1)}, u32[]{:S(2)}, u32[]{:S(2)}) collective-permute-start(bf16[1032,128]{0,1:T(8,128)(2,1)S(1)} %pad_maximum_fusion), channel_id=1, source_target_pairs={{0,4},{2,6},{4,8},{6,10},{8,12},{10,14},{12,16},{14,18},{16,20},{1... | collective-permute-start | bytes 792584 | tf_op jit(solution)/shard_map/ppermute | solution.py:43
  31.7 0.7 iota_compare_fusion.4
  32.4 3.5 %collective-permute-start.3 = (bf16[1032,128]{0,1:T(8,128)(2,1)S(1)}, bf16[1032,128]{0,1:T(8,128)(2,1)}, u32[]{:S(2)}, u32[]{:S(2)}) collective-permute-start(bf16[1032,128]{0,1:T(8,128)(2,1)S(1)} %pad_maximum_fusion), channel_id=1, source_target_pairs={{0,2},{2,4},{4,6},{6,8},{8,10},{10,12},{12,14},{14,16},{16,18},{18... | collective-permute-start | bytes 792584 | tf_op jit(solution)/shard_map/ppermute | solution.py:43
  35.9 0.4 collective-permute-done.1
  36.3 0.7 copy-done.4
  37.0 0.8 slice_convert_fusion.6
  37.9 2.1 copy.156
  40.0 1.8 slice_convert_fusion.5
  41.8 2.0 copy.157
  43.8 0.7 collective-permute-done.3
  44.5 1.8 slice_convert_fusion.4
  46.3 2.0 copy.158
  48.4 0.7 slice_convert_fusion.12
  49.0 0.7 slice_convert_fusion.13
  49.8 1.6 add_convert_fusion.1
  51.5 0.6 slice_convert_fusion.11
  52.2 9.8 %collective-permute-start.5 = (bf16[1032,128]{0,1:T(8,128)(2,1)S(1)}, bf16[1032,128]{0,1:T(8,128)(2,1)}, u32[]{:S(2)}, u32[]{:S(2)}) collective-permute-start(bf16[1032,128]{0,1:T(8,128)(2,1)S(1)} %pad_maximum_fusion.1), channel_id=1, source_target_pairs={{0,18},{2,20},{4,22},{6,24},{8,26},{10,28},{12,30},{1,19},{3,21},{... | collective-permute-start | bytes 792584 | tf_op jit(solution)/shard_map/ppermute | solution.py:43
  62.0 2.0 collective-permute-start.4
  64.0 6.8 %fusion.6 = f32[16,384,128]{2,1,0:T(8,128)} fusion(f32[16,384]{1,0:T(8,128)S(1)} %copy_bitcast_fusion, pred[384,384]{1,0:T(8,128)(4,1)} %iota_compare_fusion.4, bf16[16,384,128]{1,2,0:T(8,128)(2,1)} %bitcast.139, bf16[384,2048]{1,0:T(8,128)(2,1)S(1)} %copy-done, bf16[384,2048]{1,0:T(8,128)(2,1)} %param.14), kind=kOutput, calls=%fused_computation.10 | convolution fusion | flops 1222115328 | bytes 8036352 | tf_op jit(solution)/shard_map/hts,hsd->htd/dot_general | solution.py:123
  70.8 2.0 collective-permute-start.7
  72.8 8.0 %collective-permute-start.6 = (bf16[1032,128]{0,1:T(8,128)(2,1)S(1)}, bf16[1032,128]{0,1:T(8,128)(2,1)}, u32[]{:S(2)}, u32[]{:S(2)}) collective-permute-start(bf16[1032,128]{0,1:T(8,128)(2,1)S(1)} %pad_maximum_fusion.1), channel_id=1, source_target_pairs={{0,10},{2,12},{4,14},{6,16},{8,18},{10,20},{12,22},{14,24},{16,26}... | collective-permute-start | bytes 792584 | tf_op jit(solution)/shard_map/ppermute | solution.py:43
  80.8 6.3 %collective-permute-done.4 = bf16[1032,128]{0,1:T(8,128)(2,1)} collective-permute-done((bf16[1032,128]{0,1:T(8,128)(2,1)S(1)}, bf16[1032,128]{0,1:T(8,128)(2,1)}, u32[]{:S(2)}, u32[]{:S(2)}) %collective-permute-start.4) | collective-permute-done | bytes 264224 | tf_op jit(solution)/shard_map/ppermute | solution.py:43
  87.1 1.0 slice_convert_fusion.3
  88.2 1.8 slice_convert_fusion.2
  90.0 1.0 copy.160
  91.0 2.1 copy.161
  93.1 6.2 %collective-permute-done.6 = bf16[1032,128]{0,1:T(8,128)(2,1)} collective-permute-done((bf16[1032,128]{0,1:T(8,128)(2,1)S(1)}, bf16[1032,128]{0,1:T(8,128)(2,1)}, u32[]{:S(2)}, u32[]{:S(2)}) %collective-permute-start.6) | collective-permute-done | bytes 264224 | tf_op jit(solution)/shard_map/ppermute | solution.py:43
  99.3 1.0 slice_convert_fusion.1
  100.3 1.0 copy.162
  101.3 1.0 slice_convert_fusion
  102.3 1.0 copy.163
  103.3 0.6 slice_convert_fusion.10
  104.0 0.7 slice_convert_fusion.8
  104.6 0.7 slice_convert_fusion.9
  105.3 1.7 fusion.77
  107.1 0.3 collective-permute-start.8
  107.3 1.9 multiply_convert_fusion.5
  109.4 1.0 convert_element_type.238
  110.4 3.5 %multiply_reduce_fusion = (f32[16,384]{1,0:T(8,128)S(1)}, f32[16,384,128]{2,1,0:T(8,128)S(1)}) fusion(f32[16,384,128]{2,1,0:T(8,128)} %fusion.6, bf16[16,384,128]{2,1,0:T(8,128)(2,1)} %multiply_convert_fusion.5, f32[16,128,128]{2,1,0:T(8,128)S(1)} %broadcast_select_fusion, f32[8,128,128]{2,1,0:T(8,128)S(1)} %get-tuple-element.10, ...), kind=kOutput, calls=%fused_computation.23 | convolution fusion | flops 205514752 | bytes 9986113 | tf_op jit(solution)/shard_map/htd,hde->hte/dot_general | solution.py:130
  113.9 1.0 fusion.21
  114.9 0.9 copy.166
  115.8 7.6 %fusion.15 = (f32[384]{0:T(512)S(1)}, bf16[384,2048]{1,0:T(8,128)(2,1)S(1)}) fusion(bf16[384,2048]{0,1:T(8,128)(2,1)S(1)} %bitcast.151, bf16[2048,2048]{1,0:T(8,128)(2,1)} %all-gather.2.cloned.1.call-done, bf16[384,2048]{1,0:T(8,128)(2,1)} %param.15), kind=kOutput, calls=%fused_computation.16 | convolution fusion | flops 3225943552 | bytes 13108736 | tf_op jit(solution)/shard_map/dot_general | solution.py:144
  123.4 1.9 convolution_convert_fusion
  125.4 46.7 %all_to_all.10 = bf16[32,24,2048]{2,1,0:T(8,128)(2,1)S(1)} all-to-all(bf16[32,24,2048]{2,1,0:T(8,128)(2,1)S(1)} %bitcast.142), channel_id=1, replica_groups=mesh['dp'=4,'sy'=4,'sx'=4,'sc'=2] {'sy','sx','sc'}, dimensions={0} | all-to-all | bytes 6291456 | tf_op jit(solution)/shard_map/all_to_all | solution.py:167
  172.1 7.6 %fusion.2 = f32[32,24,1408]{2,1,0:T(8,128)S(1)} fusion(bf16[32,24,2048]{2,1,0:T(8,128)(2,1)S(1)} %all_to_all.10, bf16[1,2048,1408]{2,1,0:T(8,128)(2,1)} %param.22), kind=kOutput, calls=%fused_computation.3 | convolution fusion | flops 4429185024 | bytes 13238272 | tf_op jit(solution)/shard_map/snd,df->snf/dot_general | solution.py:171
  179.8 5.8 %multiply_convert_fusion.2 = bf16[32,24,1408]{2,1,0:T(8,128)(2,1)S(1)} fusion(f32[32,24,1408]{2,1,0:T(8,128)S(1)} %fusion.2, bf16[32,24,2048]{2,1,0:T(8,128)(2,1)S(1)} %all_to_all.10, bf16[1,2048,1408]{2,1,0:T(8,128)(2,1)S(1)} %bitcast.158), kind=kOutput, calls=%fused_computation.12 | convolution fusion | flops 4435673088 | bytes 15400960 | tf_op jit(solution)/shard_map/snd,df->snf/dot_general | solution.py:168
  185.6 6.5 %fusion.10 = bf16[32,24,2048]{2,1,0:T(8,128)(2,1)} fusion(bf16[32,24,1408]{2,1,0:T(8,128)(2,1)S(1)} %multiply_convert_fusion.2, bf16[1,1408,2048]{2,1,0:T(8,128)(2,1)S(1)} %bitcast.160), kind=kOutput, calls=%fused_computation.14 | convolution fusion | flops 4430757888 | bytes 11075584 | tf_op jit(solution)/shard_map/snf,fd->snd/dot_general | solution.py:173
  192.1 4.9 %all-to-all-start.1 = ((bf16[32,24,2048]{2,1,0:T(8,128)(2,1)}), bf16[32,24,2048]{2,1,0:T(8,128)(2,1)}, u32[]{:S(2)}, u32[]{:S(2)}) async-start(bf16[32,24,2048]{2,1,0:T(8,128)(2,1)} %fusion.10), calls=%async_computation.1 | async-start | bytes 6291456 | tf_op jit(solution)/shard_map/all_to_all | solution.py:176
  197.2 41.8 %all-to-all-done.1 = bf16[32,24,2048]{2,1,0:T(8,128)(2,1)} async-done(((bf16[32,24,2048]{2,1,0:T(8,128)(2,1)}), bf16[32,24,2048]{2,1,0:T(8,128)(2,1)}, u32[]{:S(2)}, u32[]{:S(2)}) %all-to-all-start.1) | async-done | bytes 3145760 | tf_op jit(solution)/shard_map/all_to_all | solution.py:176
  239.1 3.4 %fusion.34 = f32[384,2048]{1,0:T(8,128)S(1)} fusion(bf16[768,2048]{1,0:T(8,128)(2,1)} %bitcast.40, f32[768]{0:T(1024)S(1)} %broadcast_in_dim.17, s32[768]{0:T(1024)S(1)} %eq.33), kind=kOutput, calls=%fused_computation.47 | convolution fusion | flops 1209139200 | bytes 6297600 | tf_op jit(solution)/shard_map/dot_general | solution.py:181
  242.5 4.6 %fusion.19 = bf16[384,2048]{1,0:T(8,128)(2,1)} fusion(f32[384,2048]{1,0:T(8,128)S(1)} %fusion.34, bf16[384,2048]{1,0:T(8,128)(2,1)S(1)} %copy-done.9, bf16[768,2048]{1,0:T(8,128)(2,1)} %bitcast.40, f32[768]{0:T(1024)S(1)} %broadcast_in_dim.17, s32[768]{0:T(1024)S(1)} %eq.33), kind=kOutput, calls=%fused_computation.20 | convolution fusion | flops 1212874752 | bytes 9443328 | tf_op jit(solution)/shard_map/dot_general | solution.py:181
  (69 shorter events, 1.9 us)
Async XLA Ops:
  6.5 57.4 %copy-start = (bf16[384,2048]{1,0:T(8,128)(2,1)S(1)}, bf16[384,2048]{1,0:T(8,128)(2,1)}, u32[]{:S(2)}) copy-start(bf16[384,2048]{1,0:T(8,128)(2,1)} %param.12) | copy-start | bytes 4718596
  6.5 109.3 %all-gather.2.cloned.1.call-start = ((), (), s32[]{:S(2)}) async-start(), calls=%async_computation.2 | async-start | bytes 8650752 | tf_op jit(solution)/shard_map/all_gather | solution.py:146
  11.3 7.9 %copy-start.3 = (bf16[384,2048]{0,1:T(8,128)(2,1)}, bf16[384,2048]{0,1:T(8,128)(2,1)S(1)}, u32[]{:S(2)}) copy-start(bf16[384,2048]{0,1:T(8,128)(2,1)S(1)} %copy.172) | copy-start | bytes 4718596
  15.8 2.3 collective-permute-start
  15.8 4.4 %copy-start.2 = (f32[16,128,128]{2,1,0:T(8,128)S(1)}, f32[16,128,128]{2,1,0:T(8,128)}, u32[]{:S(2)}) copy-start(f32[16,128,128]{2,1,0:T(8,128)} %get-tuple-element.37) | copy-start | bytes 3145732
  22.5 13.8 %collective-permute-start.1 = (bf16[1032,128]{0,1:T(8,128)(2,1)S(1)}, bf16[1032,128]{0,1:T(8,128)(2,1)S(1)}, u32[]{:S(2)}, u32[]{:S(2)}) collective-permute-start(bf16[1032,128]{0,1:T(8,128)(2,1)S(1)} %pad_maximum_fusion), channel_id=1, source_target_pairs={{0,6},{2,8},{4,10},{6,12},{8,14},{10,16},{12,18},{14,20},{16,22},{... | collective-permute-start | bytes 792584 | tf_op jit(solution)/shard_map/ppermute | solution.py:43
  27.3 12.7 %collective-permute-start.2 = (bf16[1032,128]{0,1:T(8,128)(2,1)S(1)}, bf16[1032,128]{0,1:T(8,128)(2,1)}, u32[]{:S(2)}, u32[]{:S(2)}) collective-permute-start(bf16[1032,128]{0,1:T(8,128)(2,1)S(1)} %pad_maximum_fusion), channel_id=1, source_target_pairs={{0,4},{2,6},{4,8},{6,10},{8,12},{10,14},{12,16},{14,18},{16,20},{1... | collective-permute-start | bytes 792584 | tf_op jit(solution)/shard_map/ppermute | solution.py:43
  32.4 12.1 %collective-permute-start.3 = (bf16[1032,128]{0,1:T(8,128)(2,1)S(1)}, bf16[1032,128]{0,1:T(8,128)(2,1)}, u32[]{:S(2)}, u32[]{:S(2)}) collective-permute-start(bf16[1032,128]{0,1:T(8,128)(2,1)S(1)} %pad_maximum_fusion), channel_id=1, source_target_pairs={{0,2},{2,4},{4,6},{6,8},{8,10},{10,12},{12,14},{14,16},{16,18},{18... | collective-permute-start | bytes 792584 | tf_op jit(solution)/shard_map/ppermute | solution.py:43
  36.3 0.7 copy-start.4
  52.2 36.0 %collective-permute-start.5 = (bf16[1032,128]{0,1:T(8,128)(2,1)S(1)}, bf16[1032,128]{0,1:T(8,128)(2,1)}, u32[]{:S(2)}, u32[]{:S(2)}) collective-permute-start(bf16[1032,128]{0,1:T(8,128)(2,1)S(1)} %pad_maximum_fusion.1), channel_id=1, source_target_pairs={{0,18},{2,20},{4,22},{6,24},{8,26},{10,28},{12,30},{1,19},{3,21},{... | collective-permute-start | bytes 792584 | tf_op jit(solution)/shard_map/ppermute | solution.py:43
  62.0 25.2 %collective-permute-start.4 = (bf16[1032,128]{0,1:T(8,128)(2,1)S(1)}, bf16[1032,128]{0,1:T(8,128)(2,1)}, u32[]{:S(2)}, u32[]{:S(2)}) collective-permute-start(bf16[1032,128]{0,1:T(8,128)(2,1)S(1)} %pad_maximum_fusion.1), channel_id=1, source_target_pairs={{0,26},{2,28},{4,30},{1,27},{3,29},{5,31},{32,58},{34,60},{36,62},... | collective-permute-start | bytes 792584 | tf_op jit(solution)/shard_map/ppermute | solution.py:43
  70.8 30.5 %collective-permute-start.7 = (bf16[1032,128]{0,1:T(8,128)(2,1)S(1)}, bf16[1032,128]{0,1:T(8,128)(2,1)}, u32[]{:S(2)}, u32[]{:S(2)}) collective-permute-start(bf16[1032,128]{0,1:T(8,128)(2,1)S(1)} %pad_maximum_fusion.1), channel_id=1, source_target_pairs={{0,2},{2,4},{4,6},{6,8},{8,10},{10,12},{12,14},{14,16},{16,18},{18... | collective-permute-start | bytes 792584 | tf_op jit(solution)/shard_map/ppermute | solution.py:43
  72.8 26.5 %collective-permute-start.6 = (bf16[1032,128]{0,1:T(8,128)(2,1)S(1)}, bf16[1032,128]{0,1:T(8,128)(2,1)}, u32[]{:S(2)}, u32[]{:S(2)}) collective-permute-start(bf16[1032,128]{0,1:T(8,128)(2,1)S(1)} %pad_maximum_fusion.1), channel_id=1, source_target_pairs={{0,10},{2,12},{4,14},{6,16},{8,18},{10,20},{12,22},{14,24},{16,26}... | collective-permute-start | bytes 792584 | tf_op jit(solution)/shard_map/ppermute | solution.py:43
  103.3 5.9 %copy-start.6 = (s32[32,24]{0,1:T(8,128)S(1)}, s32[32,24]{0,1:T(8,128)}, u32[]{:S(2)}) copy-start(s32[32,24]{0,1:T(8,128)} %param.17) | copy-start | bytes 9220
  107.1 2.3 collective-permute-start.8
  115.8 7.6 %copy-start.7 = (f32[2048]{0:T(1024)S(1)}, f32[2048]{0:T(1024)}, u32[]{:S(2)}) copy-start(f32[2048]{0:T(1024)} %param.19) | copy-start | bytes 24580
  123.4 2.0 copy-start.8
  125.4 54.4 %slice-start = ((s8[5767168]{0:T(1024)(128)(4,1)}), s8[4194304]{0:T(1024)(128)(4,1)S(1)}, s32[]{:S(2)}) async-start(s8[5767168]{0:T(1024)(128)(4,1)} %bitcast.157), calls=%async_computation.3 | async-start | bytes 8388608
  172.1 7.7 %slice-start.1 = ((s8[5767168]{0:T(1024)(128)(4,1)}), s8[1572864]{0:T(1024)(128)(4,1)S(1)}, s32[]{:S(2)}) async-start(s8[5767168]{0:T(1024)(128)(4,1)} %bitcast.157), calls=%async_computation.4 | async-start | bytes 3145728
  172.1 13.5 %slice-start.2 = ((s8[5767168]{0:T(1024)(128)(4,1)}), s8[4194304]{0:T(1024)(128)(4,1)S(1)}, s32[]{:S(2)}) async-start(s8[5767168]{0:T(1024)(128)(4,1)} %bitcast.159), calls=%async_computation.5 | async-start | bytes 8388608
  179.8 5.8 %slice-start.3 = ((s8[5767168]{0:T(1024)(128)(4,1)}), s8[1572864]{0:T(1024)(128)(4,1)S(1)}, s32[]{:S(2)}) async-start(s8[5767168]{0:T(1024)(128)(4,1)} %bitcast.159), calls=%async_computation.6 | async-start | bytes 3145728
  192.1 5.0 %copy-start.5 = (f32[32,24]{0,1:T(8,128)S(1)}, f32[32,24]{0,1:T(8,128)}, u32[]{:S(2)}) copy-start(f32[32,24]{0,1:T(8,128)} %param.18) | copy-start | bytes 9220
  192.1 47.0 %all-to-all-start.1 = ((bf16[32,24,2048]{2,1,0:T(8,128)(2,1)}), bf16[32,24,2048]{2,1,0:T(8,128)(2,1)}, u32[]{:S(2)}, u32[]{:S(2)}) async-start(bf16[32,24,2048]{2,1,0:T(8,128)(2,1)} %fusion.10), calls=%async_computation.1 | async-start | bytes 6291456 | tf_op jit(solution)/shard_map/all_to_all | solution.py:176
  239.1 3.4 %copy-start.9 = (bf16[384,2048]{1,0:T(8,128)(2,1)S(1)}, bf16[384,2048]{1,0:T(8,128)(2,1)}, u32[]{:S(2)}) copy-start(bf16[384,2048]{1,0:T(8,128)(2,1)} %copy-done.8) | copy-start | bytes 4718596
  242.5 4.6 %copy-start.1 = (bf16[384,2048]{1,0:T(8,128)(2,1)S(1)}, bf16[384,2048]{1,0:T(8,128)(2,1)}, u32[]{:S(2)}) copy-start(bf16[384,2048]{1,0:T(8,128)(2,1)} %param.12) | copy-start | bytes 4718596
Sparse Core Ops, SparseCore 0:
  9.6 81.1 all-gather.1

commit v9 on v7

--- a/solution.py
+++ b/solution.py
@@ -33,7 +33,7 @@
     return (earlier[0] * jnp.exp(latter[1])[:, None, None] + latter[0], earlier[1] + latter[1])
 
 
-def exclusive_scan(state, ending, axis):
+def exclusive_scan(state, ending, axis, rider):
     count = lax.axis_size(axis)
     heads = state.shape[0]
 
@@ -45,16 +45,18 @@
     reach = 1
     while 2 * reach < count:
         covered = combine(fetch(covered, reach), covered)
+        if reach == 1:
+            covered, rider = lax.optimization_barrier((covered, rider))
         reach *= 2
     if count == 1:
-        return jnp.zeros_like(state)
+        return jnp.zeros_like(state), rider
     near = fetch(covered, 1)
     if reach + 1 < count:
         near = combine(fetch(covered, reach + 1), near)
-    return near[0]
-
-
-def carried_in(state, ending):
+    return near[0], rider
+
+
+def carried_in(state, ending, rider):
     heads = state.shape[0]
     half = heads // 2
     swap = [(0, 1), (1, 0)]
@@ -64,16 +66,17 @@
     lower = (jnp.where(first, state, other_state), jnp.where(first, ending, other_ending))
     upper = (jnp.where(first, other_state, state), jnp.where(first, other_ending, ending))
     chip_state, chip_ending = combine(lower, upper)
-    mine = exclusive_scan(
+    mine, rider = exclusive_scan(
         lax.dynamic_slice_in_dim(chip_state, core * half, half, axis=0),
         lax.dynamic_slice_in_dim(chip_ending, core * half, half, axis=0),
         CHIP_AXES,
+        rider,
     )
     theirs = lax.ppermute(mine.astype(jnp.bfloat16), CORE_AXIS, swap).astype(jnp.float32)
     before = jnp.where(
         first, jnp.concatenate([mine, theirs], axis=0), jnp.concatenate([theirs, mine], axis=0)
     )
-    return jnp.where(first, before, combine((before, 0.0), lower)[0])
+    return jnp.where(first, before, combine((before, 0.0), lower)[0]), rider
 
 
 def shards(
@@ -105,7 +108,7 @@
     local_state = jnp.einsum(
         "hsd,hse->hde", key_scaled, value_heads, preferred_element_type=jnp.float32
     )
-    incoming = carried_in(local_state, ending)
+    incoming, out_weight = carried_in(local_state, ending, out_weight)
     scores = (
         jnp.einsum("htd,hsd->hts", query_heads, key_heads, preferred_element_type=jnp.float32)
         * scaling

time: 253 us -> 249 us (0.984)
  transfers between devices with their start and end apart: 9 -> 9, of which waited for: 5 -> 7; matrix products, arithmetic and copies ran while one was open for 20% -> 14% of each run, Pallas kernels for 0% -> 0%
where the time goes in v9:
time: 249 us; the launch traced here: 248 us
  waiting for transfers between devices  68 us (27%)
  matrix products  51.3 us (21%)
  blocking collectives  46.5 us (19%)
  starting transfers between devices  30.8 us (12%)
  other arithmetic  21.3 us (9%)
  local copies, waits for them, and re-layouts  16.4 us (7%)
  between operations  13.9 us (6%)
    all_to_all x1, blocking collectives, shards(): lax.all_to_all(picked[:, window], SEQ, split_axis=0, concat_axis=0, tiled...  46.5 us
    all_to_all x1, waiting for transfers between devices, shards(): lax.all_to_all(produced, SEQ, split_axis=0, concat_axis=0, tiled=True)  41.8 us
    ppermute x5, starting transfers between devices, fetch(): return unpack(lax.ppermute(pack(*pair), axis, pairs), heads)  25.8 us
    ppermute x5, waiting for transfers between devices, fetch(): return unpack(lax.ppermute(pack(*pair), axis, pairs), heads)  23.9 us
    dot_general x2, matrix products, shards(): jnp.dot(part.astype(jnp.bfloat16), flat_returned, preferred_element_type=...  8 us
    dot_general x1, matrix products, shards(): jnp.einsum('snd,df->snf', arrived, up_weight[0], preferred_element_type=j...  7.64 us
    dot_general x1, matrix products, shards(): jnp.dot(normed, lax.all_gather(out_weight, SEQ, axis=0, tiled=True), pref...  7.59 us
    convert_element_type x5, local copies, waits for them, and re-layouts, unpack(): message[:heads * width].reshape(heads, width, width).astype(jnp.float32)  7.31 us
  transfers between devices with their start and end apart: 9, of which 7 were waited for; matrix products, arithmetic and copies ran while one was open for 14% of the time, Pallas kernels for 0%

profile of v9, /device:TPU:0, one launch (start us, length us, event | category | flops | bytes accessed | tf_op | source)
XLA Modules:
  0.0 248.3 jit_solution(10880060944369410219)
XLA Ops:
  6.5 0.9 copy_bitcast_fusion.1
  7.4 0.9 reduce-window.6
  8.3 0.2 slice_reduce_fusion
  8.7 0.1 copy.174
  8.9 1.9 copy.172
  10.8 3.6 %fusion.104 = (bf16[16,128,128]{2,1,0:T(8,128)(2,1)S(1)}, f32[16,128,128]{2,1,0:T(8,128)}) fusion(bf16[16,384,128]{1,2,0:T(8,128)(2,1)S(1)} %bitcast.145, f32[16,384]{1,0:T(8,128)S(1)} %get-tuple-element.25, bf16[384,2048]{1,0:T(8,128)(2,1)} %param.14), kind=kOutput, calls=%fused_computation.177 | convolution fusion | flops 203948032 | bytes 4743168 | tf_op jit(solution)/shard_map/hsd,hse->hde/dot_general | solution.py:108
  14.4 0.8 fusion.42
  15.3 2.3 collective-permute-done
  17.5 0.7 slice_convert_fusion.5
  18.2 0.2 fusion.67
  18.4 1.1 slice.121
  19.5 0.1 convert.6
  19.6 0.1 broadcast_select_fusion
  19.8 1.0 fusion.101
  20.8 0.1 copy.155
  21.1 3.5 %collective-permute-start.1 = (bf16[1032,128]{0,1:T(8,128)(2,1)S(1)}, bf16[1032,128]{0,1:T(8,128)(2,1)S(1)}, u32[]{:S(2)}, u32[]{:S(2)}) collective-permute-start(bf16[1032,128]{0,1:T(8,128)(2,1)S(1)} %pad_maximum_fusion), channel_id=1, source_target_pairs={{0,2},{2,4},{4,6},{6,8},{8,10},{10,12},{12,14},{14,16},{16,18},{18... | collective-permute-start | bytes 792584 | tf_op jit(solution)/shard_map/ppermute | solution.py:42
  24.6 6.5 %collective-permute-done.1 = bf16[1032,128]{0,1:T(8,128)(2,1)S(1)} collective-permute-done((bf16[1032,128]{0,1:T(8,128)(2,1)S(1)}, bf16[1032,128]{0,1:T(8,128)(2,1)S(1)}, u32[]{:S(2)}, u32[]{:S(2)}) %collective-permute-start.1) | collective-permute-done | bytes 264224 | tf_op jit(solution)/shard_map/ppermute | solution.py:42
  31.2 1.0 copy.156
  32.2 1.3 multiply_add_fusion.2
  33.6 0.9 copy.157
  34.5 1.0 pad_maximum_fusion.1
  35.5 5.9 %collective-permute-start.2 = (bf16[1032,128]{0,1:T(8,128)(2,1)S(1)}, bf16[1032,128]{0,1:T(8,128)(2,1)S(1)}, u32[]{:S(2)}, u32[]{:S(2)}) collective-permute-start(bf16[1032,128]{0,1:T(8,128)(2,1)S(1)} %pad_maximum_fusion.1), channel_id=1, source_target_pairs={{0,4},{2,6},{4,8},{6,10},{8,12},{10,14},{12,16},{14,18},{16,20},{1... | collective-permute-start | bytes 792584 | tf_op jit(solution)/shard_map/ppermute | solution.py:42
  41.4 5.7 %collective-permute-done.2 = bf16[1032,128]{0,1:T(8,128)(2,1)S(1)} collective-permute-done((bf16[1032,128]{0,1:T(8,128)(2,1)S(1)}, bf16[1032,128]{0,1:T(8,128)(2,1)S(1)}, u32[]{:S(2)}, u32[]{:S(2)}) %collective-permute-start.2) | collective-permute-done | bytes 264224 | tf_op jit(solution)/shard_map/ppermute | solution.py:42
  47.1 0.7 copy-done.5
  47.8 0.8 slice_convert_fusion.3
  48.7 2.1 copy.158
  50.8 1.2 fusion.46
  52.0 0.9 copy.159
  52.8 0.7 slice_convert_fusion.8
  53.5 1.0 pad_maximum_fusion.2
  54.5 7.6 %collective-permute-start.3 = (bf16[1032,128]{0,1:T(8,128)(2,1)S(1)}, bf16[1032,128]{0,1:T(8,128)(2,1)S(1)}, u32[]{:S(2)}, u32[]{:S(2)}) collective-permute-start(bf16[1032,128]{0,1:T(8,128)(2,1)S(1)} %pad_maximum_fusion.2), channel_id=1, source_target_pairs={{0,8},{2,10},{4,12},{6,14},{8,16},{10,18},{12,20},{14,22},{16,24},... | collective-permute-start | bytes 792584 | tf_op jit(solution)/shard_map/ppermute | solution.py:42
  62.1 0.7 iota_compare_fusion.4
  62.8 4.0 %collective-permute-done.3 = bf16[1032,128]{0,1:T(8,128)(2,1)S(1)} collective-permute-done((bf16[1032,128]{0,1:T(8,128)(2,1)S(1)}, bf16[1032,128]{0,1:T(8,128)(2,1)S(1)}, u32[]{:S(2)}, u32[]{:S(2)}) %collective-permute-start.3) | collective-permute-done | bytes 264224 | tf_op jit(solution)/shard_map/ppermute | solution.py:42
  66.8 0.7 copy-done.4
  67.5 0.8 slice_convert_fusion.2
  68.4 2.2 copy.160
  70.6 1.4 add_convert_fusion.1
  72.0 0.1 copy.161
  72.1 0.7 slice_convert_fusion.7
  72.9 5.4 %collective-permute-start.4 = (bf16[1032,128]{0,1:T(8,128)(2,1)S(1)}, bf16[1032,128]{0,1:T(8,128)(2,1)}, u32[]{:S(2)}, u32[]{:S(2)}) collective-permute-start(bf16[1032,128]{0,1:T(8,128)(2,1)S(1)} %pad_maximum_fusion.3), channel_id=1, source_target_pairs={{0,18},{2,20},{4,22},{6,24},{8,26},{10,28},{12,30},{1,19},{3,21},{... | collective-permute-start | bytes 792584 | tf_op jit(solution)/shard_map/ppermute | solution.py:42
  78.3 3.4 %collective-permute-start.5 = (bf16[1032,128]{0,1:T(8,128)(2,1)S(1)}, bf16[1032,128]{0,1:T(8,128)(2,1)}, u32[]{:S(2)}, u32[]{:S(2)}) collective-permute-start(bf16[1032,128]{0,1:T(8,128)(2,1)S(1)} %pad_maximum_fusion.3), channel_id=1, source_target_pairs={{0,2},{2,4},{4,6},{6,8},{8,10},{10,12},{12,14},{14,16},{16,18},{18... | collective-permute-start | bytes 792584 | tf_op jit(solution)/shard_map/ppermute | solution.py:42
  81.6 6.8 %fusion.6 = f32[16,384,128]{2,1,0:T(8,128)} fusion(f32[16,384]{1,0:T(8,128)S(1)} %copy_bitcast_fusion, pred[384,384]{1,0:T(8,128)(4,1)} %iota_compare_fusion.4, bf16[16,384,128]{1,2,0:T(8,128)(2,1)} %bitcast.146, bf16[384,2048]{1,0:T(8,128)(2,1)S(1)} %copy-done, bf16[384,2048]{1,0:T(8,128)(2,1)} %param.14), kind=kOutput, calls=%fused_computation.10 | convolution fusion | flops 1222115328 | bytes 8036352 | tf_op jit(solution)/shard_map/hts,hsd->htd/dot_general | solution.py:120
  88.4 2.8 %collective-permute-done.4 = bf16[1032,128]{0,1:T(8,128)(2,1)} collective-permute-done((bf16[1032,128]{0,1:T(8,128)(2,1)S(1)}, bf16[1032,128]{0,1:T(8,128)(2,1)}, u32[]{:S(2)}, u32[]{:S(2)}) %collective-permute-start.4) | collective-permute-done | bytes 264224 | tf_op jit(solution)/shard_map/ppermute | solution.py:42
  91.2 1.0 slice_convert_fusion.1
  92.2 1.0 copy.162
  93.2 4.9 %collective-permute-done.5 = bf16[1032,128]{0,1:T(8,128)(2,1)} collective-permute-done((bf16[1032,128]{0,1:T(8,128)(2,1)S(1)}, bf16[1032,128]{0,1:T(8,128)(2,1)}, u32[]{:S(2)}, u32[]{:S(2)}) %collective-permute-start.5) | collective-permute-done | bytes 264224 | tf_op jit(solution)/shard_map/ppermute | solution.py:42
  98.1 1.0 slice_convert_fusion
  99.1 1.0 copy.163
  100.1 0.7 slice_convert_fusion.6
  100.8 2.0 fusion.98
  102.8 1.8 multiply_convert_fusion.5
  104.9 3.5 %multiply_reduce_fusion = (f32[16,384]{1,0:T(8,128)S(1)}, f32[16,384,128]{2,1,0:T(8,128)S(1)}) fusion(f32[16,384,128]{2,1,0:T(8,128)} %fusion.6, bf16[16,384,128]{2,1,0:T(8,128)(2,1)} %multiply_convert_fusion.5, f32[16,128,128]{2,1,0:T(8,128)S(1)} %broadcast_select_fusion, f32[8,128,128]{2,1,0:T(8,128)S(1)} %get-tuple-element.16, ...), kind=kOutput, calls=%fused_computation.23 | convolution fusion | flops 205514752 | bytes 9986113 | tf_op jit(solution)/shard_map/htd,hde->hte/dot_general | solution.py:127
  108.4 1.0 fusion.21
  109.4 0.9 copy.166
  110.3 7.6 %fusion.15 = (f32[384]{0:T(512)S(1)}, bf16[384,2048]{1,0:T(8,128)(2,1)S(1)}) fusion(bf16[384,2048]{0,1:T(8,128)(2,1)S(1)} %bitcast.157, bf16[2048,2048]{1,0:T(8,128)(2,1)} %all-gather.2.cloned.1.call-done, bf16[384,2048]{1,0:T(8,128)(2,1)} %param.15), kind=kOutput, calls=%fused_computation.16 | convolution fusion | flops 3225943552 | bytes 13108736 | tf_op jit(solution)/shard_map/dot_general | solution.py:141
  118.0 1.9 convolution_convert_fusion
  119.9 46.5 %all_to_all.10 = bf16[32,24,2048]{2,1,0:T(8,128)(2,1)S(1)} all-to-all(bf16[32,24,2048]{2,1,0:T(8,128)(2,1)S(1)} %bitcast.151), channel_id=1, replica_groups=mesh['dp'=4,'sy'=4,'sx'=4,'sc'=2] {'sy','sx','sc'}, dimensions={0} | all-to-all | bytes 6291456 | tf_op jit(solution)/shard_map/all_to_all | solution.py:164
  166.4 7.6 %fusion.2 = f32[32,24,1408]{2,1,0:T(8,128)S(1)} fusion(bf16[32,24,2048]{2,1,0:T(8,128)(2,1)S(1)} %all_to_all.10, bf16[1,2048,1408]{2,1,0:T(8,128)(2,1)} %param.22), kind=kOutput, calls=%fused_computation.3 | convolution fusion | flops 4429185024 | bytes 13238272 | tf_op jit(solution)/shard_map/snd,df->snf/dot_general | solution.py:168
  174.1 5.8 %multiply_convert_fusion.2 = bf16[32,24,1408]{2,1,0:T(8,128)(2,1)S(1)} fusion(f32[32,24,1408]{2,1,0:T(8,128)S(1)} %fusion.2, bf16[32,24,2048]{2,1,0:T(8,128)(2,1)S(1)} %all_to_all.10, bf16[1,2048,1408]{2,1,0:T(8,128)(2,1)S(1)} %bitcast.166), kind=kOutput, calls=%fused_computation.12 | convolution fusion | flops 4435673088 | bytes 15400960 | tf_op jit(solution)/shard_map/snd,df->snf/dot_general | solution.py:165
  179.9 6.6 %fusion.10 = bf16[32,24,2048]{2,1,0:T(8,128)(2,1)} fusion(bf16[32,24,1408]{2,1,0:T(8,128)(2,1)S(1)} %multiply_convert_fusion.2, bf16[1,1408,2048]{2,1,0:T(8,128)(2,1)S(1)} %bitcast.168), kind=kOutput, calls=%fused_computation.14 | convolution fusion | flops 4430757888 | bytes 11075584 | tf_op jit(solution)/shard_map/snf,fd->snd/dot_general | solution.py:170
  186.5 5.0 %all-to-all-start.1 = ((bf16[32,24,2048]{2,1,0:T(8,128)(2,1)}), bf16[32,24,2048]{2,1,0:T(8,128)(2,1)}, u32[]{:S(2)}, u32[]{:S(2)}) async-start(bf16[32,24,2048]{2,1,0:T(8,128)(2,1)} %fusion.10), calls=%async_computation.1 | async-start | bytes 6291456 | tf_op jit(solution)/shard_map/all_to_all | solution.py:173
  191.6 41.8 %all-to-all-done.1 = bf16[32,24,2048]{2,1,0:T(8,128)(2,1)} async-done(((bf16[32,24,2048]{2,1,0:T(8,128)(2,1)}), bf16[32,24,2048]{2,1,0:T(8,128)(2,1)}, u32[]{:S(2)}, u32[]{:S(2)}) %all-to-all-start.1) | async-done | bytes 3145760 | tf_op jit(solution)/shard_map/all_to_all | solution.py:173
  233.5 3.4 %fusion.34 = f32[384,2048]{1,0:T(8,128)S(1)} fusion(bf16[768,2048]{1,0:T(8,128)(2,1)} %bitcast.44, f32[768]{0:T(1024)S(1)} %broadcast_in_dim.21, s32[768]{0:T(1024)S(1)} %eq.33), kind=kOutput, calls=%fused_computation.47 | convolution fusion | flops 1209139200 | bytes 6297600 | tf_op jit(solution)/shard_map/dot_general | solution.py:178
  236.9 4.6 %fusion.19 = bf16[384,2048]{1,0:T(8,128)(2,1)} fusion(f32[384,2048]{1,0:T(8,128)S(1)} %fusion.34, bf16[384,2048]{1,0:T(8,128)(2,1)S(1)} %copy-done.10, bf16[768,2048]{1,0:T(8,128)(2,1)} %bitcast.44, f32[768]{0:T(1024)S(1)} %broadcast_in_dim.21, s32[768]{0:T(1024)S(1)} %eq.33), kind=kOutput, calls=%fused_computation.20 | convolution fusion | flops 1212874752 | bytes 9443328 | tf_op jit(solution)/shard_map/dot_general | solution.py:178
  (71 shorter events, 1.3 us)
Async XLA Ops:
  6.5 75.1 %copy-start = (bf16[384,2048]{1,0:T(8,128)(2,1)S(1)}, bf16[384,2048]{1,0:T(8,128)(2,1)}, u32[]{:S(2)}) copy-start(bf16[384,2048]{1,0:T(8,128)(2,1)} %param.12) | copy-start | bytes 4718596
  6.5 103.8 %all-gather.2.cloned.1.call-start = ((), (), s32[]{:S(2)}) async-start(), calls=%async_computation.2 | async-start | bytes 8650752 | tf_op jit(solution)/shard_map/all_gather | solution.py:143
  10.8 8.7 %copy-start.3 = (bf16[384,2048]{0,1:T(8,128)(2,1)}, bf16[384,2048]{0,1:T(8,128)(2,1)S(1)}, u32[]{:S(2)}) copy-start(bf16[384,2048]{0,1:T(8,128)(2,1)S(1)} %copy.172) | copy-start | bytes 4718596
  15.3 2.3 collective-permute-start
  15.3 4.3 %copy-start.2 = (f32[16,128,128]{2,1,0:T(8,128)S(1)}, f32[16,128,128]{2,1,0:T(8,128)}, u32[]{:S(2)}) copy-start(f32[16,128,128]{2,1,0:T(8,128)} %get-tuple-element.46) | copy-start | bytes 3145732
  21.1 10.1 %collective-permute-start.1 = (bf16[1032,128]{0,1:T(8,128)(2,1)S(1)}, bf16[1032,128]{0,1:T(8,128)(2,1)S(1)}, u32[]{:S(2)}, u32[]{:S(2)}) collective-permute-start(bf16[1032,128]{0,1:T(8,128)(2,1)S(1)} %pad_maximum_fusion), channel_id=1, source_target_pairs={{0,2},{2,4},{4,6},{6,8},{8,10},{10,12},{12,14},{14,16},{16,18},{18... | collective-permute-start | bytes 792584 | tf_op jit(solution)/shard_map/ppermute | solution.py:42
  35.5 11.6 %collective-permute-start.2 = (bf16[1032,128]{0,1:T(8,128)(2,1)S(1)}, bf16[1032,128]{0,1:T(8,128)(2,1)S(1)}, u32[]{:S(2)}, u32[]{:S(2)}) collective-permute-start(bf16[1032,128]{0,1:T(8,128)(2,1)S(1)} %pad_maximum_fusion.1), channel_id=1, source_target_pairs={{0,4},{2,6},{4,8},{6,10},{8,12},{10,14},{12,16},{14,18},{16,20},{1... | collective-permute-start | bytes 792584 | tf_op jit(solution)/shard_map/ppermute | solution.py:42
  47.1 0.7 copy-start.5
  54.5 12.3 %collective-permute-start.3 = (bf16[1032,128]{0,1:T(8,128)(2,1)S(1)}, bf16[1032,128]{0,1:T(8,128)(2,1)S(1)}, u32[]{:S(2)}, u32[]{:S(2)}) collective-permute-start(bf16[1032,128]{0,1:T(8,128)(2,1)S(1)} %pad_maximum_fusion.2), channel_id=1, source_target_pairs={{0,8},{2,10},{4,12},{6,14},{8,16},{10,18},{12,20},{14,22},{16,24},... | collective-permute-start | bytes 792584 | tf_op jit(solution)/shard_map/ppermute | solution.py:42
  66.8 0.7 copy-start.4
  72.9 18.4 %collective-permute-start.4 = (bf16[1032,128]{0,1:T(8,128)(2,1)S(1)}, bf16[1032,128]{0,1:T(8,128)(2,1)}, u32[]{:S(2)}, u32[]{:S(2)}) collective-permute-start(bf16[1032,128]{0,1:T(8,128)(2,1)S(1)} %pad_maximum_fusion.3), channel_id=1, source_target_pairs={{0,18},{2,20},{4,22},{6,24},{8,26},{10,28},{12,30},{1,19},{3,21},{... | collective-permute-start | bytes 792584 | tf_op jit(solution)/shard_map/ppermute | solution.py:42
  78.3 19.8 %collective-permute-start.5 = (bf16[1032,128]{0,1:T(8,128)(2,1)S(1)}, bf16[1032,128]{0,1:T(8,128)(2,1)}, u32[]{:S(2)}, u32[]{:S(2)}) collective-permute-start(bf16[1032,128]{0,1:T(8,128)(2,1)S(1)} %pad_maximum_fusion.3), channel_id=1, source_target_pairs={{0,2},{2,4},{4,6},{6,8},{8,10},{10,12},{12,14},{14,16},{16,18},{18... | collective-permute-start | bytes 792584 | tf_op jit(solution)/shard_map/ppermute | solution.py:42
  99.1 5.6 %copy-start.7 = (s32[32,24]{0,1:T(8,128)S(1)}, s32[32,24]{0,1:T(8,128)}, u32[]{:S(2)}) copy-start(s32[32,24]{0,1:T(8,128)} %param.17) | copy-start | bytes 9220
  102.8 2.0 collective-permute-start.6
  110.3 7.6 %copy-start.8 = (f32[2048]{0:T(1024)S(1)}, f32[2048]{0:T(1024)}, u32[]{:S(2)}) copy-start(f32[2048]{0:T(1024)} %param.19) | copy-start | bytes 24580
  117.9 2.0 copy-start.9
  119.9 54.2 %slice-start = ((s8[5767168]{0:T(1024)(128)(4,1)}), s8[4194304]{0:T(1024)(128)(4,1)S(1)}, s32[]{:S(2)}) async-start(s8[5767168]{0:T(1024)(128)(4,1)} %bitcast.165), calls=%async_computation.3 | async-start | bytes 8388608
  166.4 7.7 %slice-start.1 = ((s8[5767168]{0:T(1024)(128)(4,1)}), s8[1572864]{0:T(1024)(128)(4,1)S(1)}, s32[]{:S(2)}) async-start(s8[5767168]{0:T(1024)(128)(4,1)} %bitcast.165), calls=%async_computation.4 | async-start | bytes 3145728
  166.4 13.5 %slice-start.2 = ((s8[5767168]{0:T(1024)(128)(4,1)}), s8[4194304]{0:T(1024)(128)(4,1)S(1)}, s32[]{:S(2)}) async-start(s8[5767168]{0:T(1024)(128)(4,1)} %bitcast.167), calls=%async_computation.5 | async-start | bytes 8388608
  174.1 5.8 %slice-start.3 = ((s8[5767168]{0:T(1024)(128)(4,1)}), s8[1572864]{0:T(1024)(128)(4,1)S(1)}, s32[]{:S(2)}) async-start(s8[5767168]{0:T(1024)(128)(4,1)} %bitcast.167), calls=%async_computation.6 | async-start | bytes 3145728
  186.5 5.0 %copy-start.6 = (f32[32,24]{0,1:T(8,128)S(1)}, f32[32,24]{0,1:T(8,128)}, u32[]{:S(2)}) copy-start(f32[32,24]{0,1:T(8,128)} %param.18) | copy-start | bytes 9220
  186.5 47.0 %all-to-all-start.1 = ((bf16[32,24,2048]{2,1,0:T(8,128)(2,1)}), bf16[32,24,2048]{2,1,0:T(8,128)(2,1)}, u32[]{:S(2)}, u32[]{:S(2)}) async-start(bf16[32,24,2048]{2,1,0:T(8,128)(2,1)} %fusion.10), calls=%async_computation.1 | async-start | bytes 6291456 | tf_op jit(solution)/shard_map/all_to_all | solution.py:173
  233.5 3.4 %copy-start.10 = (bf16[384,2048]{1,0:T(8,128)(2,1)S(1)}, bf16[384,2048]{1,0:T(8,128)(2,1)}, u32[]{:S(2)}) copy-start(bf16[384,2048]{1,0:T(8,128)(2,1)} %copy-done.9) | copy-start | bytes 4718596
  236.9 4.6 %copy-start.1 = (bf16[384,2048]{1,0:T(8,128)(2,1)S(1)}, bf16[384,2048]{1,0:T(8,128)(2,1)}, u32[]{:S(2)}) copy-start(bf16[384,2048]{1,0:T(8,128)(2,1)} %param.12) | copy-start | bytes 4718596
Sparse Core Ops, SparseCore 0:
  33.7 65.3 all-gather.1

commit v10 on v9

--- a/solution.py
+++ b/solution.py
@@ -7,6 +7,7 @@
 CHIP_AXES = ("sy", "sx")
 CORE_AXIS = "sc"
 CHUNKS = 1
+SCATTER_PIECES = 1
 
 
 def pack(state, ending):
@@ -173,7 +174,7 @@
         returned = lax.all_to_all(produced, SEQ, split_axis=0, concat_axis=0, tiled=True)
         flat_returned = returned.reshape(-1, model_width)
         remaining = spread_weight[:, :, window].reshape(length, -1)
-        for _ in range(2):
+        for _ in range(SCATTER_PIECES):
             part = lax.reduce_precision(remaining, exponent_bits=8, mantissa_bits=7)
             total = total + jnp.dot(
                 part.astype(jnp.bfloat16), flat_returned, preferred_element_type=jnp.float32

time: 249 us -> 246 us (0.988)
  matrix products: 51.3 us -> 47.9 us
    dot_general x2 -> x1, matrix products: 8 us -> 4.56 us  [shards(): jnp.dot(part.astype(jnp.bfloat16), flat_returned, preferred_element_type=...]
  transfers between devices with their start and end apart: 9 -> 9, of which waited for: 7 -> 7; matrix products, arithmetic and copies ran while one was open for 14% -> 15% of each run, Pallas kernels for 0% -> 0%
where the time goes in v10:
time: 246 us; the launch traced here: 245 us
  waiting for transfers between devices  68 us (28%)
  matrix products  47.9 us (19%)
  blocking collectives  46.5 us (19%)
  starting transfers between devices  30.8 us (13%)
  other arithmetic  21.3 us (9%)
  local copies, waits for them, and re-layouts  16.4 us (7%)
  between operations  13.8 us (6%)
    all_to_all x1, blocking collectives, shards(): lax.all_to_all(picked[:, window], SEQ, split_axis=0, concat_axis=0, tiled...  46.5 us
    all_to_all x1, waiting for transfers between devices, shards(): lax.all_to_all(produced, SEQ, split_axis=0, concat_axis=0, tiled=True)  41.8 us
    ppermute x5, starting transfers between devices, fetch(): return unpack(lax.ppermute(pack(*pair), axis, pairs), heads)  25.8 us
    ppermute x5, waiting for transfers between devices, fetch(): return unpack(lax.ppermute(pack(*pair), axis, pairs), heads)  23.9 us
    dot_general x1, matrix products, shards(): jnp.einsum('snd,df->snf', arrived, up_weight[0], preferred_element_type=j...  7.64 us
    dot_general x1, matrix products, shards(): jnp.dot(normed, lax.all_gather(out_weight, SEQ, axis=0, tiled=True), pref...  7.59 us
    convert_element_type x5, local copies, waits for them, and re-layouts, unpack(): message[:heads * width].reshape(heads, width, width).astype(jnp.float32)  7.31 us
    dot_general x1, matrix products, shards(): jnp.einsum('hts,hsd->htd', attend_weights, value_heads, preferred_element...  6.76 us
  transfers between devices with their start and end apart: 9, of which 7 were waited for; matrix products, arithmetic and copies ran while one was open for 15% of the time, Pallas kernels for 0%

profile of v10, /device:TPU:0, one launch (start us, length us, event | category | flops | bytes accessed | tf_op | source)
XLA Modules:
  0.0 244.9 jit_solution(732674279572451302)
XLA Ops:
  6.5 0.9 copy_bitcast_fusion.1
  7.4 0.9 reduce-window.6
  8.3 0.2 slice_reduce_fusion
  8.7 0.1 copy.174
  8.8 0.1 subtract_exponential_fusion
  8.9 1.9 copy.172
  10.8 3.6 %fusion.95 = (bf16[16,128,128]{2,1,0:T(8,128)(2,1)S(1)}, f32[16,128,128]{2,1,0:T(8,128)}) fusion(bf16[16,384,128]{1,2,0:T(8,128)(2,1)S(1)} %bitcast.144, f32[16,384]{1,0:T(8,128)S(1)} %get-tuple-element.25, bf16[384,2048]{1,0:T(8,128)(2,1)} %param.14), kind=kOutput, calls=%fused_computation.168 | convolution fusion | flops 203948032 | bytes 4743168 | tf_op jit(solution)/shard_map/hsd,hse->hde/dot_general | solution.py:109
  14.4 0.8 fusion.34
  15.3 2.3 collective-permute-done
  17.5 0.7 slice_convert_fusion.5
  18.2 0.2 fusion.59
  18.4 1.1 slice.121
  19.5 0.1 convert.6
  19.6 0.1 broadcast_select_fusion
  19.8 1.0 fusion.92
  20.8 0.1 copy.155
  21.1 3.5 %collective-permute-start.1 = (bf16[1032,128]{0,1:T(8,128)(2,1)S(1)}, bf16[1032,128]{0,1:T(8,128)(2,1)S(1)}, u32[]{:S(2)}, u32[]{:S(2)}) collective-permute-start(bf16[1032,128]{0,1:T(8,128)(2,1)S(1)} %pad_maximum_fusion), channel_id=1, source_target_pairs={{0,2},{2,4},{4,6},{6,8},{8,10},{10,12},{12,14},{14,16},{16,18},{18... | collective-permute-start | bytes 792584 | tf_op jit(solution)/shard_map/ppermute | solution.py:43
  24.6 6.5 %collective-permute-done.1 = bf16[1032,128]{0,1:T(8,128)(2,1)S(1)} collective-permute-done((bf16[1032,128]{0,1:T(8,128)(2,1)S(1)}, bf16[1032,128]{0,1:T(8,128)(2,1)S(1)}, u32[]{:S(2)}, u32[]{:S(2)}) %collective-permute-start.1) | collective-permute-done | bytes 264224 | tf_op jit(solution)/shard_map/ppermute | solution.py:43
  31.2 1.0 copy.156
  32.2 1.3 multiply_add_fusion.2
  33.6 0.9 copy.157
  34.5 1.0 pad_maximum_fusion.1
  35.5 5.9 %collective-permute-start.2 = (bf16[1032,128]{0,1:T(8,128)(2,1)S(1)}, bf16[1032,128]{0,1:T(8,128)(2,1)S(1)}, u32[]{:S(2)}, u32[]{:S(2)}) collective-permute-start(bf16[1032,128]{0,1:T(8,128)(2,1)S(1)} %pad_maximum_fusion.1), channel_id=1, source_target_pairs={{0,4},{2,6},{4,8},{6,10},{8,12},{10,14},{12,16},{14,18},{16,20},{1... | collective-permute-start | bytes 792584 | tf_op jit(solution)/shard_map/ppermute | solution.py:43
  41.4 5.7 %collective-permute-done.2 = bf16[1032,128]{0,1:T(8,128)(2,1)S(1)} collective-permute-done((bf16[1032,128]{0,1:T(8,128)(2,1)S(1)}, bf16[1032,128]{0,1:T(8,128)(2,1)S(1)}, u32[]{:S(2)}, u32[]{:S(2)}) %collective-permute-start.2) | collective-permute-done | bytes 264224 | tf_op jit(solution)/shard_map/ppermute | solution.py:43
  47.1 0.7 copy-done.5
  47.8 0.8 slice_convert_fusion.3
  48.7 2.1 copy.158
  50.8 1.2 fusion.38
  52.0 0.9 copy.159
  52.8 0.7 slice_convert_fusion.8
  53.5 1.0 pad_maximum_fusion.2
  54.5 7.6 %collective-permute-start.3 = (bf16[1032,128]{0,1:T(8,128)(2,1)S(1)}, bf16[1032,128]{0,1:T(8,128)(2,1)S(1)}, u32[]{:S(2)}, u32[]{:S(2)}) collective-permute-start(bf16[1032,128]{0,1:T(8,128)(2,1)S(1)} %pad_maximum_fusion.2), channel_id=1, source_target_pairs={{0,8},{2,10},{4,12},{6,14},{8,16},{10,18},{12,20},{14,22},{16,24},... | collective-permute-start | bytes 792584 | tf_op jit(solution)/shard_map/ppermute | solution.py:43
  62.1 0.7 iota_compare_fusion.4
  62.8 4.0 %collective-permute-done.3 = bf16[1032,128]{0,1:T(8,128)(2,1)S(1)} collective-permute-done((bf16[1032,128]{0,1:T(8,128)(2,1)S(1)}, bf16[1032,128]{0,1:T(8,128)(2,1)S(1)}, u32[]{:S(2)}, u32[]{:S(2)}) %collective-permute-start.3) | collective-permute-done | bytes 264224 | tf_op jit(solution)/shard_map/ppermute | solution.py:43
  66.8 0.7 copy-done.4
  67.5 0.8 slice_convert_fusion.2
  68.4 2.2 copy.160
  70.6 1.4 add_convert_fusion.1
  72.0 0.1 copy.161
  72.1 0.7 slice_convert_fusion.7
  72.9 5.4 %collective-permute-start.4 = (bf16[1032,128]{0,1:T(8,128)(2,1)S(1)}, bf16[1032,128]{0,1:T(8,128)(2,1)}, u32[]{:S(2)}, u32[]{:S(2)}) collective-permute-start(bf16[1032,128]{0,1:T(8,128)(2,1)S(1)} %pad_maximum_fusion.3), channel_id=1, source_target_pairs={{0,18},{2,20},{4,22},{6,24},{8,26},{10,28},{12,30},{1,19},{3,21},{... | collective-permute-start | bytes 792584 | tf_op jit(solution)/shard_map/ppermute | solution.py:43
  78.3 3.4 %collective-permute-start.5 = (bf16[1032,128]{0,1:T(8,128)(2,1)S(1)}, bf16[1032,128]{0,1:T(8,128)(2,1)}, u32[]{:S(2)}, u32[]{:S(2)}) collective-permute-start(bf16[1032,128]{0,1:T(8,128)(2,1)S(1)} %pad_maximum_fusion.3), channel_id=1, source_target_pairs={{0,2},{2,4},{4,6},{6,8},{8,10},{10,12},{12,14},{14,16},{16,18},{18... | collective-permute-start | bytes 792584 | tf_op jit(solution)/shard_map/ppermute | solution.py:43
  81.6 6.8 %fusion.6 = f32[16,384,128]{2,1,0:T(8,128)} fusion(f32[16,384]{1,0:T(8,128)S(1)} %copy_bitcast_fusion, pred[384,384]{1,0:T(8,128)(4,1)} %iota_compare_fusion.4, bf16[16,384,128]{1,2,0:T(8,128)(2,1)} %bitcast.145, bf16[384,2048]{1,0:T(8,128)(2,1)S(1)} %copy-done, bf16[384,2048]{1,0:T(8,128)(2,1)} %param.14), kind=kOutput, calls=%fused_computation.10 | convolution fusion | flops 1222115328 | bytes 8036352 | tf_op jit(solution)/shard_map/hts,hsd->htd/dot_general | solution.py:121
  88.4 2.8 %collective-permute-done.4 = bf16[1032,128]{0,1:T(8,128)(2,1)} collective-permute-done((bf16[1032,128]{0,1:T(8,128)(2,1)S(1)}, bf16[1032,128]{0,1:T(8,128)(2,1)}, u32[]{:S(2)}, u32[]{:S(2)}) %collective-permute-start.4) | collective-permute-done | bytes 264224 | tf_op jit(solution)/shard_map/ppermute | solution.py:43
  91.2 1.0 slice_convert_fusion.1
  92.2 1.0 copy.162
  93.2 4.9 %collective-permute-done.5 = bf16[1032,128]{0,1:T(8,128)(2,1)} collective-permute-done((bf16[1032,128]{0,1:T(8,128)(2,1)S(1)}, bf16[1032,128]{0,1:T(8,128)(2,1)}, u32[]{:S(2)}, u32[]{:S(2)}) %collective-permute-start.5) | collective-permute-done | bytes 264224 | tf_op jit(solution)/shard_map/ppermute | solution.py:43
  98.1 1.0 slice_convert_fusion
  99.1 1.0 copy.163
  100.1 0.7 slice_convert_fusion.6
  100.8 2.0 fusion.89
  102.8 1.8 multiply_convert_fusion.5
  104.9 3.5 %multiply_reduce_fusion = (f32[16,384]{1,0:T(8,128)S(1)}, f32[16,384,128]{2,1,0:T(8,128)S(1)}) fusion(f32[16,384,128]{2,1,0:T(8,128)} %fusion.6, bf16[16,384,128]{2,1,0:T(8,128)(2,1)} %multiply_convert_fusion.5, f32[16,128,128]{2,1,0:T(8,128)S(1)} %broadcast_select_fusion, f32[8,128,128]{2,1,0:T(8,128)S(1)} %get-tuple-element.16, ...), kind=kOutput, calls=%fused_computation.22 | convolution fusion | flops 205514752 | bytes 9986113 | tf_op jit(solution)/shard_map/htd,hde->hte/dot_general | solution.py:128
  108.4 1.0 fusion.20
  109.4 0.9 copy.166
  110.3 7.6 %fusion.15 = (f32[384]{0:T(512)S(1)}, bf16[384,2048]{1,0:T(8,128)(2,1)S(1)}) fusion(bf16[384,2048]{0,1:T(8,128)(2,1)S(1)} %bitcast.156, bf16[2048,2048]{1,0:T(8,128)(2,1)} %all-gather.2.cloned.1.call-done, bf16[384,2048]{1,0:T(8,128)(2,1)} %param.15), kind=kOutput, calls=%fused_computation.16 | convolution fusion | flops 3225943552 | bytes 13108736 | tf_op jit(solution)/shard_map/dot_general | solution.py:142
  118.0 1.9 convolution_convert_fusion
  119.9 46.5 %all_to_all.10 = bf16[32,24,2048]{2,1,0:T(8,128)(2,1)S(1)} all-to-all(bf16[32,24,2048]{2,1,0:T(8,128)(2,1)S(1)} %bitcast.150), channel_id=1, replica_groups=mesh['dp'=4,'sy'=4,'sx'=4,'sc'=2] {'sy','sx','sc'}, dimensions={0} | all-to-all | bytes 6291456 | tf_op jit(solution)/shard_map/all_to_all | solution.py:165
  166.4 7.6 %fusion.2 = f32[32,24,1408]{2,1,0:T(8,128)S(1)} fusion(bf16[32,24,2048]{2,1,0:T(8,128)(2,1)S(1)} %all_to_all.10, bf16[1,2048,1408]{2,1,0:T(8,128)(2,1)} %param.22), kind=kOutput, calls=%fused_computation.3 | convolution fusion | flops 4429185024 | bytes 13238272 | tf_op jit(solution)/shard_map/snd,df->snf/dot_general | solution.py:169
  174.1 5.8 %multiply_convert_fusion.2 = bf16[32,24,1408]{2,1,0:T(8,128)(2,1)S(1)} fusion(f32[32,24,1408]{2,1,0:T(8,128)S(1)} %fusion.2, bf16[32,24,2048]{2,1,0:T(8,128)(2,1)S(1)} %all_to_all.10, bf16[1,2048,1408]{2,1,0:T(8,128)(2,1)S(1)} %bitcast.165), kind=kOutput, calls=%fused_computation.12 | convolution fusion | flops 4435673088 | bytes 15400960 | tf_op jit(solution)/shard_map/snd,df->snf/dot_general | solution.py:166
  179.9 6.6 %fusion.10 = bf16[32,24,2048]{2,1,0:T(8,128)(2,1)} fusion(bf16[32,24,1408]{2,1,0:T(8,128)(2,1)S(1)} %multiply_convert_fusion.2, bf16[1,1408,2048]{2,1,0:T(8,128)(2,1)S(1)} %bitcast.167), kind=kOutput, calls=%fused_computation.14 | convolution fusion | flops 4430757888 | bytes 11075584 | tf_op jit(solution)/shard_map/snf,fd->snd/dot_general | solution.py:171
  186.5 5.0 %all-to-all-start.1 = ((bf16[32,24,2048]{2,1,0:T(8,128)(2,1)}), bf16[32,24,2048]{2,1,0:T(8,128)(2,1)}, u32[]{:S(2)}, u32[]{:S(2)}) async-start(bf16[32,24,2048]{2,1,0:T(8,128)(2,1)} %fusion.10), calls=%async_computation.1 | async-start | bytes 6291456 | tf_op jit(solution)/shard_map/all_to_all | solution.py:174
  191.6 41.8 %all-to-all-done.1 = bf16[32,24,2048]{2,1,0:T(8,128)(2,1)} async-done(((bf16[32,24,2048]{2,1,0:T(8,128)(2,1)}), bf16[32,24,2048]{2,1,0:T(8,128)(2,1)}, u32[]{:S(2)}, u32[]{:S(2)}) %all-to-all-start.1) | async-done | bytes 3145760 | tf_op jit(solution)/shard_map/all_to_all | solution.py:174
  233.5 4.6 %fusion.18 = bf16[384,2048]{1,0:T(8,128)(2,1)} fusion(bf16[384,2048]{1,0:T(8,128)(2,1)S(1)} %copy-done.10, bf16[768,2048]{1,0:T(8,128)(2,1)} %bitcast.44, f32[768]{0:T(1024)S(1)} %broadcast_in_dim.21, s32[768]{0:T(1024)S(1)} %eq.33), kind=kOutput, calls=%fused_computation.19 | convolution fusion | flops 1211498496 | bytes 6297600 | tf_op jit(solution)/shard_map/dot_general | solution.py:179
  (70 shorter events, 1.2 us)
Async XLA Ops:
  6.5 75.1 %copy-start = (bf16[384,2048]{1,0:T(8,128)(2,1)S(1)}, bf16[384,2048]{1,0:T(8,128)(2,1)}, u32[]{:S(2)}) copy-start(bf16[384,2048]{1,0:T(8,128)(2,1)} %param.12) | copy-start | bytes 4718596
  6.5 103.8 %all-gather.2.cloned.1.call-start = ((), (), s32[]{:S(2)}) async-start(), calls=%async_computation.2 | async-start | bytes 8650752 | tf_op jit(solution)/shard_map/all_gather | solution.py:144
  10.8 8.7 %copy-start.3 = (bf16[384,2048]{0,1:T(8,128)(2,1)}, bf16[384,2048]{0,1:T(8,128)(2,1)S(1)}, u32[]{:S(2)}) copy-start(bf16[384,2048]{0,1:T(8,128)(2,1)S(1)} %copy.172) | copy-start | bytes 4718596
  15.3 2.3 collective-permute-start
  15.3 4.3 %copy-start.2 = (f32[16,128,128]{2,1,0:T(8,128)S(1)}, f32[16,128,128]{2,1,0:T(8,128)}, u32[]{:S(2)}) copy-start(f32[16,128,128]{2,1,0:T(8,128)} %get-tuple-element.46) | copy-start | bytes 3145732
  21.1 10.1 %collective-permute-start.1 = (bf16[1032,128]{0,1:T(8,128)(2,1)S(1)}, bf16[1032,128]{0,1:T(8,128)(2,1)S(1)}, u32[]{:S(2)}, u32[]{:S(2)}) collective-permute-start(bf16[1032,128]{0,1:T(8,128)(2,1)S(1)} %pad_maximum_fusion), channel_id=1, source_target_pairs={{0,2},{2,4},{4,6},{6,8},{8,10},{10,12},{12,14},{14,16},{16,18},{18... | collective-permute-start | bytes 792584 | tf_op jit(solution)/shard_map/ppermute | solution.py:43
  35.5 11.6 %collective-permute-start.2 = (bf16[1032,128]{0,1:T(8,128)(2,1)S(1)}, bf16[1032,128]{0,1:T(8,128)(2,1)S(1)}, u32[]{:S(2)}, u32[]{:S(2)}) collective-permute-start(bf16[1032,128]{0,1:T(8,128)(2,1)S(1)} %pad_maximum_fusion.1), channel_id=1, source_target_pairs={{0,4},{2,6},{4,8},{6,10},{8,12},{10,14},{12,16},{14,18},{16,20},{1... | collective-permute-start | bytes 792584 | tf_op jit(solution)/shard_map/ppermute | solution.py:43
  47.1 0.7 copy-start.5
  54.5 12.3 %collective-permute-start.3 = (bf16[1032,128]{0,1:T(8,128)(2,1)S(1)}, bf16[1032,128]{0,1:T(8,128)(2,1)S(1)}, u32[]{:S(2)}, u32[]{:S(2)}) collective-permute-start(bf16[1032,128]{0,1:T(8,128)(2,1)S(1)} %pad_maximum_fusion.2), channel_id=1, source_target_pairs={{0,8},{2,10},{4,12},{6,14},{8,16},{10,18},{12,20},{14,22},{16,24},... | collective-permute-start | bytes 792584 | tf_op jit(solution)/shard_map/ppermute | solution.py:43
  66.8 0.7 copy-start.4
  72.9 18.4 %collective-permute-start.4 = (bf16[1032,128]{0,1:T(8,128)(2,1)S(1)}, bf16[1032,128]{0,1:T(8,128)(2,1)}, u32[]{:S(2)}, u32[]{:S(2)}) collective-permute-start(bf16[1032,128]{0,1:T(8,128)(2,1)S(1)} %pad_maximum_fusion.3), channel_id=1, source_target_pairs={{0,18},{2,20},{4,22},{6,24},{8,26},{10,28},{12,30},{1,19},{3,21},{... | collective-permute-start | bytes 792584 | tf_op jit(solution)/shard_map/ppermute | solution.py:43
  78.3 19.8 %collective-permute-start.5 = (bf16[1032,128]{0,1:T(8,128)(2,1)S(1)}, bf16[1032,128]{0,1:T(8,128)(2,1)}, u32[]{:S(2)}, u32[]{:S(2)}) collective-permute-start(bf16[1032,128]{0,1:T(8,128)(2,1)S(1)} %pad_maximum_fusion.3), channel_id=1, source_target_pairs={{0,2},{2,4},{4,6},{6,8},{8,10},{10,12},{12,14},{14,16},{16,18},{18... | collective-permute-start | bytes 792584 | tf_op jit(solution)/shard_map/ppermute | solution.py:43
  99.1 5.6 %copy-start.7 = (s32[32,24]{0,1:T(8,128)S(1)}, s32[32,24]{0,1:T(8,128)}, u32[]{:S(2)}) copy-start(s32[32,24]{0,1:T(8,128)} %param.17) | copy-start | bytes 9220
  102.8 2.0 collective-permute-start.6
  110.3 7.6 %copy-start.8 = (f32[2048]{0:T(1024)S(1)}, f32[2048]{0:T(1024)}, u32[]{:S(2)}) copy-start(f32[2048]{0:T(1024)} %param.19) | copy-start | bytes 24580
  117.9 2.0 copy-start.9
  119.9 54.2 %slice-start = ((s8[5767168]{0:T(1024)(128)(4,1)}), s8[4194304]{0:T(1024)(128)(4,1)S(1)}, s32[]{:S(2)}) async-start(s8[5767168]{0:T(1024)(128)(4,1)} %bitcast.164), calls=%async_computation.3 | async-start | bytes 8388608
  166.4 7.7 %slice-start.1 = ((s8[5767168]{0:T(1024)(128)(4,1)}), s8[1572864]{0:T(1024)(128)(4,1)S(1)}, s32[]{:S(2)}) async-start(s8[5767168]{0:T(1024)(128)(4,1)} %bitcast.164), calls=%async_computation.4 | async-start | bytes 3145728
  166.4 13.5 %slice-start.2 = ((s8[5767168]{0:T(1024)(128)(4,1)}), s8[4194304]{0:T(1024)(128)(4,1)S(1)}, s32[]{:S(2)}) async-start(s8[5767168]{0:T(1024)(128)(4,1)} %bitcast.166), calls=%async_computation.5 | async-start | bytes 8388608
  174.1 5.8 %slice-start.3 = ((s8[5767168]{0:T(1024)(128)(4,1)}), s8[1572864]{0:T(1024)(128)(4,1)S(1)}, s32[]{:S(2)}) async-start(s8[5767168]{0:T(1024)(128)(4,1)} %bitcast.166), calls=%async_computation.6 | async-start | bytes 3145728
  186.5 5.0 %copy-start.6 = (f32[32,24]{0,1:T(8,128)S(1)}, f32[32,24]{0,1:T(8,128)}, u32[]{:S(2)}) copy-start(f32[32,24]{0,1:T(8,128)} %param.18) | copy-start | bytes 9220
  186.5 47.0 %copy-start.10 = (bf16[384,2048]{1,0:T(8,128)(2,1)S(1)}, bf16[384,2048]{1,0:T(8,128)(2,1)}, u32[]{:S(2)}) copy-start(bf16[384,2048]{1,0:T(8,128)(2,1)} %copy-done.9) | copy-start | bytes 4718596
  186.5 47.0 %all-to-all-start.1 = ((bf16[32,24,2048]{2,1,0:T(8,128)(2,1)}), bf16[32,24,2048]{2,1,0:T(8,128)(2,1)}, u32[]{:S(2)}, u32[]{:S(2)}) async-start(bf16[32,24,2048]{2,1,0:T(8,128)(2,1)} %fusion.10), calls=%async_computation.1 | async-start | bytes 6291456 | tf_op jit(solution)/shard_map/all_to_all | solution.py:174
  233.5 4.6 %copy-start.1 = (bf16[384,2048]{1,0:T(8,128)(2,1)S(1)}, bf16[384,2048]{1,0:T(8,128)(2,1)}, u32[]{:S(2)}) copy-start(bf16[384,2048]{1,0:T(8,128)(2,1)} %param.12) | copy-start | bytes 4718596
Sparse Core Ops, SparseCore 0:
  33.7 65.3 all-gather.1

commit v11 on v10

--- a/solution.py
+++ b/solution.py
@@ -7,6 +7,7 @@
 CHIP_AXES = ("sy", "sx")
 CORE_AXIS = "sc"
 CHUNKS = 1
+RADIX = 4
 SCATTER_PIECES = 1
 
 
@@ -44,16 +45,21 @@
 
     covered = (state, ending)
     reach = 1
-    while 2 * reach < count:
-        covered = combine(fetch(covered, reach), covered)
+    while reach * RADIX < count:
+        gathered = covered
+        for multiple in range(1, RADIX):
+            gathered = combine(fetch(covered, multiple * reach), gathered)
+        covered = gathered
         if reach == 1:
             covered, rider = lax.optimization_barrier((covered, rider))
-        reach *= 2
+        reach *= RADIX
     if count == 1:
         return jnp.zeros_like(state), rider
     near = fetch(covered, 1)
-    if reach + 1 < count:
-        near = combine(fetch(covered, reach + 1), near)
+    distance = 1 + reach
+    while distance < count:
+        near = combine(fetch(covered, distance), near)
+        distance += reach
     return near[0], rider
 
 

time: 246 us -> 247 us (level)
    ppermute x5 -> x7, waiting for transfers between devices: 23.9 us -> 14.7 us  [fetch(): return unpack(lax.ppermute(pack(*pair), axis, pairs), heads)]
    all_gather x1, waiting for transfers between devices: 0.02 us -> 6.98 us  [shards(): lax.all_gather(out_weight, SEQ, axis=0, tiled=True)]
    convert_element_type x6 -> x8, other arithmetic: 3.82 us -> 8.42 us  [unpack(): message[:heads * width].reshape(heads, width, width).astype(jnp.float32)]
    convert_element_type x5 -> x7, local copies, waits for them, and re-layouts: 7.31 us -> 11.2 us  [unpack(): message[:heads * width].reshape(heads, width, width).astype(jnp.float32)]
    convert_element_type x4 -> x1, other arithmetic: 3.53 us -> 0.15 us  [pack(): state.astype(jnp.bfloat16).reshape(heads * rows, width)]
    ppermute x5 -> x7, starting transfers between devices: 25.8 us -> 27.7 us  [fetch(): return unpack(lax.ppermute(pack(*pair), axis, pairs), heads)]
  transfers between devices with their start and end apart: 9 -> 11, of which waited for: 7 -> 7; matrix products, arithmetic and copies ran while one was open for 15% -> 12% of each run, Pallas kernels for 0% -> 0%
where the time goes in v11:
time: 247 us; the launch traced here: 246 us
  waiting for transfers between devices  65.8 us (27%)
  matrix products  48 us (19%)
  blocking collectives  45.2 us (18%)
  starting transfers between devices  33 us (13%)
  other arithmetic  21.8 us (9%)
  local copies, waits for them, and re-layouts  18.6 us (8%)
  between operations  13.8 us (6%)
    all_to_all x1, blocking collectives, shards(): lax.all_to_all(picked[:, window], SEQ, split_axis=0, concat_axis=0, tiled...  45.2 us
    all_to_all x1, waiting for transfers between devices, shards(): lax.all_to_all(produced, SEQ, split_axis=0, concat_axis=0, tiled=True)  41.8 us
    ppermute x7, starting transfers between devices, fetch(): return unpack(lax.ppermute(pack(*pair), axis, pairs), heads)  27.7 us
    ppermute x7, waiting for transfers between devices, fetch(): return unpack(lax.ppermute(pack(*pair), axis, pairs), heads)  14.7 us
    convert_element_type x7, local copies, waits for them, and re-layouts, unpack(): message[:heads * width].reshape(heads, width, width).astype(jnp.float32)  11.2 us
    convert_element_type x8, other arithmetic, unpack(): message[:heads * width].reshape(heads, width, width).astype(jnp.float32)  8.42 us
    dot_general x1, matrix products, shards(): jnp.einsum('snd,df->snf', arrived, up_weight[0], preferred_element_type=j...  7.64 us
    dot_general x1, matrix products, shards(): jnp.dot(normed, lax.all_gather(out_weight, SEQ, axis=0, tiled=True), pref...  7.59 us
  transfers between devices with their start and end apart: 11, of which 7 were waited for; matrix products, arithmetic and copies ran while one was open for 12% of the time, Pallas kernels for 0%

profile of v11, /device:TPU:0, one launch (start us, length us, event | category | flops | bytes accessed | tf_op | source)
XLA Modules:
  0.0 246.2 jit_solution(8152671224414617295)
XLA Ops:
  6.5 0.9 copy_bitcast_fusion.1
  7.4 0.9 reduce-window.6
  8.3 0.2 slice_reduce_fusion
  8.9 1.9 copy.172
  10.8 3.6 %fusion.72 = (bf16[16,128,128]{2,1,0:T(8,128)(2,1)S(1)}, f32[16,128,128]{2,1,0:T(8,128)}) fusion(bf16[16,384,128]{1,2,0:T(8,128)(2,1)S(1)} %bitcast.136, f32[16,384]{1,0:T(8,128)S(1)} %get-tuple-element.27, bf16[384,2048]{1,0:T(8,128)(2,1)} %param.14), kind=kOutput, calls=%fused_computation.141 | convolution fusion | flops 203948032 | bytes 4743168 | tf_op jit(solution)/shard_map/hsd,hse->hde/dot_general | solution.py:115
  14.4 0.8 fusion.34
  15.3 2.3 collective-permute-done
  17.5 0.7 slice_convert_fusion.7
  18.2 0.2 fusion.48
  18.4 1.1 slice.161
  19.5 0.1 convert.8
  19.6 0.1 broadcast_select_fusion
  19.8 0.1 fusion.70
  20.0 0.9 copy.155
  20.9 1.0 pad_maximum_fusion
  21.9 4.8 %collective-permute-start.1 = (bf16[1032,128]{0,1:T(8,128)(2,1)S(1)}, bf16[1032,128]{0,1:T(8,128)(2,1)S(1)}, u32[]{:S(2)}, u32[]{:S(2)}) collective-permute-start(bf16[1032,128]{0,1:T(8,128)(2,1)S(1)} %pad_maximum_fusion), channel_id=1, source_target_pairs={{0,6},{2,8},{4,10},{6,12},{8,14},{10,16},{12,18},{14,20},{16,22},{... | collective-permute-start | bytes 792584 | tf_op jit(solution)/shard_map/ppermute | solution.py:44
  26.7 2.2 collective-permute-start.3
  28.9 4.9 %collective-permute-start.2 = (bf16[1032,128]{0,1:T(8,128)(2,1)S(1)}, bf16[1032,128]{0,1:T(8,128)(2,1)S(1)}, u32[]{:S(2)}, u32[]{:S(2)}) collective-permute-start(bf16[1032,128]{0,1:T(8,128)(2,1)S(1)} %pad_maximum_fusion), channel_id=1, source_target_pairs={{0,4},{2,6},{4,8},{6,10},{8,12},{10,14},{12,16},{14,18},{16,20},{1... | collective-permute-start | bytes 792584 | tf_op jit(solution)/shard_map/ppermute | solution.py:44
  33.9 2.4 collective-permute-done.3
  36.3 5.2 %collective-permute-done.2 = bf16[1032,128]{0,1:T(8,128)(2,1)S(1)} collective-permute-done((bf16[1032,128]{0,1:T(8,128)(2,1)S(1)}, bf16[1032,128]{0,1:T(8,128)(2,1)S(1)}, u32[]{:S(2)}, u32[]{:S(2)}) %collective-permute-start.2) | collective-permute-done | bytes 264224 | tf_op jit(solution)/shard_map/ppermute | solution.py:44
  41.5 0.7 copy-done.4
  42.3 0.9 slice_convert_fusion.6
  43.1 2.1 copy.156
  45.2 1.8 slice_convert_fusion.5
  47.0 2.1 copy.157
  49.0 0.8 slice_convert_fusion.4
  49.9 2.0 copy.158
  51.9 1.6 add_add_fusion.1
  53.6 0.1 copy.159
  53.8 6.6 %collective-permute-start.5 = (bf16[1032,128]{0,1:T(8,128)(2,1)S(1)}, bf16[1032,128]{0,1:T(8,128)(2,1)}, u32[]{:S(2)}, u32[]{:S(2)}) collective-permute-start(bf16[1032,128]{0,1:T(8,128)(2,1)S(1)} %pad_maximum_fusion.1), channel_id=1, source_target_pairs={{0,18},{2,20},{4,22},{6,24},{8,26},{10,28},{12,30},{1,19},{3,21},{... | collective-permute-start | bytes 792584 | tf_op jit(solution)/shard_map/ppermute | solution.py:44
  60.4 2.0 collective-permute-start.4
  62.4 6.7 %fusion.6 = f32[16,384,128]{2,1,0:T(8,128)} fusion(f32[16,384]{1,0:T(8,128)S(1)} %copy_bitcast_fusion, pred[384,384]{1,0:T(8,128)(4,1)S(1)} %iota_compare_fusion.4, bf16[16,384,128]{1,2,0:T(8,128)(2,1)} %bitcast.137, bf16[384,2048]{1,0:T(8,128)(2,1)S(1)} %copy-done, bf16[384,2048]{1,0:T(8,128)(2,1)} %param.14), kind=kOutput, calls=%fused_computation.10 | convolution fusion | flops 1222115328 | bytes 8036352 | tf_op jit(solution)/shard_map/hts,hsd->htd/dot_general | solution.py:127
  69.1 5.2 %collective-permute-start.7 = (bf16[1032,128]{0,1:T(8,128)(2,1)S(1)}, bf16[1032,128]{0,1:T(8,128)(2,1)}, u32[]{:S(2)}, u32[]{:S(2)}) collective-permute-start(bf16[1032,128]{0,1:T(8,128)(2,1)S(1)} %pad_maximum_fusion.1), channel_id=1, source_target_pairs={{0,2},{2,4},{4,6},{6,8},{8,10},{10,12},{12,14},{14,16},{16,18},{18... | collective-permute-start | bytes 792584 | tf_op jit(solution)/shard_map/ppermute | solution.py:44
  74.2 2.0 collective-permute-start.6
  76.3 0.2 collective-permute-done.4
  76.4 1.0 slice_convert_fusion.3
  77.5 1.8 slice_convert_fusion.2
  79.2 1.1 copy.160
  80.3 2.1 copy.161
  82.4 6.9 %collective-permute-done.6 = bf16[1032,128]{0,1:T(8,128)(2,1)} collective-permute-done((bf16[1032,128]{0,1:T(8,128)(2,1)S(1)}, bf16[1032,128]{0,1:T(8,128)(2,1)}, u32[]{:S(2)}, u32[]{:S(2)}) %collective-permute-start.6) | collective-permute-done | bytes 264224 | tf_op jit(solution)/shard_map/ppermute | solution.py:44
  89.3 1.0 slice_convert_fusion.1
  90.3 1.0 copy.162
  91.3 1.0 slice_convert_fusion
  92.3 1.0 copy.163
  93.3 0.7 slice_convert_fusion.10
  94.0 0.7 slice_convert_fusion.8
  94.7 0.7 slice_convert_fusion.9
  95.4 1.7 fusion.68
  97.1 0.3 collective-permute-start.8
  97.4 1.9 multiply_convert_fusion.5
  99.4 1.0 convert_element_type.235
  100.5 3.7 %multiply_reduce_fusion = (f32[16,384]{1,0:T(8,128)S(1)}, f32[16,384,128]{2,1,0:T(8,128)S(1)}) fusion(f32[16,384,128]{2,1,0:T(8,128)} %fusion.6, bf16[16,384,128]{2,1,0:T(8,128)(2,1)} %multiply_convert_fusion.5, f32[16,128,128]{2,1,0:T(8,128)S(1)} %broadcast_select_fusion, f32[8,128,128]{2,1,0:T(8,128)S(1)} %get-tuple-element.16, ...), kind=kOutput, calls=%fused_computation.22 | convolution fusion | flops 205514752 | bytes 9986113 | tf_op jit(solution)/shard_map/htd,hde->hte/dot_general | solution.py:134
  104.1 1.0 fusion.20
  105.1 0.9 copy.166
  106.0 7.0 %all-gather.2.cloned.1.call-done = bf16[2048,2048]{1,0:T(8,128)(2,1)} async-done(((bf16[64,2048]{1,0:T(8,128)(2,1)}), bf16[2048,2048]{1,0:T(8,128)(2,1)}) %all-gather.2.cloned.1.call-update) | async-done | bytes 8388624 | tf_op jit(solution)/shard_map/all_gather | solution.py:150
  113.0 7.6 %fusion.15 = (f32[384]{0:T(512)S(1)}, bf16[384,2048]{1,0:T(8,128)(2,1)S(1)}) fusion(bf16[384,2048]{0,1:T(8,128)(2,1)S(1)} %bitcast.149, bf16[2048,2048]{1,0:T(8,128)(2,1)} %all-gather.2.cloned.1.call-done, bf16[384,2048]{1,0:T(8,128)(2,1)} %param.15), kind=kOutput, calls=%fused_computation.16 | convolution fusion | flops 3225943552 | bytes 13108736 | tf_op jit(solution)/shard_map/dot_general | solution.py:148
  120.6 1.9 convolution_convert_fusion
  122.6 45.2 %all_to_all.10 = bf16[32,24,2048]{2,1,0:T(8,128)(2,1)S(1)} all-to-all(bf16[32,24,2048]{2,1,0:T(8,128)(2,1)S(1)} %bitcast.140), channel_id=1, replica_groups=mesh['dp'=4,'sy'=4,'sx'=4,'sc'=2] {'sy','sx','sc'}, dimensions={0} | all-to-all | bytes 6291456 | tf_op jit(solution)/shard_map/all_to_all | solution.py:171
  167.8 7.6 %fusion.2 = f32[32,24,1408]{2,1,0:T(8,128)S(1)} fusion(bf16[32,24,2048]{2,1,0:T(8,128)(2,1)S(1)} %all_to_all.10, bf16[1,2048,1408]{2,1,0:T(8,128)(2,1)} %param.22), kind=kOutput, calls=%fused_computation.3 | convolution fusion | flops 4429185024 | bytes 13238272 | tf_op jit(solution)/shard_map/snd,df->snf/dot_general | solution.py:175
  175.5 5.8 %multiply_convert_fusion.2 = bf16[32,24,1408]{2,1,0:T(8,128)(2,1)S(1)} fusion(f32[32,24,1408]{2,1,0:T(8,128)S(1)} %fusion.2, bf16[32,24,2048]{2,1,0:T(8,128)(2,1)S(1)} %all_to_all.10, bf16[1,2048,1408]{2,1,0:T(8,128)(2,1)S(1)} %bitcast.156), kind=kOutput, calls=%fused_computation.12 | convolution fusion | flops 4435673088 | bytes 15400960 | tf_op jit(solution)/shard_map/snd,df->snf/dot_general | solution.py:172
  181.3 6.6 %fusion.10 = bf16[32,24,2048]{2,1,0:T(8,128)(2,1)} fusion(bf16[32,24,1408]{2,1,0:T(8,128)(2,1)S(1)} %multiply_convert_fusion.2, bf16[1,1408,2048]{2,1,0:T(8,128)(2,1)S(1)} %bitcast.158), kind=kOutput, calls=%fused_computation.14 | convolution fusion | flops 4430757888 | bytes 11075584 | tf_op jit(solution)/shard_map/snf,fd->snd/dot_general | solution.py:177
  187.8 5.0 %all-to-all-start.1 = ((bf16[32,24,2048]{2,1,0:T(8,128)(2,1)}), bf16[32,24,2048]{2,1,0:T(8,128)(2,1)}, u32[]{:S(2)}, u32[]{:S(2)}) async-start(bf16[32,24,2048]{2,1,0:T(8,128)(2,1)} %fusion.10), calls=%async_computation.1 | async-start | bytes 6291456 | tf_op jit(solution)/shard_map/all_to_all | solution.py:180
  193.0 41.8 %all-to-all-done.1 = bf16[32,24,2048]{2,1,0:T(8,128)(2,1)} async-done(((bf16[32,24,2048]{2,1,0:T(8,128)(2,1)}), bf16[32,24,2048]{2,1,0:T(8,128)(2,1)}, u32[]{:S(2)}, u32[]{:S(2)}) %all-to-all-start.1) | async-done | bytes 3145760 | tf_op jit(solution)/shard_map/all_to_all | solution.py:180
  234.8 4.6 %fusion.18 = bf16[384,2048]{1,0:T(8,128)(2,1)} fusion(bf16[384,2048]{1,0:T(8,128)(2,1)S(1)} %copy-done.9, bf16[768,2048]{1,0:T(8,128)(2,1)} %bitcast.40, f32[768]{0:T(1024)S(1)} %broadcast_in_dim.17, s32[768]{0:T(1024)S(1)} %eq.33), kind=kOutput, calls=%fused_computation.19 | convolution fusion | flops 1211498496 | bytes 6297600 | tf_op jit(solution)/shard_map/dot_general | solution.py:185
  (68 shorter events, 1.2 us)
Async XLA Ops:
  6.5 55.9 %copy-start = (bf16[384,2048]{1,0:T(8,128)(2,1)S(1)}, bf16[384,2048]{1,0:T(8,128)(2,1)}, u32[]{:S(2)}) copy-start(bf16[384,2048]{1,0:T(8,128)(2,1)} %param.12) | copy-start | bytes 4718596
  6.5 106.5 %all-gather.2.cloned.1.call-start = ((), (), s32[]{:S(2)}) async-start(), calls=%async_computation.2 | async-start | bytes 8650752 | tf_op jit(solution)/shard_map/all_gather | solution.py:150
  10.8 8.7 %copy-start.3 = (bf16[384,2048]{0,1:T(8,128)(2,1)}, bf16[384,2048]{0,1:T(8,128)(2,1)S(1)}, u32[]{:S(2)}) copy-start(bf16[384,2048]{0,1:T(8,128)(2,1)S(1)} %copy.172) | copy-start | bytes 4718596
  15.3 2.3 collective-permute-start
  15.3 4.3 %copy-start.2 = (f32[16,128,128]{2,1,0:T(8,128)S(1)}, f32[16,128,128]{2,1,0:T(8,128)}, u32[]{:S(2)}) copy-start(f32[16,128,128]{2,1,0:T(8,128)} %get-tuple-element.42) | copy-start | bytes 3145732
  21.9 11.9 %collective-permute-start.1 = (bf16[1032,128]{0,1:T(8,128)(2,1)S(1)}, bf16[1032,128]{0,1:T(8,128)(2,1)S(1)}, u32[]{:S(2)}, u32[]{:S(2)}) collective-permute-start(bf16[1032,128]{0,1:T(8,128)(2,1)S(1)} %pad_maximum_fusion), channel_id=1, source_target_pairs={{0,6},{2,8},{4,10},{6,12},{8,14},{10,16},{12,18},{14,20},{16,22},{... | collective-permute-start | bytes 792584 | tf_op jit(solution)/shard_map/ppermute | solution.py:44
  26.7 9.6 %collective-permute-start.3 = (bf16[1032,128]{0,1:T(8,128)(2,1)S(1)}, bf16[1032,128]{0,1:T(8,128)(2,1)S(1)}, u32[]{:S(2)}, u32[]{:S(2)}) collective-permute-start(bf16[1032,128]{0,1:T(8,128)(2,1)S(1)} %pad_maximum_fusion), channel_id=1, source_target_pairs={{0,2},{2,4},{4,6},{6,8},{8,10},{10,12},{12,14},{14,16},{16,18},{18... | collective-permute-start | bytes 792584 | tf_op jit(solution)/shard_map/ppermute | solution.py:44
  28.9 12.6 %collective-permute-start.2 = (bf16[1032,128]{0,1:T(8,128)(2,1)S(1)}, bf16[1032,128]{0,1:T(8,128)(2,1)S(1)}, u32[]{:S(2)}, u32[]{:S(2)}) collective-permute-start(bf16[1032,128]{0,1:T(8,128)(2,1)S(1)} %pad_maximum_fusion), channel_id=1, source_target_pairs={{0,4},{2,6},{4,8},{6,10},{8,12},{10,14},{12,16},{14,18},{16,20},{1... | collective-permute-start | bytes 792584 | tf_op jit(solution)/shard_map/ppermute | solution.py:44
  41.5 0.7 copy-start.4
  53.8 23.7 %collective-permute-start.5 = (bf16[1032,128]{0,1:T(8,128)(2,1)S(1)}, bf16[1032,128]{0,1:T(8,128)(2,1)}, u32[]{:S(2)}, u32[]{:S(2)}) collective-permute-start(bf16[1032,128]{0,1:T(8,128)(2,1)S(1)} %pad_maximum_fusion.1), channel_id=1, source_target_pairs={{0,18},{2,20},{4,22},{6,24},{8,26},{10,28},{12,30},{1,19},{3,21},{... | collective-permute-start | bytes 792584 | tf_op jit(solution)/shard_map/ppermute | solution.py:44
  60.4 16.0 %collective-permute-start.4 = (bf16[1032,128]{0,1:T(8,128)(2,1)S(1)}, bf16[1032,128]{0,1:T(8,128)(2,1)}, u32[]{:S(2)}, u32[]{:S(2)}) collective-permute-start(bf16[1032,128]{0,1:T(8,128)(2,1)S(1)} %pad_maximum_fusion.1), channel_id=1, source_target_pairs={{0,26},{2,28},{4,30},{1,27},{3,29},{5,31},{32,58},{34,60},{36,62},... | collective-permute-start | bytes 792584 | tf_op jit(solution)/shard_map/ppermute | solution.py:44
  69.1 22.2 %collective-permute-start.7 = (bf16[1032,128]{0,1:T(8,128)(2,1)S(1)}, bf16[1032,128]{0,1:T(8,128)(2,1)}, u32[]{:S(2)}, u32[]{:S(2)}) collective-permute-start(bf16[1032,128]{0,1:T(8,128)(2,1)S(1)} %pad_maximum_fusion.1), channel_id=1, source_target_pairs={{0,2},{2,4},{4,6},{6,8},{8,10},{10,12},{12,14},{14,16},{16,18},{18... | collective-permute-start | bytes 792584 | tf_op jit(solution)/shard_map/ppermute | solution.py:44
  74.2 15.0 %collective-permute-start.6 = (bf16[1032,128]{0,1:T(8,128)(2,1)S(1)}, bf16[1032,128]{0,1:T(8,128)(2,1)}, u32[]{:S(2)}, u32[]{:S(2)}) collective-permute-start(bf16[1032,128]{0,1:T(8,128)(2,1)S(1)} %pad_maximum_fusion.1), channel_id=1, source_target_pairs={{0,10},{2,12},{4,14},{6,16},{8,18},{10,20},{12,22},{14,24},{16,26}... | collective-permute-start | bytes 792584 | tf_op jit(solution)/shard_map/ppermute | solution.py:44
  93.3 5.9 %copy-start.6 = (s32[32,24]{0,1:T(8,128)S(1)}, s32[32,24]{0,1:T(8,128)}, u32[]{:S(2)}) copy-start(s32[32,24]{0,1:T(8,128)} %param.17) | copy-start | bytes 9220
  97.1 2.3 collective-permute-start.8
  113.0 7.6 %copy-start.7 = (f32[2048]{0:T(1024)S(1)}, f32[2048]{0:T(1024)}, u32[]{:S(2)}) copy-start(f32[2048]{0:T(1024)} %param.19) | copy-start | bytes 24580
  120.6 2.0 copy-start.8
  122.6 52.9 %slice-start = ((s8[5767168]{0:T(1024)(128)(4,1)}), s8[4194304]{0:T(1024)(128)(4,1)S(1)}, s32[]{:S(2)}) async-start(s8[5767168]{0:T(1024)(128)(4,1)} %bitcast.155), calls=%async_computation.3 | async-start | bytes 8388608
  167.8 7.7 %slice-start.1 = ((s8[5767168]{0:T(1024)(128)(4,1)}), s8[1572864]{0:T(1024)(128)(4,1)S(1)}, s32[]{:S(2)}) async-start(s8[5767168]{0:T(1024)(128)(4,1)} %bitcast.155), calls=%async_computation.4 | async-start | bytes 3145728
  167.8 13.5 %slice-start.2 = ((s8[5767168]{0:T(1024)(128)(4,1)}), s8[4194304]{0:T(1024)(128)(4,1)S(1)}, s32[]{:S(2)}) async-start(s8[5767168]{0:T(1024)(128)(4,1)} %bitcast.157), calls=%async_computation.5 | async-start | bytes 8388608
  175.5 5.8 %slice-start.3 = ((s8[5767168]{0:T(1024)(128)(4,1)}), s8[1572864]{0:T(1024)(128)(4,1)S(1)}, s32[]{:S(2)}) async-start(s8[5767168]{0:T(1024)(128)(4,1)} %bitcast.157), calls=%async_computation.6 | async-start | bytes 3145728
  187.8 5.0 %copy-start.5 = (f32[32,24]{0,1:T(8,128)S(1)}, f32[32,24]{0,1:T(8,128)}, u32[]{:S(2)}) copy-start(f32[32,24]{0,1:T(8,128)} %param.18) | copy-start | bytes 9220
  187.8 47.0 %copy-start.9 = (bf16[384,2048]{1,0:T(8,128)(2,1)S(1)}, bf16[384,2048]{1,0:T(8,128)(2,1)}, u32[]{:S(2)}) copy-start(bf16[384,2048]{1,0:T(8,128)(2,1)} %copy-done.8) | copy-start | bytes 4718596
  187.8 47.0 %all-to-all-start.1 = ((bf16[32,24,2048]{2,1,0:T(8,128)(2,1)}), bf16[32,24,2048]{2,1,0:T(8,128)(2,1)}, u32[]{:S(2)}, u32[]{:S(2)}) async-start(bf16[32,24,2048]{2,1,0:T(8,128)(2,1)} %fusion.10), calls=%async_computation.1 | async-start | bytes 6291456 | tf_op jit(solution)/shard_map/all_to_all | solution.py:180
  234.8 4.6 %copy-start.1 = (bf16[384,2048]{1,0:T(8,128)(2,1)S(1)}, bf16[384,2048]{1,0:T(8,128)(2,1)}, u32[]{:S(2)}) copy-start(bf16[384,2048]{1,0:T(8,128)(2,1)} %param.12) | copy-start | bytes 4718596
Sparse Core Ops, SparseCore 0:
  53.6 59.3 all-gather.1

commit v12 on v10

--- a/solution.py
+++ b/solution.py
@@ -109,7 +109,12 @@
     local_state = jnp.einsum(
         "hsd,hse->hde", key_scaled, value_heads, preferred_element_type=jnp.float32
     )
-    incoming, out_weight = carried_in(local_state, ending, out_weight)
+    query_scaled = (
+        query_heads.astype(jnp.float32) * (jnp.exp(running) * scaling)[:, :, None]
+    ).astype(jnp.bfloat16)
+    incoming, (out_weight, query_scaled) = carried_in(
+        local_state, ending, (out_weight, query_scaled)
+    )
     scores = (
         jnp.einsum("htd,hsd->hts", query_heads, key_heads, preferred_element_type=jnp.float32)
         * scaling
@@ -121,9 +126,6 @@
     within = jnp.einsum(
         "hts,hsd->htd", attend_weights, value_heads, preferred_element_type=jnp.float32
     )
-    query_scaled = (
-        query_heads.astype(jnp.float32) * (jnp.exp(running) * scaling)[:, :, None]
-    ).astype(jnp.bfloat16)
     within, query_scaled = lax.optimization_barrier((within, query_scaled))
     across = jnp.einsum(
         "htd,hde->hte",

time: 246 us -> 252 us (1.024)
  waiting for transfers between devices: 68 us -> 74.5 us
    ppermute x5, waiting for transfers between devices: 23.9 us -> 30.3 us  [fetch(): return unpack(lax.ppermute(pack(*pair), axis, pairs), heads)]
  transfers between devices with their start and end apart: 9 -> 9, of which waited for: 7 -> 7; matrix products, arithmetic and copies ran while one was open for 15% -> 14% of each run, Pallas kernels for 0% -> 0%
where the time goes in v12:
time: 252 us
  waiting for transfers between devices  74.5 us (30%)
  matrix products  47.8 us (19%)
  blocking collectives  46.5 us (18%)
  starting transfers between devices  30.1 us (12%)
  other arithmetic  21.8 us (9%)
  local copies, waits for them, and re-layouts  17.1 us (7%)
  between operations  13.8 us (5%)
    all_to_all x1, blocking collectives, shards(): lax.all_to_all(picked[:, window], SEQ, split_axis=0, concat_axis=0, tiled...  46.5 us
    all_to_all x1, waiting for transfers between devices, shards(): lax.all_to_all(produced, SEQ, split_axis=0, concat_axis=0, tiled=True)  41.8 us
    ppermute x5, waiting for transfers between devices, fetch(): return unpack(lax.ppermute(pack(*pair), axis, pairs), heads)  30.3 us
    ppermute x5, starting transfers between devices, fetch(): return unpack(lax.ppermute(pack(*pair), axis, pairs), heads)  25.1 us
    dot_general x1, matrix products, shards(): jnp.einsum('snd,df->snf', arrived, up_weight[0], preferred_element_type=j...  7.64 us
    dot_general x1, matrix products, shards(): jnp.dot(normed, lax.all_gather(out_weight, SEQ, axis=0, tiled=True), pref...  7.58 us
    convert_element_type x5, local copies, waits for them, and re-layouts, unpack(): message[:heads * width].reshape(heads, width, width).astype(jnp.float32)  7.38 us
    dot_general x1, matrix products, shards(): jnp.einsum('hts,hsd->htd', attend_weights, value_heads, preferred_element...  6.71 us
  transfers between devices with their start and end apart: 9, of which 7 were waited for; matrix products, arithmetic and copies ran while one was open for 14% of the time, Pallas kernels for 0%

profile of v12, /device:TPU:0, one launch (start us, length us, event | category | flops | bytes accessed | tf_op | source)
XLA Modules:
  0.0 251.6 jit_solution(12482487757273417622)
XLA Ops:
  6.5 0.9 copy_bitcast_fusion.1
  7.4 0.9 reduce-window.6
  8.3 0.2 slice_reduce_fusion
  8.5 0.6 copy-done.7
  9.5 1.9 copy.172
  11.4 3.6 %fusion.95 = (bf16[16,128,128]{2,1,0:T(8,128)(2,1)S(1)}, f32[16,128,128]{2,1,0:T(8,128)}) fusion(bf16[16,384,128]{1,2,0:T(8,128)(2,1)S(1)} %bitcast.144, f32[16,384]{1,0:T(8,128)S(1)} %get-tuple-element.28, bf16[384,2048]{1,0:T(8,128)(2,1)} %param.14), kind=kOutput, calls=%fused_computation.168 | convolution fusion | flops 203948032 | bytes 4743168 | tf_op jit(solution)/shard_map/hsd,hse->hde/dot_general | solution.py:109
  15.0 0.8 fusion.34
  15.9 2.3 collective-permute-done
  18.1 0.7 slice_convert_fusion.5
  18.8 0.2 fusion.59
  19.0 1.1 slice.121
  20.1 0.1 convert.6
  20.2 0.5 fusion.88
  20.7 0.1 broadcast_select_fusion
  20.9 1.0 fusion.92
  21.9 0.1 copy.155
  22.2 3.5 %collective-permute-start.1 = (bf16[1032,128]{0,1:T(8,128)(2,1)S(1)}, bf16[1032,128]{0,1:T(8,128)(2,1)S(1)}, u32[]{:S(2)}, u32[]{:S(2)}) collective-permute-start(bf16[1032,128]{0,1:T(8,128)(2,1)S(1)} %pad_maximum_fusion), channel_id=1, source_target_pairs={{0,2},{2,4},{4,6},{6,8},{8,10},{10,12},{12,14},{14,16},{16,18},{18... | collective-permute-start | bytes 792584 | tf_op jit(solution)/shard_map/ppermute | solution.py:43
  25.7 1.9 multiply_convert_fusion.4
  27.6 4.6 %collective-permute-done.1 = bf16[1032,128]{0,1:T(8,128)(2,1)S(1)} collective-permute-done((bf16[1032,128]{0,1:T(8,128)(2,1)S(1)}, bf16[1032,128]{0,1:T(8,128)(2,1)S(1)}, u32[]{:S(2)}, u32[]{:S(2)}) %collective-permute-start.1) | collective-permute-done | bytes 264224 | tf_op jit(solution)/shard_map/ppermute | solution.py:43
  32.3 1.0 copy.156
  33.3 1.3 multiply_add_fusion.2
  34.7 0.9 copy.157
  35.6 1.0 pad_maximum_fusion.1
  36.6 5.9 %collective-permute-start.2 = (bf16[1032,128]{0,1:T(8,128)(2,1)S(1)}, bf16[1032,128]{0,1:T(8,128)(2,1)S(1)}, u32[]{:S(2)}, u32[]{:S(2)}) collective-permute-start(bf16[1032,128]{0,1:T(8,128)(2,1)S(1)} %pad_maximum_fusion.1), channel_id=1, source_target_pairs={{0,4},{2,6},{4,8},{6,10},{8,12},{10,14},{12,16},{14,18},{16,20},{1... | collective-permute-start | bytes 792584 | tf_op jit(solution)/shard_map/ppermute | solution.py:43
  42.5 5.7 %collective-permute-done.2 = bf16[1032,128]{0,1:T(8,128)(2,1)S(1)} collective-permute-done((bf16[1032,128]{0,1:T(8,128)(2,1)S(1)}, bf16[1032,128]{0,1:T(8,128)(2,1)S(1)}, u32[]{:S(2)}, u32[]{:S(2)}) %collective-permute-start.2) | collective-permute-done | bytes 264224 | tf_op jit(solution)/shard_map/ppermute | solution.py:43
  48.2 0.7 copy-done.5
  48.9 0.8 slice_convert_fusion.3
  49.8 2.1 copy.158
  51.9 1.2 fusion.38
  53.0 0.9 copy.159
  53.9 0.7 slice_convert_fusion.8
  54.6 1.0 pad_maximum_fusion.2
  55.6 7.6 %collective-permute-start.3 = (bf16[1032,128]{0,1:T(8,128)(2,1)S(1)}, bf16[1032,128]{0,1:T(8,128)(2,1)S(1)}, u32[]{:S(2)}, u32[]{:S(2)}) collective-permute-start(bf16[1032,128]{0,1:T(8,128)(2,1)S(1)} %pad_maximum_fusion.2), channel_id=1, source_target_pairs={{0,8},{2,10},{4,12},{6,14},{8,16},{10,18},{12,20},{14,22},{16,24},... | collective-permute-start | bytes 792584 | tf_op jit(solution)/shard_map/ppermute | solution.py:43
  63.2 4.7 %collective-permute-done.3 = bf16[1032,128]{0,1:T(8,128)(2,1)S(1)} collective-permute-done((bf16[1032,128]{0,1:T(8,128)(2,1)S(1)}, bf16[1032,128]{0,1:T(8,128)(2,1)S(1)}, u32[]{:S(2)}, u32[]{:S(2)}) %collective-permute-start.3) | collective-permute-done | bytes 264224 | tf_op jit(solution)/shard_map/ppermute | solution.py:43
  67.9 0.7 copy-done.4
  68.7 0.8 slice_convert_fusion.2
  69.5 2.2 copy.160
  71.7 1.4 add_convert_fusion.1
  73.1 0.1 copy.161
  73.2 0.7 slice_convert_fusion.7
  74.0 4.7 %collective-permute-start.4 = (bf16[1032,128]{0,1:T(8,128)(2,1)S(1)}, bf16[1032,128]{0,1:T(8,128)(2,1)S(1)}, u32[]{:S(2)}, u32[]{:S(2)}) collective-permute-start(bf16[1032,128]{0,1:T(8,128)(2,1)S(1)} %pad_maximum_fusion.3), channel_id=1, source_target_pairs={{0,18},{2,20},{4,22},{6,24},{8,26},{10,28},{12,30},{1,19},{3,21},{... | collective-permute-start | bytes 792584 | tf_op jit(solution)/shard_map/ppermute | solution.py:43
  78.7 3.4 %collective-permute-start.5 = (bf16[1032,128]{0,1:T(8,128)(2,1)S(1)}, bf16[1032,128]{0,1:T(8,128)(2,1)}, u32[]{:S(2)}, u32[]{:S(2)}) collective-permute-start(bf16[1032,128]{0,1:T(8,128)(2,1)S(1)} %pad_maximum_fusion.3), channel_id=1, source_target_pairs={{0,2},{2,4},{4,6},{6,8},{8,10},{10,12},{12,14},{14,16},{16,18},{18... | collective-permute-start | bytes 792584 | tf_op jit(solution)/shard_map/ppermute | solution.py:43
  82.0 0.7 iota_compare_fusion.4
  82.8 9.6 %collective-permute-done.4 = bf16[1032,128]{0,1:T(8,128)(2,1)S(1)} collective-permute-done((bf16[1032,128]{0,1:T(8,128)(2,1)S(1)}, bf16[1032,128]{0,1:T(8,128)(2,1)S(1)}, u32[]{:S(2)}, u32[]{:S(2)}) %collective-permute-start.4) | collective-permute-done | bytes 264224 | tf_op jit(solution)/shard_map/ppermute | solution.py:43
  92.4 1.0 copy.162
  93.4 5.8 %collective-permute-done.5 = bf16[1032,128]{0,1:T(8,128)(2,1)} collective-permute-done((bf16[1032,128]{0,1:T(8,128)(2,1)S(1)}, bf16[1032,128]{0,1:T(8,128)(2,1)}, u32[]{:S(2)}, u32[]{:S(2)}) %collective-permute-start.5) | collective-permute-done | bytes 264224 | tf_op jit(solution)/shard_map/ppermute | solution.py:43
  99.2 1.0 slice_convert_fusion
  100.2 1.1 copy.163
  101.3 0.7 slice_convert_fusion.6
  102.0 2.0 fusion.89
  104.0 6.7 %fusion.6 = f32[16,384,128]{2,1,0:T(8,128)} fusion(f32[16,384]{1,0:T(8,128)} %copy-done.7, pred[384,384]{1,0:T(8,128)(4,1)S(1)} %copy-done.6, bf16[16,384,128]{1,2,0:T(8,128)(2,1)} %bitcast.145, bf16[384,2048]{1,0:T(8,128)(2,1)S(1)} %copy-done, bf16[384,2048]{1,0:T(8,128)(2,1)} %param.14), kind=kOutput, calls=%fused_computation.10 | convolution fusion | flops 1222115328 | bytes 8036352 | tf_op jit(solution)/shard_map/hts,hsd->htd/dot_general | solution.py:126
  110.7 0.7 broadcast_subtract_fusion
  111.7 3.5 %multiply_reduce_fusion = (f32[16,384]{1,0:T(8,128)S(1)}, f32[16,384,128]{2,1,0:T(8,128)S(1)}) fusion(f32[16,384,128]{2,1,0:T(8,128)} %fusion.6, bf16[16,384,128]{2,1,0:T(8,128)(2,1)} %multiply_convert_fusion.4, f32[16,128,128]{2,1,0:T(8,128)S(1)} %broadcast_select_fusion, f32[8,128,128]{2,1,0:T(8,128)S(1)} %get-tuple-element.18, ...), kind=kOutput, calls=%fused_computation.22 | convolution fusion | flops 205514752 | bytes 9986113 | tf_op jit(solution)/shard_map/htd,hde->hte/dot_general | solution.py:130
  115.2 1.0 fusion.20
  116.2 0.9 copy.166
  117.1 7.6 %fusion.15 = (f32[384]{0:T(512)S(1)}, bf16[384,2048]{1,0:T(8,128)(2,1)S(1)}) fusion(bf16[384,2048]{0,1:T(8,128)(2,1)S(1)} %bitcast.156, bf16[2048,2048]{1,0:T(8,128)(2,1)} %all-gather.2.cloned.1.call-done, bf16[384,2048]{1,0:T(8,128)(2,1)} %param.15), kind=kOutput, calls=%fused_computation.16 | convolution fusion | flops 3225943552 | bytes 13108736 | tf_op jit(solution)/shard_map/dot_general | solution.py:144
  124.7 1.9 convolution_convert_fusion
  126.7 46.5 %all_to_all.10 = bf16[32,24,2048]{2,1,0:T(8,128)(2,1)S(1)} all-to-all(bf16[32,24,2048]{2,1,0:T(8,128)(2,1)S(1)} %bitcast.150), channel_id=1, replica_groups=mesh['dp'=4,'sy'=4,'sx'=4,'sc'=2] {'sy','sx','sc'}, dimensions={0} | all-to-all | bytes 6291456 | tf_op jit(solution)/shard_map/all_to_all | solution.py:167
  173.2 7.6 %fusion.2 = f32[32,24,1408]{2,1,0:T(8,128)S(1)} fusion(bf16[32,24,2048]{2,1,0:T(8,128)(2,1)S(1)} %all_to_all.10, bf16[1,2048,1408]{2,1,0:T(8,128)(2,1)} %param.22), kind=kOutput, calls=%fused_computation.3 | convolution fusion | flops 4429185024 | bytes 13238272 | tf_op jit(solution)/shard_map/snd,df->snf/dot_general | solution.py:171
  180.9 5.8 %multiply_convert_fusion.2 = bf16[32,24,1408]{2,1,0:T(8,128)(2,1)S(1)} fusion(f32[32,24,1408]{2,1,0:T(8,128)S(1)} %fusion.2, bf16[32,24,2048]{2,1,0:T(8,128)(2,1)S(1)} %all_to_all.10, bf16[1,2048,1408]{2,1,0:T(8,128)(2,1)S(1)} %bitcast.165), kind=kOutput, calls=%fused_computation.12 | convolution fusion | flops 4435673088 | bytes 15400960 | tf_op jit(solution)/shard_map/snd,df->snf/dot_general | solution.py:168
  186.7 6.5 %fusion.10 = bf16[32,24,2048]{2,1,0:T(8,128)(2,1)} fusion(bf16[32,24,1408]{2,1,0:T(8,128)(2,1)S(1)} %multiply_convert_fusion.2, bf16[1,1408,2048]{2,1,0:T(8,128)(2,1)S(1)} %bitcast.167), kind=kOutput, calls=%fused_computation.14 | convolution fusion | flops 4430757888 | bytes 11075584 | tf_op jit(solution)/shard_map/snf,fd->snd/dot_general | solution.py:173
  193.2 4.9 %all-to-all-start.1 = ((bf16[32,24,2048]{2,1,0:T(8,128)(2,1)}), bf16[32,24,2048]{2,1,0:T(8,128)(2,1)}, u32[]{:S(2)}, u32[]{:S(2)}) async-start(bf16[32,24,2048]{2,1,0:T(8,128)(2,1)} %fusion.10), calls=%async_computation.1 | async-start | bytes 6291456 | tf_op jit(solution)/shard_map/all_to_all | solution.py:176
  198.4 41.8 %all-to-all-done.1 = bf16[32,24,2048]{2,1,0:T(8,128)(2,1)} async-done(((bf16[32,24,2048]{2,1,0:T(8,128)(2,1)}), bf16[32,24,2048]{2,1,0:T(8,128)(2,1)}, u32[]{:S(2)}, u32[]{:S(2)}) %all-to-all-start.1) | async-done | bytes 3145760 | tf_op jit(solution)/shard_map/all_to_all | solution.py:176
  240.2 4.6 %fusion.18 = bf16[384,2048]{1,0:T(8,128)(2,1)} fusion(bf16[384,2048]{1,0:T(8,128)(2,1)S(1)} %copy-done.11, bf16[768,2048]{1,0:T(8,128)(2,1)} %bitcast.44, f32[768]{0:T(1024)S(1)} %broadcast_in_dim.21, s32[768]{0:T(1024)S(1)} %eq.33), kind=kOutput, calls=%fused_computation.19 | convolution fusion | flops 1211498496 | bytes 6297600 | tf_op jit(solution)/shard_map/dot_general | solution.py:181
  (72 shorter events, 1.4 us)
Async XLA Ops:
  6.5 19.2 %copy-start = (bf16[384,2048]{1,0:T(8,128)(2,1)S(1)}, bf16[384,2048]{1,0:T(8,128)(2,1)}, u32[]{:S(2)}) copy-start(bf16[384,2048]{1,0:T(8,128)(2,1)} %param.12) | copy-start | bytes 4718596
  6.5 110.5 %all-gather.2.cloned.1.call-start = ((), (), s32[]{:S(2)}) async-start(), calls=%async_computation.2 | async-start | bytes 8650752 | tf_op jit(solution)/shard_map/all_gather | solution.py:146
  8.5 0.6 copy-start.7
  11.4 8.7 %copy-start.3 = (bf16[384,2048]{0,1:T(8,128)(2,1)}, bf16[384,2048]{0,1:T(8,128)(2,1)S(1)}, u32[]{:S(2)}) copy-start(bf16[384,2048]{0,1:T(8,128)(2,1)S(1)} %copy.172) | copy-start | bytes 4718596
  15.9 2.3 collective-permute-start
  15.9 4.9 %copy-start.2 = (f32[16,128,128]{2,1,0:T(8,128)S(1)}, f32[16,128,128]{2,1,0:T(8,128)}, u32[]{:S(2)}) copy-start(f32[16,128,128]{2,1,0:T(8,128)} %get-tuple-element.48) | copy-start | bytes 3145732
  22.2 10.1 %collective-permute-start.1 = (bf16[1032,128]{0,1:T(8,128)(2,1)S(1)}, bf16[1032,128]{0,1:T(8,128)(2,1)S(1)}, u32[]{:S(2)}, u32[]{:S(2)}) collective-permute-start(bf16[1032,128]{0,1:T(8,128)(2,1)S(1)} %pad_maximum_fusion), channel_id=1, source_target_pairs={{0,2},{2,4},{4,6},{6,8},{8,10},{10,12},{12,14},{14,16},{16,18},{18... | collective-permute-start | bytes 792584 | tf_op jit(solution)/shard_map/ppermute | solution.py:43
  36.6 11.6 %collective-permute-start.2 = (bf16[1032,128]{0,1:T(8,128)(2,1)S(1)}, bf16[1032,128]{0,1:T(8,128)(2,1)S(1)}, u32[]{:S(2)}, u32[]{:S(2)}) collective-permute-start(bf16[1032,128]{0,1:T(8,128)(2,1)S(1)} %pad_maximum_fusion.1), channel_id=1, source_target_pairs={{0,4},{2,6},{4,8},{6,10},{8,12},{10,14},{12,16},{14,18},{16,20},{1... | collective-permute-start | bytes 792584 | tf_op jit(solution)/shard_map/ppermute | solution.py:43
  48.2 0.7 copy-start.5
  55.6 12.3 %collective-permute-start.3 = (bf16[1032,128]{0,1:T(8,128)(2,1)S(1)}, bf16[1032,128]{0,1:T(8,128)(2,1)S(1)}, u32[]{:S(2)}, u32[]{:S(2)}) collective-permute-start(bf16[1032,128]{0,1:T(8,128)(2,1)S(1)} %pad_maximum_fusion.2), channel_id=1, source_target_pairs={{0,8},{2,10},{4,12},{6,14},{8,16},{10,18},{12,20},{14,22},{16,24},... | collective-permute-start | bytes 792584 | tf_op jit(solution)/shard_map/ppermute | solution.py:43
  67.9 0.7 copy-start.4
  74.0 18.4 %collective-permute-start.4 = (bf16[1032,128]{0,1:T(8,128)(2,1)S(1)}, bf16[1032,128]{0,1:T(8,128)(2,1)S(1)}, u32[]{:S(2)}, u32[]{:S(2)}) collective-permute-start(bf16[1032,128]{0,1:T(8,128)(2,1)S(1)} %pad_maximum_fusion.3), channel_id=1, source_target_pairs={{0,18},{2,20},{4,22},{6,24},{8,26},{10,28},{12,30},{1,19},{3,21},{... | collective-permute-start | bytes 792584 | tf_op jit(solution)/shard_map/ppermute | solution.py:43
  78.7 20.5 %collective-permute-start.5 = (bf16[1032,128]{0,1:T(8,128)(2,1)S(1)}, bf16[1032,128]{0,1:T(8,128)(2,1)}, u32[]{:S(2)}, u32[]{:S(2)}) collective-permute-start(bf16[1032,128]{0,1:T(8,128)(2,1)S(1)} %pad_maximum_fusion.3), channel_id=1, source_target_pairs={{0,2},{2,4},{4,6},{6,8},{8,10},{10,12},{12,14},{14,16},{16,18},{18... | collective-permute-start | bytes 792584 | tf_op jit(solution)/shard_map/ppermute | solution.py:43
  99.2 4.8 %copy-start.6 = (pred[384,384]{1,0:T(8,128)(4,1)S(1)}, pred[384,384]{1,0:T(8,128)(4,1)}, u32[]{:S(2)}) copy-start(pred[384,384]{1,0:T(8,128)(4,1)} %iota_compare_fusion.4) | copy-start | bytes 442372
  104.0 7.6 %collective-permute-start.6 = (bf16[8,128,128]{2,1,0:T(8,128)(2,1)}, bf16[8,128,128]{2,1,0:T(8,128)(2,1)S(1)}, u32[]{:S(2)}, u32[]{:S(2)}) collective-permute-start(bf16[8,128,128]{2,1,0:T(8,128)(2,1)} %get-tuple-element.17), channel_id=1, source_target_pairs={{0,1},{1,0},{2,3},{3,2},{4,5},{5,4},{6,7},{7,6},{8,9},{9,8},{10,11... | collective-permute-start | bytes 786440 | tf_op jit(solution)/shard_map/ppermute | solution.py:76
  117.1 7.6 %copy-start.9 = (f32[2048]{0:T(1024)S(1)}, f32[2048]{0:T(1024)}, u32[]{:S(2)}) copy-start(f32[2048]{0:T(1024)} %param.19) | copy-start | bytes 24580
  124.7 2.0 copy-start.10
  126.7 54.2 %slice-start = ((s8[5767168]{0:T(1024)(128)(4,1)}), s8[4194304]{0:T(1024)(128)(4,1)S(1)}, s32[]{:S(2)}) async-start(s8[5767168]{0:T(1024)(128)(4,1)} %bitcast.164), calls=%async_computation.3 | async-start | bytes 8388608
  173.2 7.7 %slice-start.1 = ((s8[5767168]{0:T(1024)(128)(4,1)}), s8[1572864]{0:T(1024)(128)(4,1)S(1)}, s32[]{:S(2)}) async-start(s8[5767168]{0:T(1024)(128)(4,1)} %bitcast.164), calls=%async_computation.4 | async-start | bytes 3145728
  173.2 13.5 %slice-start.2 = ((s8[5767168]{0:T(1024)(128)(4,1)}), s8[4194304]{0:T(1024)(128)(4,1)S(1)}, s32[]{:S(2)}) async-start(s8[5767168]{0:T(1024)(128)(4,1)} %bitcast.166), calls=%async_computation.5 | async-start | bytes 8388608
  180.9 5.8 %slice-start.3 = ((s8[5767168]{0:T(1024)(128)(4,1)}), s8[1572864]{0:T(1024)(128)(4,1)S(1)}, s32[]{:S(2)}) async-start(s8[5767168]{0:T(1024)(128)(4,1)} %bitcast.166), calls=%async_computation.6 | async-start | bytes 3145728
  193.2 5.0 %copy-start.8 = (f32[32,24]{0,1:T(8,128)S(1)}, f32[32,24]{0,1:T(8,128)}, u32[]{:S(2)}) copy-start(f32[32,24]{0,1:T(8,128)} %param.18) | copy-start | bytes 9220
  193.2 47.0 %copy-start.11 = (bf16[384,2048]{1,0:T(8,128)(2,1)S(1)}, bf16[384,2048]{1,0:T(8,128)(2,1)}, u32[]{:S(2)}) copy-start(bf16[384,2048]{1,0:T(8,128)(2,1)} %copy-done.10) | copy-start | bytes 4718596
  193.2 47.0 %all-to-all-start.1 = ((bf16[32,24,2048]{2,1,0:T(8,128)(2,1)}), bf16[32,24,2048]{2,1,0:T(8,128)(2,1)}, u32[]{:S(2)}, u32[]{:S(2)}) async-start(bf16[32,24,2048]{2,1,0:T(8,128)(2,1)} %fusion.10), calls=%async_computation.1 | async-start | bytes 6291456 | tf_op jit(solution)/shard_map/all_to_all | solution.py:176
  240.2 4.6 %copy-start.1 = (bf16[384,2048]{1,0:T(8,128)(2,1)S(1)}, bf16[384,2048]{1,0:T(8,128)(2,1)}, u32[]{:S(2)}) copy-start(bf16[384,2048]{1,0:T(8,128)(2,1)} %param.12) | copy-start | bytes 4718596
Sparse Core Ops, SparseCore 0:
  34.8 65.3 all-gather.1

commit v13 on v10

--- a/solution.py
+++ b/solution.py
@@ -109,7 +109,17 @@
     local_state = jnp.einsum(
         "hsd,hse->hde", key_scaled, value_heads, preferred_element_type=jnp.float32
     )
-    incoming, out_weight = carried_in(local_state, ending, out_weight)
+    planes, rows_count = lax.axis_size("dp"), lax.axis_size("sy")
+    plane, row = lax.axis_index("dp"), lax.axis_index("sy")
+    turned = [
+        (z * rows_count + (y + z) % rows_count, z * rows_count + y)
+        for z in range(planes)
+        for y in range(rows_count)
+    ]
+    shifted = lax.ppermute(out_weight, ("dp", "sy"), turned)
+    row_block = lax.all_gather(shifted, ("sx", "sc"), axis=0, tiled=True)
+    blocks = lax.all_gather(row_block, "dp", axis=0)
+    incoming, _ = carried_in(local_state, ending, ending)
     scores = (
         jnp.einsum("htd,hsd->hts", query_heads, key_heads, preferred_element_type=jnp.float32)
         * scaling
@@ -139,11 +149,8 @@
         .transpose(1, 0, 2)
         .reshape(length, model_width)
     )
-    attended = jnp.dot(
-        normed,
-        lax.all_gather(out_weight, SEQ, axis=0, tiled=True),
-        preferred_element_type=jnp.float32,
-    )
+    rolled = jnp.roll(normed.reshape(length, planes, -1), -row, axis=1)
+    attended = jnp.einsum("tzk,zkd->td", rolled, blocks, preferred_element_type=jnp.float32)
     residual = (stream.astype(jnp.float32) + attended).astype(jnp.bfloat16)
     widened = residual.astype(jnp.float32)
     mixed_in = (

time: 246 us -> 275 us (1.12)
  waiting for transfers between devices: 68 us -> 96.3 us
    all_gather x1 -> x2, waiting for transfers between devices: 0.02 us -> 35.8 us  [the longest x1 35.7 us: shards(): row_block = lax.all_gather(shifted, ('sx', 'sc'), axis=0, tiled=True)]
    ppermute x5, waiting for transfers between devices: 23.9 us -> 16.7 us  [fetch(): return unpack(lax.ppermute(pack(*pair), axis, pairs), heads)]
  transfers between devices with their start and end apart: 9 -> 11, of which waited for: 7 -> 6; matrix products, arithmetic and copies ran while one was open for 15% -> 18% of each run, Pallas kernels for 0% -> 0%
where the time goes in v13:
time: 275 us; the launch traced here: 274 us
  waiting for transfers between devices  96.3 us (35%)
  matrix products  47.5 us (17%)
  blocking collectives  45.5 us (17%)
  starting transfers between devices  32 us (12%)
  other arithmetic  21.4 us (8%)
  local copies, waits for them, and re-layouts  17.6 us (6%)
  between operations  13.8 us (5%)
    all_to_all x1, blocking collectives, shards(): lax.all_to_all(picked[:, window], SEQ, split_axis=0, concat_axis=0, tiled...  45.5 us
    all_to_all x1, waiting for transfers between devices, shards(): lax.all_to_all(produced, SEQ, split_axis=0, concat_axis=0, tiled=True)  41.8 us
    all_gather x1, waiting for transfers between devices, shards(): row_block = lax.all_gather(shifted, ('sx', 'sc'), axis=0, tiled=True)  35.7 us
    ppermute x5, starting transfers between devices, fetch(): return unpack(lax.ppermute(pack(*pair), axis, pairs), heads)  25.1 us
    ppermute x5, waiting for transfers between devices, fetch(): return unpack(lax.ppermute(pack(*pair), axis, pairs), heads)  16.7 us
    dot_general x1, matrix products, shards(): jnp.einsum('snd,df->snf', arrived, up_weight[0], preferred_element_type=j...  7.64 us
    dot_general x1, matrix products, shards(): jnp.einsum('tzk,zkd->td', rolled, blocks, preferred_element_type=jnp.floa...  7.39 us
    convert_element_type x5, local copies, waits for them, and re-layouts, unpack(): message[:heads * width].reshape(heads, width, width).astype(jnp.float32)  7.12 us
  transfers between devices with their start and end apart: 11, of which 6 were waited for; matrix products, arithmetic and copies ran while one was open for 18% of the time, Pallas kernels for 0%

profile of v13, /device:TPU:0, one launch (start us, length us, event | category | flops | bytes accessed | tf_op | source)
XLA Modules:
  0.0 274.2 jit_solution(12707582090393923469)
XLA Ops:
  6.5 1.7 collective-permute-start.7
  8.3 0.7 copy-done.4
  9.0 0.7 copy_bitcast_fusion.1
  9.8 0.9 reduce-window.6
  10.6 0.2 slice_reduce_fusion
  11.1 35.7 %all-gather.4.cloned.1.call-done = bf16[512,2048]{1,0:T(8,128)(2,1)} async-done(((bf16[64,2048]{1,0:T(8,128)(2,1)}), bf16[512,2048]{1,0:T(8,128)(2,1)}) %all-gather.4.cloned.1.call-update) | async-done | bytes 2097168 | tf_op jit(solution)/shard_map/all_gather | solution.py:120
  47.0 1.9 copy.184
  49.0 3.6 %fusion.100 = (bf16[16,128,128]{2,1,0:T(8,128)(2,1)S(1)}, f32[16,128,128]{2,1,0:T(8,128)}) fusion(bf16[16,384,128]{1,2,0:T(8,128)(2,1)S(1)} %bitcast.149, f32[16,384]{1,0:T(8,128)S(1)} %get-tuple-element.23, bf16[384,2048]{1,0:T(8,128)(2,1)} %param.14), kind=kOutput, calls=%fused_computation.174 | convolution fusion | flops 203948032 | bytes 4743168 | tf_op jit(solution)/shard_map/hsd,hse->hde/dot_general | solution.py:109
  52.5 0.8 fusion.37
  53.3 0.2 collective-permute-start
  53.6 2.0 collective-permute-done
  55.6 1.1 slice.121
  56.8 0.7 slice_convert_fusion.5
  57.5 0.2 fusion.62
  57.8 0.1 broadcast_select_fusion
  57.9 1.0 fusion.97
  58.9 0.1 copy.165
  59.2 2.2 collective-permute-start.1
  61.4 6.6 %collective-permute-done.1 = bf16[1032,128]{0,1:T(8,128)(2,1)S(1)} collective-permute-done((bf16[1032,128]{0,1:T(8,128)(2,1)S(1)}, bf16[1032,128]{0,1:T(8,128)(2,1)S(1)}, u32[]{:S(2)}, u32[]{:S(2)}) %collective-permute-start.1) | collective-permute-done | bytes 264224 | tf_op jit(solution)/shard_map/ppermute | solution.py:43
  68.1 1.0 copy.166
  69.1 1.3 multiply_add_fusion.2
  70.5 0.9 copy.167
  71.4 1.0 pad_maximum_fusion.1
  72.3 6.2 %collective-permute-start.2 = (bf16[1032,128]{0,1:T(8,128)(2,1)S(1)}, bf16[1032,128]{0,1:T(8,128)(2,1)S(1)}, u32[]{:S(2)}, u32[]{:S(2)}) collective-permute-start(bf16[1032,128]{0,1:T(8,128)(2,1)S(1)} %pad_maximum_fusion.1), channel_id=1, source_target_pairs={{0,4},{2,6},{4,8},{6,10},{8,12},{10,14},{12,16},{14,18},{16,20},{1... | collective-permute-start | bytes 792584 | tf_op jit(solution)/shard_map/ppermute | solution.py:43
  78.6 5.9 %collective-permute-done.2 = bf16[1032,128]{0,1:T(8,128)(2,1)S(1)} collective-permute-done((bf16[1032,128]{0,1:T(8,128)(2,1)S(1)}, bf16[1032,128]{0,1:T(8,128)(2,1)S(1)}, u32[]{:S(2)}, u32[]{:S(2)}) %collective-permute-start.2) | collective-permute-done | bytes 264224 | tf_op jit(solution)/shard_map/ppermute | solution.py:43
  84.4 0.7 copy-done.6
  85.2 0.8 slice_convert_fusion.3
  86.0 2.1 copy.168
  88.1 1.2 fusion.41
  89.3 0.9 copy.169
  90.1 0.7 slice_convert_fusion.8
  90.8 1.0 pad_maximum_fusion.2
  91.8 8.2 %collective-permute-start.3 = (bf16[1032,128]{0,1:T(8,128)(2,1)S(1)}, bf16[1032,128]{0,1:T(8,128)(2,1)S(1)}, u32[]{:S(2)}, u32[]{:S(2)}) collective-permute-start(bf16[1032,128]{0,1:T(8,128)(2,1)S(1)} %pad_maximum_fusion.2), channel_id=1, source_target_pairs={{0,8},{2,10},{4,12},{6,14},{8,16},{10,18},{12,20},{14,22},{16,24},... | collective-permute-start | bytes 792584 | tf_op jit(solution)/shard_map/ppermute | solution.py:43
  100.0 0.7 iota_compare_fusion.4
  100.7 4.2 %collective-permute-done.3 = bf16[1032,128]{0,1:T(8,128)(2,1)S(1)} collective-permute-done((bf16[1032,128]{0,1:T(8,128)(2,1)S(1)}, bf16[1032,128]{0,1:T(8,128)(2,1)S(1)}, u32[]{:S(2)}, u32[]{:S(2)}) %collective-permute-start.3) | collective-permute-done | bytes 264224 | tf_op jit(solution)/shard_map/ppermute | solution.py:43
  104.9 0.7 copy-done.5
  105.6 0.8 slice_convert_fusion.2
  106.5 2.0 copy.170
  108.5 1.4 add_convert_fusion
  109.9 0.1 copy.171
  110.0 0.7 slice_convert_fusion.7
  110.8 4.5 %collective-permute-start.4 = (bf16[1032,128]{0,1:T(8,128)(2,1)S(1)}, bf16[1032,128]{0,1:T(8,128)(2,1)}, u32[]{:S(2)}, u32[]{:S(2)}) collective-permute-start(bf16[1032,128]{0,1:T(8,128)(2,1)S(1)} %pad_maximum_fusion.3), channel_id=1, source_target_pairs={{0,18},{2,20},{4,22},{6,24},{8,26},{10,28},{12,30},{1,19},{3,21},{... | collective-permute-start | bytes 792584 | tf_op jit(solution)/shard_map/ppermute | solution.py:43
  115.3 4.0 %collective-permute-start.5 = (bf16[1032,128]{0,1:T(8,128)(2,1)S(1)}, bf16[1032,128]{0,1:T(8,128)(2,1)}, u32[]{:S(2)}, u32[]{:S(2)}) collective-permute-start(bf16[1032,128]{0,1:T(8,128)(2,1)S(1)} %pad_maximum_fusion.3), channel_id=1, source_target_pairs={{0,2},{2,4},{4,6},{6,8},{8,10},{10,12},{12,14},{14,16},{16,18},{18... | collective-permute-start | bytes 792584 | tf_op jit(solution)/shard_map/ppermute | solution.py:43
  119.3 6.7 %fusion.6 = f32[16,384,128]{2,1,0:T(8,128)} fusion(f32[16,384]{1,0:T(8,128)S(1)} %copy_bitcast_fusion, pred[384,384]{1,0:T(8,128)(4,1)} %iota_compare_fusion.4, bf16[16,384,128]{1,2,0:T(8,128)(2,1)} %bitcast.150, bf16[384,2048]{1,0:T(8,128)(2,1)S(1)} %copy-done, bf16[384,2048]{1,0:T(8,128)(2,1)} %param.14), kind=kOutput, calls=%fused_computation.10 | convolution fusion | flops 1222115328 | bytes 8036352 | tf_op jit(solution)/shard_map/hts,hsd->htd/dot_general | solution.py:131
  126.0 1.0 slice_convert_fusion.1
  127.0 1.0 copy.172
  127.9 1.0 slice_convert_fusion
  129.0 1.0 copy.173
  129.9 0.7 slice_convert_fusion.6
  130.6 2.1 fusion.94
  132.7 1.8 multiply_convert_fusion.5
  134.8 3.5 %multiply_reduce_fusion = (f32[16,384]{1,0:T(8,128)S(1)}, f32[16,384,128]{2,1,0:T(8,128)S(1)}) fusion(f32[16,384,128]{2,1,0:T(8,128)} %fusion.6, bf16[16,384,128]{2,1,0:T(8,128)(2,1)} %multiply_convert_fusion.5, f32[16,128,128]{2,1,0:T(8,128)S(1)} %broadcast_select_fusion, f32[8,128,128]{2,1,0:T(8,128)S(1)} %get-tuple-element.14, ...), kind=kOutput, calls=%fused_computation.25 | convolution fusion | flops 205514752 | bytes 9986113 | tf_op jit(solution)/shard_map/htd,hde->hte/dot_general | solution.py:138
  138.3 1.0 fusion.21
  139.3 0.9 copy.176
  140.2 0.8 copy.177
  141.0 7.4 %fusion.15 = (f32[384]{0:T(512)S(1)}, bf16[384,2048]{1,0:T(8,128)(2,1)S(1)}) fusion(bf16[4,512,2048]{2,1,0:T(8,128)(2,1)} %bitcast.168, s32[]{:T(128)S(6)} %select_n.76, bf16[384,4,512]{2,0,1:T(8,128)(2,1)S(1)} %copy.177, bf16[384,2048]{1,0:T(8,128)(2,1)} %param.15), kind=kOutput, calls=%fused_computation.16 | convolution fusion | flops 3226729984 | bytes 13108740 | tf_op jit(solution)/shard_map/tzk,zkd->td/dot_general | solution.py:153
  148.4 1.9 convolution_convert_fusion
  150.3 45.5 %all_to_all.10 = bf16[32,24,2048]{2,1,0:T(8,128)(2,1)S(1)} all-to-all(bf16[32,24,2048]{2,1,0:T(8,128)(2,1)S(1)} %bitcast.155), channel_id=1, replica_groups=mesh['dp'=4,'sy'=4,'sx'=4,'sc'=2] {'sy','sx','sc'}, dimensions={0} | all-to-all | bytes 6291456 | tf_op jit(solution)/shard_map/all_to_all | solution.py:172
  195.8 7.6 %fusion.2 = f32[32,24,1408]{2,1,0:T(8,128)S(1)} fusion(bf16[32,24,2048]{2,1,0:T(8,128)(2,1)S(1)} %all_to_all.10, bf16[1,2048,1408]{2,1,0:T(8,128)(2,1)} %param.22), kind=kOutput, calls=%fused_computation.3 | convolution fusion | flops 4429185024 | bytes 13238272 | tf_op jit(solution)/shard_map/snd,df->snf/dot_general | solution.py:176
  203.5 5.8 %multiply_convert_fusion.2 = bf16[32,24,1408]{2,1,0:T(8,128)(2,1)S(1)} fusion(f32[32,24,1408]{2,1,0:T(8,128)S(1)} %fusion.2, bf16[32,24,2048]{2,1,0:T(8,128)(2,1)S(1)} %all_to_all.10, bf16[1,2048,1408]{2,1,0:T(8,128)(2,1)S(1)} %bitcast.170), kind=kOutput, calls=%fused_computation.12 | convolution fusion | flops 4435673088 | bytes 15400960 | tf_op jit(solution)/shard_map/snd,df->snf/dot_general | solution.py:173
  209.3 6.5 %fusion.10 = bf16[32,24,2048]{2,1,0:T(8,128)(2,1)} fusion(bf16[32,24,1408]{2,1,0:T(8,128)(2,1)S(1)} %multiply_convert_fusion.2, bf16[1,1408,2048]{2,1,0:T(8,128)(2,1)S(1)} %bitcast.172), kind=kOutput, calls=%fused_computation.14 | convolution fusion | flops 4430757888 | bytes 11075584 | tf_op jit(solution)/shard_map/snf,fd->snd/dot_general | solution.py:178
  215.8 4.9 %all-to-all-start.1 = ((bf16[32,24,2048]{2,1,0:T(8,128)(2,1)}), bf16[32,24,2048]{2,1,0:T(8,128)(2,1)}, u32[]{:S(2)}, u32[]{:S(2)}) async-start(bf16[32,24,2048]{2,1,0:T(8,128)(2,1)} %fusion.10), calls=%async_computation.1 | async-start | bytes 6291456 | tf_op jit(solution)/shard_map/all_to_all | solution.py:181
  221.0 41.8 %all-to-all-done.1 = bf16[32,24,2048]{2,1,0:T(8,128)(2,1)} async-done(((bf16[32,24,2048]{2,1,0:T(8,128)(2,1)}), bf16[32,24,2048]{2,1,0:T(8,128)(2,1)}, u32[]{:S(2)}, u32[]{:S(2)}) %all-to-all-start.1) | async-done | bytes 3145760 | tf_op jit(solution)/shard_map/all_to_all | solution.py:181
  262.8 4.6 %fusion.18 = bf16[384,2048]{1,0:T(8,128)(2,1)} fusion(bf16[384,2048]{1,0:T(8,128)(2,1)S(1)} %copy-done.11, bf16[768,2048]{1,0:T(8,128)(2,1)} %bitcast.46, f32[768]{0:T(1024)S(1)} %broadcast_in_dim.21, s32[768]{0:T(1024)S(1)} %eq.36), kind=kOutput, calls=%fused_computation.19 | convolution fusion | flops 1211498496 | bytes 6297600 | tf_op jit(solution)/shard_map/dot_general | solution.py:186
  (78 shorter events, 1.6 us)
Async XLA Ops:
  6.5 112.7 %copy-start = (bf16[384,2048]{1,0:T(8,128)(2,1)S(1)}, bf16[384,2048]{1,0:T(8,128)(2,1)}, u32[]{:S(2)}) copy-start(bf16[384,2048]{1,0:T(8,128)(2,1)} %param.12) | copy-start | bytes 4718596
  6.5 40.3 %all-gather.4.cloned.1.call-start = ((), (), s32[]{:S(2)}) async-start(), calls=%async_computation.2 | async-start | bytes 2359296 | tf_op jit(solution)/shard_map/all_gather | solution.py:120
  6.5 1.7 collective-permute-start.7
  8.3 0.7 copy-start.4
  9.0 132.0 %all-gather.6.cloned.1.call-start = ((), (), s32[]{:S(2)}) async-start(), calls=%async_computation.3 | async-start | bytes 10485760 | tf_op jit(solution)/shard_map/all_gather | solution.py:121
  48.9 7.8 %copy-start.3 = (bf16[384,2048]{0,1:T(8,128)(2,1)}, bf16[384,2048]{0,1:T(8,128)(2,1)S(1)}, u32[]{:S(2)}) copy-start(bf16[384,2048]{0,1:T(8,128)(2,1)S(1)} %copy.184) | copy-start | bytes 4718596
  53.3 2.3 collective-permute-start
  53.6 4.2 %copy-start.2 = (f32[16,128,128]{2,1,0:T(8,128)S(1)}, f32[16,128,128]{2,1,0:T(8,128)}, u32[]{:S(2)}) copy-start(f32[16,128,128]{2,1,0:T(8,128)} %get-tuple-element.44) | copy-start | bytes 3145732
  59.2 8.9 %collective-permute-start.1 = (bf16[1032,128]{0,1:T(8,128)(2,1)S(1)}, bf16[1032,128]{0,1:T(8,128)(2,1)S(1)}, u32[]{:S(2)}, u32[]{:S(2)}) collective-permute-start(bf16[1032,128]{0,1:T(8,128)(2,1)S(1)} %pad_maximum_fusion), channel_id=1, source_target_pairs={{0,2},{2,4},{4,6},{6,8},{8,10},{10,12},{12,14},{14,16},{16,18},{18... | collective-permute-start | bytes 792584 | tf_op jit(solution)/shard_map/ppermute | solution.py:43
  72.3 12.1 %collective-permute-start.2 = (bf16[1032,128]{0,1:T(8,128)(2,1)S(1)}, bf16[1032,128]{0,1:T(8,128)(2,1)S(1)}, u32[]{:S(2)}, u32[]{:S(2)}) collective-permute-start(bf16[1032,128]{0,1:T(8,128)(2,1)S(1)} %pad_maximum_fusion.1), channel_id=1, source_target_pairs={{0,4},{2,6},{4,8},{6,10},{8,12},{10,14},{12,16},{14,18},{16,20},{1... | collective-permute-start | bytes 792584 | tf_op jit(solution)/shard_map/ppermute | solution.py:43
  84.4 0.7 copy-start.6
  91.8 13.1 %collective-permute-start.3 = (bf16[1032,128]{0,1:T(8,128)(2,1)S(1)}, bf16[1032,128]{0,1:T(8,128)(2,1)S(1)}, u32[]{:S(2)}, u32[]{:S(2)}) collective-permute-start(bf16[1032,128]{0,1:T(8,128)(2,1)S(1)} %pad_maximum_fusion.2), channel_id=1, source_target_pairs={{0,8},{2,10},{4,12},{6,14},{8,16},{10,18},{12,20},{14,22},{16,24},... | collective-permute-start | bytes 792584 | tf_op jit(solution)/shard_map/ppermute | solution.py:43
  104.9 0.7 copy-start.5
  110.8 15.2 %collective-permute-start.4 = (bf16[1032,128]{0,1:T(8,128)(2,1)S(1)}, bf16[1032,128]{0,1:T(8,128)(2,1)}, u32[]{:S(2)}, u32[]{:S(2)}) collective-permute-start(bf16[1032,128]{0,1:T(8,128)(2,1)S(1)} %pad_maximum_fusion.3), channel_id=1, source_target_pairs={{0,18},{2,20},{4,22},{6,24},{8,26},{10,28},{12,30},{1,19},{3,21},{... | collective-permute-start | bytes 792584 | tf_op jit(solution)/shard_map/ppermute | solution.py:43
  115.3 12.7 %collective-permute-start.5 = (bf16[1032,128]{0,1:T(8,128)(2,1)S(1)}, bf16[1032,128]{0,1:T(8,128)(2,1)}, u32[]{:S(2)}, u32[]{:S(2)}) collective-permute-start(bf16[1032,128]{0,1:T(8,128)(2,1)S(1)} %pad_maximum_fusion.3), channel_id=1, source_target_pairs={{0,2},{2,4},{4,6},{6,8},{8,10},{10,12},{12,14},{14,16},{16,18},{18... | collective-permute-start | bytes 792584 | tf_op jit(solution)/shard_map/ppermute | solution.py:43
  128.9 5.6 %copy-start.8 = (s32[32,24]{0,1:T(8,128)S(1)}, s32[32,24]{0,1:T(8,128)}, u32[]{:S(2)}) copy-start(s32[32,24]{0,1:T(8,128)} %param.17) | copy-start | bytes 9220
  132.7 2.0 collective-permute-start.6
  141.0 7.4 %copy-start.9 = (f32[2048]{0:T(1024)S(1)}, f32[2048]{0:T(1024)}, u32[]{:S(2)}) copy-start(f32[2048]{0:T(1024)} %param.19) | copy-start | bytes 24580
  148.4 2.0 copy-start.10
  150.3 53.2 %slice-start = ((s8[5767168]{0:T(1024)(128)(4,1)}), s8[4194304]{0:T(1024)(128)(4,1)S(1)}, s32[]{:S(2)}) async-start(s8[5767168]{0:T(1024)(128)(4,1)} %bitcast.169), calls=%async_computation.4 | async-start | bytes 8388608
  195.8 7.7 %slice-start.1 = ((s8[5767168]{0:T(1024)(128)(4,1)}), s8[1572864]{0:T(1024)(128)(4,1)S(1)}, s32[]{:S(2)}) async-start(s8[5767168]{0:T(1024)(128)(4,1)} %bitcast.169), calls=%async_computation.5 | async-start | bytes 3145728
  195.8 13.5 %slice-start.2 = ((s8[5767168]{0:T(1024)(128)(4,1)}), s8[4194304]{0:T(1024)(128)(4,1)S(1)}, s32[]{:S(2)}) async-start(s8[5767168]{0:T(1024)(128)(4,1)} %bitcast.171), calls=%async_computation.6 | async-start | bytes 8388608
  203.5 5.8 %slice-start.3 = ((s8[5767168]{0:T(1024)(128)(4,1)}), s8[1572864]{0:T(1024)(128)(4,1)S(1)}, s32[]{:S(2)}) async-start(s8[5767168]{0:T(1024)(128)(4,1)} %bitcast.171), calls=%async_computation.7 | async-start | bytes 3145728
  215.8 5.0 %copy-start.7 = (f32[32,24]{0,1:T(8,128)S(1)}, f32[32,24]{0,1:T(8,128)}, u32[]{:S(2)}) copy-start(f32[32,24]{0,1:T(8,128)} %param.18) | copy-start | bytes 9220
  215.8 47.0 %copy-start.11 = (bf16[384,2048]{1,0:T(8,128)(2,1)S(1)}, bf16[384,2048]{1,0:T(8,128)(2,1)}, u32[]{:S(2)}) copy-start(bf16[384,2048]{1,0:T(8,128)(2,1)} %copy-done.10) | copy-start | bytes 4718596
  215.8 47.0 %all-to-all-start.1 = ((bf16[32,24,2048]{2,1,0:T(8,128)(2,1)}), bf16[32,24,2048]{2,1,0:T(8,128)(2,1)}, u32[]{:S(2)}, u32[]{:S(2)}) async-start(bf16[32,24,2048]{2,1,0:T(8,128)(2,1)} %fusion.10), calls=%async_computation.1 | async-start | bytes 6291456 | tf_op jit(solution)/shard_map/all_to_all | solution.py:181
  262.8 4.6 %copy-start.1 = (bf16[384,2048]{1,0:T(8,128)(2,1)S(1)}, bf16[384,2048]{1,0:T(8,128)(2,1)}, u32[]{:S(2)}) copy-start(bf16[384,2048]{1,0:T(8,128)(2,1)} %param.12) | copy-start | bytes 4718596
Sparse Core Ops, SparseCore 0:
  9.1 37.6 all-gather.3
  48.5 83.6 all-gather.5

commit v14 on v10

--- a/solution.py
+++ b/solution.py
@@ -59,7 +59,6 @@
 
 def carried_in(state, ending, rider):
     heads = state.shape[0]
-    half = heads // 2
     swap = [(0, 1), (1, 0)]
     core = lax.axis_index(CORE_AXIS)
     first = core == 0
@@ -67,16 +66,7 @@
     lower = (jnp.where(first, state, other_state), jnp.where(first, ending, other_ending))
     upper = (jnp.where(first, other_state, state), jnp.where(first, other_ending, ending))
     chip_state, chip_ending = combine(lower, upper)
-    mine, rider = exclusive_scan(
-        lax.dynamic_slice_in_dim(chip_state, core * half, half, axis=0),
-        lax.dynamic_slice_in_dim(chip_ending, core * half, half, axis=0),
-        CHIP_AXES,
-        rider,
-    )
-    theirs = lax.ppermute(mine.astype(jnp.bfloat16), CORE_AXIS, swap).astype(jnp.float32)
-    before = jnp.where(
-        first, jnp.concatenate([mine, theirs], axis=0), jnp.concatenate([theirs, mine], axis=0)
-    )
+    before, rider = exclusive_scan(chip_state, chip_ending, CHIP_AXES, rider)
     return jnp.where(first, before, combine((before, 0.0), lower)[0]), rider
 
 

time: 246 us -> 254 us (1.033)
  waiting for transfers between devices: 68 us -> 96.7 us
  other arithmetic: 21.3 us -> 11.3 us
  local copies, waits for them, and re-layouts: 16.4 us -> 10.5 us
  starting transfers between devices: 30.8 us -> 27.9 us
    ppermute x5, waiting for transfers between devices: 23.9 us -> 52.7 us  [fetch(): return unpack(lax.ppermute(pack(*pair), axis, pairs), heads)]
    convert_element_type x5 -> x0, local copies, waits for them, and re-layouts: 7.31 us -> none  [unpack(): message[:heads * width].reshape(heads, width, width).astype(jnp.float32)]
    convert_element_type x8 -> x0, other arithmetic: 5.9 us -> none  [the longest x6 3.82 us: unpack(): message[:heads * width].reshape(heads, width, width).astype(jnp.float32)]
    slice x1 -> x7, local copies, waits for them, and re-layouts: 1.08 us -> 4.35 us  [unpack(): message[:heads * width].reshape(heads, width, width).astype(jnp.float32)]
    ppermute x5, starting transfers between devices: 25.8 us -> 22.9 us  [fetch(): return unpack(lax.ppermute(pack(*pair), axis, pairs), heads)]
    convert_element_type x4, other arithmetic: 3.53 us -> 0.89 us  [pack(): state.astype(jnp.bfloat16).reshape(heads * rows, width)]
  transfers between devices with their start and end apart: 9 -> 8, of which waited for: 7 -> 7; matrix products, arithmetic and copies ran while one was open for 15% -> 9% of each run, Pallas kernels for 0% -> 0%
where the time goes in v14:
time: 254 us; the launch traced here: 253 us
  waiting for transfers between devices  96.7 us (38%)
  matrix products  46.3 us (18%)
  blocking collectives  46.3 us (18%)
  starting transfers between devices  27.9 us (11%)
  between operations  13.9 us (5%)
  other arithmetic  11.3 us (4%)
  local copies, waits for them, and re-layouts  10.5 us (4%)
    ppermute x5, waiting for transfers between devices, fetch(): return unpack(lax.ppermute(pack(*pair), axis, pairs), heads)  52.7 us
    all_to_all x1, blocking collectives, shards(): lax.all_to_all(picked[:, window], SEQ, split_axis=0, concat_axis=0, tiled...  46.3 us
    all_to_all x1, waiting for transfers between devices, shards(): lax.all_to_all(produced, SEQ, split_axis=0, concat_axis=0, tiled=True)  41.8 us
    ppermute x5, starting transfers between devices, fetch(): return unpack(lax.ppermute(pack(*pair), axis, pairs), heads)  22.9 us
    dot_general x1, matrix products, shards(): jnp.einsum('snd,df->snf', arrived, up_weight[0], preferred_element_type=j...  7.64 us
    dot_general x1, matrix products, shards(): jnp.dot(normed, lax.all_gather(out_weight, SEQ, axis=0, tiled=True), pref...  7.58 us
    dot_general x1, matrix products, shards(): jnp.einsum('hts,hsd->htd', attend_weights, value_heads, preferred_element...  6.69 us
    dot_general x1, matrix products, shards(): jnp.einsum('snf,fd->snd', activated, down_weight[0], preferred_element_ty...  6.59 us
  transfers between devices with their start and end apart: 8, of which 7 were waited for; matrix products, arithmetic and copies ran while one was open for 9% of the time, Pallas kernels for 0%

profile of v14, /device:TPU:0, one launch (start us, length us, event | category | flops | bytes accessed | tf_op | source)
XLA Modules:
  0.0 253.0 jit_solution(2897449829420794950)
XLA Ops:
  6.5 0.9 copy_bitcast_fusion.1
  7.4 0.9 reduce-window.6
  8.3 0.2 slice_reduce_fusion
  8.4 0.1 copy_bitcast_fusion
  8.5 0.1 slice.120
  8.6 0.1 copy.174
  8.7 0.1 copy.176
  8.8 0.1 subtract_exponential_fusion
  8.9 2.6 %copy.173 = bf16[384,2048]{0,1:T(8,128)(2,1)} copy(bf16[384,2048]{1,0:T(8,128)(2,1)} %param.13) | data formatting | bytes 3145728 | tf_op jit(solution)/shard_map/reshape | solution.py:93
  11.5 2.5 fusion.85
  14.0 0.9 fusion.45
  14.9 2.1 collective-permute-done
  17.1 0.1 copy.175
  17.2 0.1 copy.177
  17.3 0.3 fusion.44
  17.6 3.5 %collective-permute-start.1 = (bf16[2064,128]{1,0:T(8,128)(2,1)S(1)}, bf16[2064,128]{1,0:T(8,128)(2,1)S(1)}, u32[]{:S(2)}, u32[]{:S(2)}) collective-permute-start(bf16[2064,128]{1,0:T(8,128)(2,1)S(1)} %fusion.46), channel_id=1, source_target_pairs={{0,2},{2,4},{4,6},{6,8},{8,10},{10,12},{12,14},{14,16},{16,18},{18... | collective-permute-start | bytes 1585160 | tf_op jit(solution)/shard_map/ppermute | solution.py:43
  21.2 11.5 %collective-permute-done.1 = bf16[2064,128]{1,0:T(8,128)(2,1)S(1)} collective-permute-done((bf16[2064,128]{1,0:T(8,128)(2,1)S(1)}, bf16[2064,128]{1,0:T(8,128)(2,1)S(1)}, u32[]{:S(2)}, u32[]{:S(2)}) %collective-permute-start.1) | collective-permute-done | bytes 528416 | tf_op jit(solution)/shard_map/ppermute | solution.py:43
  32.7 0.2 fusion.57
  33.0 1.6 fusion.38
  34.6 0.1 convert_element_type.197
  34.7 0.1 copy.178
  34.8 0.9 fusion.47
  35.7 5.9 %collective-permute-start.2 = (bf16[2064,128]{1,0:T(8,128)(2,1)}, bf16[2064,128]{1,0:T(8,128)(2,1)S(1)}, u32[]{:S(2)}, u32[]{:S(2)}) collective-permute-start(bf16[2064,128]{1,0:T(8,128)(2,1)} %fusion.47), channel_id=1, source_target_pairs={{0,4},{2,6},{4,8},{6,10},{8,12},{10,14},{12,16},{14,18},{16,20},{1... | collective-permute-start | bytes 1585160 | tf_op jit(solution)/shard_map/ppermute | solution.py:43
  41.7 12.5 %collective-permute-done.2 = bf16[2064,128]{1,0:T(8,128)(2,1)S(1)} collective-permute-done((bf16[2064,128]{1,0:T(8,128)(2,1)}, bf16[2064,128]{1,0:T(8,128)(2,1)S(1)}, u32[]{:S(2)}, u32[]{:S(2)}) %collective-permute-start.2) | collective-permute-done | bytes 528416 | tf_op jit(solution)/shard_map/ppermute | solution.py:43
  54.2 0.2 fusion.56
  54.4 0.6 copy-done.5
  55.0 0.1 copy.179
  55.1 1.1 slice.128
  56.2 0.2 fusion.39
  56.4 0.8 fusion.48
  57.2 9.2 %collective-permute-start.3 = (bf16[2064,128]{1,0:T(8,128)(2,1)}, bf16[2064,128]{1,0:T(8,128)(2,1)}, u32[]{:S(2)}, u32[]{:S(2)}) collective-permute-start(bf16[2064,128]{1,0:T(8,128)(2,1)} %fusion.48), channel_id=1, source_target_pairs={{0,8},{2,10},{4,12},{6,14},{8,16},{10,18},{12,20},{14,22},{16,24},... | collective-permute-start | bytes 1585160 | tf_op jit(solution)/shard_map/ppermute | solution.py:43
  66.5 6.7 %fusion.6 = f32[16,384,128]{2,1,0:T(8,128)} fusion(f32[16,384]{1,0:T(8,128)S(1)} %copy_bitcast_fusion, pred[384,384]{1,0:T(8,128)(4,1)S(1)} %iota_compare_fusion.4, bf16[16,384,128]{1,2,0:T(8,128)(2,1)} %bitcast.135, bf16[384,2048]{1,0:T(8,128)(2,1)} %param.14, bf16[384,2048]{1,0:T(8,128)(2,1)S(1)} %copy-done), kind=kOutput, calls=%fused_computation.10 | convolution fusion | flops 1222115328 | bytes 8036352 | tf_op jit(solution)/shard_map/hts,hsd->htd/dot_general | solution.py:111
  73.2 8.3 %collective-permute-done.3 = bf16[2064,128]{1,0:T(8,128)(2,1)} collective-permute-done((bf16[2064,128]{1,0:T(8,128)(2,1)}, bf16[2064,128]{1,0:T(8,128)(2,1)}, u32[]{:S(2)}, u32[]{:S(2)}) %collective-permute-start.3) | collective-permute-done | bytes 528416 | tf_op jit(solution)/shard_map/ppermute | solution.py:43
  81.4 0.7 slice_convert_fusion.1
  82.1 0.2 fusion.55
  82.3 0.1 copy.180
  82.4 1.1 slice.133
  83.5 0.3 fusion.36
  83.9 0.8 fusion.49
  84.7 2.1 collective-permute-start.4
  86.8 2.1 collective-permute-start.5
  88.9 1.0 multiply_convert_fusion.5
  89.9 0.1 copy.168
  90.0 0.1 eq.33
  90.1 12.8 %collective-permute-done.4 = bf16[2064,128]{1,0:T(8,128)(2,1)} collective-permute-done((bf16[2064,128]{1,0:T(8,128)(2,1)}, bf16[2064,128]{1,0:T(8,128)(2,1)}, u32[]{:S(2)}, u32[]{:S(2)}) %collective-permute-start.4) | collective-permute-done | bytes 528416 | tf_op jit(solution)/shard_map/ppermute | solution.py:43
  102.9 1.1 slice.138
  104.0 7.6 %collective-permute-done.5 = bf16[2064,128]{1,0:T(8,128)(2,1)} collective-permute-done((bf16[2064,128]{1,0:T(8,128)(2,1)}, bf16[2064,128]{1,0:T(8,128)(2,1)}, u32[]{:S(2)}, u32[]{:S(2)}) %collective-permute-start.5) | collective-permute-done | bytes 528416 | tf_op jit(solution)/shard_map/ppermute | solution.py:43
  111.6 1.1 slice.143
  112.7 0.7 slice_convert_fusion
  113.4 0.2 fusion.54
  113.6 3.1 %multiply_reduce_fusion = (f32[16,384]{1,0:T(8,128)S(1)}, f32[16,384,128]{2,1,0:T(8,128)S(1)}) fusion(f32[16,384,128]{2,1,0:T(8,128)} %fusion.6, bf16[16,384,128]{2,1,0:T(8,128)(2,1)S(1)} %multiply_convert_fusion.5, bf16[16,128,128]{2,1,0:T(8,128)(2,1)S(1)} %bitcast.141, bf16[16,128,128]{2,1,0:T(8,128)(2,1)S(1)} %bitcast.140, ...), kind=kOutput, calls=%fused_computation.22 | convolution fusion | flops 206301184 | bytes 10510465 | tf_op jit(solution)/shard_map/htd,hde->hte/dot_general | solution.py:118
  116.7 1.0 fusion.20
  117.7 0.9 copy.167
  118.6 7.6 %fusion.15 = (f32[384]{0:T(512)S(1)}, bf16[384,2048]{1,0:T(8,128)(2,1)S(1)}) fusion(bf16[384,2048]{0,1:T(8,128)(2,1)S(1)} %bitcast.149, bf16[2048,2048]{1,0:T(8,128)(2,1)} %all-gather.2.cloned.1.call-done, bf16[384,2048]{1,0:T(8,128)(2,1)} %param.15), kind=kOutput, calls=%fused_computation.16 | convolution fusion | flops 3225943552 | bytes 13108736 | tf_op jit(solution)/shard_map/dot_general | solution.py:132
  126.3 1.9 convolution_convert_fusion
  128.2 46.3 %all_to_all.10 = bf16[32,24,2048]{2,1,0:T(8,128)(2,1)S(1)} all-to-all(bf16[32,24,2048]{2,1,0:T(8,128)(2,1)S(1)} %bitcast.139), channel_id=1, replica_groups=mesh['dp'=4,'sy'=4,'sx'=4,'sc'=2] {'sy','sx','sc'}, dimensions={0} | all-to-all | bytes 6291456 | tf_op jit(solution)/shard_map/all_to_all | solution.py:155
  174.5 7.6 %fusion.2 = f32[32,24,1408]{2,1,0:T(8,128)S(1)} fusion(bf16[32,24,2048]{2,1,0:T(8,128)(2,1)S(1)} %all_to_all.10, bf16[1,2048,1408]{2,1,0:T(8,128)(2,1)} %param.22), kind=kOutput, calls=%fused_computation.3 | convolution fusion | flops 4429185024 | bytes 13238272 | tf_op jit(solution)/shard_map/snd,df->snf/dot_general | solution.py:159
  182.2 5.8 %multiply_convert_fusion.2 = bf16[32,24,1408]{2,1,0:T(8,128)(2,1)S(1)} fusion(f32[32,24,1408]{2,1,0:T(8,128)S(1)} %fusion.2, bf16[32,24,2048]{2,1,0:T(8,128)(2,1)S(1)} %all_to_all.10, bf16[1,2048,1408]{2,1,0:T(8,128)(2,1)S(1)} %bitcast.154), kind=kOutput, calls=%fused_computation.12 | convolution fusion | flops 4435673088 | bytes 15400960 | tf_op jit(solution)/shard_map/snd,df->snf/dot_general | solution.py:156
  188.0 6.6 %fusion.10 = bf16[32,24,2048]{2,1,0:T(8,128)(2,1)} fusion(bf16[32,24,1408]{2,1,0:T(8,128)(2,1)S(1)} %multiply_convert_fusion.2, bf16[1,1408,2048]{2,1,0:T(8,128)(2,1)S(1)} %bitcast.156), kind=kOutput, calls=%fused_computation.14 | convolution fusion | flops 4430757888 | bytes 11075584 | tf_op jit(solution)/shard_map/snf,fd->snd/dot_general | solution.py:161
  194.6 5.0 %all-to-all-start.1 = ((bf16[32,24,2048]{2,1,0:T(8,128)(2,1)}), bf16[32,24,2048]{2,1,0:T(8,128)(2,1)}, u32[]{:S(2)}, u32[]{:S(2)}) async-start(bf16[32,24,2048]{2,1,0:T(8,128)(2,1)} %fusion.10), calls=%async_computation.1 | async-start | bytes 6291456 | tf_op jit(solution)/shard_map/all_to_all | solution.py:164
  199.6 0.1 copy.169
  199.7 0.1 broadcast_in_dim.21
  199.8 41.8 %all-to-all-done.1 = bf16[32,24,2048]{2,1,0:T(8,128)(2,1)} async-done(((bf16[32,24,2048]{2,1,0:T(8,128)(2,1)}), bf16[32,24,2048]{2,1,0:T(8,128)(2,1)}, u32[]{:S(2)}, u32[]{:S(2)}) %all-to-all-start.1) | async-done | bytes 3145760 | tf_op jit(solution)/shard_map/all_to_all | solution.py:164
  241.6 4.6 %fusion.18 = bf16[384,2048]{1,0:T(8,128)(2,1)} fusion(bf16[384,2048]{1,0:T(8,128)(2,1)S(1)} %copy-done.10, bf16[768,2048]{1,0:T(8,128)(2,1)} %bitcast.38, f32[768]{0:T(1024)S(1)} %broadcast_in_dim.21, s32[768]{0:T(1024)S(1)} %eq.33), kind=kOutput, calls=%fused_computation.19 | convolution fusion | flops 1211498496 | bytes 6297600 | tf_op jit(solution)/shard_map/dot_general | solution.py:169
  (64 shorter events, 0.5 us)
Async XLA Ops:
  6.5 60.0 %copy-start = (bf16[384,2048]{1,0:T(8,128)(2,1)S(1)}, bf16[384,2048]{1,0:T(8,128)(2,1)}, u32[]{:S(2)}) copy-start(bf16[384,2048]{1,0:T(8,128)(2,1)} %param.12) | copy-start | bytes 4718596
  6.5 112.1 %all-gather.2.cloned.1.call-start = ((), (), s32[]{:S(2)}) async-start(), calls=%async_computation.2 | async-start | bytes 8650752 | tf_op jit(solution)/shard_map/all_gather | solution.py:134
  14.0 18.9 %copy-start.2 = (f32[16,128,128]{2,1,0:T(8,128)}, f32[16,128,128]{2,1,0:T(8,128)S(1)}, u32[]{:S(2)}) copy-start(f32[16,128,128]{2,1,0:T(8,128)S(1)} %get-tuple-element.42) | copy-start | bytes 3145732
  14.9 2.1 collective-permute-start
  17.1 17.5 %copy-start.4 = (bf16[2064,128]{1,0:T(8,128)(2,1)}, bf16[2064,128]{1,0:T(8,128)(2,1)S(1)}, u32[]{:S(2)}) copy-start(bf16[2064,128]{1,0:T(8,128)(2,1)S(1)} %collective-permute-done) | copy-start | bytes 1585156
  17.6 15.1 %collective-permute-start.1 = (bf16[2064,128]{1,0:T(8,128)(2,1)S(1)}, bf16[2064,128]{1,0:T(8,128)(2,1)S(1)}, u32[]{:S(2)}, u32[]{:S(2)}) collective-permute-start(bf16[2064,128]{1,0:T(8,128)(2,1)S(1)} %fusion.46), channel_id=1, source_target_pairs={{0,2},{2,4},{4,6},{6,8},{8,10},{10,12},{12,14},{14,16},{16,18},{18... | collective-permute-start | bytes 1585160 | tf_op jit(solution)/shard_map/ppermute | solution.py:43
  35.7 18.5 %collective-permute-start.2 = (bf16[2064,128]{1,0:T(8,128)(2,1)}, bf16[2064,128]{1,0:T(8,128)(2,1)S(1)}, u32[]{:S(2)}, u32[]{:S(2)}) collective-permute-start(bf16[2064,128]{1,0:T(8,128)(2,1)} %fusion.47), channel_id=1, source_target_pairs={{0,4},{2,6},{4,8},{6,10},{8,12},{10,14},{12,16},{14,18},{16,20},{1... | collective-permute-start | bytes 1585160 | tf_op jit(solution)/shard_map/ppermute | solution.py:43
  54.2 0.8 copy-start.5
  57.2 24.2 %collective-permute-start.3 = (bf16[2064,128]{1,0:T(8,128)(2,1)}, bf16[2064,128]{1,0:T(8,128)(2,1)}, u32[]{:S(2)}, u32[]{:S(2)}) collective-permute-start(bf16[2064,128]{1,0:T(8,128)(2,1)} %fusion.48), channel_id=1, source_target_pairs={{0,8},{2,10},{4,12},{6,14},{8,16},{10,18},{12,20},{14,22},{16,24},... | collective-permute-start | bytes 1585160 | tf_op jit(solution)/shard_map/ppermute | solution.py:43
  83.9 6.0 %copy-start.7 = (s32[32,24]{0,1:T(8,128)S(1)}, s32[32,24]{0,1:T(8,128)}, u32[]{:S(2)}) copy-start(s32[32,24]{0,1:T(8,128)} %param.17) | copy-start | bytes 9220
  84.7 18.2 %collective-permute-start.4 = (bf16[2064,128]{1,0:T(8,128)(2,1)}, bf16[2064,128]{1,0:T(8,128)(2,1)}, u32[]{:S(2)}, u32[]{:S(2)}) collective-permute-start(bf16[2064,128]{1,0:T(8,128)(2,1)} %fusion.49), channel_id=1, source_target_pairs={{0,18},{2,20},{4,22},{6,24},{8,26},{10,28},{12,30},{1,19},{3,21},{... | collective-permute-start | bytes 1585160 | tf_op jit(solution)/shard_map/ppermute | solution.py:43
  86.8 24.9 %collective-permute-start.5 = (bf16[2064,128]{1,0:T(8,128)(2,1)}, bf16[2064,128]{1,0:T(8,128)(2,1)}, u32[]{:S(2)}, u32[]{:S(2)}) collective-permute-start(bf16[2064,128]{1,0:T(8,128)(2,1)} %fusion.49), channel_id=1, source_target_pairs={{0,2},{2,4},{4,6},{6,8},{8,10},{10,12},{12,14},{14,16},{16,18},{18... | collective-permute-start | bytes 1585160 | tf_op jit(solution)/shard_map/ppermute | solution.py:43
  89.9 23.7 %copy-start.3 = (f32[16,128,128]{2,1,0:T(8,128)S(1)}, f32[16,128,128]{2,1,0:T(8,128)}, u32[]{:S(2)}) copy-start(f32[16,128,128]{2,1,0:T(8,128)} %copy-done.2) | copy-start | bytes 3145732
  89.9 23.7 %slice-start = ((bf16[2064,128]{1,0:T(8,128)(2,1)}), bf16[2048,128]{1,0:T(8,128)(2,1)S(1)}, s32[]{:S(2)}) async-start(bf16[2064,128]{1,0:T(8,128)(2,1)} %copy-done.4), calls=%async_computation.3 | async-start | bytes 1048576 | tf_op jit(solution)/shard_map/slice | solution.py:28
  118.6 7.6 %copy-start.8 = (f32[2048]{0:T(1024)S(1)}, f32[2048]{0:T(1024)}, u32[]{:S(2)}) copy-start(f32[2048]{0:T(1024)} %param.19) | copy-start | bytes 24580
  126.2 2.0 copy-start.9
  128.2 54.0 %slice-start.1 = ((s8[5767168]{0:T(1024)(128)(4,1)}), s8[4194304]{0:T(1024)(128)(4,1)S(1)}, s32[]{:S(2)}) async-start(s8[5767168]{0:T(1024)(128)(4,1)} %bitcast.153), calls=%async_computation.4 | async-start | bytes 8388608
  174.5 7.7 %slice-start.2 = ((s8[5767168]{0:T(1024)(128)(4,1)}), s8[1572864]{0:T(1024)(128)(4,1)S(1)}, s32[]{:S(2)}) async-start(s8[5767168]{0:T(1024)(128)(4,1)} %bitcast.153), calls=%async_computation.5 | async-start | bytes 3145728
  174.5 13.5 %slice-start.3 = ((s8[5767168]{0:T(1024)(128)(4,1)}), s8[4194304]{0:T(1024)(128)(4,1)S(1)}, s32[]{:S(2)}) async-start(s8[5767168]{0:T(1024)(128)(4,1)} %bitcast.155), calls=%async_computation.6 | async-start | bytes 8388608
  182.2 5.8 %slice-start.4 = ((s8[5767168]{0:T(1024)(128)(4,1)}), s8[1572864]{0:T(1024)(128)(4,1)S(1)}, s32[]{:S(2)}) async-start(s8[5767168]{0:T(1024)(128)(4,1)} %bitcast.155), calls=%async_computation.7 | async-start | bytes 3145728
  194.6 5.0 %copy-start.6 = (f32[32,24]{0,1:T(8,128)S(1)}, f32[32,24]{0,1:T(8,128)}, u32[]{:S(2)}) copy-start(f32[32,24]{0,1:T(8,128)} %param.18) | copy-start | bytes 9220
  194.6 47.0 %copy-start.10 = (bf16[384,2048]{1,0:T(8,128)(2,1)S(1)}, bf16[384,2048]{1,0:T(8,128)(2,1)}, u32[]{:S(2)}) copy-start(bf16[384,2048]{1,0:T(8,128)(2,1)} %copy-done.9) | copy-start | bytes 4718596
  194.6 47.0 %all-to-all-start.1 = ((bf16[32,24,2048]{2,1,0:T(8,128)(2,1)}), bf16[32,24,2048]{2,1,0:T(8,128)(2,1)}, u32[]{:S(2)}, u32[]{:S(2)}) async-start(bf16[32,24,2048]{2,1,0:T(8,128)(2,1)} %fusion.10), calls=%async_computation.1 | async-start | bytes 6291456 | tf_op jit(solution)/shard_map/all_to_all | solution.py:164
  241.6 4.6 %copy-start.1 = (bf16[384,2048]{1,0:T(8,128)(2,1)S(1)}, bf16[384,2048]{1,0:T(8,128)(2,1)}, u32[]{:S(2)}) copy-start(bf16[384,2048]{1,0:T(8,128)(2,1)} %param.12) | copy-start | bytes 4718596
Sparse Core Ops, SparseCore 0:
  34.7 62.5 all-gather.1

commit v15 on v10

--- a/solution.py
+++ b/solution.py
@@ -46,7 +46,7 @@
     reach = 1
     while 2 * reach < count:
         covered = combine(fetch(covered, reach), covered)
-        if reach == 1:
+        if reach == 2:
             covered, rider = lax.optimization_barrier((covered, rider))
         reach *= 2
     if count == 1:

time: 246 us -> 247 us (level)
    all_gather x1, waiting for transfers between devices: 0.02 us -> 7.21 us  [shards(): lax.all_gather(out_weight, SEQ, axis=0, tiled=True)]
    ppermute x5, waiting for transfers between devices: 23.9 us -> 17.5 us  [fetch(): return unpack(lax.ppermute(pack(*pair), axis, pairs), heads)]
  transfers between devices with their start and end apart: 9 -> 9, of which waited for: 7 -> 6; matrix products, arithmetic and copies ran while one was open for 15% -> 12% of each run, Pallas kernels for 0% -> 0%
where the time goes in v15:
time: 247 us; the launch traced here: 246 us
  waiting for transfers between devices  68.4 us (28%)
  matrix products  48.8 us (20%)
  blocking collectives  44.8 us (18%)
  starting transfers between devices  29.6 us (12%)
  other arithmetic  22.6 us (9%)
  local copies, waits for them, and re-layouts  18.2 us (7%)
  between operations  13.8 us (6%)
    all_to_all x1, blocking collectives, shards(): lax.all_to_all(picked[:, window], SEQ, split_axis=0, concat_axis=0, tiled...  44.8 us
    all_to_all x1, waiting for transfers between devices, shards(): lax.all_to_all(produced, SEQ, split_axis=0, concat_axis=0, tiled=True)  41.8 us
    ppermute x5, starting transfers between devices, fetch(): return unpack(lax.ppermute(pack(*pair), axis, pairs), heads)  24.5 us
    ppermute x5, waiting for transfers between devices, fetch(): return unpack(lax.ppermute(pack(*pair), axis, pairs), heads)  17.5 us
    convert_element_type x5, local copies, waits for them, and re-layouts, unpack(): message[:heads * width].reshape(heads, width, width).astype(jnp.float32)  8.13 us
    dot_general x1, matrix products, shards(): jnp.dot(normed, lax.all_gather(out_weight, SEQ, axis=0, tiled=True), pref...  8.03 us
    dot_general x1, matrix products, shards(): jnp.einsum('snd,df->snf', arrived, up_weight[0], preferred_element_type=j...  7.64 us
    all_gather x1, waiting for transfers between devices, shards(): lax.all_gather(out_weight, SEQ, axis=0, tiled=True)  7.21 us
  transfers between devices with their start and end apart: 9, of which 6 were waited for; matrix products, arithmetic and copies ran while one was open for 12% of the time, Pallas kernels for 0%

profile of v15, /device:TPU:0, one launch (start us, length us, event | category | flops | bytes accessed | tf_op | source)
XLA Modules:
  0.0 246.3 jit_solution(9041766453527545706)
XLA Ops:
  6.5 0.9 copy_bitcast_fusion.1
  7.4 0.9 reduce-window.6
  8.3 0.2 slice_reduce_fusion
  8.7 0.1 copy.174
  8.8 0.1 subtract_exponential_fusion
  8.9 2.6 %copy.172 = bf16[384,2048]{0,1:T(8,128)(2,1)} copy(bf16[384,2048]{1,0:T(8,128)(2,1)} %param.13) | data formatting | bytes 3145728 | tf_op jit(solution)/shard_map/reshape | solution.py:103
  11.5 3.5 %fusion.95 = (bf16[16,128,128]{2,1,0:T(8,128)(2,1)S(1)}, f32[16,128,128]{2,1,0:T(8,128)}) fusion(bf16[16,384,128]{1,2,0:T(8,128)(2,1)} %bitcast.144, f32[16,384]{1,0:T(8,128)S(1)} %get-tuple-element.25, bf16[384,2048]{1,0:T(8,128)(2,1)} %param.14), kind=kOutput, calls=%fused_computation.168 | convolution fusion | flops 203948032 | bytes 4743168 | tf_op jit(solution)/shard_map/hsd,hse->hde/dot_general | solution.py:109
  15.1 0.1 collective-permute-start
  15.2 1.9 collective-permute-done
  17.1 0.2 fusion.59
  17.3 0.1 convert.6
  17.4 0.1 broadcast_select_fusion
  17.6 0.1 fusion.92
  17.8 0.8 copy.155
  18.7 1.0 pad_maximum_fusion
  19.7 3.5 %collective-permute-start.1 = (bf16[1032,128]{0,1:T(8,128)(2,1)S(1)}, bf16[1032,128]{0,1:T(8,128)(2,1)S(1)}, u32[]{:S(2)}, u32[]{:S(2)}) collective-permute-start(bf16[1032,128]{0,1:T(8,128)(2,1)S(1)} %pad_maximum_fusion), channel_id=1, source_target_pairs={{0,2},{2,4},{4,6},{6,8},{8,10},{10,12},{12,14},{14,16},{16,18},{18... | collective-permute-start | bytes 792584 | tf_op jit(solution)/shard_map/ppermute | solution.py:43
  23.2 6.5 %collective-permute-done.1 = bf16[1032,128]{0,1:T(8,128)(2,1)S(1)} collective-permute-done((bf16[1032,128]{0,1:T(8,128)(2,1)S(1)}, bf16[1032,128]{0,1:T(8,128)(2,1)S(1)}, u32[]{:S(2)}, u32[]{:S(2)}) %collective-permute-start.1) | collective-permute-done | bytes 264224 | tf_op jit(solution)/shard_map/ppermute | solution.py:43
  29.8 0.7 copy-done.5
  30.5 0.9 slice_convert_fusion.4
  31.3 2.1 copy.156
  33.4 1.2 fusion.38
  34.6 0.8 copy.157
  35.4 0.7 slice_convert_fusion.9
  36.1 1.0 pad_maximum_fusion.1
  37.1 5.9 %collective-permute-start.2 = (bf16[1032,128]{0,1:T(8,128)(2,1)S(1)}, bf16[1032,128]{0,1:T(8,128)(2,1)S(1)}, u32[]{:S(2)}, u32[]{:S(2)}) collective-permute-start(bf16[1032,128]{0,1:T(8,128)(2,1)S(1)} %pad_maximum_fusion.1), channel_id=1, source_target_pairs={{0,4},{2,6},{4,8},{6,10},{8,12},{10,14},{12,16},{14,18},{16,20},{1... | collective-permute-start | bytes 792584 | tf_op jit(solution)/shard_map/ppermute | solution.py:43
  43.0 5.7 %collective-permute-done.2 = bf16[1032,128]{0,1:T(8,128)(2,1)S(1)} collective-permute-done((bf16[1032,128]{0,1:T(8,128)(2,1)S(1)}, bf16[1032,128]{0,1:T(8,128)(2,1)S(1)}, u32[]{:S(2)}, u32[]{:S(2)}) %collective-permute-start.2) | collective-permute-done | bytes 264224 | tf_op jit(solution)/shard_map/ppermute | solution.py:43
  48.7 0.9 slice_convert_fusion.3
  49.6 2.0 copy.158
  51.6 2.2 multiply_add_fusion.1
  53.9 1.1 convert_element_type.208
  55.0 0.9 copy.159
  55.9 1.0 pad_maximum_fusion.2
  56.9 7.5 %collective-permute-start.3 = (bf16[1032,128]{0,1:T(8,128)(2,1)S(1)}, bf16[1032,128]{0,1:T(8,128)(2,1)S(1)}, u32[]{:S(2)}, u32[]{:S(2)}) collective-permute-start(bf16[1032,128]{0,1:T(8,128)(2,1)S(1)} %pad_maximum_fusion.2), channel_id=1, source_target_pairs={{0,8},{2,10},{4,12},{6,14},{8,16},{10,18},{12,20},{14,22},{16,24},... | collective-permute-start | bytes 792584 | tf_op jit(solution)/shard_map/ppermute | solution.py:43
  64.4 0.7 iota_compare_fusion.4
  65.1 5.3 %collective-permute-done.3 = bf16[1032,128]{0,1:T(8,128)(2,1)S(1)} collective-permute-done((bf16[1032,128]{0,1:T(8,128)(2,1)S(1)}, bf16[1032,128]{0,1:T(8,128)(2,1)S(1)}, u32[]{:S(2)}, u32[]{:S(2)}) %collective-permute-start.3) | collective-permute-done | bytes 264224 | tf_op jit(solution)/shard_map/ppermute | solution.py:43
  70.3 0.7 copy-done.4
  71.0 0.8 slice_convert_fusion.2
  71.9 2.0 copy.160
  73.9 1.2 add_convert_fusion.1
  75.1 0.1 copy.161
  75.3 0.7 slice_convert_fusion.7
  76.0 4.4 %collective-permute-start.4 = (bf16[1032,128]{0,1:T(8,128)(2,1)S(1)}, bf16[1032,128]{0,1:T(8,128)(2,1)}, u32[]{:S(2)}, u32[]{:S(2)}) collective-permute-start(bf16[1032,128]{0,1:T(8,128)(2,1)S(1)} %pad_maximum_fusion.3), channel_id=1, source_target_pairs={{0,18},{2,20},{4,22},{6,24},{8,26},{10,28},{12,30},{1,19},{3,21},{... | collective-permute-start | bytes 792584 | tf_op jit(solution)/shard_map/ppermute | solution.py:43
  80.4 3.2 %collective-permute-start.5 = (bf16[1032,128]{0,1:T(8,128)(2,1)S(1)}, bf16[1032,128]{0,1:T(8,128)(2,1)}, u32[]{:S(2)}, u32[]{:S(2)}) collective-permute-start(bf16[1032,128]{0,1:T(8,128)(2,1)S(1)} %pad_maximum_fusion.3), channel_id=1, source_target_pairs={{0,2},{2,4},{4,6},{6,8},{8,10},{10,12},{12,14},{14,16},{16,18},{18... | collective-permute-start | bytes 792584 | tf_op jit(solution)/shard_map/ppermute | solution.py:43
  83.6 6.7 %fusion.6 = f32[16,384,128]{2,1,0:T(8,128)} fusion(f32[16,384]{1,0:T(8,128)S(1)} %copy_bitcast_fusion, pred[384,384]{1,0:T(8,128)(4,1)} %iota_compare_fusion.4, bf16[16,384,128]{1,2,0:T(8,128)(2,1)} %bitcast.145, bf16[384,2048]{1,0:T(8,128)(2,1)S(1)} %copy-done, bf16[384,2048]{1,0:T(8,128)(2,1)} %param.14), kind=kOutput, calls=%fused_computation.10 | convolution fusion | flops 1222115328 | bytes 8036352 | tf_op jit(solution)/shard_map/hts,hsd->htd/dot_general | solution.py:121
  90.3 1.1 slice_convert_fusion.1
  91.4 1.0 copy.162
  92.4 1.0 slice_convert_fusion
  93.4 1.0 copy.163
  94.4 0.6 slice_convert_fusion.6
  95.0 2.0 fusion.89
  97.1 1.8 multiply_convert_fusion.5
  99.2 3.7 %multiply_reduce_fusion = (f32[16,384]{1,0:T(8,128)S(1)}, f32[16,384,128]{2,1,0:T(8,128)S(1)}) fusion(f32[16,384,128]{2,1,0:T(8,128)} %fusion.6, bf16[16,384,128]{2,1,0:T(8,128)(2,1)} %multiply_convert_fusion.5, f32[16,128,128]{2,1,0:T(8,128)S(1)} %broadcast_select_fusion, f32[8,128,128]{2,1,0:T(8,128)S(1)} %get-tuple-element.16, ...), kind=kOutput, calls=%fused_computation.22 | convolution fusion | flops 205514752 | bytes 9986113 | tf_op jit(solution)/shard_map/htd,hde->hte/dot_general | solution.py:128
  102.9 1.0 fusion.20
  103.9 1.6 copy.166
  105.4 7.2 %all-gather.2.cloned.1.call-done = bf16[2048,2048]{1,0:T(8,128)(2,1)} async-done(((bf16[64,2048]{1,0:T(8,128)(2,1)}), bf16[2048,2048]{1,0:T(8,128)(2,1)}) %all-gather.2.cloned.1.call-update) | async-done | bytes 8388624 | tf_op jit(solution)/shard_map/all_gather | solution.py:144
  112.6 8.0 %fusion.15 = (f32[384]{0:T(512)S(1)}, bf16[384,2048]{1,0:T(8,128)(2,1)S(1)}) fusion(bf16[384,2048]{0,1:T(8,128)(2,1)} %bitcast.156, bf16[2048,2048]{1,0:T(8,128)(2,1)} %all-gather.2.cloned.1.call-done, bf16[384,2048]{1,0:T(8,128)(2,1)} %param.15), kind=kOutput, calls=%fused_computation.16 | convolution fusion | flops 3225943552 | bytes 13108736 | tf_op jit(solution)/shard_map/dot_general | solution.py:142
  120.7 1.9 convolution_convert_fusion
  122.6 44.8 %all_to_all.10 = bf16[32,24,2048]{2,1,0:T(8,128)(2,1)S(1)} all-to-all(bf16[32,24,2048]{2,1,0:T(8,128)(2,1)S(1)} %bitcast.150), channel_id=1, replica_groups=mesh['dp'=4,'sy'=4,'sx'=4,'sc'=2] {'sy','sx','sc'}, dimensions={0} | all-to-all | bytes 6291456 | tf_op jit(solution)/shard_map/all_to_all | solution.py:165
  167.4 7.6 %fusion.2 = f32[32,24,1408]{2,1,0:T(8,128)S(1)} fusion(bf16[32,24,2048]{2,1,0:T(8,128)(2,1)S(1)} %all_to_all.10, bf16[1,2048,1408]{2,1,0:T(8,128)(2,1)} %param.22), kind=kOutput, calls=%fused_computation.3 | convolution fusion | flops 4429185024 | bytes 13238272 | tf_op jit(solution)/shard_map/snd,df->snf/dot_general | solution.py:169
  175.1 5.8 %multiply_convert_fusion.2 = bf16[32,24,1408]{2,1,0:T(8,128)(2,1)S(1)} fusion(f32[32,24,1408]{2,1,0:T(8,128)S(1)} %fusion.2, bf16[32,24,2048]{2,1,0:T(8,128)(2,1)S(1)} %all_to_all.10, bf16[1,2048,1408]{2,1,0:T(8,128)(2,1)S(1)} %bitcast.165), kind=kOutput, calls=%fused_computation.12 | convolution fusion | flops 4435673088 | bytes 15400960 | tf_op jit(solution)/shard_map/snd,df->snf/dot_general | solution.py:166
  180.9 6.5 %fusion.10 = bf16[32,24,2048]{2,1,0:T(8,128)(2,1)} fusion(bf16[32,24,1408]{2,1,0:T(8,128)(2,1)S(1)} %multiply_convert_fusion.2, bf16[1,1408,2048]{2,1,0:T(8,128)(2,1)S(1)} %bitcast.167), kind=kOutput, calls=%fused_computation.14 | convolution fusion | flops 4430757888 | bytes 11075584 | tf_op jit(solution)/shard_map/snf,fd->snd/dot_general | solution.py:171
  187.5 4.9 %all-to-all-start.1 = ((bf16[32,24,2048]{2,1,0:T(8,128)(2,1)}), bf16[32,24,2048]{2,1,0:T(8,128)(2,1)}, u32[]{:S(2)}, u32[]{:S(2)}) async-start(bf16[32,24,2048]{2,1,0:T(8,128)(2,1)} %fusion.10), calls=%async_computation.1 | async-start | bytes 6291456 | tf_op jit(solution)/shard_map/all_to_all | solution.py:174
  192.6 41.8 %all-to-all-done.1 = bf16[32,24,2048]{2,1,0:T(8,128)(2,1)} async-done(((bf16[32,24,2048]{2,1,0:T(8,128)(2,1)}), bf16[32,24,2048]{2,1,0:T(8,128)(2,1)}, u32[]{:S(2)}, u32[]{:S(2)}) %all-to-all-start.1) | async-done | bytes 3145760 | tf_op jit(solution)/shard_map/all_to_all | solution.py:174
  234.4 5.0 %fusion.18 = bf16[384,2048]{1,0:T(8,128)(2,1)} fusion(bf16[384,2048]{1,0:T(8,128)(2,1)} %copy-done.9, bf16[768,2048]{1,0:T(8,128)(2,1)} %bitcast.44, f32[768]{0:T(1024)S(1)} %broadcast_in_dim.21, s32[768]{0:T(1024)S(1)} %eq.33), kind=kOutput, calls=%fused_computation.19 | convolution fusion | flops 1211498496 | bytes 6297600 | tf_op jit(solution)/shard_map/dot_general | solution.py:179
  (68 shorter events, 1.2 us)
Async XLA Ops:
  6.5 77.1 %copy-start = (bf16[384,2048]{1,0:T(8,128)(2,1)S(1)}, bf16[384,2048]{1,0:T(8,128)(2,1)}, u32[]{:S(2)}) copy-start(bf16[384,2048]{1,0:T(8,128)(2,1)} %param.12) | copy-start | bytes 4718596
  6.5 106.1 %all-gather.2.cloned.1.call-start = ((), (), s32[]{:S(2)}) async-start(), calls=%async_computation.2 | async-start | bytes 8650752 | tf_op jit(solution)/shard_map/all_gather | solution.py:144
  15.1 2.0 collective-permute-start
  15.2 2.3 copy-start.2
  19.7 10.1 %collective-permute-start.1 = (bf16[1032,128]{0,1:T(8,128)(2,1)S(1)}, bf16[1032,128]{0,1:T(8,128)(2,1)S(1)}, u32[]{:S(2)}, u32[]{:S(2)}) collective-permute-start(bf16[1032,128]{0,1:T(8,128)(2,1)S(1)} %pad_maximum_fusion), channel_id=1, source_target_pairs={{0,2},{2,4},{4,6},{6,8},{8,10},{10,12},{12,14},{14,16},{16,18},{18... | collective-permute-start | bytes 792584 | tf_op jit(solution)/shard_map/ppermute | solution.py:43
  29.8 0.7 copy-start.5
  37.1 11.6 %collective-permute-start.2 = (bf16[1032,128]{0,1:T(8,128)(2,1)S(1)}, bf16[1032,128]{0,1:T(8,128)(2,1)S(1)}, u32[]{:S(2)}, u32[]{:S(2)}) collective-permute-start(bf16[1032,128]{0,1:T(8,128)(2,1)S(1)} %pad_maximum_fusion.1), channel_id=1, source_target_pairs={{0,4},{2,6},{4,8},{6,10},{8,12},{10,14},{12,16},{14,18},{16,20},{1... | collective-permute-start | bytes 792584 | tf_op jit(solution)/shard_map/ppermute | solution.py:43
  53.9 20.1 %copy-start.3 = (f32[8,128,128]{2,1,0:T(8,128)S(1)}, f32[8,128,128]{2,1,0:T(8,128)}, u32[]{:S(2)}) copy-start(f32[8,128,128]{2,1,0:T(8,128)} %multiply_add_fusion.1) | copy-start | bytes 1572868
  56.9 13.4 %collective-permute-start.3 = (bf16[1032,128]{0,1:T(8,128)(2,1)S(1)}, bf16[1032,128]{0,1:T(8,128)(2,1)S(1)}, u32[]{:S(2)}, u32[]{:S(2)}) collective-permute-start(bf16[1032,128]{0,1:T(8,128)(2,1)S(1)} %pad_maximum_fusion.2), channel_id=1, source_target_pairs={{0,8},{2,10},{4,12},{6,14},{8,16},{10,18},{12,20},{14,22},{16,24},... | collective-permute-start | bytes 792584 | tf_op jit(solution)/shard_map/ppermute | solution.py:43
  70.3 0.7 copy-start.4
  76.0 14.3 %collective-permute-start.4 = (bf16[1032,128]{0,1:T(8,128)(2,1)S(1)}, bf16[1032,128]{0,1:T(8,128)(2,1)}, u32[]{:S(2)}, u32[]{:S(2)}) collective-permute-start(bf16[1032,128]{0,1:T(8,128)(2,1)S(1)} %pad_maximum_fusion.3), channel_id=1, source_target_pairs={{0,18},{2,20},{4,22},{6,24},{8,26},{10,28},{12,30},{1,19},{3,21},{... | collective-permute-start | bytes 792584 | tf_op jit(solution)/shard_map/ppermute | solution.py:43
  80.4 12.0 %collective-permute-start.5 = (bf16[1032,128]{0,1:T(8,128)(2,1)S(1)}, bf16[1032,128]{0,1:T(8,128)(2,1)}, u32[]{:S(2)}, u32[]{:S(2)}) collective-permute-start(bf16[1032,128]{0,1:T(8,128)(2,1)S(1)} %pad_maximum_fusion.3), channel_id=1, source_target_pairs={{0,2},{2,4},{4,6},{6,8},{8,10},{10,12},{12,14},{14,16},{16,18},{18... | collective-permute-start | bytes 792584 | tf_op jit(solution)/shard_map/ppermute | solution.py:43
  93.4 5.5 %copy-start.7 = (s32[32,24]{0,1:T(8,128)S(1)}, s32[32,24]{0,1:T(8,128)}, u32[]{:S(2)}) copy-start(s32[32,24]{0,1:T(8,128)} %param.17) | copy-start | bytes 9220
  97.1 2.0 collective-permute-start.6
  112.6 8.1 %copy-start.8 = (f32[2048]{0:T(1024)S(1)}, f32[2048]{0:T(1024)}, u32[]{:S(2)}) copy-start(f32[2048]{0:T(1024)} %param.19) | copy-start | bytes 24580
  120.7 2.0 copy-start.9
  122.6 52.5 %slice-start = ((s8[5767168]{0:T(1024)(128)(4,1)}), s8[4194304]{0:T(1024)(128)(4,1)S(1)}, s32[]{:S(2)}) async-start(s8[5767168]{0:T(1024)(128)(4,1)} %bitcast.164), calls=%async_computation.3 | async-start | bytes 8388608
  167.4 7.7 %slice-start.1 = ((s8[5767168]{0:T(1024)(128)(4,1)}), s8[1572864]{0:T(1024)(128)(4,1)S(1)}, s32[]{:S(2)}) async-start(s8[5767168]{0:T(1024)(128)(4,1)} %bitcast.164), calls=%async_computation.4 | async-start | bytes 3145728
  167.4 13.5 %slice-start.2 = ((s8[5767168]{0:T(1024)(128)(4,1)}), s8[4194304]{0:T(1024)(128)(4,1)S(1)}, s32[]{:S(2)}) async-start(s8[5767168]{0:T(1024)(128)(4,1)} %bitcast.166), calls=%async_computation.5 | async-start | bytes 8388608
  175.1 5.8 %slice-start.3 = ((s8[5767168]{0:T(1024)(128)(4,1)}), s8[1572864]{0:T(1024)(128)(4,1)S(1)}, s32[]{:S(2)}) async-start(s8[5767168]{0:T(1024)(128)(4,1)} %bitcast.166), calls=%async_computation.6 | async-start | bytes 3145728
  187.5 5.0 %copy-start.6 = (f32[32,24]{0,1:T(8,128)S(1)}, f32[32,24]{0,1:T(8,128)}, u32[]{:S(2)}) copy-start(f32[32,24]{0,1:T(8,128)} %param.18) | copy-start | bytes 9220
  187.5 47.0 %all-to-all-start.1 = ((bf16[32,24,2048]{2,1,0:T(8,128)(2,1)}), bf16[32,24,2048]{2,1,0:T(8,128)(2,1)}, u32[]{:S(2)}, u32[]{:S(2)}) async-start(bf16[32,24,2048]{2,1,0:T(8,128)(2,1)} %fusion.10), calls=%async_computation.1 | async-start | bytes 6291456 | tf_op jit(solution)/shard_map/all_to_all | solution.py:174
  234.4 5.0 %copy-start.1 = (bf16[384,2048]{1,0:T(8,128)(2,1)S(1)}, bf16[384,2048]{1,0:T(8,128)(2,1)}, u32[]{:S(2)}) copy-start(bf16[384,2048]{1,0:T(8,128)(2,1)} %param.12) | copy-start | bytes 4718596
Sparse Core Ops, SparseCore 0:
  54.0 58.5 all-gather.1

commit v16 on v10

--- a/solution.py
+++ b/solution.py
@@ -172,14 +172,16 @@
             "snf,fd->snd", activated, down_weight[0], preferred_element_type=jnp.float32
         ).astype(jnp.bfloat16)
         returned = lax.all_to_all(produced, SEQ, split_axis=0, concat_axis=0, tiled=True)
-        flat_returned = returned.reshape(-1, model_width)
         remaining = spread_weight[:, :, window].reshape(length, -1)
+        pieces = []
         for _ in range(SCATTER_PIECES):
             part = lax.reduce_precision(remaining, exponent_bits=8, mantissa_bits=7)
-            total = total + jnp.dot(
-                part.astype(jnp.bfloat16), flat_returned, preferred_element_type=jnp.float32
-            )
+            pieces.append(part.astype(jnp.bfloat16))
             remaining = remaining - part
+        pieces, returned = lax.optimization_barrier((pieces, returned))
+        flat_returned = returned.reshape(-1, model_width)
+        for part in pieces:
+            total = total + jnp.dot(part, flat_returned, preferred_element_type=jnp.float32)
     return total.astype(jnp.bfloat16)
 
 

time: 246 us -> 246 us (level)
  no operation moved by 1% of the time
where the time goes in v16:
time: 246 us; the launch traced here: 245 us
  waiting for transfers between devices  67.9 us (28%)
  matrix products  48.4 us (20%)
  blocking collectives  46.5 us (19%)
  starting transfers between devices  30.8 us (13%)
  other arithmetic  21.5 us (9%)
  local copies, waits for them, and re-layouts  16.4 us (7%)
  between operations  13.8 us (6%)
    all_to_all x1, blocking collectives, shards(): lax.all_to_all(picked[:, window], SEQ, split_axis=0, concat_axis=0, tiled...  46.5 us
    all_to_all x1, waiting for transfers between devices, shards(): lax.all_to_all(produced, SEQ, split_axis=0, concat_axis=0, tiled=True)  41.6 us
    ppermute x5, starting transfers between devices, fetch(): return unpack(lax.ppermute(pack(*pair), axis, pairs), heads)  25.8 us
    ppermute x5, waiting for transfers between devices, fetch(): return unpack(lax.ppermute(pack(*pair), axis, pairs), heads)  23.9 us
    dot_general x1, matrix products, shards(): jnp.einsum('snd,df->snf', arrived, up_weight[0], preferred_element_type=j...  7.65 us
    dot_general x1, matrix products, shards(): jnp.dot(normed, lax.all_gather(out_weight, SEQ, axis=0, tiled=True), pref...  7.59 us
    convert_element_type x5, local copies, waits for them, and re-layouts, unpack(): message[:heads * width].reshape(heads, width, width).astype(jnp.float32)  7.31 us
    dot_general x1, matrix products, shards(): jnp.einsum('hts,hsd->htd', attend_weights, value_heads, preferred_element...  6.76 us
  transfers between devices with their start and end apart: 9, of which 7 were waited for; matrix products, arithmetic and copies ran while one was open for 15% of the time, Pallas kernels for 0%

profile of v16, /device:TPU:0, one launch (start us, length us, event | category | flops | bytes accessed | tf_op | source)
XLA Modules:
  0.0 245.2 jit_solution(4677539583566830225)
XLA Ops:
  6.5 0.9 copy_bitcast_fusion.1
  7.4 0.9 reduce-window.6
  8.3 0.2 slice_reduce_fusion
  8.7 0.1 copy.174
  8.9 1.9 copy.172
  10.8 3.6 %fusion.91 = (bf16[16,128,128]{2,1,0:T(8,128)(2,1)S(1)}, f32[16,128,128]{2,1,0:T(8,128)}) fusion(bf16[16,384,128]{1,2,0:T(8,128)(2,1)S(1)} %bitcast.145, f32[16,384]{1,0:T(8,128)S(1)} %get-tuple-element.29, bf16[384,2048]{1,0:T(8,128)(2,1)} %param.14), kind=kOutput, calls=%fused_computation.164 | convolution fusion | flops 203948032 | bytes 4743168 | tf_op jit(solution)/shard_map/hsd,hse->hde/dot_general | solution.py:109
  14.4 0.8 fusion.31
  15.3 2.3 collective-permute-done
  17.5 0.7 slice_convert_fusion.5
  18.2 0.2 fusion.56
  18.4 1.1 slice.121
  19.5 0.1 convert.6
  19.6 0.1 broadcast_select_fusion
  19.8 1.0 fusion.88
  20.8 0.1 copy.155
  21.1 3.5 %collective-permute-start.1 = (bf16[1032,128]{0,1:T(8,128)(2,1)S(1)}, bf16[1032,128]{0,1:T(8,128)(2,1)S(1)}, u32[]{:S(2)}, u32[]{:S(2)}) collective-permute-start(bf16[1032,128]{0,1:T(8,128)(2,1)S(1)} %pad_maximum_fusion), channel_id=1, source_target_pairs={{0,2},{2,4},{4,6},{6,8},{8,10},{10,12},{12,14},{14,16},{16,18},{18... | collective-permute-start | bytes 792584 | tf_op jit(solution)/shard_map/ppermute | solution.py:43
  24.6 6.5 %collective-permute-done.1 = bf16[1032,128]{0,1:T(8,128)(2,1)S(1)} collective-permute-done((bf16[1032,128]{0,1:T(8,128)(2,1)S(1)}, bf16[1032,128]{0,1:T(8,128)(2,1)S(1)}, u32[]{:S(2)}, u32[]{:S(2)}) %collective-permute-start.1) | collective-permute-done | bytes 264224 | tf_op jit(solution)/shard_map/ppermute | solution.py:43
  31.2 1.0 copy.156
  32.2 1.3 multiply_add_fusion.2
  33.6 0.9 copy.157
  34.5 1.0 pad_maximum_fusion.1
  35.5 5.9 %collective-permute-start.2 = (bf16[1032,128]{0,1:T(8,128)(2,1)S(1)}, bf16[1032,128]{0,1:T(8,128)(2,1)S(1)}, u32[]{:S(2)}, u32[]{:S(2)}) collective-permute-start(bf16[1032,128]{0,1:T(8,128)(2,1)S(1)} %pad_maximum_fusion.1), channel_id=1, source_target_pairs={{0,4},{2,6},{4,8},{6,10},{8,12},{10,14},{12,16},{14,18},{16,20},{1... | collective-permute-start | bytes 792584 | tf_op jit(solution)/shard_map/ppermute | solution.py:43
  41.4 5.7 %collective-permute-done.2 = bf16[1032,128]{0,1:T(8,128)(2,1)S(1)} collective-permute-done((bf16[1032,128]{0,1:T(8,128)(2,1)S(1)}, bf16[1032,128]{0,1:T(8,128)(2,1)S(1)}, u32[]{:S(2)}, u32[]{:S(2)}) %collective-permute-start.2) | collective-permute-done | bytes 264224 | tf_op jit(solution)/shard_map/ppermute | solution.py:43
  47.1 0.7 copy-done.5
  47.8 0.9 slice_convert_fusion.3
  48.7 2.1 copy.158
  50.8 1.2 fusion.35
  52.0 0.9 copy.159
  52.8 0.7 slice_convert_fusion.8
  53.5 1.0 pad_maximum_fusion.2
  54.5 7.6 %collective-permute-start.3 = (bf16[1032,128]{0,1:T(8,128)(2,1)S(1)}, bf16[1032,128]{0,1:T(8,128)(2,1)S(1)}, u32[]{:S(2)}, u32[]{:S(2)}) collective-permute-start(bf16[1032,128]{0,1:T(8,128)(2,1)S(1)} %pad_maximum_fusion.2), channel_id=1, source_target_pairs={{0,8},{2,10},{4,12},{6,14},{8,16},{10,18},{12,20},{14,22},{16,24},... | collective-permute-start | bytes 792584 | tf_op jit(solution)/shard_map/ppermute | solution.py:43
  62.1 0.7 iota_compare_fusion.4
  62.8 4.0 %collective-permute-done.3 = bf16[1032,128]{0,1:T(8,128)(2,1)S(1)} collective-permute-done((bf16[1032,128]{0,1:T(8,128)(2,1)S(1)}, bf16[1032,128]{0,1:T(8,128)(2,1)S(1)}, u32[]{:S(2)}, u32[]{:S(2)}) %collective-permute-start.3) | collective-permute-done | bytes 264224 | tf_op jit(solution)/shard_map/ppermute | solution.py:43
  66.8 0.7 copy-done.4
  67.6 0.8 slice_convert_fusion.2
  68.4 2.2 copy.160
  70.6 1.4 add_convert_fusion.1
  72.0 0.1 copy.161
  72.1 0.7 slice_convert_fusion.7
  72.9 5.4 %collective-permute-start.4 = (bf16[1032,128]{0,1:T(8,128)(2,1)S(1)}, bf16[1032,128]{0,1:T(8,128)(2,1)}, u32[]{:S(2)}, u32[]{:S(2)}) collective-permute-start(bf16[1032,128]{0,1:T(8,128)(2,1)S(1)} %pad_maximum_fusion.3), channel_id=1, source_target_pairs={{0,18},{2,20},{4,22},{6,24},{8,26},{10,28},{12,30},{1,19},{3,21},{... | collective-permute-start | bytes 792584 | tf_op jit(solution)/shard_map/ppermute | solution.py:43
  78.3 3.3 %collective-permute-start.5 = (bf16[1032,128]{0,1:T(8,128)(2,1)S(1)}, bf16[1032,128]{0,1:T(8,128)(2,1)}, u32[]{:S(2)}, u32[]{:S(2)}) collective-permute-start(bf16[1032,128]{0,1:T(8,128)(2,1)S(1)} %pad_maximum_fusion.3), channel_id=1, source_target_pairs={{0,2},{2,4},{4,6},{6,8},{8,10},{10,12},{12,14},{14,16},{16,18},{18... | collective-permute-start | bytes 792584 | tf_op jit(solution)/shard_map/ppermute | solution.py:43
  81.6 6.8 %fusion.6 = f32[16,384,128]{2,1,0:T(8,128)} fusion(f32[16,384]{1,0:T(8,128)S(1)} %copy_bitcast_fusion, pred[384,384]{1,0:T(8,128)(4,1)} %iota_compare_fusion.4, bf16[16,384,128]{1,2,0:T(8,128)(2,1)} %bitcast.146, bf16[384,2048]{1,0:T(8,128)(2,1)S(1)} %copy-done, bf16[384,2048]{1,0:T(8,128)(2,1)} %param.14), kind=kOutput, calls=%fused_computation.10 | convolution fusion | flops 1222115328 | bytes 8036352 | tf_op jit(solution)/shard_map/hts,hsd->htd/dot_general | solution.py:121
  88.4 2.9 %collective-permute-done.4 = bf16[1032,128]{0,1:T(8,128)(2,1)} collective-permute-done((bf16[1032,128]{0,1:T(8,128)(2,1)S(1)}, bf16[1032,128]{0,1:T(8,128)(2,1)}, u32[]{:S(2)}, u32[]{:S(2)}) %collective-permute-start.4) | collective-permute-done | bytes 264224 | tf_op jit(solution)/shard_map/ppermute | solution.py:43
  91.2 1.0 slice_convert_fusion.1
  92.2 1.0 copy.162
  93.2 4.9 %collective-permute-done.5 = bf16[1032,128]{0,1:T(8,128)(2,1)} collective-permute-done((bf16[1032,128]{0,1:T(8,128)(2,1)S(1)}, bf16[1032,128]{0,1:T(8,128)(2,1)}, u32[]{:S(2)}, u32[]{:S(2)}) %collective-permute-start.5) | collective-permute-done | bytes 264224 | tf_op jit(solution)/shard_map/ppermute | solution.py:43
  98.1 1.0 slice_convert_fusion
  99.1 1.0 copy.163
  100.1 0.6 slice_convert_fusion.6
  100.7 2.0 fusion.85
  102.8 1.8 multiply_convert_fusion.5
  104.8 3.5 %multiply_reduce_fusion = (f32[16,384]{1,0:T(8,128)S(1)}, f32[16,384,128]{2,1,0:T(8,128)S(1)}) fusion(f32[16,384,128]{2,1,0:T(8,128)} %fusion.6, bf16[16,384,128]{2,1,0:T(8,128)(2,1)} %multiply_convert_fusion.5, f32[16,128,128]{2,1,0:T(8,128)S(1)} %broadcast_select_fusion, f32[8,128,128]{2,1,0:T(8,128)S(1)} %get-tuple-element.20, ...), kind=kOutput, calls=%fused_computation.22 | convolution fusion | flops 205514752 | bytes 9986113 | tf_op jit(solution)/shard_map/htd,hde->hte/dot_general | solution.py:128
  108.4 1.0 fusion.20
  109.4 0.9 copy.166
  110.3 7.6 %fusion.15 = (f32[384]{0:T(512)S(1)}, bf16[384,2048]{1,0:T(8,128)(2,1)S(1)}) fusion(bf16[384,2048]{0,1:T(8,128)(2,1)S(1)} %bitcast.157, bf16[2048,2048]{1,0:T(8,128)(2,1)} %all-gather.2.cloned.1.call-done, bf16[384,2048]{1,0:T(8,128)(2,1)} %param.15), kind=kOutput, calls=%fused_computation.16 | convolution fusion | flops 3225943552 | bytes 13108736 | tf_op jit(solution)/shard_map/dot_general | solution.py:142
  117.9 1.9 convolution_convert_fusion
  119.9 46.5 %all_to_all.10 = bf16[32,24,2048]{2,1,0:T(8,128)(2,1)S(1)} all-to-all(bf16[32,24,2048]{2,1,0:T(8,128)(2,1)S(1)} %bitcast.151), channel_id=1, replica_groups=mesh['dp'=4,'sy'=4,'sx'=4,'sc'=2] {'sy','sx','sc'}, dimensions={0} | all-to-all | bytes 6291456 | tf_op jit(solution)/shard_map/all_to_all | solution.py:165
  166.4 7.6 %fusion.2 = f32[32,24,1408]{2,1,0:T(8,128)S(1)} fusion(bf16[32,24,2048]{2,1,0:T(8,128)(2,1)S(1)} %all_to_all.10, bf16[1,2048,1408]{2,1,0:T(8,128)(2,1)} %param.22), kind=kOutput, calls=%fused_computation.3 | convolution fusion | flops 4429185024 | bytes 13238272 | tf_op jit(solution)/shard_map/snd,df->snf/dot_general | solution.py:169
  174.1 5.8 %multiply_convert_fusion.2 = bf16[32,24,1408]{2,1,0:T(8,128)(2,1)S(1)} fusion(f32[32,24,1408]{2,1,0:T(8,128)S(1)} %fusion.2, bf16[32,24,2048]{2,1,0:T(8,128)(2,1)S(1)} %all_to_all.10, bf16[1,2048,1408]{2,1,0:T(8,128)(2,1)S(1)} %bitcast.166), kind=kOutput, calls=%fused_computation.12 | convolution fusion | flops 4435673088 | bytes 15400960 | tf_op jit(solution)/shard_map/snd,df->snf/dot_general | solution.py:166
  179.9 6.5 %fusion.10 = bf16[32,24,2048]{2,1,0:T(8,128)(2,1)} fusion(bf16[32,24,1408]{2,1,0:T(8,128)(2,1)S(1)} %multiply_convert_fusion.2, bf16[1,1408,2048]{2,1,0:T(8,128)(2,1)S(1)} %bitcast.168), kind=kOutput, calls=%fused_computation.14 | convolution fusion | flops 4430757888 | bytes 11075584 | tf_op jit(solution)/shard_map/snf,fd->snd/dot_general | solution.py:171
  186.4 4.9 %all-to-all-start.1 = ((bf16[32,24,2048]{2,1,0:T(8,128)(2,1)}), bf16[32,24,2048]{2,1,0:T(8,128)(2,1)}, u32[]{:S(2)}, u32[]{:S(2)}) async-start(bf16[32,24,2048]{2,1,0:T(8,128)(2,1)} %fusion.10), calls=%async_computation.1 | async-start | bytes 6291456 | tf_op jit(solution)/shard_map/all_to_all | solution.py:174
  191.6 0.2 reduce-precision_convert_fusion
  191.7 41.6 %all-to-all-done.1 = bf16[32,24,2048]{2,1,0:T(8,128)(2,1)} async-done(((bf16[32,24,2048]{2,1,0:T(8,128)(2,1)}), bf16[32,24,2048]{2,1,0:T(8,128)(2,1)}, u32[]{:S(2)}, u32[]{:S(2)}) %all-to-all-start.1) | async-done | bytes 3145760 | tf_op jit(solution)/shard_map/all_to_all | solution.py:174
  233.4 5.0 %fusion.18 = bf16[384,2048]{1,0:T(8,128)(2,1)} fusion(bf16[384,2048]{1,0:T(8,128)(2,1)} %copy-done.9, bf16[384,768]{1,0:T(8,128)(2,1)S(1)} %reduce-precision_convert_fusion, bf16[768,2048]{1,0:T(8,128)(2,1)} %bitcast.44), kind=kOutput, calls=%fused_computation.19 | convolution fusion | flops 1210318848 | bytes 6881280 | tf_op jit(solution)/shard_map/dot_general | solution.py:184
  (69 shorter events, 1.3 us)
Async XLA Ops:
  6.5 75.1 %copy-start = (bf16[384,2048]{1,0:T(8,128)(2,1)S(1)}, bf16[384,2048]{1,0:T(8,128)(2,1)}, u32[]{:S(2)}) copy-start(bf16[384,2048]{1,0:T(8,128)(2,1)} %param.12) | copy-start | bytes 4718596
  6.5 103.7 %all-gather.2.cloned.1.call-start = ((), (), s32[]{:S(2)}) async-start(), calls=%async_computation.2 | async-start | bytes 8650752 | tf_op jit(solution)/shard_map/all_gather | solution.py:144
  10.8 8.7 %copy-start.3 = (bf16[384,2048]{0,1:T(8,128)(2,1)}, bf16[384,2048]{0,1:T(8,128)(2,1)S(1)}, u32[]{:S(2)}) copy-start(bf16[384,2048]{0,1:T(8,128)(2,1)S(1)} %copy.172) | copy-start | bytes 4718596
  15.3 2.3 collective-permute-start
  15.3 4.3 %copy-start.2 = (f32[16,128,128]{2,1,0:T(8,128)S(1)}, f32[16,128,128]{2,1,0:T(8,128)}, u32[]{:S(2)}) copy-start(f32[16,128,128]{2,1,0:T(8,128)} %get-tuple-element.50) | copy-start | bytes 3145732
  21.1 10.1 %collective-permute-start.1 = (bf16[1032,128]{0,1:T(8,128)(2,1)S(1)}, bf16[1032,128]{0,1:T(8,128)(2,1)S(1)}, u32[]{:S(2)}, u32[]{:S(2)}) collective-permute-start(bf16[1032,128]{0,1:T(8,128)(2,1)S(1)} %pad_maximum_fusion), channel_id=1, source_target_pairs={{0,2},{2,4},{4,6},{6,8},{8,10},{10,12},{12,14},{14,16},{16,18},{18... | collective-permute-start | bytes 792584 | tf_op jit(solution)/shard_map/ppermute | solution.py:43
  35.5 11.6 %collective-permute-start.2 = (bf16[1032,128]{0,1:T(8,128)(2,1)S(1)}, bf16[1032,128]{0,1:T(8,128)(2,1)S(1)}, u32[]{:S(2)}, u32[]{:S(2)}) collective-permute-start(bf16[1032,128]{0,1:T(8,128)(2,1)S(1)} %pad_maximum_fusion.1), channel_id=1, source_target_pairs={{0,4},{2,6},{4,8},{6,10},{8,12},{10,14},{12,16},{14,18},{16,20},{1... | collective-permute-start | bytes 792584 | tf_op jit(solution)/shard_map/ppermute | solution.py:43
  47.1 0.7 copy-start.5
  54.5 12.3 %collective-permute-start.3 = (bf16[1032,128]{0,1:T(8,128)(2,1)S(1)}, bf16[1032,128]{0,1:T(8,128)(2,1)S(1)}, u32[]{:S(2)}, u32[]{:S(2)}) collective-permute-start(bf16[1032,128]{0,1:T(8,128)(2,1)S(1)} %pad_maximum_fusion.2), channel_id=1, source_target_pairs={{0,8},{2,10},{4,12},{6,14},{8,16},{10,18},{12,20},{14,22},{16,24},... | collective-permute-start | bytes 792584 | tf_op jit(solution)/shard_map/ppermute | solution.py:43
  66.8 0.7 copy-start.4
  72.9 18.4 %collective-permute-start.4 = (bf16[1032,128]{0,1:T(8,128)(2,1)S(1)}, bf16[1032,128]{0,1:T(8,128)(2,1)}, u32[]{:S(2)}, u32[]{:S(2)}) collective-permute-start(bf16[1032,128]{0,1:T(8,128)(2,1)S(1)} %pad_maximum_fusion.3), channel_id=1, source_target_pairs={{0,18},{2,20},{4,22},{6,24},{8,26},{10,28},{12,30},{1,19},{3,21},{... | collective-permute-start | bytes 792584 | tf_op jit(solution)/shard_map/ppermute | solution.py:43
  78.3 19.8 %collective-permute-start.5 = (bf16[1032,128]{0,1:T(8,128)(2,1)S(1)}, bf16[1032,128]{0,1:T(8,128)(2,1)}, u32[]{:S(2)}, u32[]{:S(2)}) collective-permute-start(bf16[1032,128]{0,1:T(8,128)(2,1)S(1)} %pad_maximum_fusion.3), channel_id=1, source_target_pairs={{0,2},{2,4},{4,6},{6,8},{8,10},{10,12},{12,14},{14,16},{16,18},{18... | collective-permute-start | bytes 792584 | tf_op jit(solution)/shard_map/ppermute | solution.py:43
  99.1 5.5 %copy-start.7 = (s32[32,24]{0,1:T(8,128)S(1)}, s32[32,24]{0,1:T(8,128)}, u32[]{:S(2)}) copy-start(s32[32,24]{0,1:T(8,128)} %param.17) | copy-start | bytes 9220
  102.8 2.0 collective-permute-start.6
  110.3 7.6 %copy-start.8 = (f32[2048]{0:T(1024)S(1)}, f32[2048]{0:T(1024)}, u32[]{:S(2)}) copy-start(f32[2048]{0:T(1024)} %param.19) | copy-start | bytes 24580
  117.9 2.0 copy-start.9
  119.8 54.2 %slice-start = ((s8[5767168]{0:T(1024)(128)(4,1)}), s8[4194304]{0:T(1024)(128)(4,1)S(1)}, s32[]{:S(2)}) async-start(s8[5767168]{0:T(1024)(128)(4,1)} %bitcast.165), calls=%async_computation.3 | async-start | bytes 8388608
  166.4 7.7 %slice-start.1 = ((s8[5767168]{0:T(1024)(128)(4,1)}), s8[1572864]{0:T(1024)(128)(4,1)S(1)}, s32[]{:S(2)}) async-start(s8[5767168]{0:T(1024)(128)(4,1)} %bitcast.165), calls=%async_computation.4 | async-start | bytes 3145728
  166.4 13.5 %slice-start.2 = ((s8[5767168]{0:T(1024)(128)(4,1)}), s8[4194304]{0:T(1024)(128)(4,1)S(1)}, s32[]{:S(2)}) async-start(s8[5767168]{0:T(1024)(128)(4,1)} %bitcast.167), calls=%async_computation.5 | async-start | bytes 8388608
  174.1 5.8 %slice-start.3 = ((s8[5767168]{0:T(1024)(128)(4,1)}), s8[1572864]{0:T(1024)(128)(4,1)S(1)}, s32[]{:S(2)}) async-start(s8[5767168]{0:T(1024)(128)(4,1)} %bitcast.167), calls=%async_computation.6 | async-start | bytes 3145728
  186.4 5.0 %copy-start.6 = (f32[32,24]{0,1:T(8,128)S(1)}, f32[32,24]{0,1:T(8,128)}, u32[]{:S(2)}) copy-start(f32[32,24]{0,1:T(8,128)} %param.18) | copy-start | bytes 9220
  186.4 47.0 %all-to-all-start.1 = ((bf16[32,24,2048]{2,1,0:T(8,128)(2,1)}), bf16[32,24,2048]{2,1,0:T(8,128)(2,1)}, u32[]{:S(2)}, u32[]{:S(2)}) async-start(bf16[32,24,2048]{2,1,0:T(8,128)(2,1)} %fusion.10), calls=%async_computation.1 | async-start | bytes 6291456 | tf_op jit(solution)/shard_map/all_to_all | solution.py:174
  233.4 5.0 %copy-start.1 = (bf16[384,2048]{1,0:T(8,128)(2,1)S(1)}, bf16[384,2048]{1,0:T(8,128)(2,1)}, u32[]{:S(2)}) copy-start(bf16[384,2048]{1,0:T(8,128)(2,1)} %param.12) | copy-start | bytes 4718596
Sparse Core Ops, SparseCore 0:
  33.7 65.3 all-gather.1
